TPU v7x, 32 devices: a whole 2x2x4 slice. The times are simulated.
32 devices in a mesh: tile: 8 (over z, x), pred: 4 (over y, core).
Axes of the slice: x: 2, y: 2, z: 4, core: 2. Of those that a mesh axis runs over, the one named last changes fastest.
Arguments:
- covariates: bfloat16 [64, 1024, 8192], P('pred', 'tile'), may hold values from -1.5 to 1.5
- target: float32 [1024, 8192], P('tile'), may hold values from -6 to 6
- land: int32 [1024, 8192], P('tile'), may hold values 0 or 1
- coefs: float32 [64, 64, 512], P('pred', 'tile'), may hold values from -6 to 6
- first_moment: float32 [64, 64, 512], P('pred', 'tile'), may hold values from -3 to 3
- second_moment: float32 [64, 64, 512], P('pred', 'tile'), may hold values from 0.05 to 1
- smoothing: float32 [64], P('pred'), may hold values from 0.01 to 0.1
Outputs:
- fitted: float32 [1024, 8192], P(('tile', 'pred'))
- residual: float32 [1024, 8192], P(('tile', 'pred'))
- gradient: float32 [64, 64, 512], P('pred', 'tile')
- new_coefs: float32 [64, 64, 512], P('pred', 'tile')
- new_first: float32 [64, 64, 512], P('pred', 'tile')
- new_second: float32 [64, 64, 512], P('pred', 'tile')
Inputs may be any that keep to these rules, and one draw needn't show every extreme that they name: land is 1 on land cells and 0 elsewhere.
All inputs are finite; a program needn't handle non-finite values. No bound on the sum of `land` on one device may be relied on, other than what follows from the above.
Results may differ from a plain program's by a relative error of at most 0.0003.
Values sent between devices are 32-bit elements; how exact they have to be, the bound alone decides.
No kernel may reach another device: no remote copies, remote signals or barrier semaphores. Data moves between devices by JAX's collectives and lax.ppermute only.
A program may use at most 128 MiB of HBM per device.

v0:
```python
import jax
import jax.numpy as jnp
from jax import lax
from jax.experimental import pallas as pl
from jax.experimental.pallas import tpu as pltpu
from jax.sharding import PartitionSpec as P

H = 16
TN = 512
L = 256
CHUNKS = 4
LEAD = 8


def extended(array, sides, width):
    for axis, dim in sides:
        peers, length = (lax.axis_size(axis), array.shape[dim])
        up = [(i, (i + 1) % peers) for i in range(peers - 1)]
        down = [(j, i) for i, j in up]
        last = lax.slice_in_dim(array, length - width, length, axis=dim)
        first = lax.slice_in_dim(array, 0, width, axis=dim)
        before = lax.ppermute(last, axis, up)
        after = lax.ppermute(first, axis, down)
        array = jnp.concatenate([before, array, after], axis=dim)
    return array


def from_behind(block, axis, distance):
    devices = range(lax.axis_size(axis))
    route = [(i - distance, i) for i in devices if i - distance in devices]
    return lax.ppermute(block, axis, route)


def weights_of(u):
    return [
        (1.0 - u) * (1.0 - u) * (1.0 - u) / 6.0,
        (3.0 * u * u * u - 6.0 * u * u + 4.0) / 6.0,
        (-3.0 * u * u * u + 3.0 * u * u + 3.0 * u + 1.0) / 6.0,
        u * u * u / 6.0,
    ]


def weight_table(spacing):
    u = (jnp.arange(spacing, dtype=jnp.float32) + 0.5) / spacing
    return jnp.stack(weights_of(u))


def block_basis(window):
    n = jnp.arange(window, dtype=jnp.int32)[:, None]
    j = jnp.arange(TN, dtype=jnp.int32)[None, :]
    u = ((j % H).astype(jnp.float32) + 0.5) / H
    values = weights_of(u)
    offset = n - LEAD + 1 - j // H
    basis = jnp.zeros((window, TN), jnp.float32)
    for dd in range(4):
        basis = jnp.where(offset == dd, values[dd], basis)
    return basis


def banded_along(padded, ny):
    knots = padded.shape[-1]
    per_block = TN // H
    window = 4 * per_block
    blocks = ny // TN
    right = per_block * (blocks - 1) + window - knots - LEAD
    cpad = jnp.pad(padded, ((0, 0), (0, 0), (LEAD, right)))
    cwin = jnp.stack([cpad[..., per_block * b : per_block * b + window] for b in range(blocks)], axis=2)
    along = jnp.einsum("pkbn,nj->pkbj", cwin, block_basis(window), precision=lax.Precision.HIGHEST)
    return along.reshape(padded.shape[:2] + (ny,))


def banded_data(back, knots):
    npred, nrow, ny = back.shape
    per_block = TN // H
    window = 4 * per_block
    blocks = ny // TN
    back4 = back.reshape(npred, nrow, blocks, TN)
    dwin = jnp.einsum("pkbj,nj->pkbn", back4, block_basis(window), precision=lax.Precision.HIGHEST)
    total = None
    for a in range(4):
        part = dwin[..., a * per_block : (a + 1) * per_block]
        part = jnp.pad(part, ((0, 0), (0, 0), (a, 3 - a), (0, 0)))
        total = part if total is None else total + part
    total = total.reshape(npred, nrow, (blocks + 3) * per_block)
    return total[..., LEAD : LEAD + knots]


def fit_kernel(w_ref, cov_ref, a_ref, o_ref):
    npred = cov_ref.shape[0]
    nint = cov_ref.shape[1] // H
    for s in range(TN // L):
        cols = pl.ds(s * L, L)
        w = [w_ref[d] for d in range(4)]
        for m in range(nint):
            rows = pl.ds(m * H, H)

            def body(p, acc):
                surf = w[0] * a_ref[p, pl.ds(m + 1, 1), cols]
                for d in range(1, 4):
                    surf = surf + w[d] * a_ref[p, pl.ds(m + 1 + d, 1), cols]
                return acc + cov_ref[p, rows, cols].astype(jnp.float32) * surf

            acc = lax.fori_loop(0, npred, body, jnp.zeros((H, L), jnp.float32), unroll=True)
            o_ref[rows, cols] = acc


def back_kernel(w_ref, cov_ref, r_ref, o_ref, rw_ref):
    npred = cov_ref.shape[0]
    nint = cov_ref.shape[1] // H
    for s in range(TN // L):
        cols = pl.ds(s * L, L)
        for d in range(4):
            for m in range(nint):
                rw_ref[d, pl.ds(m * H, H), :] = w_ref[d] * r_ref[pl.ds(m * H, H), cols]

        def body(p, carry):
            o_ref[p, pl.ds(0, 1), cols] = jnp.zeros((1, L), jnp.float32)
            accs = {}
            for m in range(nint):
                c = cov_ref[p, pl.ds(m * H, H), cols].astype(jnp.float32)
                for d in range(4):
                    prod = c * rw_ref[d, pl.ds(m * H, H), :]
                    half = prod[0:8] + prod[8:16]
                    r = m + 1 + d
                    accs[r] = half if r not in accs else accs[r] + half
                done = m + 1
                o_ref[p, pl.ds(done, 1), cols] = jnp.sum(accs.pop(done), axis=0, keepdims=True)
            for r in sorted(accs):
                o_ref[p, pl.ds(r, 1), cols] = jnp.sum(accs[r], axis=0, keepdims=True)
            return carry

        lax.fori_loop(0, npred, body, 0)


def fit_chunk(wl, cov, along, chunk, width):
    npred, rows, _ = cov.shape
    nrow = along.shape[1]
    off = chunk * (width // TN)
    return pl.pallas_call(
        fit_kernel,
        grid=(width // TN,),
        in_specs=[
            pl.BlockSpec((4, H, L), lambda j: (0, 0, 0)),
            pl.BlockSpec((npred, rows, TN), lambda j: (0, 0, j + off)),
            pl.BlockSpec((npred, nrow, TN), lambda j: (0, 0, j + off)),
        ],
        out_specs=pl.BlockSpec((rows, TN), lambda j: (0, j)),
        out_shape=jax.ShapeDtypeStruct((rows, width), jnp.float32),
        compiler_params=pltpu.CompilerParams(dimension_semantics=("arbitrary",)),
    )(wl, cov, along)


def back_chunk(wl, cov, resid, chunk, nrow):
    npred, rows, _ = cov.shape
    width = resid.shape[1]
    off = chunk * (width // TN)
    return pl.pallas_call(
        back_kernel,
        grid=(width // TN,),
        in_specs=[
            pl.BlockSpec((4, H, L), lambda j: (0, 0, 0)),
            pl.BlockSpec((npred, rows, TN), lambda j: (0, 0, j + off)),
            pl.BlockSpec((rows, TN), lambda j: (0, j)),
        ],
        out_specs=pl.BlockSpec((npred, nrow, TN), lambda j: (0, 0, j)),
        out_shape=jax.ShapeDtypeStruct((npred, nrow, width), jnp.float32),
        scratch_shapes=[pltpu.VMEM((4, rows, L), jnp.float32)],
        compiler_params=pltpu.CompilerParams(dimension_semantics=("arbitrary",)),
    )(wl, cov, resid)


def penalty(padded, count):
    stencil = [1.0, -4.0, 6.0, -4.0, 1.0]
    along_rows = None
    for ii in range(5):
        term = stencil[ii] * padded[..., ii : ii + count, :]
        along_rows = term if along_rows is None else along_rows + term
    centre = padded[..., 2 : count + 2, :]
    width = centre.shape[-1]
    wide = jnp.pad(centre, [(0, 0)] * (centre.ndim - 1) + [(2, 2)])
    for ii in range(5):
        along_rows = along_rows + stencil[ii] * wide[..., ii : ii + width]
    return along_rows


def local(covariates, target, land, coefs, first_moment, second_moment, smoothing):
    npred, rows, ny = covariates.shape
    count = coefs.shape[1]
    knots = coefs.shape[2]
    share = rows // lax.axis_size("pred")
    start = lax.axis_index("pred") * share
    wl = jnp.broadcast_to(weight_table(H)[:, :, None], (4, H, L))
    padded = extended(coefs, (("tile", 1),), 2)
    along = banded_along(padded, ny)
    nrow = padded.shape[1]
    target_blk = lax.dynamic_slice_in_dim(target, start, share, 0)
    land_blk = lax.dynamic_slice_in_dim(land, start, share, 0).astype(jnp.float32)
    width = ny // CHUNKS
    fitted_parts, resid_parts, back_parts = [], [], []
    for c in range(CHUNKS):
        partial = fit_chunk(wl, covariates, along, c, width)
        fitted_c = lax.psum_scatter(partial, "pred", scatter_dimension=0, tiled=True)
        cols = slice(c * width, (c + 1) * width)
        resid_c = land_blk[:, cols] * (target_blk[:, cols] - fitted_c)
        resid_full = lax.all_gather(resid_c, "pred", axis=0, tiled=True)
        back_parts.append(back_chunk(wl, covariates, resid_full, c, nrow))
        fitted_parts.append(fitted_c)
        resid_parts.append(resid_c)
    fitted = jnp.concatenate(fitted_parts, axis=1)
    residual = jnp.concatenate(resid_parts, axis=1)
    back = jnp.concatenate(back_parts, axis=2)
    grad_pad = -(1.0 / H) * banded_data(back, knots)
    inner = grad_pad[:, 2 : count + 2]
    from_below = from_behind(grad_pad[:, count + 2 :], "tile", 1)
    from_above = from_behind(grad_pad[:, :2], "tile", -1)
    middle = jnp.zeros((inner.shape[0], count - 2, inner.shape[2]), jnp.float32)
    low_add = jnp.concatenate([from_below, middle], axis=1)
    high_add = jnp.concatenate([middle, from_above], axis=1)
    data = inner + low_add + high_add
    gradient = data + smoothing[:, None, None] * penalty(padded, count)
    new_first = 0.9 * first_moment + 0.1 * gradient
    new_second = 0.99 * second_moment + 0.01 * gradient * gradient
    new_coefs = coefs - 0.1 * new_first / (jnp.sqrt(new_second) + 1e-08)
    return (fitted, residual, gradient, new_coefs, new_first, new_second)


def solution(mesh):
    in_specs = (
        P("pred", "tile", None),
        P("tile", None),
        P("tile", None),
        P("pred", "tile", None),
        P("pred", "tile", None),
        P("pred", "tile", None),
        P("pred"),
    )
    out_specs = (
        P(("tile", "pred"), None),
        P(("tile", "pred"), None),
        P("pred", "tile", None),
        P("pred", "tile", None),
        P("pred", "tile", None),
        P("pred", "tile", None),
    )
    return jax.shard_map(local, mesh=mesh, in_specs=in_specs, out_specs=out_specs, check_vma=False)
```

profile of v0, /device:TPU:0, one launch (start us, length us, event | category | flops | bytes accessed | tf_op | source)
XLA Modules:
  0.0 302.4 jit_solution(5141606847638783377)
XLA Ops:
  7.2 1.1 copy.688
  8.3 1.3 collective-permute-start.1
  9.7 5.5 %collective-permute-start = (f32[16,2,512]{2,0,1:T(8,128)S(1)}, f32[16,2,512]{2,0,1:T(8,128)S(1)}, u32[]{:S(2)}, u32[]{:S(2)}) collective-permute-start(f32[16,2,512]{2,0,1:T(8,128)S(1)} %get-tuple-element.136), channel_id=1, source_target_pairs={{0,4},{4,8},{8,12},{12,16},{16,20},{20,24},{24,28},{1,5},{5,9},{9,... | collective-permute-start | bytes 196616 | tf_op jit(solution)/shard_map/ppermute | solution.py:22
  15.2 1.9 collective-permute-done
  17.2 1.1 constant_dynamic-update-slice_fusion.3
  18.4 0.7 copy-done.4
  19.1 0.5 fusion.49
  19.5 0.1 copy.706
  19.6 0.1 copy.704
  19.7 0.1 copy.705
  19.9 0.1 copy.703
  20.0 0.1 copy.702
  20.1 0.1 copy.701
  20.2 0.1 copy.700
  20.3 0.1 copy.699
  20.4 0.1 copy.698
  20.6 0.1 copy.696
  20.7 0.1 copy.695
  21.0 0.1 copy.693
  21.1 0.1 copy.692
  21.3 2.5 stack.75
  23.8 7.2 %fusion = f32[16,12,16,512]{3,2,0,1:T(8,128)} fusion(f32[16,12,16,128]{3,2,1,0:T(8,128)S(1)} %stack.75, f32[512]{0:T(512)S(1)} %get-tuple-element.147, f32[512]{0:T(512)S(1)} %get-tuple-element.148, f32[512]{0:T(512)S(1)} %get-tuple-element.146, f32[512]{0:T(512)S(1)} %get-tuple-element.145, s32[512]{0:T(512)S(1)} %add_select_fusion, s32[128]{0:T(128)S(1)} %iota_add_fusion), kind=kOutput, calls=%fused_computation.2 | convolution fusion | flops 2416508928 | bytes 7875072 | tf_op jit(solution)/shard_map/pkbn,nj->pkbj/dot_general | solution.py:68
  31.0 7.1 %reshape.213 = f32[16,12,8192]{2,0,1:T(8,128)} reshape(f32[16,12,16,512]{3,2,0,1:T(8,128)} %fusion) | data formatting | bytes 12582912 | tf_op jit(solution)/shard_map/reshape | solution.py:69
  38.2 9.8 %copy.708.a_ref = f32[16,12,8192]{2,1,0:T(8,128)} copy(f32[16,12,8192]{2,0,1:T(8,128)} %reshape.213) | data formatting | bytes 12582912 | tf_op jit(solution)/shard_map/reshape | solution.py:69
  48.0 0.7 broadcast_in_dim.55.w_ref
  48.7 9.0 %shard_map.121 = f32[128,2048]{1,0:T(8,128)} custom-call(f32[4,16,256]{2,1,0:T(8,128)} %broadcast_in_dim.55.w_ref, bf16[16,128,8192]{2,1,0:T(8,128)(2,1)} %cov_ref.15, f32[16,12,8192]{2,1,0:T(8,128)} %copy.708.a_ref), custom_call_target="tpu_custom_call" | custom-call | tf_op jit(solution)/shard_map/pallas_call | solution.py:139
  57.8 0.2 reduce-scatter.9.cloned.1.call-start
  58.0 9.1 %shard_map.120 = f32[128,2048]{1,0:T(8,128)} custom-call(f32[4,16,256]{2,1,0:T(8,128)} %broadcast_in_dim.55.w_ref, bf16[16,128,8192]{2,1,0:T(8,128)(2,1)} %cov_ref.15, f32[16,12,8192]{2,1,0:T(8,128)} %copy.708.a_ref), custom_call_target="tpu_custom_call" | custom-call | tf_op jit(solution)/shard_map/pallas_call | solution.py:139
  67.1 9.3 %shard_map.118 = f32[128,2048]{1,0:T(8,128)} custom-call(f32[4,16,256]{2,1,0:T(8,128)} %broadcast_in_dim.55.w_ref, bf16[16,128,8192]{2,1,0:T(8,128)(2,1)} %cov_ref.15, f32[16,12,8192]{2,1,0:T(8,128)} %copy.708.a_ref), custom_call_target="tpu_custom_call" | custom-call | tf_op jit(solution)/shard_map/pallas_call | solution.py:139
  76.5 9.2 %shard_map.119 = f32[128,2048]{1,0:T(8,128)} custom-call(f32[4,16,256]{2,1,0:T(8,128)} %broadcast_in_dim.55.w_ref, bf16[16,128,8192]{2,1,0:T(8,128)(2,1)} %cov_ref.15, f32[16,12,8192]{2,1,0:T(8,128)} %copy.708.a_ref), custom_call_target="tpu_custom_call" | custom-call | tf_op jit(solution)/shard_map/pallas_call | solution.py:139
  85.8 1.3 dynamic-slice_convert_fusion
  87.2 27.1 %reduce-scatter.9.cloned.1.call-done = f32[32,2048]{1,0:T(8,128)} async-done(((f32[128,2048]{1,0:T(8,128)}), f32[32,2048]{1,0:T(8,128)}) %reduce-scatter.9.cloned.1.call-update) | async-done | bytes 262160 | tf_op jit(solution)/shard_map/reduce_scatter | solution.py:202
  114.3 27.5 %reduce-scatter.5.cloned.1.call-done = f32[32,2048]{1,0:T(8,128)} async-done(((f32[128,2048]{1,0:T(8,128)}), f32[32,2048]{1,0:T(8,128)}) %reduce-scatter.5.cloned.1.call-update) | async-done | bytes 262160 | tf_op jit(solution)/shard_map/reduce_scatter | solution.py:202
  141.8 27.5 %reduce-scatter.7.cloned.1.call-done = f32[32,2048]{1,0:T(8,128)} async-done(((f32[128,2048]{1,0:T(8,128)}), f32[32,2048]{1,0:T(8,128)}) %reduce-scatter.7.cloned.1.call-update) | async-done | bytes 262160 | tf_op jit(solution)/shard_map/reduce_scatter | solution.py:202
  169.2 2.5 fusion.19
  171.8 0.5 all-gather.7.cloned.1.call-update
  172.4 0.7 all-gather.9.cloned.1.call-update
  173.2 0.7 all-gather.5.cloned.1.call-update
  173.9 2.2 pad_maximum_fusion.2
  176.1 12.6 %all-gather.11.cloned.1.call-done.r_ref = f32[128,2048]{1,0:T(8,128)} async-done(((f32[32,2048]{1,0:T(8,128)}), f32[128,2048]{1,0:T(8,128)}) %all-gather.11.cloned.1.call-update) | async-done | bytes 1048592 | tf_op jit(solution)/shard_map/all_gather | solution.py:205
  188.7 11.1 %shard_map.125 = f32[16,12,2048]{2,1,0:T(8,128)} custom-call(f32[4,16,256]{2,1,0:T(8,128)} %broadcast_in_dim.55.w_ref, bf16[16,128,8192]{2,1,0:T(8,128)(2,1)} %cov_ref.15, f32[128,2048]{1,0:T(8,128)} %all-gather.11.cloned.1.call-done.r_ref), custom_call_target="tpu_custom_call" | custom-call | tf_op jit(solution)/shard_map/pallas_call | solution.py:157
  199.8 7.7 %all-gather.7.cloned.1.call-done.r_ref = f32[128,2048]{1,0:T(8,128)} async-done(((f32[32,2048]{1,0:T(8,128)}), f32[128,2048]{1,0:T(8,128)}) %all-gather.7.cloned.1.call-update) | async-done | bytes 1048592 | tf_op jit(solution)/shard_map/all_gather | solution.py:205
  207.4 11.1 %shard_map.123 = f32[16,12,2048]{2,1,0:T(8,128)} custom-call(f32[4,16,256]{2,1,0:T(8,128)} %broadcast_in_dim.55.w_ref, bf16[16,128,8192]{2,1,0:T(8,128)(2,1)} %cov_ref.15, f32[128,2048]{1,0:T(8,128)} %all-gather.7.cloned.1.call-done.r_ref), custom_call_target="tpu_custom_call" | custom-call | tf_op jit(solution)/shard_map/pallas_call | solution.py:157
  218.5 7.8 %all-gather.9.cloned.1.call-done.r_ref = f32[128,2048]{1,0:T(8,128)} async-done(((f32[32,2048]{1,0:T(8,128)}), f32[128,2048]{1,0:T(8,128)}) %all-gather.9.cloned.1.call-update) | async-done | bytes 1048592 | tf_op jit(solution)/shard_map/all_gather | solution.py:205
  226.3 11.1 %shard_map.124 = f32[16,12,2048]{2,1,0:T(8,128)} custom-call(f32[4,16,256]{2,1,0:T(8,128)} %broadcast_in_dim.55.w_ref, bf16[16,128,8192]{2,1,0:T(8,128)(2,1)} %cov_ref.15, f32[128,2048]{1,0:T(8,128)} %all-gather.9.cloned.1.call-done.r_ref), custom_call_target="tpu_custom_call" | custom-call | tf_op jit(solution)/shard_map/pallas_call | solution.py:157
  237.4 7.8 %all-gather.5.cloned.1.call-done.r_ref = f32[128,2048]{1,0:T(8,128)} async-done(((f32[32,2048]{1,0:T(8,128)}), f32[128,2048]{1,0:T(8,128)}) %all-gather.5.cloned.1.call-update) | async-done | bytes 1048592 | tf_op jit(solution)/shard_map/all_gather | solution.py:205
  245.2 11.7 %shard_map.122 = f32[16,12,2048]{2,1,0:T(8,128)} custom-call(f32[4,16,256]{2,1,0:T(8,128)} %broadcast_in_dim.55.w_ref, bf16[16,128,8192]{2,1,0:T(8,128)(2,1)} %cov_ref.15, f32[128,2048]{1,0:T(8,128)} %all-gather.5.cloned.1.call-done.r_ref), custom_call_target="tpu_custom_call" | custom-call | tf_op jit(solution)/shard_map/pallas_call | solution.py:157
  256.9 5.5 %pad_maximum_fusion = f32[16,12,8192]{2,1,0:T(8,128)} fusion(f32[16,12,2048]{2,1,0:T(8,128)S(1)} %copy-done, f32[16,12,2048]{2,1,0:T(8,128)} %shard_map.124, f32[16,12,2048]{2,1,0:T(8,128)} %shard_map.123, f32[16,12,2048]{2,1,0:T(8,128)} %shard_map.122), kind=kLoop, calls=%fused_computation | loop fusion | flops 4718592 | bytes 12582912 | tf_op jit(solution)/shard_map/concatenate | solution.py:211
  262.4 8.2 %reshape.217 = f32[16,12,16,512]{3,2,1,0:T(8,128)} reshape(f32[16,12,8192]{2,1,0:T(8,128)} %pad_maximum_fusion) | data formatting | bytes 12582912 | tf_op jit(solution)/shard_map/reshape | solution.py:77
  270.5 7.4 %fusion.20 = f32[16,12,16,128]{3,2,1,0:T(8,128)S(1)} fusion(f32[16,12,16,512]{3,2,1,0:T(8,128)} %reshape.217, f32[512]{0:T(512)S(1)} %get-tuple-element.147, f32[512]{0:T(512)S(1)} %get-tuple-element.148, f32[512]{0:T(512)S(1)} %get-tuple-element.146, f32[512]{0:T(512)S(1)} %get-tuple-element.145, s32[512]{0:T(512)S(1)} %add_select_fusion, ...), kind=kOutput, calls=%fused_computation.47 | convolution fusion | flops 2416508928 | bytes 7875072 | tf_op jit(solution)/shard_map/pkbj,nj->pkbn/dot_general | solution.py:78
  278.0 1.4 fusion.85
  279.3 1.1 pad_add_fusion
  280.5 0.5 reshape.218
  281.1 0.2 slice.207
  281.3 0.3 copy_multiply_fusion
  281.6 3.5 %collective-permute-start.2 = (f32[16,2,512]{2,0,1:T(8,128)S(1)}, f32[16,2,512]{2,0,1:T(8,128)S(1)}, u32[]{:S(2)}, u32[]{:S(2)}) collective-permute-start(f32[16,2,512]{2,0,1:T(8,128)S(1)} %get-tuple-element.114), channel_id=1, source_target_pairs={{0,4},{4,8},{8,12},{12,16},{16,20},{20,24},{24,28},{1,5},{5,9},{9,... | collective-permute-start | bytes 196616 | tf_op jit(solution)/shard_map/ppermute | solution.py:31
  285.1 1.3 collective-permute-start.3
  286.5 1.0 pad_maximum_fusion.1
  287.5 3.8 %collective-permute-done.3 = f32[16,2,512]{2,0,1:T(8,128)S(1)} collective-permute-done((f32[16,2,512]{2,0,1:T(8,128)S(1)}, f32[16,2,512]{2,0,1:T(8,128)S(1)}, u32[]{:S(2)}, u32[]{:S(2)}) %collective-permute-start.3) | collective-permute-done | bytes 65568 | tf_op jit(solution)/shard_map/ppermute | solution.py:31
  291.3 0.8 divide_subtract_fusion
  292.1 0.9 copy.723
  292.9 0.9 copy.724
  293.8 0.9 copy.725
  294.7 0.9 copy.722
  (54 shorter events, 0.9 us)
Async XLA Ops:
  7.2 80.0 %reduce-scatter.11.cloned.1.call-start = ((), (), s32[]{:S(2)}) async-start(), calls=%async_computation.7 | async-start | bytes 1310720 | tf_op jit(solution)/shard_map/reduce_scatter | solution.py:202
  8.3 8.9 %copy-start.2 = (f32[16,8,512]{2,0,1:T(8,128)}, f32[16,8,512]{2,0,1:T(8,128)S(1)}, u32[]{:S(2)}) copy-start(f32[16,8,512]{2,0,1:T(8,128)S(1)} %copy.688) | copy-start | bytes 786436
  8.3 10.0 %collective-permute-start.1 = (f32[16,2,512]{2,0,1:T(8,128)S(1)}, f32[16,2,512]{2,0,1:T(8,128)S(1)}, u32[]{:S(2)}, u32[]{:S(2)}) collective-permute-start(f32[16,2,512]{2,0,1:T(8,128)S(1)} %get-tuple-element.135), channel_id=1, source_target_pairs={{4,0},{8,4},{12,8},{16,12},{20,16},{24,20},{28,24},{5,1},{9,5},{13... | collective-permute-start | bytes 196616 | tf_op jit(solution)/shard_map/ppermute | solution.py:23
  9.7 7.5 %collective-permute-start = (f32[16,2,512]{2,0,1:T(8,128)S(1)}, f32[16,2,512]{2,0,1:T(8,128)S(1)}, u32[]{:S(2)}, u32[]{:S(2)}) collective-permute-start(f32[16,2,512]{2,0,1:T(8,128)S(1)} %get-tuple-element.136), channel_id=1, source_target_pairs={{0,4},{4,8},{8,12},{12,16},{16,20},{20,24},{24,28},{1,5},{5,9},{9,... | collective-permute-start | bytes 196616 | tf_op jit(solution)/shard_map/ppermute | solution.py:22
  18.3 0.7 copy-start.4
  57.8 56.6 %reduce-scatter.9.cloned.1.call-start = ((), (), s32[]{:S(2)}) async-start(), calls=%async_computation.6 | async-start | bytes 1310720 | tf_op jit(solution)/shard_map/reduce_scatter | solution.py:202
  67.1 74.7 %reduce-scatter.5.cloned.1.call-start = ((), (), s32[]{:S(2)}) async-start(), calls=%async_computation.4 | async-start | bytes 1310720 | tf_op jit(solution)/shard_map/reduce_scatter | solution.py:202
  76.5 92.7 %reduce-scatter.7.cloned.1.call-start = ((), (), s32[]{:S(2)}) async-start(), calls=%async_computation.5 | async-start | bytes 1310720 | tf_op jit(solution)/shard_map/reduce_scatter | solution.py:202
  85.8 102.9 %all-gather.11.cloned.1.call-start = ((), (), s32[]{:S(2)}) async-start(), calls=%async_computation.11 | async-start | bytes 1310720 | tf_op jit(solution)/shard_map/all_gather | solution.py:205
  171.8 35.6 %all-gather.7.cloned.1.call-start = ((), (), s32[]{:S(2)}) async-start(), calls=%async_computation.9 | async-start | bytes 1310720 | tf_op jit(solution)/shard_map/all_gather | solution.py:205
  172.4 53.9 %all-gather.9.cloned.1.call-start = ((), (), s32[]{:S(2)}) async-start(), calls=%async_computation.10 | async-start | bytes 1310720 | tf_op jit(solution)/shard_map/all_gather | solution.py:205
  173.1 72.1 %all-gather.5.cloned.1.call-start = ((), (), s32[]{:S(2)}) async-start(), calls=%async_computation.8 | async-start | bytes 1310720 | tf_op jit(solution)/shard_map/all_gather | solution.py:205
  237.4 19.5 %copy-start = (f32[16,12,2048]{2,1,0:T(8,128)S(1)}, f32[16,12,2048]{2,1,0:T(8,128)}, u32[]{:S(2)}) copy-start(f32[16,12,2048]{2,1,0:T(8,128)} %shard_map.125) | copy-start | bytes 4718596
  281.0 5.4 %copy-start.6 = (f32[32,2048]{1,0:T(8,128)S(1)}, f32[32,2048]{1,0:T(8,128)}, u32[]{:S(2)}) copy-start(f32[32,2048]{1,0:T(8,128)} %reduce-scatter.11.cloned.1.call-done) | copy-start | bytes 786436
  281.0 5.4 %copy-start.7 = (f32[32,2048]{1,0:T(8,128)S(1)}, f32[32,2048]{1,0:T(8,128)}, u32[]{:S(2)}) copy-start(f32[32,2048]{1,0:T(8,128)} %reduce-scatter.9.cloned.1.call-done) | copy-start | bytes 786436
  281.0 5.4 %copy-start.8 = (f32[32,2048]{1,0:T(8,128)S(1)}, f32[32,2048]{1,0:T(8,128)}, u32[]{:S(2)}) copy-start(f32[32,2048]{1,0:T(8,128)} %reduce-scatter.5.cloned.1.call-done) | copy-start | bytes 786436
  281.0 5.4 %copy-start.9 = (f32[32,2048]{1,0:T(8,128)S(1)}, f32[32,2048]{1,0:T(8,128)}, u32[]{:S(2)}) copy-start(f32[32,2048]{1,0:T(8,128)} %reduce-scatter.7.cloned.1.call-done) | copy-start | bytes 786436
  281.0 10.2 %copy-start.1 = (f32[16,8,512]{2,1,0:T(8,128)S(1)}, f32[16,8,512]{2,1,0:T(8,128)}, u32[]{:S(2)}) copy-start(f32[16,8,512]{2,1,0:T(8,128)} %param.10) | copy-start | bytes 786436
  281.1 10.2 %copy-start.3 = (f32[16,8,512]{2,0,1:T(8,128)S(1)}, f32[16,8,512]{2,0,1:T(8,128)}, u32[]{:S(2)}) copy-start(f32[16,8,512]{2,0,1:T(8,128)} %copy-done.2) | copy-start | bytes 786436
  281.1 10.2 %copy-start.5 = (f32[16,10,512]{2,0,1:T(8,128)S(1)}, f32[16,10,512]{2,0,1:T(8,128)}, u32[]{:S(2)}) copy-start(f32[16,10,512]{2,0,1:T(8,128)} %copy-done.4) | copy-start | bytes 983044
  281.1 10.2 %copy-start.10 = (f32[16,8,512]{2,1,0:T(8,128)S(1)}, f32[16,8,512]{2,1,0:T(8,128)}, u32[]{:S(2)}) copy-start(f32[16,8,512]{2,1,0:T(8,128)} %param.11) | copy-start | bytes 786436
  281.1 10.2 %copy-start.11 = (f32[16,8,512]{2,1,0:T(8,128)S(1)}, f32[16,8,512]{2,1,0:T(8,128)}, u32[]{:S(2)}) copy-start(f32[16,8,512]{2,1,0:T(8,128)} %param.12) | copy-start | bytes 786436
  281.1 10.2 %copy-start.12 = (f32[16]{0:T(128)S(1)}, f32[16]{0:T(128)}, u32[]{:S(2)}) copy-start(f32[16]{0:T(128)} %param.13) | copy-start | bytes 196
  281.6 5.9 %collective-permute-start.2 = (f32[16,2,512]{2,0,1:T(8,128)S(1)}, f32[16,2,512]{2,0,1:T(8,128)S(1)}, u32[]{:S(2)}, u32[]{:S(2)}) collective-permute-start(f32[16,2,512]{2,0,1:T(8,128)S(1)} %get-tuple-element.114), channel_id=1, source_target_pairs={{0,4},{4,8},{8,12},{12,16},{16,20},{20,24},{24,28},{1,5},{5,9},{9,... | collective-permute-start | bytes 196616 | tf_op jit(solution)/shard_map/ppermute | solution.py:31
  285.1 6.2 %collective-permute-start.3 = (f32[16,2,512]{2,0,1:T(8,128)S(1)}, f32[16,2,512]{2,0,1:T(8,128)S(1)}, u32[]{:S(2)}, u32[]{:S(2)}) collective-permute-start(f32[16,2,512]{2,0,1:T(8,128)S(1)} %get-tuple-element.115), channel_id=1, source_target_pairs={{4,0},{8,4},{12,8},{16,12},{20,16},{24,20},{28,24},{5,1},{9,5},{13... | collective-permute-start | bytes 196616 | tf_op jit(solution)/shard_map/ppermute | solution.py:31
Sparse Core Ops, SparseCore 0:
  57.9 28.1 reduce-scatter.10
  89.4 24.8 reduce-scatter.8
  116.8 24.8 reduce-scatter.4
  144.3 24.8 reduce-scatter.6
  171.9 16.7 all-gather.10
  190.7 16.7 all-gather.6
  209.5 16.7 all-gather.8
  228.4 16.7 all-gather.4
where the time goes:
time: 303 us; the launch traced here: 302 us
  waiting for transfers between devices  126 us (42%)
  Pallas kernels  81.5 us (27%)
  local copies, waits for them, and re-layouts  39 us (13%)
  other arithmetic  14.8 us (5%)
  matrix products  14.7 us (5%)
  between operations  14.6 us (5%)
  starting transfers between devices  12.1 us (4%)
    reduce_scatter x4, waiting for transfers between devices, local(): lax.psum_scatter(partial, 'pred', scatter_dimension=0, tiled=True)  82.1 us
    pallas_call x4, Pallas kernels, back_chunk(): pl.pallas_call(back_kernel, grid=(width // TN,), in_specs=[pl.BlockSpec((...  44.9 us
    pallas_call x4, Pallas kernels, fit_chunk(): pl.pallas_call(fit_kernel, grid=(width // TN,), in_specs=[pl.BlockSpec((4...  36.7 us
    all_gather x4, waiting for transfers between devices, local(): resid_full = lax.all_gather(resid_c, 'pred', axis=0, tiled=True)  35.9 us
    reshape x2, local copies, waits for them, and re-layouts, banded_along(): return along.reshape(padded.shape[:2] + (ny,))  17 us
    reshape x1, local copies, waits for them, and re-layouts, banded_data(): back4 = back.reshape(npred, nrow, blocks, TN)  8.15 us
    dot_general x1, matrix products, banded_data(): jnp.einsum('pkbj,nj->pkbn', back4, block_basis(window), precision=lax.Pre...  7.43 us
    dot_general x1, matrix products, banded_along(): jnp.einsum('pkbn,nj->pkbj', cwin, block_basis(window), precision=lax.Prec...  7.25 us
  transfers between devices with their start and end apart: 12, of which 9 were waited for; matrix products, arithmetic and copies ran while one was open for 2% of the time, Pallas kernels for 20%

commit v1 on v0

--- a/solution.py
+++ b/solution.py
@@ -64,18 +64,15 @@
     blocks = ny // TN
     right = per_block * (blocks - 1) + window - knots - LEAD
     cpad = jnp.pad(padded, ((0, 0), (0, 0), (LEAD, right)))
-    cwin = jnp.stack([cpad[..., per_block * b : per_block * b + window] for b in range(blocks)], axis=2)
-    along = jnp.einsum("pkbn,nj->pkbj", cwin, block_basis(window), precision=lax.Precision.HIGHEST)
-    return along.reshape(padded.shape[:2] + (ny,))
-
-
-def banded_data(back, knots):
-    npred, nrow, ny = back.shape
+    cwin = jnp.stack([cpad[..., per_block * b : per_block * b + window] for b in range(blocks)], axis=1)
+    return jnp.einsum("pbkn,nj->pbkj", cwin, block_basis(window), precision=lax.Precision.HIGHEST)
+
+
+def banded_data(back4, knots):
+    npred, blocks, nrow, _ = back4.shape
     per_block = TN // H
     window = 4 * per_block
-    blocks = ny // TN
-    back4 = back.reshape(npred, nrow, blocks, TN)
-    dwin = jnp.einsum("pkbj,nj->pkbn", back4, block_basis(window), precision=lax.Precision.HIGHEST)
+    dwin = jnp.einsum("pbkj,nj->pkbn", back4, block_basis(window), precision=lax.Precision.HIGHEST)
     total = None
     for a in range(4):
         part = dwin[..., a * per_block : (a + 1) * per_block]
@@ -83,6 +80,31 @@
         total = part if total is None else total + part
     total = total.reshape(npred, nrow, (blocks + 3) * per_block)
     return total[..., LEAD : LEAD + knots]
+
+
+def allreduce_rows(x, axis):
+    n = lax.axis_size(axis)
+    idx = lax.axis_index(axis)
+    bits = []
+    bit = 1
+    while bit < n:
+        bits.append(bit)
+        bit *= 2
+    cur = x
+    for bit in bits:
+        half = cur.shape[0] // 2
+        mine = (idx // bit) % 2
+        pair = cur.reshape((2, half) + cur.shape[1:])
+        keep = lax.dynamic_index_in_dim(pair, mine, 0, keepdims=False)
+        send = lax.dynamic_index_in_dim(pair, 1 - mine, 0, keepdims=False)
+        cur = keep + lax.ppermute(send, axis, [(i, i ^ bit) for i in range(n)])
+    for bit in reversed(bits):
+        mine = (idx // bit) % 2
+        other = lax.ppermute(cur, axis, [(i, i ^ bit) for i in range(n)])
+        first = jnp.where(mine == 0, cur, other)
+        second = jnp.where(mine == 0, other, cur)
+        cur = jnp.concatenate([first, second], axis=0)
+    return cur
 
 
 def fit_kernel(w_ref, cov_ref, a_ref, o_ref):
@@ -95,26 +117,28 @@
             rows = pl.ds(m * H, H)
 
             def body(p, acc):
-                surf = w[0] * a_ref[p, pl.ds(m + 1, 1), cols]
+                surf = w[0] * a_ref[p, 0, pl.ds(m + 1, 1), cols]
                 for d in range(1, 4):
-                    surf = surf + w[d] * a_ref[p, pl.ds(m + 1 + d, 1), cols]
+                    surf = surf + w[d] * a_ref[p, 0, pl.ds(m + 1 + d, 1), cols]
                 return acc + cov_ref[p, rows, cols].astype(jnp.float32) * surf
 
             acc = lax.fori_loop(0, npred, body, jnp.zeros((H, L), jnp.float32), unroll=True)
             o_ref[rows, cols] = acc
 
 
-def back_kernel(w_ref, cov_ref, r_ref, o_ref, rw_ref):
+def back_kernel(w_ref, cov_ref, t_ref, y_ref, g_ref, o_ref, rw_ref):
     npred = cov_ref.shape[0]
     nint = cov_ref.shape[1] // H
     for s in range(TN // L):
         cols = pl.ds(s * L, L)
-        for d in range(4):
-            for m in range(nint):
-                rw_ref[d, pl.ds(m * H, H), :] = w_ref[d] * r_ref[pl.ds(m * H, H), cols]
+        for m in range(nint):
+            rows = pl.ds(m * H, H)
+            resid = g_ref[rows, cols].astype(jnp.float32) * (y_ref[rows, cols] - t_ref[rows, cols])
+            for d in range(4):
+                rw_ref[d, rows, :] = w_ref[d] * resid
 
         def body(p, carry):
-            o_ref[p, pl.ds(0, 1), cols] = jnp.zeros((1, L), jnp.float32)
+            o_ref[p, 0, pl.ds(0, 1), cols] = jnp.zeros((1, L), jnp.float32)
             accs = {}
             for m in range(nint):
                 c = cov_ref[p, pl.ds(m * H, H), cols].astype(jnp.float32)
@@ -124,9 +148,9 @@
                     r = m + 1 + d
                     accs[r] = half if r not in accs else accs[r] + half
                 done = m + 1
-                o_ref[p, pl.ds(done, 1), cols] = jnp.sum(accs.pop(done), axis=0, keepdims=True)
+                o_ref[p, 0, pl.ds(done, 1), cols] = jnp.sum(accs.pop(done), axis=0, keepdims=True)
             for r in sorted(accs):
-                o_ref[p, pl.ds(r, 1), cols] = jnp.sum(accs[r], axis=0, keepdims=True)
+                o_ref[p, 0, pl.ds(r, 1), cols] = jnp.sum(accs[r], axis=0, keepdims=True)
             return carry
 
         lax.fori_loop(0, npred, body, 0)
@@ -134,7 +158,7 @@
 
 def fit_chunk(wl, cov, along, chunk, width):
     npred, rows, _ = cov.shape
-    nrow = along.shape[1]
+    nrow = along.shape[2]
     off = chunk * (width // TN)
     return pl.pallas_call(
         fit_kernel,
@@ -142,7 +166,7 @@
         in_specs=[
             pl.BlockSpec((4, H, L), lambda j: (0, 0, 0)),
             pl.BlockSpec((npred, rows, TN), lambda j: (0, 0, j + off)),
-            pl.BlockSpec((npred, nrow, TN), lambda j: (0, 0, j + off)),
+            pl.BlockSpec((npred, 1, nrow, TN), lambda j: (0, j + off, 0, 0)),
         ],
         out_specs=pl.BlockSpec((rows, TN), lambda j: (0, j)),
         out_shape=jax.ShapeDtypeStruct((rows, width), jnp.float32),
@@ -150,9 +174,9 @@
     )(wl, cov, along)
 
 
-def back_chunk(wl, cov, resid, chunk, nrow):
+def back_chunk(wl, cov, total, target, land, chunk, nrow):
     npred, rows, _ = cov.shape
-    width = resid.shape[1]
+    width = total.shape[1]
     off = chunk * (width // TN)
     return pl.pallas_call(
         back_kernel,
@@ -161,12 +185,14 @@
             pl.BlockSpec((4, H, L), lambda j: (0, 0, 0)),
             pl.BlockSpec((npred, rows, TN), lambda j: (0, 0, j + off)),
             pl.BlockSpec((rows, TN), lambda j: (0, j)),
+            pl.BlockSpec((rows, TN), lambda j: (0, j + off)),
+            pl.BlockSpec((rows, TN), lambda j: (0, j + off)),
         ],
-        out_specs=pl.BlockSpec((npred, nrow, TN), lambda j: (0, 0, j)),
-        out_shape=jax.ShapeDtypeStruct((npred, nrow, width), jnp.float32),
+        out_specs=pl.BlockSpec((npred, 1, nrow, TN), lambda j: (0, j, 0, 0)),
+        out_shape=jax.ShapeDtypeStruct((npred, width // TN, nrow, TN), jnp.float32),
         scratch_shapes=[pltpu.VMEM((4, rows, L), jnp.float32)],
         compiler_params=pltpu.CompilerParams(dimension_semantics=("arbitrary",)),
-    )(wl, cov, resid)
+    )(wl, cov, total, target, land)
 
 
 def penalty(padded, count):
@@ -196,19 +222,15 @@
     target_blk = lax.dynamic_slice_in_dim(target, start, share, 0)
     land_blk = lax.dynamic_slice_in_dim(land, start, share, 0).astype(jnp.float32)
     width = ny // CHUNKS
-    fitted_parts, resid_parts, back_parts = [], [], []
+    fitted_parts, back_parts = [], []
     for c in range(CHUNKS):
         partial = fit_chunk(wl, covariates, along, c, width)
-        fitted_c = lax.psum_scatter(partial, "pred", scatter_dimension=0, tiled=True)
-        cols = slice(c * width, (c + 1) * width)
-        resid_c = land_blk[:, cols] * (target_blk[:, cols] - fitted_c)
-        resid_full = lax.all_gather(resid_c, "pred", axis=0, tiled=True)
-        back_parts.append(back_chunk(wl, covariates, resid_full, c, nrow))
-        fitted_parts.append(fitted_c)
-        resid_parts.append(resid_c)
+        total = allreduce_rows(partial, "pred")
+        back_parts.append(back_chunk(wl, covariates, total, target, land, c, nrow))
+        fitted_parts.append(lax.dynamic_slice_in_dim(total, start, share, 0))
     fitted = jnp.concatenate(fitted_parts, axis=1)
-    residual = jnp.concatenate(resid_parts, axis=1)
-    back = jnp.concatenate(back_parts, axis=2)
+    residual = land_blk * (target_blk - fitted)
+    back = jnp.concatenate(back_parts, axis=1)
     grad_pad = -(1.0 / H) * banded_data(back, knots)
     inner = grad_pad[:, 2 : count + 2]
     from_below = from_behind(grad_pad[:, count + 2 :], "tile", 1)

time: 303 us -> 203 us (0.67)
  waiting for transfers between devices: 126 us -> 39.7 us
  local copies, waits for them, and re-layouts: 39 us -> 18.8 us
  starting transfers between devices: 12.1 us -> 26.4 us
  between operations: 14.6 us -> 1.39 us
  other arithmetic: 14.8 us -> 18.2 us
    reduce_scatter x4 -> x0, waiting for transfers between devices: 82.1 us -> none  [local(): lax.psum_scatter(partial, 'pred', scatter_dimension=0, tiled=True)]
    all_gather x4 -> x0, waiting for transfers between devices: 35.9 us -> none  [local(): resid_full = lax.all_gather(resid_c, 'pred', axis=0, tiled=True)]
    ppermute x0 -> x16, waiting for transfers between devices: none -> 34.7 us  [the longest x8 19.3 us: allreduce_rows(): other = lax.ppermute(cur, axis, [(i, i ^ bit) for i in range(n)])]
    reshape x3 -> x0, local copies, waits for them, and re-layouts: 25.1 us -> none  [the longest x2 17 us: banded_along(): return along.reshape(padded.shape[:2] + (ny,))]
    ppermute x0 -> x16, starting transfers between devices: none -> 13.6 us  [the longest x8 8.21 us: allreduce_rows(): other = lax.ppermute(cur, axis, [(i, i ^ bit) for i in range(n)])]
    squeeze x0 -> x8, local copies, waits for them, and re-layouts: none -> 4.04 us  [allreduce_rows(): send = lax.dynamic_index_in_dim(pair, 1 - mine, 0, keepdims=False)]
    concatenate x3 -> x13, other arithmetic: 8.77 us -> 11 us  [the longest x12 7.33 us: allreduce_rows(): cur = jnp.concatenate([first, second], axis=0)]
  transfers between devices with their start and end apart: 12 -> 20, of which waited for: 9 -> 10; matrix products, arithmetic and copies ran while one was open for 2% -> 7% of each run, Pallas kernels for 20% -> 8%
where the time goes in v1:
time: 203 us; the launch traced here: 202 us
  Pallas kernels  80.2 us (40%)
  waiting for transfers between devices  39.7 us (20%)
  starting transfers between devices  26.4 us (13%)
  local copies, waits for them, and re-layouts  18.8 us (9%)
  other arithmetic  18.2 us (9%)
  matrix products  17.6 us (9%)
    pallas_call x4, Pallas kernels, back_chunk(): pl.pallas_call(back_kernel, grid=(width // TN,), in_specs=[pl.BlockSpec((...  46.2 us
    pallas_call x4, Pallas kernels, fit_chunk(): pl.pallas_call(fit_kernel, grid=(width // TN,), in_specs=[pl.BlockSpec((4...  34 us
    ppermute x8, waiting for transfers between devices, allreduce_rows(): other = lax.ppermute(cur, axis, [(i, i ^ bit) for i in range(n)])  19.3 us
    ppermute x8, waiting for transfers between devices, allreduce_rows(): cur = keep + lax.ppermute(send, axis, [(i, i ^ bit) for i in range(n)])  15.4 us
    dot_general x1, matrix products, banded_along(): jnp.einsum('pbkn,nj->pbkj', cwin, block_basis(window), precision=lax.Prec...  9.28 us
    dot_general x1, matrix products, banded_data(): jnp.einsum('pbkj,nj->pkbn', back4, block_basis(window), precision=lax.Pre...  8.28 us
    ppermute x8, starting transfers between devices, allreduce_rows(): other = lax.ppermute(cur, axis, [(i, i ^ bit) for i in range(n)])  8.21 us
    concatenate x12, other arithmetic, allreduce_rows(): cur = jnp.concatenate([first, second], axis=0)  7.33 us
  transfers between devices with their start and end apart: 20, of which 10 were waited for; matrix products, arithmetic and copies ran while one was open for 7% of the time, Pallas kernels for 8%

profile of v1, /device:TPU:0, one launch (start us, length us, event | category | flops | bytes accessed | tf_op | source)
XLA Modules:
  0.0 202.2 jit_solution(13597383688224947366)
XLA Ops:
  0.6 1.1 copy.663
  1.8 0.7 copy-done.6
  2.5 1.3 collective-permute-start.1
  3.8 5.5 %collective-permute-start = (f32[16,2,512]{2,0,1:T(8,128)S(1)}, f32[16,2,512]{2,0,1:T(8,128)S(1)}, u32[]{:S(2)}, u32[]{:S(2)}) collective-permute-start(f32[16,2,512]{2,0,1:T(8,128)S(1)} %get-tuple-element.150), channel_id=1, source_target_pairs={{0,4},{4,8},{8,12},{12,16},{16,20},{20,24},{24,28},{1,5},{5,9},{9,... | collective-permute-start | bytes 196616 | tf_op jit(solution)/shard_map/ppermute | solution.py:22
  9.4 1.9 collective-permute-done
  11.3 1.1 constant_dynamic-update-slice_fusion.3
  12.5 0.7 copy-done.8
  13.1 0.5 fusion.53
  15.4 2.7 %stack.75 = f32[16,16,12,128]{3,1,2,0:T(8,128)S(1)} concatenate(f32[16,1,12,128]{3,1,2,0:T(1,128)S(1)} %copy.666, f32[16,1,12,128]{3,1,2,0:T(1,128)S(1)} %copy.667, f32[16,1,12,128]{3,1,2,0:T(1,128)S(1)} %copy.668, f32[16,1,12,128]{3,1,2,0:T(1,128)S(1)} %copy.669, f32[16,1,12,128]{3,1,2,0:T(1,128)S(1)} %copy.670, f32[16,1,12,128]{3,1,2,0:T(1,128)S(1)} %copy.671, ...), dimensions={1} | concatenate | bytes 3145728 | tf_op jit(solution)/shard_map/stack | solution.py:67
  18.1 9.3 %fusion.2.a_ref = f32[16,16,12,512]{3,2,1,0:T(8,128)} fusion(f32[16,16,12,128]{3,1,2,0:T(8,128)S(1)} %stack.75, f32[512]{0:T(512)S(1)} %get-tuple-element.157, f32[512]{0:T(512)S(1)} %get-tuple-element.158, f32[512]{0:T(512)S(1)} %get-tuple-element.156, f32[512]{0:T(512)S(1)} %get-tuple-element.155, s32[512]{0:T(512)S(1)} %add_select_fusion, ...), kind=kOutput, calls=%fused_computation.4 | convolution fusion | flops 2416508928 | bytes 7875072 | tf_op jit(solution)/shard_map/pbkn,nj->pbkj/dot_general | solution.py:68
  27.3 0.7 broadcast_in_dim.55.w_ref
  28.0 8.4 %shard_map.120 = f32[128,2048]{1,0:T(8,128)} custom-call(f32[4,16,256]{2,1,0:T(8,128)} %broadcast_in_dim.55.w_ref, bf16[16,128,8192]{2,1,0:T(8,128)(2,1)} %cov_ref.15, f32[16,16,12,512]{3,2,1,0:T(8,128)} %fusion.2.a_ref), custom_call_target="tpu_custom_call" | custom-call | tf_op jit(solution)/shard_map/pallas_call | solution.py:163
  36.5 8.5 %shard_map.119 = f32[128,2048]{1,0:T(8,128)} custom-call(f32[4,16,256]{2,1,0:T(8,128)} %broadcast_in_dim.55.w_ref, bf16[16,128,8192]{2,1,0:T(8,128)(2,1)} %cov_ref.15, f32[16,16,12,512]{3,2,1,0:T(8,128)} %fusion.2.a_ref), custom_call_target="tpu_custom_call" | custom-call | tf_op jit(solution)/shard_map/pallas_call | solution.py:163
  45.0 0.9 dynamic-slice_bitcast_fusion.1
  45.9 1.9 dynamic-slice_bitcast_fusion.2
  47.7 8.4 %shard_map.118 = f32[128,2048]{1,0:T(8,128)} custom-call(f32[4,16,256]{2,1,0:T(8,128)} %broadcast_in_dim.55.w_ref, bf16[16,128,8192]{2,1,0:T(8,128)(2,1)} %cov_ref.15, f32[16,16,12,512]{3,2,1,0:T(8,128)} %fusion.2.a_ref), custom_call_target="tpu_custom_call" | custom-call | tf_op jit(solution)/shard_map/pallas_call | solution.py:163
  56.2 8.5 %shard_map.121 = f32[128,2048]{1,0:T(8,128)} custom-call(f32[4,16,256]{2,1,0:T(8,128)} %broadcast_in_dim.55.w_ref, bf16[16,128,8192]{2,1,0:T(8,128)(2,1)} %cov_ref.15, f32[16,16,12,512]{3,2,1,0:T(8,128)} %fusion.2.a_ref), custom_call_target="tpu_custom_call" | custom-call | tf_op jit(solution)/shard_map/pallas_call | solution.py:163
  64.7 0.5 collective-permute-start.6
  65.2 1.2 dynamic-slice_bitcast_fusion
  66.6 0.5 collective-permute-start.2
  67.1 1.1 bitcast_add_fusion.1
  68.2 2.0 collective-permute-start.11
  70.3 0.2 collective-permute-start.7
  70.6 2.0 collective-permute-start.15
  72.9 4.6 %collective-permute-done.11 = f32[32,2048]{1,0:T(8,128)S(1)} collective-permute-done((f32[32,2048]{1,0:T(8,128)S(1)}, f32[32,2048]{1,0:T(8,128)S(1)}, u32[]{:S(2)}, u32[]{:S(2)}) %collective-permute-start.11) | collective-permute-done | bytes 262176 | tf_op jit(solution)/shard_map/ppermute | solution.py:100
  77.5 2.0 collective-permute-start.12
  79.5 3.6 %collective-permute-done.7 = f32[32,2048]{1,0:T(8,128)S(1)} collective-permute-done((f32[32,2048]{1,0:T(8,128)S(1)}, f32[32,2048]{1,0:T(8,128)S(1)}, u32[]{:S(2)}, u32[]{:S(2)}) %collective-permute-start.7) | collective-permute-done | bytes 262176 | tf_op jit(solution)/shard_map/ppermute | solution.py:100
  83.1 2.0 collective-permute-start.8
  85.1 3.6 %collective-permute-done.15 = f32[32,2048]{1,0:T(8,128)S(1)} collective-permute-done((f32[32,2048]{1,0:T(8,128)S(1)}, f32[32,2048]{1,0:T(8,128)S(1)}, u32[]{:S(2)}, u32[]{:S(2)}) %collective-permute-start.15) | collective-permute-done | bytes 262176 | tf_op jit(solution)/shard_map/ppermute | solution.py:100
  88.7 2.0 collective-permute-start.16
  90.7 3.6 %collective-permute-done.3 = f32[32,2048]{1,0:T(8,128)S(1)} collective-permute-done((f32[32,2048]{1,0:T(8,128)S(1)}, f32[32,2048]{1,0:T(8,128)S(1)}, u32[]{:S(2)}, u32[]{:S(2)}) %collective-permute-start.3) | collective-permute-done | bytes 262176 | tf_op jit(solution)/shard_map/ppermute | solution.py:100
  94.3 2.0 collective-permute-start.4
  96.3 3.6 %collective-permute-done.12 = f32[32,2048]{1,0:T(8,128)S(1)} collective-permute-done((f32[32,2048]{1,0:T(8,128)S(1)}, f32[32,2048]{1,0:T(8,128)S(1)}, u32[]{:S(2)}, u32[]{:S(2)}) %collective-permute-start.12) | collective-permute-done | bytes 262176 | tf_op jit(solution)/shard_map/ppermute | solution.py:103
  100.1 5.4 %collective-permute-done.8 = f32[32,2048]{1,0:T(8,128)S(1)} collective-permute-done((f32[32,2048]{1,0:T(8,128)S(1)}, f32[32,2048]{1,0:T(8,128)S(1)}, u32[]{:S(2)}, u32[]{:S(2)}) %collective-permute-start.8) | collective-permute-done | bytes 262176 | tf_op jit(solution)/shard_map/ppermute | solution.py:103
  105.7 5.4 %collective-permute-done.16 = f32[32,2048]{1,0:T(8,128)S(1)} collective-permute-done((f32[32,2048]{1,0:T(8,128)S(1)}, f32[32,2048]{1,0:T(8,128)S(1)}, u32[]{:S(2)}, u32[]{:S(2)}) %collective-permute-start.16) | collective-permute-done | bytes 262176 | tf_op jit(solution)/shard_map/ppermute | solution.py:103
  111.3 4.8 %collective-permute-done.4 = f32[32,2048]{1,0:T(8,128)S(1)} collective-permute-done((f32[32,2048]{1,0:T(8,128)S(1)}, f32[32,2048]{1,0:T(8,128)S(1)}, u32[]{:S(2)}, u32[]{:S(2)}) %collective-permute-start.4) | collective-permute-done | bytes 262176 | tf_op jit(solution)/shard_map/ppermute | solution.py:103
  116.5 0.8 fusion.18
  117.2 0.7 fusion.19
  118.0 1.0 pad_maximum_fusion.3.t_ref
  119.1 0.8 fusion.17
  119.9 1.1 pad_maximum_fusion.2.t_ref
  120.9 1.0 pad_maximum_fusion.4.t_ref
  122.1 0.8 fusion.20
  122.8 1.0 pad_maximum_fusion.1.t_ref
  123.9 11.3 %shard_map.124 = f32[16,4,12,512]{3,2,1,0:T(8,128)} custom-call(f32[4,16,256]{2,1,0:T(8,128)} %broadcast_in_dim.55.w_ref, bf16[16,128,8192]{2,1,0:T(8,128)(2,1)} %cov_ref.15, f32[128,2048]{1,0:T(8,128)} %pad_maximum_fusion.3.t_ref, f32[128,8192]{1,0:T(8,128)} %y_ref.7, s32[128,8192]{1,0:T(8,128)} %g_ref.7), custom_call_target="tpu_custom_call" | custom-call | tf_op jit(solution)/shard_map/pallas_call | solution.py:181
  135.2 11.4 %shard_map.123 = f32[16,4,12,512]{3,2,1,0:T(8,128)} custom-call(f32[4,16,256]{2,1,0:T(8,128)} %broadcast_in_dim.55.w_ref, bf16[16,128,8192]{2,1,0:T(8,128)(2,1)} %cov_ref.15, f32[128,2048]{1,0:T(8,128)} %pad_maximum_fusion.2.t_ref, f32[128,8192]{1,0:T(8,128)} %y_ref.7, s32[128,8192]{1,0:T(8,128)} %g_ref.7), custom_call_target="tpu_custom_call" | custom-call | tf_op jit(solution)/shard_map/pallas_call | solution.py:181
  146.6 12.0 %shard_map.122 = f32[16,4,12,512]{3,2,1,0:T(8,128)} custom-call(f32[4,16,256]{2,1,0:T(8,128)} %broadcast_in_dim.55.w_ref, bf16[16,128,8192]{2,1,0:T(8,128)(2,1)} %cov_ref.15, f32[128,2048]{1,0:T(8,128)} %pad_maximum_fusion.1.t_ref, f32[128,8192]{1,0:T(8,128)} %y_ref.7, s32[128,8192]{1,0:T(8,128)} %g_ref.7), custom_call_target="tpu_custom_call" | custom-call | tf_op jit(solution)/shard_map/pallas_call | solution.py:181
  158.6 11.5 %shard_map.125 = f32[16,4,12,512]{3,2,1,0:T(8,128)} custom-call(f32[4,16,256]{2,1,0:T(8,128)} %broadcast_in_dim.55.w_ref, bf16[16,128,8192]{2,1,0:T(8,128)(2,1)} %cov_ref.15, f32[128,2048]{1,0:T(8,128)} %pad_maximum_fusion.4.t_ref, f32[128,8192]{1,0:T(8,128)} %y_ref.7, s32[128,8192]{1,0:T(8,128)} %g_ref.7), custom_call_target="tpu_custom_call" | custom-call | tf_op jit(solution)/shard_map/pallas_call | solution.py:181
  170.1 3.6 %pad_maximum_fusion = f32[16,16,12,512]{3,2,1,0:T(8,128)S(1)} fusion(f32[16,4,12,512]{3,2,1,0:T(8,128)} %shard_map.125, f32[16,4,12,512]{3,2,1,0:T(8,128)S(1)} %copy-done, f32[16,4,12,512]{3,2,1,0:T(8,128)} %shard_map.123, f32[16,4,12,512]{3,2,1,0:T(8,128)} %shard_map.122), kind=kLoop, calls=%fused_computation | loop fusion | flops 4718592 | bytes 12582912 | tf_op jit(solution)/shard_map/concatenate | solution.py:233
  173.7 8.3 %fusion.4 = f32[16,12,16,128]{3,2,1,0:T(8,128)S(1)} fusion(f32[16,16,12,512]{3,2,1,0:T(8,128)S(1)} %pad_maximum_fusion, f32[512]{0:T(512)S(1)} %get-tuple-element.157, f32[512]{0:T(512)S(1)} %get-tuple-element.158, f32[512]{0:T(512)S(1)} %get-tuple-element.156, f32[512]{0:T(512)S(1)} %get-tuple-element.155, s32[512]{0:T(512)S(1)} %add_select_fusion, ...), kind=kOutput, calls=%fused_computation.6 | convolution fusion | flops 2416508928 | bytes 7875072 | tf_op jit(solution)/shard_map/pbkj,nj->pkbn/dot_general | solution.py:75
  182.0 1.4 fusion.89
  183.4 1.1 pad_add_fusion
  184.5 0.5 reshape.241
  185.1 0.2 slice.171
  185.3 0.3 copy_multiply_fusion
  185.6 4.5 %collective-permute-start.18 = (f32[16,2,512]{2,0,1:T(8,128)S(1)}, f32[16,2,512]{2,0,1:T(8,128)S(1)}, u32[]{:S(2)}, u32[]{:S(2)}) collective-permute-start(f32[16,2,512]{2,0,1:T(8,128)S(1)} %get-tuple-element.128), channel_id=1, source_target_pairs={{0,4},{4,8},{8,12},{12,16},{16,20},{20,24},{24,28},{1,5},{5,9},{9,... | collective-permute-start | bytes 196616 | tf_op jit(solution)/shard_map/ppermute | solution.py:31
  190.2 1.4 collective-permute-start.19
  191.7 3.1 %subtract_multiply_fusion = (f32[32,8192]{1,0:T(8,128)}, f32[32,8192]{1,0:T(8,128)}) fusion(f32[128,8192]{1,0:T(8,128)} %y_ref.7, s32[]{:T(128)S(6)} %select_n.245, s32[128,8192]{1,0:T(8,128)} %g_ref.7, f32[32,2048]{1,0:T(8,128)S(1)} %copy-done.12, f32[32,2048]{1,0:T(8,128)S(1)} %copy-done.10, f32[32,2048]{1,0:T(8,128)S(1)} %copy-done.11, ...), kind=kLoop, calls=%fused_computation.20 | loop fusion | flops 1572864 | bytes 5242884 | tf_op jit(solution)/shard_map/mul | solution.py:232
  194.8 3.2 %collective-permute-done.19 = f32[16,2,512]{2,0,1:T(8,128)S(1)} collective-permute-done((f32[16,2,512]{2,0,1:T(8,128)S(1)}, f32[16,2,512]{2,0,1:T(8,128)S(1)}, u32[]{:S(2)}, u32[]{:S(2)}) %collective-permute-start.19) | collective-permute-done | bytes 65568 | tf_op jit(solution)/shard_map/ppermute | solution.py:31
  198.0 0.8 divide_subtract_fusion
  198.8 0.9 copy.696
  199.6 0.9 copy.697
  200.5 0.9 copy.698
  201.3 0.9 copy.695
  (100 shorter events, 3.6 us)
Async XLA Ops:
  1.7 0.7 copy-start.6
  2.5 10.0 %collective-permute-start.1 = (f32[16,2,512]{2,0,1:T(8,128)S(1)}, f32[16,2,512]{2,0,1:T(8,128)S(1)}, u32[]{:S(2)}, u32[]{:S(2)}) collective-permute-start(f32[16,2,512]{2,0,1:T(8,128)S(1)} %get-tuple-element.149), channel_id=1, source_target_pairs={{4,0},{8,4},{12,8},{16,12},{20,16},{24,20},{28,24},{5,1},{9,5},{13... | collective-permute-start | bytes 196616 | tf_op jit(solution)/shard_map/ppermute | solution.py:23
  3.8 7.5 %collective-permute-start = (f32[16,2,512]{2,0,1:T(8,128)S(1)}, f32[16,2,512]{2,0,1:T(8,128)S(1)}, u32[]{:S(2)}, u32[]{:S(2)}) collective-permute-start(f32[16,2,512]{2,0,1:T(8,128)S(1)} %get-tuple-element.150), channel_id=1, source_target_pairs={{0,4},{4,8},{8,12},{12,16},{16,20},{20,24},{24,28},{1,5},{5,9},{9,... | collective-permute-start | bytes 196616 | tf_op jit(solution)/shard_map/ppermute | solution.py:22
  12.4 0.7 copy-start.8
  36.5 8.5 %copy-start.4 = (f32[128,2048]{1,0:T(8,128)S(1)}, f32[128,2048]{1,0:T(8,128)}, u32[]{:S(2)}) copy-start(f32[128,2048]{1,0:T(8,128)} %shard_map.120) | copy-start | bytes 3145732
  45.9 21.2 %collective-permute-start.10 = (f32[64,2048]{1,0:T(8,128)}, f32[64,2048]{1,0:T(8,128)}, u32[]{:S(2)}, u32[]{:S(2)}) collective-permute-start(f32[64,2048]{1,0:T(8,128)} %dynamic-slice_bitcast_fusion.1), channel_id=1, source_target_pairs={{0,1},{1,0},{2,3},{3,2},{4,5},{5,4},{6,7},{7,6},{8,9},{9,8},{10,11... | collective-permute-start | bytes 1572872 | tf_op jit(solution)/shard_map/ppermute | solution.py:100
  56.2 10.3 %copy-start.1 = (f32[128,2048]{1,0:T(8,128)S(1)}, f32[128,2048]{1,0:T(8,128)}, u32[]{:S(2)}) copy-start(f32[128,2048]{1,0:T(8,128)} %shard_map.118) | copy-start | bytes 3145732
  64.7 5.5 %collective-permute-start.6 = (f32[64,2048]{1,0:T(8,128)}, f32[64,2048]{1,0:T(8,128)S(1)}, u32[]{:S(2)}, u32[]{:S(2)}) collective-permute-start(f32[64,2048]{1,0:T(8,128)} %dynamic-slice_bitcast_fusion.2), channel_id=1, source_target_pairs={{0,1},{1,0},{2,3},{3,2},{4,5},{5,4},{6,7},{7,6},{8,9},{9,8},{10,11... | collective-permute-start | bytes 1572872 | tf_op jit(solution)/shard_map/ppermute | solution.py:100
  65.2 5.0 %copy-start.3 = (f32[128,2048]{1,0:T(8,128)S(1)}, f32[128,2048]{1,0:T(8,128)}, u32[]{:S(2)}) copy-start(f32[128,2048]{1,0:T(8,128)} %shard_map.119) | copy-start | bytes 3145732
  66.4 4.1 %collective-permute-start.14 = (f32[64,2048]{1,0:T(8,128)S(1)}, f32[64,2048]{1,0:T(8,128)S(1)}, u32[]{:S(2)}, u32[]{:S(2)}) collective-permute-start(f32[64,2048]{1,0:T(8,128)S(1)} %dynamic-slice_bitcast_fusion), channel_id=1, source_target_pairs={{0,1},{1,0},{2,3},{3,2},{4,5},{5,4},{6,7},{7,6},{8,9},{9,8},{10,11... | collective-permute-start | bytes 1572872 | tf_op jit(solution)/shard_map/ppermute | solution.py:100
  66.5 4.0 %copy-start.2 = (f32[128,2048]{1,0:T(8,128)S(1)}, f32[128,2048]{1,0:T(8,128)}, u32[]{:S(2)}) copy-start(f32[128,2048]{1,0:T(8,128)} %shard_map.121) | copy-start | bytes 3145732
  66.6 6.0 %collective-permute-start.2 = (f32[64,2048]{1,0:T(8,128)S(1)}, f32[64,2048]{1,0:T(8,128)S(1)}, u32[]{:S(2)}, u32[]{:S(2)}) collective-permute-start(f32[64,2048]{1,0:T(8,128)S(1)} %dynamic-slice_bitcast_fusion.3), channel_id=1, source_target_pairs={{0,1},{1,0},{2,3},{3,2},{4,5},{5,4},{6,7},{7,6},{8,9},{9,8},{10,11... | collective-permute-start | bytes 1572872 | tf_op jit(solution)/shard_map/ppermute | solution.py:100
  68.2 9.2 %collective-permute-start.11 = (f32[32,2048]{1,0:T(8,128)S(1)}, f32[32,2048]{1,0:T(8,128)S(1)}, u32[]{:S(2)}, u32[]{:S(2)}) collective-permute-start(f32[32,2048]{1,0:T(8,128)S(1)} %dynamic-slice_bitcast_fusion.5), channel_id=1, source_target_pairs={{0,2},{1,3},{2,0},{3,1},{4,6},{5,7},{6,4},{7,5},{8,10},{9,11},{10,... | collective-permute-start | bytes 786440 | tf_op jit(solution)/shard_map/ppermute | solution.py:100
  70.3 12.8 %collective-permute-start.7 = (f32[32,2048]{1,0:T(8,128)S(1)}, f32[32,2048]{1,0:T(8,128)S(1)}, u32[]{:S(2)}, u32[]{:S(2)}) collective-permute-start(f32[32,2048]{1,0:T(8,128)S(1)} %dynamic-slice_bitcast_fusion.6), channel_id=1, source_target_pairs={{0,2},{1,3},{2,0},{3,1},{4,6},{5,7},{6,4},{7,5},{8,10},{9,11},{10,... | collective-permute-start | bytes 786440 | tf_op jit(solution)/shard_map/ppermute | solution.py:100
  70.6 18.1 %collective-permute-start.15 = (f32[32,2048]{1,0:T(8,128)S(1)}, f32[32,2048]{1,0:T(8,128)S(1)}, u32[]{:S(2)}, u32[]{:S(2)}) collective-permute-start(f32[32,2048]{1,0:T(8,128)S(1)} %dynamic-slice_bitcast_fusion.4), channel_id=1, source_target_pairs={{0,2},{1,3},{2,0},{3,1},{4,6},{5,7},{6,4},{7,5},{8,10},{9,11},{10,... | collective-permute-start | bytes 786440 | tf_op jit(solution)/shard_map/ppermute | solution.py:100
  72.7 21.6 %collective-permute-start.3 = (f32[32,2048]{1,0:T(8,128)S(1)}, f32[32,2048]{1,0:T(8,128)S(1)}, u32[]{:S(2)}, u32[]{:S(2)}) collective-permute-start(f32[32,2048]{1,0:T(8,128)S(1)} %dynamic-slice_bitcast_fusion.7), channel_id=1, source_target_pairs={{0,2},{1,3},{2,0},{3,1},{4,6},{5,7},{6,4},{7,5},{8,10},{9,11},{10,... | collective-permute-start | bytes 786440 | tf_op jit(solution)/shard_map/ppermute | solution.py:100
  77.5 22.4 %collective-permute-start.12 = (f32[32,2048]{1,0:T(8,128)S(1)}, f32[32,2048]{1,0:T(8,128)S(1)}, u32[]{:S(2)}, u32[]{:S(2)}) collective-permute-start(f32[32,2048]{1,0:T(8,128)S(1)} %bitcast_add_fusion.5), channel_id=1, source_target_pairs={{0,2},{1,3},{2,0},{3,1},{4,6},{5,7},{6,4},{7,5},{8,10},{9,11},{10,... | collective-permute-start | bytes 786440 | tf_op jit(solution)/shard_map/ppermute | solution.py:103
  83.1 22.4 %collective-permute-start.8 = (f32[32,2048]{1,0:T(8,128)S(1)}, f32[32,2048]{1,0:T(8,128)S(1)}, u32[]{:S(2)}, u32[]{:S(2)}) collective-permute-start(f32[32,2048]{1,0:T(8,128)S(1)} %bitcast_add_fusion.6), channel_id=1, source_target_pairs={{0,2},{1,3},{2,0},{3,1},{4,6},{5,7},{6,4},{7,5},{8,10},{9,11},{10,... | collective-permute-start | bytes 786440 | tf_op jit(solution)/shard_map/ppermute | solution.py:103
  88.7 22.4 %collective-permute-start.16 = (f32[32,2048]{1,0:T(8,128)S(1)}, f32[32,2048]{1,0:T(8,128)S(1)}, u32[]{:S(2)}, u32[]{:S(2)}) collective-permute-start(f32[32,2048]{1,0:T(8,128)S(1)} %bitcast_add_fusion.4), channel_id=1, source_target_pairs={{0,2},{1,3},{2,0},{3,1},{4,6},{5,7},{6,4},{7,5},{8,10},{9,11},{10,... | collective-permute-start | bytes 786440 | tf_op jit(solution)/shard_map/ppermute | solution.py:103
  94.3 21.8 %collective-permute-start.4 = (f32[32,2048]{1,0:T(8,128)S(1)}, f32[32,2048]{1,0:T(8,128)S(1)}, u32[]{:S(2)}, u32[]{:S(2)}) collective-permute-start(f32[32,2048]{1,0:T(8,128)S(1)} %bitcast_add_fusion.7), channel_id=1, source_target_pairs={{0,2},{1,3},{2,0},{3,1},{4,6},{5,7},{6,4},{7,5},{8,10},{9,11},{10,... | collective-permute-start | bytes 786440 | tf_op jit(solution)/shard_map/ppermute | solution.py:103
  100.0 16.3 %collective-permute-start.13 = (f32[64,2048]{1,0:T(8,128)S(1)}, f32[64,2048]{1,0:T(8,128)S(1)}, u32[]{:S(2)}, u32[]{:S(2)}) collective-permute-start(f32[64,2048]{1,0:T(8,128)S(1)} %pad_maximum_fusion.8), channel_id=1, source_target_pairs={{0,1},{1,0},{2,3},{3,2},{4,5},{5,4},{6,7},{7,6},{8,9},{9,8},{10,11... | collective-permute-start | bytes 1572872 | tf_op jit(solution)/shard_map/ppermute | solution.py:103
  105.6 10.7 %collective-permute-start.9 = (f32[64,2048]{1,0:T(8,128)S(1)}, f32[64,2048]{1,0:T(8,128)S(1)}, u32[]{:S(2)}, u32[]{:S(2)}) collective-permute-start(f32[64,2048]{1,0:T(8,128)S(1)} %pad_maximum_fusion.7), channel_id=1, source_target_pairs={{0,1},{1,0},{2,3},{3,2},{4,5},{5,4},{6,7},{7,6},{8,9},{9,8},{10,11... | collective-permute-start | bytes 1572872 | tf_op jit(solution)/shard_map/ppermute | solution.py:103
  111.2 7.8 %collective-permute-start.17 = (f32[64,2048]{1,0:T(8,128)S(1)}, f32[64,2048]{1,0:T(8,128)S(1)}, u32[]{:S(2)}, u32[]{:S(2)}) collective-permute-start(f32[64,2048]{1,0:T(8,128)S(1)} %pad_maximum_fusion.9), channel_id=1, source_target_pairs={{0,1},{1,0},{2,3},{3,2},{4,5},{5,4},{6,7},{7,6},{8,9},{9,8},{10,11... | collective-permute-start | bytes 1572872 | tf_op jit(solution)/shard_map/ppermute | solution.py:103
  116.2 5.8 %collective-permute-start.5 = (f32[64,2048]{1,0:T(8,128)S(1)}, f32[64,2048]{1,0:T(8,128)S(1)}, u32[]{:S(2)}, u32[]{:S(2)}) collective-permute-start(f32[64,2048]{1,0:T(8,128)S(1)} %pad_maximum_fusion.6), channel_id=1, source_target_pairs={{0,1},{1,0},{2,3},{3,2},{4,5},{5,4},{6,7},{7,6},{8,9},{9,8},{10,11... | collective-permute-start | bytes 1572872 | tf_op jit(solution)/shard_map/ppermute | solution.py:103
  158.6 11.5 %copy-start = (f32[16,4,12,512]{3,2,1,0:T(8,128)S(1)}, f32[16,4,12,512]{3,2,1,0:T(8,128)}, u32[]{:S(2)}) copy-start(f32[16,4,12,512]{3,2,1,0:T(8,128)} %shard_map.124) | copy-start | bytes 4718596
  185.1 6.6 %copy-start.10 = (f32[32,2048]{1,0:T(8,128)S(1)}, f32[32,2048]{1,0:T(8,128)}, u32[]{:S(2)}) copy-start(f32[32,2048]{1,0:T(8,128)} %fusion.18) | copy-start | bytes 786436
  185.1 6.6 %copy-start.11 = (f32[32,2048]{1,0:T(8,128)S(1)}, f32[32,2048]{1,0:T(8,128)}, u32[]{:S(2)}) copy-start(f32[32,2048]{1,0:T(8,128)} %fusion.19) | copy-start | bytes 786436
  185.1 6.6 %copy-start.12 = (f32[32,2048]{1,0:T(8,128)S(1)}, f32[32,2048]{1,0:T(8,128)}, u32[]{:S(2)}) copy-start(f32[32,2048]{1,0:T(8,128)} %fusion.17) | copy-start | bytes 786436
  185.1 6.6 %copy-start.13 = (f32[32,2048]{1,0:T(8,128)S(1)}, f32[32,2048]{1,0:T(8,128)}, u32[]{:S(2)}) copy-start(f32[32,2048]{1,0:T(8,128)} %fusion.20) | copy-start | bytes 786436
  185.6 9.2 %collective-permute-start.18 = (f32[16,2,512]{2,0,1:T(8,128)S(1)}, f32[16,2,512]{2,0,1:T(8,128)S(1)}, u32[]{:S(2)}, u32[]{:S(2)}) collective-permute-start(f32[16,2,512]{2,0,1:T(8,128)S(1)} %get-tuple-element.128), channel_id=1, source_target_pairs={{0,4},{4,8},{8,12},{12,16},{16,20},{20,24},{24,28},{1,5},{5,9},{9,... | collective-permute-start | bytes 196616 | tf_op jit(solution)/shard_map/ppermute | solution.py:31
  190.1 7.8 %copy-start.5 = (f32[16,8,512]{2,1,0:T(8,128)S(1)}, f32[16,8,512]{2,1,0:T(8,128)}, u32[]{:S(2)}) copy-start(f32[16,8,512]{2,1,0:T(8,128)} %param.10) | copy-start | bytes 786436
  190.1 7.8 %copy-start.7 = (f32[16,8,512]{2,0,1:T(8,128)S(1)}, f32[16,8,512]{2,0,1:T(8,128)}, u32[]{:S(2)}) copy-start(f32[16,8,512]{2,0,1:T(8,128)} %copy-done.6) | copy-start | bytes 786436
  190.2 7.8 %copy-start.9 = (f32[16,10,512]{2,0,1:T(8,128)S(1)}, f32[16,10,512]{2,0,1:T(8,128)}, u32[]{:S(2)}) copy-start(f32[16,10,512]{2,0,1:T(8,128)} %copy-done.8) | copy-start | bytes 983044
  190.2 7.8 %copy-start.14 = (f32[16,8,512]{2,1,0:T(8,128)S(1)}, f32[16,8,512]{2,1,0:T(8,128)}, u32[]{:S(2)}) copy-start(f32[16,8,512]{2,1,0:T(8,128)} %param.11) | copy-start | bytes 786436
  190.2 7.8 %copy-start.15 = (f32[16,8,512]{2,1,0:T(8,128)S(1)}, f32[16,8,512]{2,1,0:T(8,128)}, u32[]{:S(2)}) copy-start(f32[16,8,512]{2,1,0:T(8,128)} %param.12) | copy-start | bytes 786436
  190.2 7.8 %copy-start.16 = (f32[16]{0:T(128)S(1)}, f32[16]{0:T(128)}, u32[]{:S(2)}) copy-start(f32[16]{0:T(128)} %param.13) | copy-start | bytes 196
  190.2 7.8 %collective-permute-start.19 = (f32[16,2,512]{2,0,1:T(8,128)S(1)}, f32[16,2,512]{2,0,1:T(8,128)S(1)}, u32[]{:S(2)}, u32[]{:S(2)}) collective-permute-start(f32[16,2,512]{2,0,1:T(8,128)S(1)} %get-tuple-element.129), channel_id=1, source_target_pairs={{4,0},{8,4},{12,8},{16,12},{20,16},{24,20},{28,24},{5,1},{9,5},{13... | collective-permute-start | bytes 196616 | tf_op jit(solution)/shard_map/ppermute | solution.py:31

commit v2 on v1

--- a/solution.py
+++ b/solution.py
@@ -65,14 +65,14 @@
     right = per_block * (blocks - 1) + window - knots - LEAD
     cpad = jnp.pad(padded, ((0, 0), (0, 0), (LEAD, right)))
     cwin = jnp.stack([cpad[..., per_block * b : per_block * b + window] for b in range(blocks)], axis=1)
-    return jnp.einsum("pbkn,nj->pbkj", cwin, block_basis(window), precision=lax.Precision.HIGHEST)
+    return jnp.einsum("pbkn,nj->pbkj", cwin, block_basis(window), precision=lax.Precision.HIGH)
 
 
 def banded_data(back4, knots):
     npred, blocks, nrow, _ = back4.shape
     per_block = TN // H
     window = 4 * per_block
-    dwin = jnp.einsum("pbkj,nj->pkbn", back4, block_basis(window), precision=lax.Precision.HIGHEST)
+    dwin = jnp.einsum("pbkj,nj->pkbn", back4, block_basis(window), precision=lax.Precision.HIGH)
     total = None
     for a in range(4):
         part = dwin[..., a * per_block : (a + 1) * per_block]
@@ -82,7 +82,7 @@
     return total[..., LEAD : LEAD + knots]
 
 
-def allreduce_rows(x, axis):
+def reduce_steps(x, axis):
     n = lax.axis_size(axis)
     idx = lax.axis_index(axis)
     bits = []
@@ -90,21 +90,26 @@
     while bit < n:
         bits.append(bit)
         bit *= 2
-    cur = x
+    steps = []
     for bit in bits:
-        half = cur.shape[0] // 2
-        mine = (idx // bit) % 2
-        pair = cur.reshape((2, half) + cur.shape[1:])
-        keep = lax.dynamic_index_in_dim(pair, mine, 0, keepdims=False)
-        send = lax.dynamic_index_in_dim(pair, 1 - mine, 0, keepdims=False)
-        cur = keep + lax.ppermute(send, axis, [(i, i ^ bit) for i in range(n)])
+        def halve(cur, bit=bit):
+            half = cur.shape[0] // 2
+            mine = (idx // bit) % 2
+            pair = cur.reshape((2, half) + cur.shape[1:])
+            keep = lax.dynamic_index_in_dim(pair, mine, 0, keepdims=False)
+            send = lax.dynamic_index_in_dim(pair, 1 - mine, 0, keepdims=False)
+            return send, lambda recv: keep + recv
+        steps.append((bit, halve))
     for bit in reversed(bits):
-        mine = (idx // bit) % 2
-        other = lax.ppermute(cur, axis, [(i, i ^ bit) for i in range(n)])
-        first = jnp.where(mine == 0, cur, other)
-        second = jnp.where(mine == 0, other, cur)
-        cur = jnp.concatenate([first, second], axis=0)
-    return cur
+        def double(cur, bit=bit):
+            mine = (idx // bit) % 2
+            def finish(other):
+                first = jnp.where(mine == 0, cur, other)
+                second = jnp.where(mine == 0, other, cur)
+                return jnp.concatenate([first, second], axis=0)
+            return cur, finish
+        steps.append((bit, double))
+    return [(bit, fn, [(i, i ^ bit) for i in range(n)]) for bit, fn in steps]
 
 
 def fit_kernel(w_ref, cov_ref, a_ref, o_ref):
@@ -171,6 +176,11 @@
         out_specs=pl.BlockSpec((rows, TN), lambda j: (0, j)),
         out_shape=jax.ShapeDtypeStruct((rows, width), jnp.float32),
         compiler_params=pltpu.CompilerParams(dimension_semantics=("arbitrary",)),
+        cost_estimate=pl.CostEstimate(
+            flops=10 * npred * rows * width,
+            transcendentals=0,
+            bytes_accessed=2 * npred * rows * width + 4 * npred * nrow * width + 4 * rows * width,
+        ),
     )(wl, cov, along)
 
 
@@ -192,6 +202,11 @@
         out_shape=jax.ShapeDtypeStruct((npred, width // TN, nrow, TN), jnp.float32),
         scratch_shapes=[pltpu.VMEM((4, rows, L), jnp.float32)],
         compiler_params=pltpu.CompilerParams(dimension_semantics=("arbitrary",)),
+        cost_estimate=pl.CostEstimate(
+            flops=10 * npred * rows * width,
+            transcendentals=0,
+            bytes_accessed=2 * npred * rows * width + 12 * rows * width + 4 * npred * nrow * width,
+        ),
     )(wl, cov, total, target, land)
 
 
@@ -222,12 +237,43 @@
     target_blk = lax.dynamic_slice_in_dim(target, start, share, 0)
     land_blk = lax.dynamic_slice_in_dim(land, start, share, 0).astype(jnp.float32)
     width = ny // CHUNKS
-    fitted_parts, back_parts = [], []
+    steps = reduce_steps(jnp.zeros((rows, width), jnp.float32), "pred")
+    nsteps = len(steps)
+    state = [None] * CHUNKS
+    fitted_parts = [None] * CHUNKS
+    back_parts = [None] * CHUNKS
+    state[0] = fit_chunk(wl, covariates, along, 0, width)
+    for s in range(1, CHUNKS + nsteps + 1):
+        pending = []
+        for c in range(CHUNKS):
+            k = s - c - 1
+            if 0 <= k < nsteps:
+                _, fn, pairs = steps[k]
+                send, finish = fn(state[c])
+                pending.append((c, finish, lax.ppermute(send, "pred", pairs)))
+        filler = None
+        if s < CHUNKS:
+            filler = ("fit", s)
+        elif 0 <= s - nsteps - 1 < CHUNKS:
+            filler = ("back", s - nsteps - 1)
+        recvs = [r for _, _, r in pending]
+        if filler is not None:
+            kind, c = filler
+            if kind == "fit":
+                out = fit_chunk(wl, covariates, along, c, width)
+            else:
+                out = back_chunk(wl, covariates, state[c], target, land, c, nrow)
+            recvs, out = lax.optimization_barrier((recvs, out))
+            if kind == "fit":
+                state[c] = out
+            else:
+                back_parts[c] = out
+        for (c, finish, _), r in zip(pending, recvs):
+            state[c] = finish(r)
     for c in range(CHUNKS):
-        partial = fit_chunk(wl, covariates, along, c, width)
-        total = allreduce_rows(partial, "pred")
-        back_parts.append(back_chunk(wl, covariates, total, target, land, c, nrow))
-        fitted_parts.append(lax.dynamic_slice_in_dim(total, start, share, 0))
+        if back_parts[c] is None:
+            back_parts[c] = back_chunk(wl, covariates, state[c], target, land, c, nrow)
+        fitted_parts[c] = lax.dynamic_slice_in_dim(state[c], start, share, 0)
     fitted = jnp.concatenate(fitted_parts, axis=1)
     residual = land_blk * (target_blk - fitted)
     back = jnp.concatenate(back_parts, axis=1)

time: 203 us -> 180 us (0.89)
  waiting for transfers between devices: 39.7 us -> 18.1 us
  other arithmetic: 18.2 us -> 26.7 us
  matrix products: 17.6 us -> 12.1 us
  starting transfers between devices: 26.4 us -> 22.5 us
    ppermute x16, waiting for transfers between devices: 34.7 us -> 13 us  [local(): pending.append((c, finish, lax.ppermute(send, 'pred', pairs)))]
    ppermute x16, starting transfers between devices: 13.6 us -> 10.1 us  [local(): pending.append((c, finish, lax.ppermute(send, 'pred', pairs)))]
    dot_general x1, matrix products: 9.28 us -> 6 us  [banded_along(): jnp.einsum('pbkn,nj->pbkj', cwin, block_basis(window), precision=lax.Prec...]
    add x8, other arithmetic: 1.41 us -> 4.44 us  [halve(): return (send, lambda recv: keep + recv)]
    select_n x8, other arithmetic: 0.54 us -> 3.54 us  [the longest x7 2.42 us: finish(): first = jnp.where(mine == 0, cur, other)]
    concatenate x12, other arithmetic: 7.33 us -> 9.67 us  [finish(): return jnp.concatenate([first, second], axis=0)]
    dot_general x1, matrix products: 8.28 us -> 6.08 us  [banded_data(): jnp.einsum('pbkj,nj->pkbn', back4, block_basis(window), precision=lax.Pre...]
  transfers between devices with their start and end apart: 20 -> 20, of which waited for: 10 -> 5; matrix products, arithmetic and copies ran while one was open for 7% -> 8% of each run, Pallas kernels for 8% -> 34%
where the time goes in v2:
time: 180 us
  Pallas kernels  80.1 us (44%)
  other arithmetic  26.7 us (15%)
  starting transfers between devices  22.5 us (12%)
  local copies, waits for them, and re-layouts  18.6 us (10%)
  waiting for transfers between devices  18.1 us (10%)
  matrix products  12.1 us (7%)
    pallas_call x4, Pallas kernels, back_chunk(): pl.pallas_call(back_kernel, grid=(width // TN,), in_specs=[pl.BlockSpec((...  46.2 us
    pallas_call x4, Pallas kernels, fit_chunk(): pl.pallas_call(fit_kernel, grid=(width // TN,), in_specs=[pl.BlockSpec((4...  33.9 us
    ppermute x16, waiting for transfers between devices, local(): pending.append((c, finish, lax.ppermute(send, 'pred', pairs)))  13 us
    ppermute x16, starting transfers between devices, local(): pending.append((c, finish, lax.ppermute(send, 'pred', pairs)))  10.1 us
    concatenate x12, other arithmetic, finish(): return jnp.concatenate([first, second], axis=0)  9.67 us
    dot_general x1, matrix products, banded_data(): jnp.einsum('pbkj,nj->pkbn', back4, block_basis(window), precision=lax.Pre...  6.08 us
    unnamed x40, local copies, waits for them, and re-layouts  6.04 us
    dot_general x1, matrix products, banded_along(): jnp.einsum('pbkn,nj->pbkj', cwin, block_basis(window), precision=lax.Prec...  6 us
  transfers between devices with their start and end apart: 20, of which 5 were waited for; matrix products, arithmetic and copies ran while one was open for 8% of the time, Pallas kernels for 34%

profile of v2, /device:TPU:0, one launch (start us, length us, event | category | flops | bytes accessed | tf_op | source)
XLA Modules:
  0.0 179.5 jit_solution(13486721567836867641)
XLA Ops:
  0.6 1.1 copy.663
  1.8 0.7 copy-done.6
  2.5 1.3 collective-permute-start.1
  3.8 5.5 %collective-permute-start = (f32[16,2,512]{2,0,1:T(8,128)S(1)}, f32[16,2,512]{2,0,1:T(8,128)S(1)}, u32[]{:S(2)}, u32[]{:S(2)}) collective-permute-start(f32[16,2,512]{2,0,1:T(8,128)S(1)} %get-tuple-element.186), channel_id=1, source_target_pairs={{0,4},{4,8},{8,12},{12,16},{16,20},{20,24},{24,28},{1,5},{5,9},{9,... | collective-permute-start | bytes 196616 | tf_op jit(solution)/shard_map/ppermute | solution.py:22
  9.4 1.9 %collective-permute-done = f32[16,2,512]{2,0,1:T(8,128)S(1)} collective-permute-done((f32[16,2,512]{2,0,1:T(8,128)S(1)}, f32[16,2,512]{2,0,1:T(8,128)S(1)}, u32[]{:S(2)}, u32[]{:S(2)}) %collective-permute-start) | collective-permute-done | bytes 65568 | tf_op jit(solution)/shard_map/ppermute | solution.py:22
  11.3 1.1 constant_dynamic-update-slice_fusion.3
  12.5 0.7 copy-done.8
  13.2 0.5 fusion.53
  15.4 2.7 %stack.75 = f32[16,16,12,128]{3,1,2,0:T(8,128)S(1)} concatenate(f32[16,1,12,128]{3,1,2,0:T(1,128)S(1)} %copy.666, f32[16,1,12,128]{3,1,2,0:T(1,128)S(1)} %copy.667, f32[16,1,12,128]{3,1,2,0:T(1,128)S(1)} %copy.668, f32[16,1,12,128]{3,1,2,0:T(1,128)S(1)} %copy.669, f32[16,1,12,128]{3,1,2,0:T(1,128)S(1)} %copy.670, f32[16,1,12,128]{3,1,2,0:T(1,128)S(1)} %copy.671, ...), dimensions={1} | concatenate | bytes 3145728 | tf_op jit(solution)/shard_map/stack | solution.py:67
  18.1 6.0 %fusion.2.a_ref = f32[16,16,12,512]{3,2,1,0:T(8,128)} fusion(f32[16,16,12,128]{3,1,2,0:T(8,128)S(1)} %stack.75, f32[512]{0:T(512)S(1)} %get-tuple-element.193, f32[512]{0:T(512)S(1)} %get-tuple-element.194, f32[512]{0:T(512)S(1)} %get-tuple-element.192, f32[512]{0:T(512)S(1)} %get-tuple-element.191, s32[512]{0:T(512)S(1)} %add_select_fusion, ...), kind=kOutput, calls=%fused_computation.4 | convolution fusion | flops 1208549376 | bytes 7875072 | tf_op jit(solution)/shard_map/pbkn,nj->pbkj/dot_general | solution.py:68
  24.1 0.7 broadcast_in_dim.55.w_ref
  24.8 8.4 %shard_map.118 = f32[128,2048]{1,0:T(8,128)} custom-call(f32[4,16,256]{2,1,0:T(8,128)} %broadcast_in_dim.55.w_ref, bf16[16,128,8192]{2,1,0:T(8,128)(2,1)} %cov_ref.15, f32[16,16,12,512]{3,2,1,0:T(8,128)} %fusion.2.a_ref), custom_call_target="tpu_custom_call" | custom-call | flops 41943040 | bytes 11010048 | tf_op jit(solution)/shard_map/pallas_call | solution.py:168
  33.2 1.1 dynamic-slice_bitcast_fusion.3
  34.4 8.5 %shard_map.119 = f32[128,2048]{1,0:T(8,128)} custom-call(f32[4,16,256]{2,1,0:T(8,128)} %broadcast_in_dim.55.w_ref, bf16[16,128,8192]{2,1,0:T(8,128)(2,1)} %cov_ref.15, f32[16,16,12,512]{3,2,1,0:T(8,128)} %fusion.2.a_ref), custom_call_target="tpu_custom_call" | custom-call | flops 41943040 | bytes 11010048 | tf_op jit(solution)/shard_map/pallas_call | solution.py:168
  43.0 1.1 dynamic-slice_bitcast_fusion.2
  44.0 0.5 collective-permute-start.4
  44.6 0.7 dynamic-slice_bitcast_fusion.7
  45.3 1.9 %collective-permute-start.3 = (f32[32,2048]{1,0:T(8,128)}, f32[32,2048]{1,0:T(8,128)}, u32[]{:S(2)}, u32[]{:S(2)}) collective-permute-start(f32[32,2048]{1,0:T(8,128)} %dynamic-slice_bitcast_fusion.7), channel_id=1, source_target_pairs={{0,2},{1,3},{2,0},{3,1},{4,6},{5,7},{6,4},{7,5},{8,10},{9,11},{10,... | collective-permute-start | bytes 786440 | tf_op jit(solution)/shard_map/ppermute | solution.py:253
  47.2 8.5 %shard_map.120 = f32[128,2048]{1,0:T(8,128)} custom-call(f32[4,16,256]{2,1,0:T(8,128)} %broadcast_in_dim.55.w_ref, bf16[16,128,8192]{2,1,0:T(8,128)(2,1)} %cov_ref.15, f32[16,16,12,512]{3,2,1,0:T(8,128)} %fusion.2.a_ref), custom_call_target="tpu_custom_call" | custom-call | flops 41943040 | bytes 11010048 | tf_op jit(solution)/shard_map/pallas_call | solution.py:168
  55.8 1.2 bitcast_add_fusion.2
  57.2 0.8 dynamic-slice_bitcast_fusion.1
  58.0 1.0 bitcast_add_fusion.7
  59.0 2.0 %collective-permute-start.5 = (f32[32,2048]{1,0:T(8,128)S(1)}, f32[32,2048]{1,0:T(8,128)S(1)}, u32[]{:S(2)}, u32[]{:S(2)}) collective-permute-start(f32[32,2048]{1,0:T(8,128)S(1)} %bitcast_add_fusion.7), channel_id=1, source_target_pairs={{0,2},{1,3},{2,0},{3,1},{4,6},{5,7},{6,4},{7,5},{8,10},{9,11},{10,... | collective-permute-start | bytes 786440 | tf_op jit(solution)/shard_map/ppermute | solution.py:253
  61.0 8.4 %shard_map.121 = f32[128,2048]{1,0:T(8,128)} custom-call(f32[4,16,256]{2,1,0:T(8,128)} %broadcast_in_dim.55.w_ref, bf16[16,128,8192]{2,1,0:T(8,128)(2,1)} %cov_ref.15, f32[16,16,12,512]{3,2,1,0:T(8,128)} %fusion.2.a_ref), custom_call_target="tpu_custom_call" | custom-call | flops 41943040 | bytes 11010048 | tf_op jit(solution)/shard_map/pallas_call | solution.py:168
  69.4 1.3 collective-permute-done.5
  70.8 1.1 bitcast_add_fusion.6
  72.2 1.7 collective-permute-start.9
  74.2 0.5 collective-permute-start.13
  74.7 6.4 %collective-permute-done.11 = f32[32,2048]{1,0:T(8,128)S(1)} collective-permute-done((f32[32,2048]{1,0:T(8,128)S(1)}, f32[32,2048]{1,0:T(8,128)S(1)}, u32[]{:S(2)}, u32[]{:S(2)}) %collective-permute-start.11) | collective-permute-done | bytes 262176 | tf_op jit(solution)/shard_map/ppermute | solution.py:253
  81.6 5.2 %collective-permute-done.9 = f32[32,2048]{1,0:T(8,128)S(1)} collective-permute-done((f32[32,2048]{1,0:T(8,128)S(1)}, f32[32,2048]{1,0:T(8,128)S(1)}, u32[]{:S(2)}, u32[]{:S(2)}) %collective-permute-start.9) | collective-permute-done | bytes 262176 | tf_op jit(solution)/shard_map/ppermute | solution.py:253
  86.8 0.8 pad_maximum_fusion.7
  88.2 1.0 pad_maximum_fusion.1.t_ref
  89.3 12.0 %shard_map.122 = f32[16,4,12,512]{3,2,1,0:T(8,128)} custom-call(f32[4,16,256]{2,1,0:T(8,128)} %broadcast_in_dim.55.w_ref, bf16[16,128,8192]{2,1,0:T(8,128)(2,1)} %cov_ref.15, f32[128,2048]{1,0:T(8,128)} %pad_maximum_fusion.1.t_ref, f32[128,8192]{1,0:T(8,128)} %y_ref.7, s32[128,8192]{1,0:T(8,128)} %g_ref.7), custom_call_target="tpu_custom_call" | custom-call | flops 41943040 | bytes 13107200 | tf_op jit(solution)/shard_map/pallas_call | solution.py:191
  101.3 0.7 fusion.20
  102.0 1.1 broadcast_select_fusion.5
  103.1 1.0 broadcast_select_fusion.11
  104.1 0.8 pad_maximum_fusion.8
  105.2 1.0 bitcast_add_fusion.4
  106.2 1.8 collective-permute-start.16
  108.0 1.0 pad_maximum_fusion.2.t_ref
  109.0 11.4 %shard_map.123 = f32[16,4,12,512]{3,2,1,0:T(8,128)} custom-call(f32[4,16,256]{2,1,0:T(8,128)} %broadcast_in_dim.55.w_ref, bf16[16,128,8192]{2,1,0:T(8,128)(2,1)} %cov_ref.15, f32[128,2048]{1,0:T(8,128)} %pad_maximum_fusion.2.t_ref, f32[128,8192]{1,0:T(8,128)} %y_ref.7, s32[128,8192]{1,0:T(8,128)} %g_ref.7), custom_call_target="tpu_custom_call" | custom-call | flops 41943040 | bytes 13107200 | tf_op jit(solution)/shard_map/pallas_call | solution.py:191
  120.4 0.7 fusion.19
  121.2 0.8 pad_maximum_fusion.9
  122.1 1.0 pad_maximum_fusion.3.t_ref
  123.2 11.3 %shard_map.124 = f32[16,4,12,512]{3,2,1,0:T(8,128)} custom-call(f32[4,16,256]{2,1,0:T(8,128)} %broadcast_in_dim.55.w_ref, bf16[16,128,8192]{2,1,0:T(8,128)(2,1)} %cov_ref.15, f32[128,2048]{1,0:T(8,128)} %pad_maximum_fusion.3.t_ref, f32[128,8192]{1,0:T(8,128)} %y_ref.7, s32[128,8192]{1,0:T(8,128)} %g_ref.7), custom_call_target="tpu_custom_call" | custom-call | flops 41943040 | bytes 13107200 | tf_op jit(solution)/shard_map/pallas_call | solution.py:191
  134.5 0.7 fusion.18
  135.3 1.1 broadcast_select_fusion
  136.4 0.8 fusion.17
  137.1 1.0 pad_maximum_fusion.4.t_ref
  138.2 11.5 %shard_map.125 = f32[16,4,12,512]{3,2,1,0:T(8,128)} custom-call(f32[4,16,256]{2,1,0:T(8,128)} %broadcast_in_dim.55.w_ref, bf16[16,128,8192]{2,1,0:T(8,128)(2,1)} %cov_ref.15, f32[128,2048]{1,0:T(8,128)} %pad_maximum_fusion.4.t_ref, f32[128,8192]{1,0:T(8,128)} %y_ref.7, s32[128,8192]{1,0:T(8,128)} %g_ref.7), custom_call_target="tpu_custom_call" | custom-call | flops 41943040 | bytes 13107200 | tf_op jit(solution)/shard_map/pallas_call | solution.py:191
  149.7 3.7 %pad_maximum_fusion = f32[16,16,12,512]{3,2,1,0:T(8,128)S(1)} fusion(f32[16,4,12,512]{3,2,1,0:T(8,128)} %shard_map.125, f32[16,4,12,512]{3,2,1,0:T(8,128)} %shard_map.124, f32[16,4,12,512]{3,2,1,0:T(8,128)} %shard_map.123, f32[16,4,12,512]{3,2,1,0:T(8,128)S(1)} %copy-done), kind=kLoop, calls=%fused_computation | loop fusion | flops 4718592 | bytes 12582912 | tf_op jit(solution)/shard_map/concatenate | solution.py:279
  153.5 6.1 %fusion.4 = f32[16,12,16,128]{3,2,1,0:T(8,128)S(1)} fusion(f32[16,16,12,512]{3,2,1,0:T(8,128)S(1)} %pad_maximum_fusion, f32[512]{0:T(512)S(1)} %get-tuple-element.193, f32[512]{0:T(512)S(1)} %get-tuple-element.194, f32[512]{0:T(512)S(1)} %get-tuple-element.192, f32[512]{0:T(512)S(1)} %get-tuple-element.191, s32[512]{0:T(512)S(1)} %add_select_fusion, ...), kind=kOutput, calls=%fused_computation.6 | convolution fusion | flops 1208549376 | bytes 7875072 | tf_op jit(solution)/shard_map/pbkj,nj->pkbn/dot_general | solution.py:75
  159.6 1.4 fusion.89
  160.9 1.1 pad_add_fusion
  162.1 0.5 reshape.241
  163.1 4.3 %collective-permute-start.18 = (f32[16,2,512]{2,0,1:T(8,128)S(1)}, f32[16,2,512]{2,0,1:T(8,128)S(1)}, u32[]{:S(2)}, u32[]{:S(2)}) collective-permute-start(f32[16,2,512]{2,0,1:T(8,128)S(1)} %get-tuple-element.164), channel_id=1, source_target_pairs={{0,4},{4,8},{8,12},{12,16},{16,20},{20,24},{24,28},{1,5},{5,9},{9,... | collective-permute-start | bytes 196616 | tf_op jit(solution)/shard_map/ppermute | solution.py:31
  167.5 1.4 collective-permute-start.19
  169.0 3.1 %subtract_multiply_fusion = (f32[32,8192]{1,0:T(8,128)}, f32[32,8192]{1,0:T(8,128)}) fusion(f32[128,8192]{1,0:T(8,128)} %y_ref.7, s32[]{:T(128)S(6)} %select_n.245, s32[128,8192]{1,0:T(8,128)} %g_ref.7, f32[32,2048]{1,0:T(8,128)S(1)} %copy-done.13, f32[32,2048]{1,0:T(8,128)S(1)} %copy-done.12, f32[32,2048]{1,0:T(8,128)S(1)} %copy-done.11, ...), kind=kLoop, calls=%fused_computation.20 | loop fusion | flops 1572864 | bytes 5242884 | tf_op jit(solution)/shard_map/mul | solution.py:278
  172.1 3.2 %collective-permute-done.19 = f32[16,2,512]{2,0,1:T(8,128)S(1)} collective-permute-done((f32[16,2,512]{2,0,1:T(8,128)S(1)}, f32[16,2,512]{2,0,1:T(8,128)S(1)}, u32[]{:S(2)}, u32[]{:S(2)}) %collective-permute-start.19) | collective-permute-done | bytes 65568 | tf_op jit(solution)/shard_map/ppermute | solution.py:31
  175.3 0.8 divide_subtract_fusion
  176.1 0.9 copy.696
  177.0 0.9 copy.697
  177.8 0.9 copy.698
  178.7 0.9 copy.695
  (100 shorter events, 4.7 us)
Async XLA Ops:
  1.7 0.7 copy-start.6
  2.5 10.0 %collective-permute-start.1 = (f32[16,2,512]{2,0,1:T(8,128)S(1)}, f32[16,2,512]{2,0,1:T(8,128)S(1)}, u32[]{:S(2)}, u32[]{:S(2)}) collective-permute-start(f32[16,2,512]{2,0,1:T(8,128)S(1)} %get-tuple-element.185), channel_id=1, source_target_pairs={{4,0},{8,4},{12,8},{16,12},{20,16},{24,20},{28,24},{5,1},{9,5},{13... | collective-permute-start | bytes 196616 | tf_op jit(solution)/shard_map/ppermute | solution.py:23
  3.8 7.5 %collective-permute-start = (f32[16,2,512]{2,0,1:T(8,128)S(1)}, f32[16,2,512]{2,0,1:T(8,128)S(1)}, u32[]{:S(2)}, u32[]{:S(2)}) collective-permute-start(f32[16,2,512]{2,0,1:T(8,128)S(1)} %get-tuple-element.186), channel_id=1, source_target_pairs={{0,4},{4,8},{8,12},{12,16},{16,20},{20,24},{24,28},{1,5},{5,9},{9,... | collective-permute-start | bytes 196616 | tf_op jit(solution)/shard_map/ppermute | solution.py:22
  12.4 0.7 copy-start.8
  34.3 8.7 %collective-permute-start.2 = (f32[64,2048]{1,0:T(8,128)S(1)}, f32[64,2048]{1,0:T(8,128)S(1)}, u32[]{:S(2)}, u32[]{:S(2)}) collective-permute-start(f32[64,2048]{1,0:T(8,128)S(1)} %dynamic-slice_bitcast_fusion.3), channel_id=1, source_target_pairs={{0,1},{1,0},{2,3},{3,2},{4,5},{5,4},{6,7},{7,6},{8,9},{9,8},{10,11... | collective-permute-start | bytes 1572872 | tf_op jit(solution)/shard_map/ppermute | solution.py:253
  34.4 10.1 %copy-start.2 = (f32[128,2048]{1,0:T(8,128)S(1)}, f32[128,2048]{1,0:T(8,128)}, u32[]{:S(2)}) copy-start(f32[128,2048]{1,0:T(8,128)} %shard_map.118) | copy-start | bytes 3145732
  44.0 11.7 %collective-permute-start.4 = (f32[64,2048]{1,0:T(8,128)S(1)}, f32[64,2048]{1,0:T(8,128)}, u32[]{:S(2)}, u32[]{:S(2)}) collective-permute-start(f32[64,2048]{1,0:T(8,128)S(1)} %dynamic-slice_bitcast_fusion.2), channel_id=1, source_target_pairs={{0,1},{1,0},{2,3},{3,2},{4,5},{5,4},{6,7},{7,6},{8,9},{9,8},{10,11... | collective-permute-start | bytes 1572872 | tf_op jit(solution)/shard_map/ppermute | solution.py:253
  45.3 10.4 %collective-permute-start.3 = (f32[32,2048]{1,0:T(8,128)}, f32[32,2048]{1,0:T(8,128)}, u32[]{:S(2)}, u32[]{:S(2)}) collective-permute-start(f32[32,2048]{1,0:T(8,128)} %dynamic-slice_bitcast_fusion.7), channel_id=1, source_target_pairs={{0,2},{1,3},{2,0},{3,1},{4,6},{5,7},{6,4},{7,5},{8,10},{9,11},{10,... | collective-permute-start | bytes 786440 | tf_op jit(solution)/shard_map/ppermute | solution.py:253
  47.2 8.6 %copy-start.4 = (f32[128,2048]{1,0:T(8,128)S(1)}, f32[128,2048]{1,0:T(8,128)}, u32[]{:S(2)}) copy-start(f32[128,2048]{1,0:T(8,128)} %shard_map.119) | copy-start | bytes 3145732
  55.7 1.5 copy-start.3
  57.0 12.4 %collective-permute-start.6 = (f32[32,2048]{1,0:T(8,128)S(1)}, f32[32,2048]{1,0:T(8,128)}, u32[]{:S(2)}, u32[]{:S(2)}) collective-permute-start(f32[32,2048]{1,0:T(8,128)S(1)} %dynamic-slice_bitcast_fusion.6), channel_id=1, source_target_pairs={{0,2},{1,3},{2,0},{3,1},{4,6},{5,7},{6,4},{7,5},{8,10},{9,11},{10,... | collective-permute-start | bytes 786440 | tf_op jit(solution)/shard_map/ppermute | solution.py:253
  58.0 12.7 %collective-permute-start.7 = (f32[64,2048]{1,0:T(8,128)}, f32[64,2048]{1,0:T(8,128)S(1)}, u32[]{:S(2)}, u32[]{:S(2)}) collective-permute-start(f32[64,2048]{1,0:T(8,128)} %dynamic-slice_bitcast_fusion.1), channel_id=1, source_target_pairs={{0,1},{1,0},{2,3},{3,2},{4,5},{5,4},{6,7},{7,6},{8,9},{9,8},{10,11... | collective-permute-start | bytes 1572872 | tf_op jit(solution)/shard_map/ppermute | solution.py:253
  59.0 11.7 %collective-permute-start.5 = (f32[32,2048]{1,0:T(8,128)S(1)}, f32[32,2048]{1,0:T(8,128)S(1)}, u32[]{:S(2)}, u32[]{:S(2)}) collective-permute-start(f32[32,2048]{1,0:T(8,128)S(1)} %bitcast_add_fusion.7), channel_id=1, source_target_pairs={{0,2},{1,3},{2,0},{3,1},{4,6},{5,7},{6,4},{7,5},{8,10},{9,11},{10,... | collective-permute-start | bytes 786440 | tf_op jit(solution)/shard_map/ppermute | solution.py:253
  70.8 3.4 %copy-start.1 = (f32[128,2048]{1,0:T(8,128)S(1)}, f32[128,2048]{1,0:T(8,128)}, u32[]{:S(2)}) copy-start(f32[128,2048]{1,0:T(8,128)} %shard_map.121) | copy-start | bytes 3145732
  71.9 9.3 %collective-permute-start.11 = (f32[32,2048]{1,0:T(8,128)S(1)}, f32[32,2048]{1,0:T(8,128)S(1)}, u32[]{:S(2)}, u32[]{:S(2)}) collective-permute-start(f32[32,2048]{1,0:T(8,128)S(1)} %dynamic-slice_bitcast_fusion.5), channel_id=1, source_target_pairs={{0,2},{1,3},{2,0},{3,1},{4,6},{5,7},{6,4},{7,5},{8,10},{9,11},{10,... | collective-permute-start | bytes 786440 | tf_op jit(solution)/shard_map/ppermute | solution.py:253
  72.2 14.6 %collective-permute-start.9 = (f32[32,2048]{1,0:T(8,128)S(1)}, f32[32,2048]{1,0:T(8,128)S(1)}, u32[]{:S(2)}, u32[]{:S(2)}) collective-permute-start(f32[32,2048]{1,0:T(8,128)S(1)} %bitcast_add_fusion.6), channel_id=1, source_target_pairs={{0,2},{1,3},{2,0},{3,1},{4,6},{5,7},{6,4},{7,5},{8,10},{9,11},{10,... | collective-permute-start | bytes 786440 | tf_op jit(solution)/shard_map/ppermute | solution.py:253
  74.1 14.1 %collective-permute-start.8 = (f32[64,2048]{1,0:T(8,128)S(1)}, f32[64,2048]{1,0:T(8,128)S(1)}, u32[]{:S(2)}, u32[]{:S(2)}) collective-permute-start(f32[64,2048]{1,0:T(8,128)S(1)} %pad_maximum_fusion.6), channel_id=1, source_target_pairs={{0,1},{1,0},{2,3},{3,2},{4,5},{5,4},{6,7},{7,6},{8,9},{9,8},{10,11... | collective-permute-start | bytes 1572872 | tf_op jit(solution)/shard_map/ppermute | solution.py:253
  74.2 13.5 %collective-permute-start.13 = (f32[64,2048]{1,0:T(8,128)S(1)}, f32[64,2048]{1,0:T(8,128)S(1)}, u32[]{:S(2)}, u32[]{:S(2)}) collective-permute-start(f32[64,2048]{1,0:T(8,128)S(1)} %dynamic-slice_bitcast_fusion), channel_id=1, source_target_pairs={{0,1},{1,0},{2,3},{3,2},{4,5},{5,4},{6,7},{7,6},{8,9},{9,8},{10,11... | collective-permute-start | bytes 1572872 | tf_op jit(solution)/shard_map/ppermute | solution.py:253
  81.2 20.8 %collective-permute-start.12 = (f32[32,2048]{1,0:T(8,128)S(1)}, f32[32,2048]{1,0:T(8,128)}, u32[]{:S(2)}, u32[]{:S(2)}) collective-permute-start(f32[32,2048]{1,0:T(8,128)S(1)} %bitcast_add_fusion.5), channel_id=1, source_target_pairs={{0,2},{1,3},{2,0},{3,1},{4,6},{5,7},{6,4},{7,5},{8,10},{9,11},{10,... | collective-permute-start | bytes 786440 | tf_op jit(solution)/shard_map/ppermute | solution.py:253
  87.7 14.3 %collective-permute-start.10 = (f32[64,2048]{1,0:T(8,128)}, f32[64,2048]{1,0:T(8,128)}, u32[]{:S(2)}, u32[]{:S(2)}) collective-permute-start(f32[64,2048]{1,0:T(8,128)} %pad_maximum_fusion.7), channel_id=1, source_target_pairs={{0,1},{1,0},{2,3},{3,2},{4,5},{5,4},{6,7},{7,6},{8,9},{9,8},{10,11... | collective-permute-start | bytes 1572872 | tf_op jit(solution)/shard_map/ppermute | solution.py:253
  87.8 14.2 %collective-permute-start.14 = (f32[32,2048]{1,0:T(8,128)S(1)}, f32[32,2048]{1,0:T(8,128)}, u32[]{:S(2)}, u32[]{:S(2)}) collective-permute-start(f32[32,2048]{1,0:T(8,128)S(1)} %dynamic-slice_bitcast_fusion.4), channel_id=1, source_target_pairs={{0,2},{1,3},{2,0},{3,1},{4,6},{5,7},{6,4},{7,5},{8,10},{9,11},{10,... | collective-permute-start | bytes 786440 | tf_op jit(solution)/shard_map/ppermute | solution.py:253
  105.0 16.2 %collective-permute-start.15 = (f32[64,2048]{1,0:T(8,128)}, f32[64,2048]{1,0:T(8,128)S(1)}, u32[]{:S(2)}, u32[]{:S(2)}) collective-permute-start(f32[64,2048]{1,0:T(8,128)} %pad_maximum_fusion.8), channel_id=1, source_target_pairs={{0,1},{1,0},{2,3},{3,2},{4,5},{5,4},{6,7},{7,6},{8,9},{9,8},{10,11... | collective-permute-start | bytes 1572872 | tf_op jit(solution)/shard_map/ppermute | solution.py:253
  106.2 15.0 %collective-permute-start.16 = (f32[32,2048]{1,0:T(8,128)S(1)}, f32[32,2048]{1,0:T(8,128)S(1)}, u32[]{:S(2)}, u32[]{:S(2)}) collective-permute-start(f32[32,2048]{1,0:T(8,128)S(1)} %bitcast_add_fusion.4), channel_id=1, source_target_pairs={{0,2},{1,3},{2,0},{3,1},{4,6},{5,7},{6,4},{7,5},{8,10},{9,11},{10,... | collective-permute-start | bytes 786440 | tf_op jit(solution)/shard_map/ppermute | solution.py:253
  122.0 13.2 %collective-permute-start.17 = (f32[64,2048]{1,0:T(8,128)}, f32[64,2048]{1,0:T(8,128)}, u32[]{:S(2)}, u32[]{:S(2)}) collective-permute-start(f32[64,2048]{1,0:T(8,128)} %pad_maximum_fusion.9), channel_id=1, source_target_pairs={{0,1},{1,0},{2,3},{3,2},{4,5},{5,4},{6,7},{7,6},{8,9},{9,8},{10,11... | collective-permute-start | bytes 1572872 | tf_op jit(solution)/shard_map/ppermute | solution.py:253
  138.2 11.5 %copy-start = (f32[16,4,12,512]{3,2,1,0:T(8,128)S(1)}, f32[16,4,12,512]{3,2,1,0:T(8,128)}, u32[]{:S(2)}) copy-start(f32[16,4,12,512]{3,2,1,0:T(8,128)} %shard_map.122) | copy-start | bytes 4718596
  162.6 6.3 %copy-start.10 = (f32[32,2048]{1,0:T(8,128)S(1)}, f32[32,2048]{1,0:T(8,128)}, u32[]{:S(2)}) copy-start(f32[32,2048]{1,0:T(8,128)} %fusion.20) | copy-start | bytes 786436
  162.6 6.3 %copy-start.11 = (f32[32,2048]{1,0:T(8,128)S(1)}, f32[32,2048]{1,0:T(8,128)}, u32[]{:S(2)}) copy-start(f32[32,2048]{1,0:T(8,128)} %fusion.19) | copy-start | bytes 786436
  162.6 6.3 %copy-start.12 = (f32[32,2048]{1,0:T(8,128)S(1)}, f32[32,2048]{1,0:T(8,128)}, u32[]{:S(2)}) copy-start(f32[32,2048]{1,0:T(8,128)} %fusion.18) | copy-start | bytes 786436
  162.6 6.3 %copy-start.13 = (f32[32,2048]{1,0:T(8,128)S(1)}, f32[32,2048]{1,0:T(8,128)}, u32[]{:S(2)}) copy-start(f32[32,2048]{1,0:T(8,128)} %fusion.17) | copy-start | bytes 786436
  163.1 8.9 %collective-permute-start.18 = (f32[16,2,512]{2,0,1:T(8,128)S(1)}, f32[16,2,512]{2,0,1:T(8,128)S(1)}, u32[]{:S(2)}, u32[]{:S(2)}) collective-permute-start(f32[16,2,512]{2,0,1:T(8,128)S(1)} %get-tuple-element.164), channel_id=1, source_target_pairs={{0,4},{4,8},{8,12},{12,16},{16,20},{20,24},{24,28},{1,5},{5,9},{9,... | collective-permute-start | bytes 196616 | tf_op jit(solution)/shard_map/ppermute | solution.py:31
  167.4 7.8 %copy-start.5 = (f32[16,8,512]{2,1,0:T(8,128)S(1)}, f32[16,8,512]{2,1,0:T(8,128)}, u32[]{:S(2)}) copy-start(f32[16,8,512]{2,1,0:T(8,128)} %param.10) | copy-start | bytes 786436
  167.5 7.8 %copy-start.7 = (f32[16,8,512]{2,0,1:T(8,128)S(1)}, f32[16,8,512]{2,0,1:T(8,128)}, u32[]{:S(2)}) copy-start(f32[16,8,512]{2,0,1:T(8,128)} %copy-done.6) | copy-start | bytes 786436
  167.5 7.8 %copy-start.9 = (f32[16,10,512]{2,0,1:T(8,128)S(1)}, f32[16,10,512]{2,0,1:T(8,128)}, u32[]{:S(2)}) copy-start(f32[16,10,512]{2,0,1:T(8,128)} %copy-done.8) | copy-start | bytes 983044
  167.5 7.8 %copy-start.14 = (f32[16,8,512]{2,1,0:T(8,128)S(1)}, f32[16,8,512]{2,1,0:T(8,128)}, u32[]{:S(2)}) copy-start(f32[16,8,512]{2,1,0:T(8,128)} %param.11) | copy-start | bytes 786436
  167.5 7.8 %copy-start.15 = (f32[16,8,512]{2,1,0:T(8,128)S(1)}, f32[16,8,512]{2,1,0:T(8,128)}, u32[]{:S(2)}) copy-start(f32[16,8,512]{2,1,0:T(8,128)} %param.12) | copy-start | bytes 786436
  167.5 7.8 %copy-start.16 = (f32[16]{0:T(128)S(1)}, f32[16]{0:T(128)}, u32[]{:S(2)}) copy-start(f32[16]{0:T(128)} %param.13) | copy-start | bytes 196
  167.5 7.8 %collective-permute-start.19 = (f32[16,2,512]{2,0,1:T(8,128)S(1)}, f32[16,2,512]{2,0,1:T(8,128)S(1)}, u32[]{:S(2)}, u32[]{:S(2)}) collective-permute-start(f32[16,2,512]{2,0,1:T(8,128)S(1)} %get-tuple-element.165), channel_id=1, source_target_pairs={{4,0},{8,4},{12,8},{16,12},{20,16},{24,20},{28,24},{5,1},{9,5},{13... | collective-permute-start | bytes 196616 | tf_op jit(solution)/shard_map/ppermute | solution.py:31

commit v3 on v2

--- a/solution.py
+++ b/solution.py
@@ -8,7 +8,7 @@
 H = 16
 TN = 512
 L = 256
-CHUNKS = 4
+CHUNKS = 8
 LEAD = 8
 
 
@@ -72,7 +72,8 @@
     npred, blocks, nrow, _ = back4.shape
     per_block = TN // H
     window = 4 * per_block
-    dwin = jnp.einsum("pbkj,nj->pkbn", back4, block_basis(window), precision=lax.Precision.HIGH)
+    dwin = jnp.einsum("pbkj,nj->pbkn", back4, block_basis(window), precision=lax.Precision.HIGH)
+    dwin = jnp.transpose(dwin, (0, 2, 1, 3))
     total = None
     for a in range(4):
         part = dwin[..., a * per_block : (a + 1) * per_block]
@@ -149,9 +150,8 @@
                 c = cov_ref[p, pl.ds(m * H, H), cols].astype(jnp.float32)
                 for d in range(4):
                     prod = c * rw_ref[d, pl.ds(m * H, H), :]
-                    half = prod[0:8] + prod[8:16]
                     r = m + 1 + d
-                    accs[r] = half if r not in accs else accs[r] + half
+                    accs[r] = prod if r not in accs else accs[r] + prod
                 done = m + 1
                 o_ref[p, 0, pl.ds(done, 1), cols] = jnp.sum(accs.pop(done), axis=0, keepdims=True)
             for r in sorted(accs):
@@ -243,6 +243,7 @@
     fitted_parts = [None] * CHUNKS
     back_parts = [None] * CHUNKS
     state[0] = fit_chunk(wl, covariates, along, 0, width)
+    next_back = 0
     for s in range(1, CHUNKS + nsteps + 1):
         pending = []
         for c in range(CHUNKS):
@@ -251,23 +252,21 @@
                 _, fn, pairs = steps[k]
                 send, finish = fn(state[c])
                 pending.append((c, finish, lax.ppermute(send, "pred", pairs)))
-        filler = None
+        outs = []
         if s < CHUNKS:
-            filler = ("fit", s)
-        elif 0 <= s - nsteps - 1 < CHUNKS:
-            filler = ("back", s - nsteps - 1)
+            outs.append(("fit", s, fit_chunk(wl, covariates, along, s, width)))
+        if next_back < CHUNKS and next_back + nsteps + 1 <= s:
+            c = next_back
+            outs.append(("back", c, back_chunk(wl, covariates, state[c], target, land, c, nrow)))
+            next_back += 1
         recvs = [r for _, _, r in pending]
-        if filler is not None:
-            kind, c = filler
-            if kind == "fit":
-                out = fit_chunk(wl, covariates, along, c, width)
-            else:
-                out = back_chunk(wl, covariates, state[c], target, land, c, nrow)
-            recvs, out = lax.optimization_barrier((recvs, out))
-            if kind == "fit":
-                state[c] = out
-            else:
-                back_parts[c] = out
+        if outs:
+            recvs, vals = lax.optimization_barrier((recvs, [v for _, _, v in outs]))
+            for (kind, c, _), v in zip(outs, vals):
+                if kind == "fit":
+                    state[c] = v
+                else:
+                    back_parts[c] = v
         for (c, finish, _), r in zip(pending, recvs):
             state[c] = finish(r)
     for c in range(CHUNKS):

time: 180 us -> 219 us (1.22)
  Pallas kernels: 80.1 us -> 98.6 us
  waiting for transfers between devices: 18.1 us -> 3.61 us
  local copies, waits for them, and re-layouts: 18.6 us -> 32.9 us
  starting transfers between devices: 22.5 us -> 33.5 us
  other arithmetic: 26.7 us -> 35 us
    ppermute x16 -> x32, waiting for transfers between devices: 13 us -> 0.08 us  [local(): pending.append((c, finish, lax.ppermute(send, 'pred', pairs)))]
    ppermute x16 -> x32, starting transfers between devices: 10.1 us -> 21.1 us  [local(): pending.append((c, finish, lax.ppermute(send, 'pred', pairs)))]
    pallas_call x4 -> x8, Pallas kernels: 46.2 us -> 57.1 us  [back_chunk(): pl.pallas_call(back_kernel, grid=(width // TN,), in_specs=[pl.BlockSpec((...]
    unnamed x40 -> x89, local copies, waits for them, and re-layouts: 6.04 us -> 14.2 us
    pallas_call x4 -> x8, Pallas kernels: 33.9 us -> 41.5 us  [fit_chunk(): pl.pallas_call(fit_kernel, grid=(width // TN,), in_specs=[pl.BlockSpec((4...]
    unnamed x0 -> x7, other arithmetic: none -> 4.75 us
    select_n x1 -> x8, other arithmetic: 1.13 us -> 5.09 us  [finish(): second = jnp.where(mine == 0, other, cur)]
    ppermute x2, waiting for transfers between devices: 3.2 us -> 0.01 us  [from_behind(): return lax.ppermute(block, axis, route)]
  transfers between devices with their start and end apart: 20 -> 36, of which waited for: 5 -> 2; matrix products, arithmetic and copies ran while one was open for 8% -> 15% of each run, Pallas kernels for 34% -> 40%
where the time goes in v3:
time: 219 us; the launch traced here: 218 us
  Pallas kernels  98.6 us (45%)
  other arithmetic  35 us (16%)
  starting transfers between devices  33.5 us (15%)
  local copies, waits for them, and re-layouts  32.9 us (15%)
  matrix products  12.4 us (6%)
  waiting for transfers between devices  3.61 us (2%)
    pallas_call x8, Pallas kernels, back_chunk(): pl.pallas_call(back_kernel, grid=(width // TN,), in_specs=[pl.BlockSpec((...  57.1 us
    pallas_call x8, Pallas kernels, fit_chunk(): pl.pallas_call(fit_kernel, grid=(width // TN,), in_specs=[pl.BlockSpec((4...  41.5 us
    ppermute x32, starting transfers between devices, local(): pending.append((c, finish, lax.ppermute(send, 'pred', pairs)))  21.1 us
    unnamed x89, local copies, waits for them, and re-layouts  14.2 us
    concatenate x16, other arithmetic, finish(): return jnp.concatenate([first, second], axis=0)  8.18 us
    add x16, other arithmetic, halve(): return (send, lambda recv: keep + recv)  6.84 us
    dot_general x1, matrix products, banded_data(): jnp.einsum('pbkj,nj->pbkn', back4, block_basis(window), precision=lax.Pre...  6.36 us
    ppermute x2, starting transfers between devices, from_behind(): return lax.ppermute(block, axis, route)  6.29 us
  transfers between devices with their start and end apart: 36, of which 2 were waited for; matrix products, arithmetic and copies ran while one was open for 15% of the time, Pallas kernels for 40%

profile of v3, /device:TPU:0, one launch (start us, length us, event | category | flops | bytes accessed | tf_op | source)
XLA Modules:
  0.0 217.8 jit_solution(4733532979098318994)
XLA Ops:
  0.6 1.1 copy.713
  2.5 4.8 %collective-permute-start = (f32[16,2,512]{2,0,1:T(8,128)S(1)}, f32[16,2,512]{2,0,1:T(8,128)S(1)}, u32[]{:S(2)}, u32[]{:S(2)}) collective-permute-start(f32[16,2,512]{2,0,1:T(8,128)S(1)} %get-tuple-element.256), channel_id=1, source_target_pairs={{0,4},{4,8},{8,12},{12,16},{16,20},{20,24},{24,28},{1,5},{5,9},{9,... | collective-permute-start | bytes 196616 | tf_op jit(solution)/shard_map/ppermute | solution.py:22
  7.3 1.3 collective-permute-start.1
  9.2 1.1 constant_dynamic-update-slice_fusion.11
  10.3 3.1 %collective-permute-done.1 = f32[16,2,512]{2,0,1:T(8,128)S(1)} collective-permute-done((f32[16,2,512]{2,0,1:T(8,128)S(1)}, f32[16,2,512]{2,0,1:T(8,128)S(1)}, u32[]{:S(2)}, u32[]{:S(2)}) %collective-permute-start.1) | collective-permute-done | bytes 65568 | tf_op jit(solution)/shard_map/ppermute | solution.py:23
  16.5 2.7 %stack.75 = f32[16,16,12,128]{3,1,2,0:T(8,128)S(1)} concatenate(f32[16,1,12,128]{3,1,2,0:T(1,128)S(1)} %copy.716, f32[16,1,12,128]{3,1,2,0:T(1,128)S(1)} %copy.717, f32[16,1,12,128]{3,1,2,0:T(1,128)S(1)} %copy.718, f32[16,1,12,128]{3,1,2,0:T(1,128)S(1)} %copy.719, f32[16,1,12,128]{3,1,2,0:T(1,128)S(1)} %copy.720, f32[16,1,12,128]{3,1,2,0:T(1,128)S(1)} %copy.721, ...), dimensions={1} | concatenate | bytes 3145728 | tf_op jit(solution)/shard_map/stack | solution.py:67
  19.2 6.0 %fusion.a_ref = f32[16,16,12,512]{3,2,1,0:T(8,128)} fusion(f32[16,16,12,128]{3,1,2,0:T(8,128)S(1)} %stack.75, f32[512]{0:T(512)S(1)} %get-tuple-element.263, f32[512]{0:T(512)S(1)} %get-tuple-element.264, f32[512]{0:T(512)S(1)} %get-tuple-element.262, f32[512]{0:T(512)S(1)} %get-tuple-element.261, s32[512]{0:T(512)S(1)} %add_select_fusion, ...), kind=kOutput, calls=%fused_computation.1 | convolution fusion | flops 1208549376 | bytes 7875072 | tf_op jit(solution)/shard_map/pbkn,nj->pbkj/dot_general | solution.py:68
  25.9 5.1 %shard_map.118 = f32[128,1024]{1,0:T(8,128)} custom-call(f32[4,16,256]{2,1,0:T(8,128)} %broadcast_in_dim.55.w_ref, bf16[16,128,8192]{2,1,0:T(8,128)(2,1)} %cov_ref.31, f32[16,16,12,512]{3,2,1,0:T(8,128)} %fusion.a_ref), custom_call_target="tpu_custom_call" | custom-call | flops 20971520 | bytes 5505024 | tf_op jit(solution)/shard_map/pallas_call | solution.py:168
  31.1 1.0 dynamic-slice_bitcast_fusion.7
  32.2 5.2 %shard_map.119 = f32[128,1024]{1,0:T(8,128)} custom-call(f32[4,16,256]{2,1,0:T(8,128)} %broadcast_in_dim.55.w_ref, bf16[16,128,8192]{2,1,0:T(8,128)(2,1)} %cov_ref.31, f32[16,16,12,512]{3,2,1,0:T(8,128)} %fusion.a_ref), custom_call_target="tpu_custom_call" | custom-call | flops 20971520 | bytes 5505024 | tf_op jit(solution)/shard_map/pallas_call | solution.py:168
  37.4 1.0 dynamic-slice_bitcast_fusion.6
  38.9 1.6 collective-permute-start.3
  40.5 5.2 %shard_map.120 = f32[128,1024]{1,0:T(8,128)} custom-call(f32[4,16,256]{2,1,0:T(8,128)} %broadcast_in_dim.55.w_ref, bf16[16,128,8192]{2,1,0:T(8,128)(2,1)} %cov_ref.31, f32[16,16,12,512]{3,2,1,0:T(8,128)} %fusion.a_ref), custom_call_target="tpu_custom_call" | custom-call | flops 20971520 | bytes 5505024 | tf_op jit(solution)/shard_map/pallas_call | solution.py:168
  46.3 1.0 dynamic-slice_bitcast_fusion.5
  47.5 1.6 collective-permute-start.6
  49.0 5.2 %shard_map.121 = f32[128,1024]{1,0:T(8,128)} custom-call(f32[4,16,256]{2,1,0:T(8,128)} %broadcast_in_dim.55.w_ref, bf16[16,128,8192]{2,1,0:T(8,128)(2,1)} %cov_ref.31, f32[16,16,12,512]{3,2,1,0:T(8,128)} %fusion.a_ref), custom_call_target="tpu_custom_call" | custom-call | flops 20971520 | bytes 5505024 | tf_op jit(solution)/shard_map/pallas_call | solution.py:168
  55.2 1.0 dynamic-slice_bitcast_fusion.4
  56.5 1.4 collective-permute-start.10
  57.9 5.2 %shard_map.122 = f32[128,1024]{1,0:T(8,128)} custom-call(f32[4,16,256]{2,1,0:T(8,128)} %broadcast_in_dim.55.w_ref, bf16[16,128,8192]{2,1,0:T(8,128)(2,1)} %cov_ref.31, f32[16,16,12,512]{3,2,1,0:T(8,128)} %fusion.a_ref), custom_call_target="tpu_custom_call" | custom-call | flops 20971520 | bytes 5505024 | tf_op jit(solution)/shard_map/pallas_call | solution.py:168
  63.1 5.2 %shard_map.123 = f32[128,1024]{1,0:T(8,128)} custom-call(f32[4,16,256]{2,1,0:T(8,128)} %broadcast_in_dim.55.w_ref, bf16[16,128,8192]{2,1,0:T(8,128)(2,1)} %cov_ref.31, f32[16,16,12,512]{3,2,1,0:T(8,128)} %fusion.a_ref), custom_call_target="tpu_custom_call" | custom-call | flops 20971520 | bytes 5505024 | tf_op jit(solution)/shard_map/pallas_call | solution.py:168
  68.2 5.2 %shard_map.125 = f32[128,1024]{1,0:T(8,128)} custom-call(f32[4,16,256]{2,1,0:T(8,128)} %broadcast_in_dim.55.w_ref, bf16[16,128,8192]{2,1,0:T(8,128)(2,1)} %cov_ref.31, f32[16,16,12,512]{3,2,1,0:T(8,128)} %fusion.a_ref), custom_call_target="tpu_custom_call" | custom-call | flops 20971520 | bytes 5505024 | tf_op jit(solution)/shard_map/pallas_call | solution.py:168
  73.4 5.3 %shard_map.127 = f32[128,1024]{1,0:T(8,128)} custom-call(f32[4,16,256]{2,1,0:T(8,128)} %broadcast_in_dim.55.w_ref, bf16[16,128,8192]{2,1,0:T(8,128)(2,1)} %cov_ref.31, f32[16,16,12,512]{3,2,1,0:T(8,128)} %fusion.a_ref), custom_call_target="tpu_custom_call" | custom-call | flops 20971520 | bytes 5505024 | tf_op jit(solution)/shard_map/pallas_call | solution.py:168
  80.3 1.5 collective-permute-start.14
  82.8 7.6 %shard_map.124 = f32[16,2,12,512]{3,2,1,0:T(8,128)} custom-call(f32[4,16,256]{2,1,0:T(8,128)} %broadcast_in_dim.55.w_ref, bf16[16,128,8192]{2,1,0:T(8,128)(2,1)} %cov_ref.31, f32[128,1024]{1,0:T(8,128)} %pad_maximum_fusion.t_ref, f32[128,8192]{1,0:T(8,128)} %y_ref.15, s32[128,8192]{1,0:T(8,128)} %g_ref.15), custom_call_target="tpu_custom_call" | custom-call | flops 20971520 | bytes 6553600 | tf_op jit(solution)/shard_map/pallas_call | solution.py:191
  91.1 1.0 broadcast_select_fusion.12
  92.1 0.9 broadcast_select_fusion.27
  96.5 1.5 collective-permute-start.18
  98.9 7.1 %shard_map.126 = f32[16,2,12,512]{3,2,1,0:T(8,128)} custom-call(f32[4,16,256]{2,1,0:T(8,128)} %broadcast_in_dim.55.w_ref, bf16[16,128,8192]{2,1,0:T(8,128)(2,1)} %cov_ref.31, f32[128,1024]{1,0:T(8,128)} %pad_maximum_fusion.1.t_ref, f32[128,8192]{1,0:T(8,128)} %y_ref.15, s32[128,8192]{1,0:T(8,128)} %g_ref.15), custom_call_target="tpu_custom_call" | custom-call | flops 20971520 | bytes 6553600 | tf_op jit(solution)/shard_map/pallas_call | solution.py:191
  106.7 1.1 constant_dynamic-update-slice_fusion.10
  107.8 1.0 broadcast_select_fusion.10
  108.8 0.9 broadcast_select_fusion.25
  110.9 0.9 bitcast_add_fusion.11
  112.4 1.0 bitcast_add_fusion.2
  114.0 1.5 collective-permute-start.22
  116.5 7.1 %shard_map.128 = f32[16,2,12,512]{3,2,1,0:T(8,128)} custom-call(f32[4,16,256]{2,1,0:T(8,128)} %broadcast_in_dim.55.w_ref, bf16[16,128,8192]{2,1,0:T(8,128)(2,1)} %cov_ref.31, f32[128,1024]{1,0:T(8,128)} %pad_maximum_fusion.2.t_ref, f32[128,8192]{1,0:T(8,128)} %y_ref.15, s32[128,8192]{1,0:T(8,128)} %g_ref.15), custom_call_target="tpu_custom_call" | custom-call | flops 20971520 | bytes 6553600 | tf_op jit(solution)/shard_map/pallas_call | solution.py:191
  124.2 1.0 constant_dynamic-update-slice_fusion.9
  125.3 1.0 broadcast_select_fusion.8
  126.3 0.9 broadcast_select_fusion.23
  127.8 0.9 bitcast_add_fusion.10
  129.3 1.0 bitcast_add_fusion.1
  130.3 1.6 collective-permute-start.26
  132.9 7.1 %shard_map.129 = f32[16,2,12,512]{3,2,1,0:T(8,128)} custom-call(f32[4,16,256]{2,1,0:T(8,128)} %broadcast_in_dim.55.w_ref, bf16[16,128,8192]{2,1,0:T(8,128)(2,1)} %cov_ref.31, f32[128,1024]{1,0:T(8,128)} %pad_maximum_fusion.3.t_ref, f32[128,8192]{1,0:T(8,128)} %y_ref.15, s32[128,8192]{1,0:T(8,128)} %g_ref.15), custom_call_target="tpu_custom_call" | custom-call | flops 20971520 | bytes 6553600 | tf_op jit(solution)/shard_map/pallas_call | solution.py:191
  140.6 1.1 constant_dynamic-update-slice_fusion.8
  142.3 1.0 broadcast_select_fusion.6
  143.3 0.9 broadcast_select_fusion.21
  146.3 1.0 bitcast_add_fusion
  147.3 1.6 collective-permute-start.30
  149.8 7.1 %shard_map.130 = f32[16,2,12,512]{3,2,1,0:T(8,128)} custom-call(f32[4,16,256]{2,1,0:T(8,128)} %broadcast_in_dim.55.w_ref, bf16[16,128,8192]{2,1,0:T(8,128)(2,1)} %cov_ref.31, f32[128,1024]{1,0:T(8,128)} %pad_maximum_fusion.4.t_ref, f32[128,8192]{1,0:T(8,128)} %y_ref.15, s32[128,8192]{1,0:T(8,128)} %g_ref.15), custom_call_target="tpu_custom_call" | custom-call | flops 20971520 | bytes 6553600 | tf_op jit(solution)/shard_map/pallas_call | solution.py:191
  157.5 1.0 constant_dynamic-update-slice_fusion.7
  158.6 1.0 broadcast_select_fusion.4
  161.1 7.1 %shard_map.131 = f32[16,2,12,512]{3,2,1,0:T(8,128)} custom-call(f32[4,16,256]{2,1,0:T(8,128)} %broadcast_in_dim.55.w_ref, bf16[16,128,8192]{2,1,0:T(8,128)(2,1)} %cov_ref.31, f32[128,1024]{1,0:T(8,128)} %pad_maximum_fusion.5.t_ref, f32[128,8192]{1,0:T(8,128)} %y_ref.15, s32[128,8192]{1,0:T(8,128)} %g_ref.15), custom_call_target="tpu_custom_call" | custom-call | flops 20971520 | bytes 6553600 | tf_op jit(solution)/shard_map/pallas_call | solution.py:191
  168.9 1.1 constant_dynamic-update-slice_fusion.6
  171.2 7.1 %shard_map.132 = f32[16,2,12,512]{3,2,1,0:T(8,128)} custom-call(f32[4,16,256]{2,1,0:T(8,128)} %broadcast_in_dim.55.w_ref, bf16[16,128,8192]{2,1,0:T(8,128)(2,1)} %cov_ref.31, f32[128,1024]{1,0:T(8,128)} %pad_maximum_fusion.6.t_ref, f32[128,8192]{1,0:T(8,128)} %y_ref.15, s32[128,8192]{1,0:T(8,128)} %g_ref.15), custom_call_target="tpu_custom_call" | custom-call | flops 20971520 | bytes 6553600 | tf_op jit(solution)/shard_map/pallas_call | solution.py:191
  178.9 1.1 constant_dynamic-update-slice_fusion.5
  181.6 7.1 %shard_map.133 = f32[16,2,12,512]{3,2,1,0:T(8,128)} custom-call(f32[4,16,256]{2,1,0:T(8,128)} %broadcast_in_dim.55.w_ref, bf16[16,128,8192]{2,1,0:T(8,128)(2,1)} %cov_ref.31, f32[128,1024]{1,0:T(8,128)} %pad_maximum_fusion.7.t_ref, f32[128,8192]{1,0:T(8,128)} %y_ref.15, s32[128,8192]{1,0:T(8,128)} %g_ref.15), custom_call_target="tpu_custom_call" | custom-call | flops 20971520 | bytes 6553600 | tf_op jit(solution)/shard_map/pallas_call | solution.py:191
  188.7 1.0 constant_dynamic-update-slice_fusion.4
  189.8 2.3 %constant_dynamic-update-slice_fusion.3 = f32[16,16,12,512]{3,2,1,0:T(8,128)} fusion(f32[16,16,12,512]{3,2,1,0:T(8,128)} %constant_dynamic-update-slice_fusion.4, f32[16,2,12,512]{3,2,1,0:T(8,128)} %shard_map.133), kind=kLoop, calls=%fused_computation.197 | loop fusion | bytes 2097152 | tf_op jit(solution)/shard_map/concatenate | solution.py:278
  192.1 6.4 %convolution_bitcast_fusion = f32[16,12,16,128]{3,1,2,0:T(8,128)S(1)} fusion(f32[16,16,12,512]{3,2,1,0:T(8,128)} %constant_dynamic-update-slice_fusion.3, f32[512]{0:T(512)S(1)} %copy-done.26, f32[512]{0:T(512)S(1)} %copy-done.28, f32[512]{0:T(512)S(1)} %copy-done.32, f32[512]{0:T(512)S(1)} %copy-done.30, s32[512]{0:T(512)S(1)} %copy-done.34, ...), kind=kOutput, calls=%fused_computation.3 | convolution fusion | flops 1208549376 | bytes 7875072 | tf_op jit(solution)/shard_map/pbkj,nj->pbkn/dot_general | solution.py:75
  198.5 1.8 fusion.96
  201.7 1.3 reshape.271
  203.0 1.3 slice_multiply_fusion
  204.3 1.3 collective-permute-start.35
  205.6 5.0 %collective-permute-start.34 = (f32[16,2,512]{2,0,1:T(8,128)S(1)}, f32[16,2,512]{2,0,1:T(8,128)S(1)}, u32[]{:S(2)}, u32[]{:S(2)}) collective-permute-start(f32[16,2,512]{2,0,1:T(8,128)S(1)} %get-tuple-element.218), channel_id=1, source_target_pairs={{0,4},{4,8},{8,12},{12,16},{16,20},{20,24},{24,28},{1,5},{5,9},{9,... | collective-permute-start | bytes 196616 | tf_op jit(solution)/shard_map/ppermute | solution.py:31
  210.6 3.0 %subtract_multiply_fusion = f32[32,8192]{1,0:T(8,128)} fusion(f32[32,8192]{1,0:T(8,128)} %fusion.20, f32[128,8192]{1,0:T(8,128)} %y_ref.15, s32[]{:T(128)S(6)} %select_n.377, s32[128,8192]{1,0:T(8,128)} %g_ref.15), kind=kLoop, calls=%fused_computation.4 | loop fusion | flops 786432 | bytes 4194308 | tf_op jit(solution)/shard_map/mul | solution.py:277
  (225 shorter events, 37.9 us)
Async XLA Ops:
  2.5 6.7 %collective-permute-start = (f32[16,2,512]{2,0,1:T(8,128)S(1)}, f32[16,2,512]{2,0,1:T(8,128)S(1)}, u32[]{:S(2)}, u32[]{:S(2)}) collective-permute-start(f32[16,2,512]{2,0,1:T(8,128)S(1)} %get-tuple-element.256), channel_id=1, source_target_pairs={{0,4},{4,8},{8,12},{12,16},{16,20},{20,24},{24,28},{1,5},{5,9},{9,... | collective-permute-start | bytes 196616 | tf_op jit(solution)/shard_map/ppermute | solution.py:22
  7.3 6.2 %collective-permute-start.1 = (f32[16,2,512]{2,0,1:T(8,128)S(1)}, f32[16,2,512]{2,0,1:T(8,128)S(1)}, u32[]{:S(2)}, u32[]{:S(2)}) collective-permute-start(f32[16,2,512]{2,0,1:T(8,128)S(1)} %get-tuple-element.255), channel_id=1, source_target_pairs={{4,0},{8,4},{12,8},{16,12},{20,16},{24,20},{28,24},{5,1},{9,5},{13... | collective-permute-start | bytes 196616 | tf_op jit(solution)/shard_map/ppermute | solution.py:23
  8.7 10.5 %copy-start.25 = (f32[512]{0:T(512)}, f32[512]{0:T(512)S(1)}, u32[]{:S(2)}) copy-start(f32[512]{0:T(512)S(1)} %get-tuple-element.263) | copy-start | bytes 6148
  8.7 10.5 %copy-start.27 = (f32[512]{0:T(512)}, f32[512]{0:T(512)S(1)}, u32[]{:S(2)}) copy-start(f32[512]{0:T(512)S(1)} %get-tuple-element.264) | copy-start | bytes 6148
  8.7 10.5 %copy-start.29 = (f32[512]{0:T(512)}, f32[512]{0:T(512)S(1)}, u32[]{:S(2)}) copy-start(f32[512]{0:T(512)S(1)} %get-tuple-element.261) | copy-start | bytes 6148
  8.7 10.5 %copy-start.31 = (f32[512]{0:T(512)}, f32[512]{0:T(512)S(1)}, u32[]{:S(2)}) copy-start(f32[512]{0:T(512)S(1)} %get-tuple-element.262) | copy-start | bytes 6148
  8.7 10.4 %copy-start.33 = (s32[512]{0:T(512)}, s32[512]{0:T(512)S(1)}, u32[]{:S(2)}) copy-start(s32[512]{0:T(512)S(1)} %add_select_fusion) | copy-start | bytes 6148
  8.8 10.4 %copy-start.35 = (s32[128]{0:T(128)}, s32[128]{0:T(128)S(1)}, u32[]{:S(2)}) copy-start(s32[128]{0:T(128)S(1)} %iota_add_fusion) | copy-start | bytes 1540
  32.0 5.4 %collective-permute-start.2 = (f32[64,1024]{1,0:T(8,128)S(1)}, f32[64,1024]{1,0:T(8,128)S(1)}, u32[]{:S(2)}, u32[]{:S(2)}) collective-permute-start(f32[64,1024]{1,0:T(8,128)S(1)} %dynamic-slice_bitcast_fusion.7), channel_id=1, source_target_pairs={{0,1},{1,0},{2,3},{3,2},{4,5},{5,4},{6,7},{7,6},{8,9},{9,8},{10,11... | collective-permute-start | bytes 786440 | tf_op jit(solution)/shard_map/ppermute | solution.py:254
  32.2 6.7 %copy-start.13 = (f32[128,1024]{1,0:T(8,128)S(1)}, f32[128,1024]{1,0:T(8,128)}, u32[]{:S(2)}) copy-start(f32[128,1024]{1,0:T(8,128)} %shard_map.118) | copy-start | bytes 1572868
  38.4 7.4 %collective-permute-start.4 = (f32[64,1024]{1,0:T(8,128)S(1)}, f32[64,1024]{1,0:T(8,128)S(1)}, u32[]{:S(2)}, u32[]{:S(2)}) collective-permute-start(f32[64,1024]{1,0:T(8,128)S(1)} %dynamic-slice_bitcast_fusion.6), channel_id=1, source_target_pairs={{0,1},{1,0},{2,3},{3,2},{4,5},{5,4},{6,7},{7,6},{8,9},{9,8},{10,11... | collective-permute-start | bytes 786440 | tf_op jit(solution)/shard_map/ppermute | solution.py:254
  38.9 6.8 %collective-permute-start.3 = (f32[32,1024]{1,0:T(8,128)S(1)}, f32[32,1024]{1,0:T(8,128)S(1)}, u32[]{:S(2)}, u32[]{:S(2)}) collective-permute-start(f32[32,1024]{1,0:T(8,128)S(1)} %dynamic-slice_bitcast_fusion.15), channel_id=1, source_target_pairs={{0,2},{1,3},{2,0},{3,1},{4,6},{5,7},{6,4},{7,5},{8,10},{9,11},{10,... | collective-permute-start | bytes 393224 | tf_op jit(solution)/shard_map/ppermute | solution.py:254
  40.5 6.9 %copy-start.15 = (f32[128,1024]{1,0:T(8,128)S(1)}, f32[128,1024]{1,0:T(8,128)}, u32[]{:S(2)}) copy-start(f32[128,1024]{1,0:T(8,128)} %shard_map.119) | copy-start | bytes 1572868
  45.8 8.5 %collective-permute-start.5 = (f32[32,1024]{1,0:T(8,128)S(1)}, f32[32,1024]{1,0:T(8,128)S(1)}, u32[]{:S(2)}, u32[]{:S(2)}) collective-permute-start(f32[32,1024]{1,0:T(8,128)S(1)} %bitcast_add_fusion.15), channel_id=1, source_target_pairs={{0,2},{1,3},{2,0},{3,1},{4,6},{5,7},{6,4},{7,5},{8,10},{9,11},{10,... | collective-permute-start | bytes 393224 | tf_op jit(solution)/shard_map/ppermute | solution.py:254
  47.3 7.0 %collective-permute-start.7 = (f32[64,1024]{1,0:T(8,128)S(1)}, f32[64,1024]{1,0:T(8,128)S(1)}, u32[]{:S(2)}, u32[]{:S(2)}) collective-permute-start(f32[64,1024]{1,0:T(8,128)S(1)} %dynamic-slice_bitcast_fusion.5), channel_id=1, source_target_pairs={{0,1},{1,0},{2,3},{3,2},{4,5},{5,4},{6,7},{7,6},{8,9},{9,8},{10,11... | collective-permute-start | bytes 786440 | tf_op jit(solution)/shard_map/ppermute | solution.py:254
  47.5 6.8 %collective-permute-start.6 = (f32[32,1024]{1,0:T(8,128)S(1)}, f32[32,1024]{1,0:T(8,128)S(1)}, u32[]{:S(2)}, u32[]{:S(2)}) collective-permute-start(f32[32,1024]{1,0:T(8,128)S(1)} %dynamic-slice_bitcast_fusion.14), channel_id=1, source_target_pairs={{0,2},{1,3},{2,0},{3,1},{4,6},{5,7},{6,4},{7,5},{8,10},{9,11},{10,... | collective-permute-start | bytes 393224 | tf_op jit(solution)/shard_map/ppermute | solution.py:254
  49.0 7.4 %copy-start.14 = (f32[128,1024]{1,0:T(8,128)S(1)}, f32[128,1024]{1,0:T(8,128)}, u32[]{:S(2)}) copy-start(f32[128,1024]{1,0:T(8,128)} %shard_map.120) | copy-start | bytes 1572868
  54.3 24.3 %collective-permute-start.8 = (f32[64,1024]{1,0:T(8,128)S(1)}, f32[64,1024]{1,0:T(8,128)S(1)}, u32[]{:S(2)}, u32[]{:S(2)}) collective-permute-start(f32[64,1024]{1,0:T(8,128)S(1)} %pad_maximum_fusion.8), channel_id=1, source_target_pairs={{0,1},{1,0},{2,3},{3,2},{4,5},{5,4},{6,7},{7,6},{8,9},{9,8},{10,11... | collective-permute-start | bytes 786440 | tf_op jit(solution)/shard_map/ppermute | solution.py:254
  54.6 24.0 %collective-permute-start.9 = (f32[32,1024]{1,0:T(8,128)S(1)}, f32[32,1024]{1,0:T(8,128)S(1)}, u32[]{:S(2)}, u32[]{:S(2)}) collective-permute-start(f32[32,1024]{1,0:T(8,128)S(1)} %bitcast_add_fusion.14), channel_id=1, source_target_pairs={{0,2},{1,3},{2,0},{3,1},{4,6},{5,7},{6,4},{7,5},{8,10},{9,11},{10,... | collective-permute-start | bytes 393224 | tf_op jit(solution)/shard_map/ppermute | solution.py:254
  56.2 22.5 %collective-permute-start.11 = (f32[64,1024]{1,0:T(8,128)S(1)}, f32[64,1024]{1,0:T(8,128)S(1)}, u32[]{:S(2)}, u32[]{:S(2)}) collective-permute-start(f32[64,1024]{1,0:T(8,128)S(1)} %dynamic-slice_bitcast_fusion.4), channel_id=1, source_target_pairs={{0,1},{1,0},{2,3},{3,2},{4,5},{5,4},{6,7},{7,6},{8,9},{9,8},{10,11... | collective-permute-start | bytes 786440 | tf_op jit(solution)/shard_map/ppermute | solution.py:254
  56.5 22.2 %collective-permute-start.10 = (f32[32,1024]{1,0:T(8,128)S(1)}, f32[32,1024]{1,0:T(8,128)S(1)}, u32[]{:S(2)}, u32[]{:S(2)}) collective-permute-start(f32[32,1024]{1,0:T(8,128)S(1)} %dynamic-slice_bitcast_fusion.13), channel_id=1, source_target_pairs={{0,2},{1,3},{2,0},{3,1},{4,6},{5,7},{6,4},{7,5},{8,10},{9,11},{10,... | collective-permute-start | bytes 393224 | tf_op jit(solution)/shard_map/ppermute | solution.py:254
  73.4 6.2 %copy-start.12 = (f32[128,1024]{1,0:T(8,128)S(1)}, f32[128,1024]{1,0:T(8,128)}, u32[]{:S(2)}) copy-start(f32[128,1024]{1,0:T(8,128)} %shard_map.121) | copy-start | bytes 1572868
  73.4 8.4 %copy-start.11 = (f32[128,1024]{1,0:T(8,128)S(1)}, f32[128,1024]{1,0:T(8,128)}, u32[]{:S(2)}) copy-start(f32[128,1024]{1,0:T(8,128)} %shard_map.122) | copy-start | bytes 1572868
  78.7 12.4 %collective-permute-start.12 = (f32[64,1024]{1,0:T(8,128)S(1)}, f32[64,1024]{1,0:T(8,128)}, u32[]{:S(2)}, u32[]{:S(2)}) collective-permute-start(f32[64,1024]{1,0:T(8,128)S(1)} %pad_maximum_fusion.9), channel_id=1, source_target_pairs={{0,1},{1,0},{2,3},{3,2},{4,5},{5,4},{6,7},{7,6},{8,9},{9,8},{10,11... | collective-permute-start | bytes 786440 | tf_op jit(solution)/shard_map/ppermute | solution.py:254
  79.0 12.1 %collective-permute-start.13 = (f32[32,1024]{1,0:T(8,128)S(1)}, f32[32,1024]{1,0:T(8,128)}, u32[]{:S(2)}, u32[]{:S(2)}) collective-permute-start(f32[32,1024]{1,0:T(8,128)S(1)} %bitcast_add_fusion.13), channel_id=1, source_target_pairs={{0,2},{1,3},{2,0},{3,1},{4,6},{5,7},{6,4},{7,5},{8,10},{9,11},{10,... | collective-permute-start | bytes 393224 | tf_op jit(solution)/shard_map/ppermute | solution.py:254
  80.3 10.8 %collective-permute-start.14 = (f32[32,1024]{1,0:T(8,128)}, f32[32,1024]{1,0:T(8,128)}, u32[]{:S(2)}, u32[]{:S(2)}) collective-permute-start(f32[32,1024]{1,0:T(8,128)} %dynamic-slice_bitcast_fusion.12), channel_id=1, source_target_pairs={{0,2},{1,3},{2,0},{3,1},{4,6},{5,7},{6,4},{7,5},{8,10},{9,11},{10,... | collective-permute-start | bytes 393224 | tf_op jit(solution)/shard_map/ppermute | solution.py:254
  81.8 9.3 %collective-permute-start.15 = (f32[64,1024]{1,0:T(8,128)S(1)}, f32[64,1024]{1,0:T(8,128)S(1)}, u32[]{:S(2)}, u32[]{:S(2)}) collective-permute-start(f32[64,1024]{1,0:T(8,128)S(1)} %dynamic-slice_bitcast_fusion.3), channel_id=1, source_target_pairs={{0,1},{1,0},{2,3},{3,2},{4,5},{5,4},{6,7},{7,6},{8,9},{9,8},{10,11... | collective-permute-start | bytes 786440 | tf_op jit(solution)/shard_map/ppermute | solution.py:254
  90.4 7.6 %copy-start.10 = (f32[128,1024]{1,0:T(8,128)S(1)}, f32[128,1024]{1,0:T(8,128)}, u32[]{:S(2)}) copy-start(f32[128,1024]{1,0:T(8,128)} %shard_map.123) | copy-start | bytes 1572868
  93.8 14.0 %collective-permute-start.16 = (f32[64,1024]{1,0:T(8,128)}, f32[64,1024]{1,0:T(8,128)}, u32[]{:S(2)}, u32[]{:S(2)}) collective-permute-start(f32[64,1024]{1,0:T(8,128)} %pad_maximum_fusion.10), channel_id=1, source_target_pairs={{0,1},{1,0},{2,3},{3,2},{4,5},{5,4},{6,7},{7,6},{8,9},{9,8},{10,11... | collective-permute-start | bytes 786440 | tf_op jit(solution)/shard_map/ppermute | solution.py:254
  95.2 12.5 %collective-permute-start.17 = (f32[32,1024]{1,0:T(8,128)S(1)}, f32[32,1024]{1,0:T(8,128)}, u32[]{:S(2)}, u32[]{:S(2)}) collective-permute-start(f32[32,1024]{1,0:T(8,128)S(1)} %bitcast_add_fusion.12), channel_id=1, source_target_pairs={{0,2},{1,3},{2,0},{3,1},{4,6},{5,7},{6,4},{7,5},{8,10},{9,11},{10,... | collective-permute-start | bytes 393224 | tf_op jit(solution)/shard_map/ppermute | solution.py:254
  96.5 11.3 %collective-permute-start.18 = (f32[32,1024]{1,0:T(8,128)}, f32[32,1024]{1,0:T(8,128)}, u32[]{:S(2)}, u32[]{:S(2)}) collective-permute-start(f32[32,1024]{1,0:T(8,128)} %dynamic-slice_bitcast_fusion.11), channel_id=1, source_target_pairs={{0,2},{1,3},{2,0},{3,1},{4,6},{5,7},{6,4},{7,5},{8,10},{9,11},{10,... | collective-permute-start | bytes 393224 | tf_op jit(solution)/shard_map/ppermute | solution.py:254
  98.0 9.7 %collective-permute-start.19 = (f32[64,1024]{1,0:T(8,128)S(1)}, f32[64,1024]{1,0:T(8,128)}, u32[]{:S(2)}, u32[]{:S(2)}) collective-permute-start(f32[64,1024]{1,0:T(8,128)S(1)} %dynamic-slice_bitcast_fusion.2), channel_id=1, source_target_pairs={{0,1},{1,0},{2,3},{3,2},{4,5},{5,4},{6,7},{7,6},{8,9},{9,8},{10,11... | collective-permute-start | bytes 786440 | tf_op jit(solution)/shard_map/ppermute | solution.py:254
  98.9 7.8 %copy-start.3 = (f32[16,2,12,512]{3,2,1,0:T(8,128)S(1)}, f32[16,2,12,512]{3,2,1,0:T(8,128)}, u32[]{:S(2)}) copy-start(f32[16,2,12,512]{3,2,1,0:T(8,128)} %shard_map.124) | copy-start | bytes 2359300
  106.0 9.6 %copy-start.9 = (f32[128,1024]{1,0:T(8,128)S(1)}, f32[128,1024]{1,0:T(8,128)}, u32[]{:S(2)}) copy-start(f32[128,1024]{1,0:T(8,128)} %shard_map.125) | copy-start | bytes 1572868
  110.4 14.9 %collective-permute-start.20 = (f32[64,1024]{1,0:T(8,128)}, f32[64,1024]{1,0:T(8,128)}, u32[]{:S(2)}, u32[]{:S(2)}) collective-permute-start(f32[64,1024]{1,0:T(8,128)} %pad_maximum_fusion.11), channel_id=1, source_target_pairs={{0,1},{1,0},{2,3},{3,2},{4,5},{5,4},{6,7},{7,6},{8,9},{9,8},{10,11... | collective-permute-start | bytes 786440 | tf_op jit(solution)/shard_map/ppermute | solution.py:254
  111.8 13.5 %collective-permute-start.21 = (f32[32,1024]{1,0:T(8,128)S(1)}, f32[32,1024]{1,0:T(8,128)}, u32[]{:S(2)}, u32[]{:S(2)}) collective-permute-start(f32[32,1024]{1,0:T(8,128)S(1)} %bitcast_add_fusion.11), channel_id=1, source_target_pairs={{0,2},{1,3},{2,0},{3,1},{4,6},{5,7},{6,4},{7,5},{8,10},{9,11},{10,... | collective-permute-start | bytes 393224 | tf_op jit(solution)/shard_map/ppermute | solution.py:254
  114.0 11.2 %collective-permute-start.22 = (f32[32,1024]{1,0:T(8,128)}, f32[32,1024]{1,0:T(8,128)}, u32[]{:S(2)}, u32[]{:S(2)}) collective-permute-start(f32[32,1024]{1,0:T(8,128)} %dynamic-slice_bitcast_fusion.10), channel_id=1, source_target_pairs={{0,2},{1,3},{2,0},{3,1},{4,6},{5,7},{6,4},{7,5},{8,10},{9,11},{10,... | collective-permute-start | bytes 393224 | tf_op jit(solution)/shard_map/ppermute | solution.py:254
  115.6 9.7 %collective-permute-start.23 = (f32[64,1024]{1,0:T(8,128)S(1)}, f32[64,1024]{1,0:T(8,128)}, u32[]{:S(2)}, u32[]{:S(2)}) collective-permute-start(f32[64,1024]{1,0:T(8,128)S(1)} %dynamic-slice_bitcast_fusion.1), channel_id=1, source_target_pairs={{0,1},{1,0},{2,3},{3,2},{4,5},{5,4},{6,7},{7,6},{8,9},{9,8},{10,11... | collective-permute-start | bytes 786440 | tf_op jit(solution)/shard_map/ppermute | solution.py:254
  116.5 7.8 %copy-start.1 = (f32[16,2,12,512]{3,2,1,0:T(8,128)S(1)}, f32[16,2,12,512]{3,2,1,0:T(8,128)}, u32[]{:S(2)}) copy-start(f32[16,2,12,512]{3,2,1,0:T(8,128)} %shard_map.126) | copy-start | bytes 2359300
  123.6 8.4 %copy-start.8 = (f32[128,1024]{1,0:T(8,128)S(1)}, f32[128,1024]{1,0:T(8,128)}, u32[]{:S(2)}) copy-start(f32[128,1024]{1,0:T(8,128)} %shard_map.127) | copy-start | bytes 1572868
  127.3 14.4 %collective-permute-start.24 = (f32[64,1024]{1,0:T(8,128)S(1)}, f32[64,1024]{1,0:T(8,128)}, u32[]{:S(2)}, u32[]{:S(2)}) collective-permute-start(f32[64,1024]{1,0:T(8,128)S(1)} %pad_maximum_fusion.12), channel_id=1, source_target_pairs={{0,1},{1,0},{2,3},{3,2},{4,5},{5,4},{6,7},{7,6},{8,9},{9,8},{10,11... | collective-permute-start | bytes 786440 | tf_op jit(solution)/shard_map/ppermute | solution.py:254
  128.7 12.9 %collective-permute-start.25 = (f32[32,1024]{1,0:T(8,128)S(1)}, f32[32,1024]{1,0:T(8,128)}, u32[]{:S(2)}, u32[]{:S(2)}) collective-permute-start(f32[32,1024]{1,0:T(8,128)S(1)} %bitcast_add_fusion.10), channel_id=1, source_target_pairs={{0,2},{1,3},{2,0},{3,1},{4,6},{5,7},{6,4},{7,5},{8,10},{9,11},{10,... | collective-permute-start | bytes 393224 | tf_op jit(solution)/shard_map/ppermute | solution.py:254
  130.3 11.3 %collective-permute-start.26 = (f32[32,1024]{1,0:T(8,128)S(1)}, f32[32,1024]{1,0:T(8,128)S(1)}, u32[]{:S(2)}, u32[]{:S(2)}) collective-permute-start(f32[32,1024]{1,0:T(8,128)S(1)} %dynamic-slice_bitcast_fusion.9), channel_id=1, source_target_pairs={{0,2},{1,3},{2,0},{3,1},{4,6},{5,7},{6,4},{7,5},{8,10},{9,11},{10,... | collective-permute-start | bytes 393224 | tf_op jit(solution)/shard_map/ppermute | solution.py:254
  131.9 10.4 %collective-permute-start.27 = (f32[64,1024]{1,0:T(8,128)S(1)}, f32[64,1024]{1,0:T(8,128)}, u32[]{:S(2)}, u32[]{:S(2)}) collective-permute-start(f32[64,1024]{1,0:T(8,128)S(1)} %dynamic-slice_bitcast_fusion), channel_id=1, source_target_pairs={{0,1},{1,0},{2,3},{3,2},{4,5},{5,4},{6,7},{7,6},{8,9},{9,8},{10,11... | collective-permute-start | bytes 786440 | tf_op jit(solution)/shard_map/ppermute | solution.py:254
  132.8 7.8 %copy-start = (f32[16,2,12,512]{3,2,1,0:T(8,128)S(1)}, f32[16,2,12,512]{3,2,1,0:T(8,128)}, u32[]{:S(2)}) copy-start(f32[16,2,12,512]{3,2,1,0:T(8,128)} %shard_map.128) | copy-start | bytes 2359300
  144.3 14.3 %collective-permute-start.28 = (f32[64,1024]{1,0:T(8,128)S(1)}, f32[64,1024]{1,0:T(8,128)}, u32[]{:S(2)}, u32[]{:S(2)}) collective-permute-start(f32[64,1024]{1,0:T(8,128)S(1)} %pad_maximum_fusion.13), channel_id=1, source_target_pairs={{0,1},{1,0},{2,3},{3,2},{4,5},{5,4},{6,7},{7,6},{8,9},{9,8},{10,11... | collective-permute-start | bytes 786440 | tf_op jit(solution)/shard_map/ppermute | solution.py:254
  145.8 12.8 %collective-permute-start.29 = (f32[32,1024]{1,0:T(8,128)S(1)}, f32[32,1024]{1,0:T(8,128)S(1)}, u32[]{:S(2)}, u32[]{:S(2)}) collective-permute-start(f32[32,1024]{1,0:T(8,128)S(1)} %bitcast_add_fusion.9), channel_id=1, source_target_pairs={{0,2},{1,3},{2,0},{3,1},{4,6},{5,7},{6,4},{7,5},{8,10},{9,11},{10,... | collective-permute-start | bytes 393224 | tf_op jit(solution)/shard_map/ppermute | solution.py:254
  147.3 11.2 %collective-permute-start.30 = (f32[32,1024]{1,0:T(8,128)S(1)}, f32[32,1024]{1,0:T(8,128)S(1)}, u32[]{:S(2)}, u32[]{:S(2)}) collective-permute-start(f32[32,1024]{1,0:T(8,128)S(1)} %dynamic-slice_bitcast_fusion.8), channel_id=1, source_target_pairs={{0,2},{1,3},{2,0},{3,1},{4,6},{5,7},{6,4},{7,5},{8,10},{9,11},{10,... | collective-permute-start | bytes 393224 | tf_op jit(solution)/shard_map/ppermute | solution.py:254
  149.8 7.8 %copy-start.2 = (f32[16,2,12,512]{3,2,1,0:T(8,128)S(1)}, f32[16,2,12,512]{3,2,1,0:T(8,128)}, u32[]{:S(2)}) copy-start(f32[16,2,12,512]{3,2,1,0:T(8,128)} %shard_map.129) | copy-start | bytes 2359300
  159.6 10.3 %collective-permute-start.31 = (f32[64,1024]{1,0:T(8,128)S(1)}, f32[64,1024]{1,0:T(8,128)S(1)}, u32[]{:S(2)}, u32[]{:S(2)}) collective-permute-start(f32[64,1024]{1,0:T(8,128)S(1)} %pad_maximum_fusion.14), channel_id=1, source_target_pairs={{0,1},{1,0},{2,3},{3,2},{4,5},{5,4},{6,7},{7,6},{8,9},{9,8},{10,11... | collective-permute-start | bytes 786440 | tf_op jit(solution)/shard_map/ppermute | solution.py:254
  159.7 10.2 %collective-permute-start.32 = (f32[32,1024]{1,0:T(8,128)S(1)}, f32[32,1024]{1,0:T(8,128)S(1)}, u32[]{:S(2)}, u32[]{:S(2)}) collective-permute-start(f32[32,1024]{1,0:T(8,128)S(1)} %bitcast_add_fusion.8), channel_id=1, source_target_pairs={{0,2},{1,3},{2,0},{3,1},{4,6},{5,7},{6,4},{7,5},{8,10},{9,11},{10,... | collective-permute-start | bytes 393224 | tf_op jit(solution)/shard_map/ppermute | solution.py:254
  161.1 7.8 %copy-start.4 = (f32[16,2,12,512]{3,2,1,0:T(8,128)S(1)}, f32[16,2,12,512]{3,2,1,0:T(8,128)}, u32[]{:S(2)}) copy-start(f32[16,2,12,512]{3,2,1,0:T(8,128)} %shard_map.130) | copy-start | bytes 2359300
  170.1 10.0 %collective-permute-start.33 = (f32[64,1024]{1,0:T(8,128)S(1)}, f32[64,1024]{1,0:T(8,128)S(1)}, u32[]{:S(2)}, u32[]{:S(2)}) collective-permute-start(f32[64,1024]{1,0:T(8,128)S(1)} %pad_maximum_fusion.15), channel_id=1, source_target_pairs={{0,1},{1,0},{2,3},{3,2},{4,5},{5,4},{6,7},{7,6},{8,9},{9,8},{10,11... | collective-permute-start | bytes 786440 | tf_op jit(solution)/shard_map/ppermute | solution.py:254
  171.2 7.8 %copy-start.5 = (f32[16,2,12,512]{3,2,1,0:T(8,128)S(1)}, f32[16,2,12,512]{3,2,1,0:T(8,128)}, u32[]{:S(2)}) copy-start(f32[16,2,12,512]{3,2,1,0:T(8,128)} %shard_map.131) | copy-start | bytes 2359300
  181.6 7.1 %copy-start.6 = (f32[16,2,12,512]{3,2,1,0:T(8,128)S(1)}, f32[16,2,12,512]{3,2,1,0:T(8,128)}, u32[]{:S(2)}) copy-start(f32[16,2,12,512]{3,2,1,0:T(8,128)} %shard_map.132) | copy-start | bytes 2359300
  201.7 11.9 %copy-start.7 = (f32[16,8,512]{2,1,0:T(8,128)S(1)}, f32[16,8,512]{2,1,0:T(8,128)}, u32[]{:S(2)}) copy-start(f32[16,8,512]{2,1,0:T(8,128)} %param.10) | copy-start | bytes 786436
  201.7 11.9 %copy-start.17 = (f32[16,10,512]{2,0,1:T(8,128)S(1)}, f32[16,10,512]{2,0,1:T(8,128)}, u32[]{:S(2)}) copy-start(f32[16,10,512]{2,0,1:T(8,128)} %copy-done.16) | copy-start | bytes 983044
  201.7 11.9 %copy-start.19 = (f32[16,8,512]{2,0,1:T(8,128)S(1)}, f32[16,8,512]{2,0,1:T(8,128)}, u32[]{:S(2)}) copy-start(f32[16,8,512]{2,0,1:T(8,128)} %copy-done.18) | copy-start | bytes 786436
  201.7 11.9 %copy-start.21 = (f32[16,10,512]{2,0,1:T(8,128)S(1)}, f32[16,10,512]{2,0,1:T(8,128)}, u32[]{:S(2)}) copy-start(f32[16,10,512]{2,0,1:T(8,128)} %copy-done.20) | copy-start | bytes 983044
  201.7 11.9 %copy-start.37 = (f32[16]{0:T(128)S(1)}, f32[16]{0:T(128)}, u32[]{:S(2)}) copy-start(f32[16]{0:T(128)} %param.13) | copy-start | bytes 196
  203.0 10.6 %copy-start.22 = (f32[16,8,512]{2,1,0:T(8,128)S(1)}, f32[16,8,512]{2,1,0:T(8,128)}, u32[]{:S(2)}) copy-start(f32[16,8,512]{2,1,0:T(8,128)} %param.11) | copy-start | bytes 786436
  203.0 10.6 %copy-start.23 = (f32[16,8,512]{2,1,0:T(8,128)S(1)}, f32[16,8,512]{2,1,0:T(8,128)}, u32[]{:S(2)}) copy-start(f32[16,8,512]{2,1,0:T(8,128)} %param.12) | copy-start | bytes 786436
  204.3 9.3 %collective-permute-start.35 = (f32[16,2,512]{2,0,1:T(8,128)S(1)}, f32[16,2,512]{2,0,1:T(8,128)S(1)}, u32[]{:S(2)}, u32[]{:S(2)}) collective-permute-start(f32[16,2,512]{2,0,1:T(8,128)S(1)} %get-tuple-element.219), channel_id=1, source_target_pairs={{4,0},{8,4},{12,8},{16,12},{20,16},{24,20},{28,24},{5,1},{9,5},{13... | collective-permute-start | bytes 196616 | tf_op jit(solution)/shard_map/ppermute | solution.py:31
  205.6 8.0 %collective-permute-start.34 = (f32[16,2,512]{2,0,1:T(8,128)S(1)}, f32[16,2,512]{2,0,1:T(8,128)S(1)}, u32[]{:S(2)}, u32[]{:S(2)}) collective-permute-start(f32[16,2,512]{2,0,1:T(8,128)S(1)} %get-tuple-element.218), channel_id=1, source_target_pairs={{0,4},{4,8},{8,12},{12,16},{16,20},{20,24},{24,28},{1,5},{5,9},{9,... | collective-permute-start | bytes 196616 | tf_op jit(solution)/shard_map/ppermute | solution.py:31
  (10 other events, 25.6 us)

commit v4 on v3

--- a/solution.py
+++ b/solution.py
@@ -8,7 +8,7 @@
 H = 16
 TN = 512
 L = 256
-CHUNKS = 8
+CHUNKS = 4
 LEAD = 8
 
 
@@ -72,8 +72,7 @@
     npred, blocks, nrow, _ = back4.shape
     per_block = TN // H
     window = 4 * per_block
-    dwin = jnp.einsum("pbkj,nj->pbkn", back4, block_basis(window), precision=lax.Precision.HIGH)
-    dwin = jnp.transpose(dwin, (0, 2, 1, 3))
+    dwin = jnp.einsum("pbkj,nj->pkbn", back4, block_basis(window), precision=lax.Precision.HIGH)
     total = None
     for a in range(4):
         part = dwin[..., a * per_block : (a + 1) * per_block]
@@ -92,7 +91,7 @@
         bits.append(bit)
         bit *= 2
     steps = []
-    for bit in bits:
+    for bit in bits[:-1]:
         def halve(cur, bit=bit):
             half = cur.shape[0] // 2
             mine = (idx // bit) % 2
@@ -101,7 +100,11 @@
             send = lax.dynamic_index_in_dim(pair, 1 - mine, 0, keepdims=False)
             return send, lambda recv: keep + recv
         steps.append((bit, halve))
-    for bit in reversed(bits):
+    for bit in bits[-1:]:
+        def swap(cur):
+            return cur, lambda recv: cur + recv
+        steps.append((bit, swap))
+    for bit in reversed(bits[:-1]):
         def double(cur, bit=bit):
             mine = (idx // bit) % 2
             def finish(other):
@@ -150,8 +153,9 @@
                 c = cov_ref[p, pl.ds(m * H, H), cols].astype(jnp.float32)
                 for d in range(4):
                     prod = c * rw_ref[d, pl.ds(m * H, H), :]
+                    half = prod[0:8] + prod[8:16]
                     r = m + 1 + d
-                    accs[r] = prod if r not in accs else accs[r] + prod
+                    accs[r] = half if r not in accs else accs[r] + half
                 done = m + 1
                 o_ref[p, 0, pl.ds(done, 1), cols] = jnp.sum(accs.pop(done), axis=0, keepdims=True)
             for r in sorted(accs):

time: 219 us -> 174 us (0.79)
  Pallas kernels: 98.6 us -> 80.2 us
  starting transfers between devices: 33.5 us -> 20.4 us
  local copies, waits for them, and re-layouts: 32.9 us -> 20.2 us
  waiting for transfers between devices: 3.61 us -> 11.7 us
  other arithmetic: 35 us -> 27.4 us
    ppermute x32 -> x12, starting transfers between devices: 21.1 us -> 7.65 us  [local(): pending.append((c, finish, lax.ppermute(send, 'pred', pairs)))]
    pallas_call x8 -> x4, Pallas kernels: 57.1 us -> 46.3 us  [back_chunk(): pl.pallas_call(back_kernel, grid=(width // TN,), in_specs=[pl.BlockSpec((...]
    pallas_call x8 -> x4, Pallas kernels: 41.5 us -> 33.9 us  [fit_chunk(): pl.pallas_call(fit_kernel, grid=(width // TN,), in_specs=[pl.BlockSpec((4...]
    unnamed x89 -> x42, local copies, waits for them, and re-layouts: 14.2 us -> 6.85 us
    ppermute x32 -> x12, waiting for transfers between devices: 0.08 us -> 6.76 us  [local(): pending.append((c, finish, lax.ppermute(send, 'pred', pairs)))]
    select_n x8 -> x1, other arithmetic: 5.09 us -> 0.1 us  [finish(): second = jnp.where(mine == 0, other, cur)]
    unnamed x7 -> x0, other arithmetic: 4.75 us -> none
    add x0 -> x4, other arithmetic: none -> 4.55 us  [swap(): return (cur, lambda recv: cur + recv)]
  transfers between devices with their start and end apart: 36 -> 16, of which waited for: 2 -> 4; matrix products, arithmetic and copies ran while one was open for 15% -> 7% of each run, Pallas kernels for 40% -> 35%
where the time goes in v4:
time: 174 us; the launch traced here: 173 us
  Pallas kernels  80.2 us (46%)
  other arithmetic  27.4 us (16%)
  starting transfers between devices  20.4 us (12%)
  local copies, waits for them, and re-layouts  20.2 us (12%)
  matrix products  11.9 us (7%)
  waiting for transfers between devices  11.7 us (7%)
    pallas_call x4, Pallas kernels, back_chunk(): pl.pallas_call(back_kernel, grid=(width // TN,), in_specs=[pl.BlockSpec((...  46.3 us
    pallas_call x4, Pallas kernels, fit_chunk(): pl.pallas_call(fit_kernel, grid=(width // TN,), in_specs=[pl.BlockSpec((4...  33.9 us
    ppermute x12, starting transfers between devices, local(): pending.append((c, finish, lax.ppermute(send, 'pred', pairs)))  7.65 us
    concatenate x8, other arithmetic, finish(): return jnp.concatenate([first, second], axis=0)  7.15 us
    unnamed x42, local copies, waits for them, and re-layouts  6.85 us
    ppermute x12, waiting for transfers between devices, local(): pending.append((c, finish, lax.ppermute(send, 'pred', pairs)))  6.76 us
    dot_general x1, matrix products, banded_along(): jnp.einsum('pbkn,nj->pbkj', cwin, block_basis(window), precision=lax.Prec...  5.96 us
    dot_general x1, matrix products, banded_data(): jnp.einsum('pbkj,nj->pkbn', back4, block_basis(window), precision=lax.Pre...  5.95 us
  transfers between devices with their start and end apart: 16, of which 4 were waited for; matrix products, arithmetic and copies ran while one was open for 7% of the time, Pallas kernels for 35%

profile of v4, /device:TPU:0, one launch (start us, length us, event | category | flops | bytes accessed | tf_op | source)
XLA Modules:
  0.0 173.0 jit_solution(14966512813212774469)
XLA Ops:
  0.6 1.1 copy.663
  1.8 0.7 copy-done.6
  2.5 1.3 collective-permute-start.1
  3.8 5.5 %collective-permute-start = (f32[16,2,512]{2,0,1:T(8,128)S(1)}, f32[16,2,512]{2,0,1:T(8,128)S(1)}, u32[]{:S(2)}, u32[]{:S(2)}) collective-permute-start(f32[16,2,512]{2,0,1:T(8,128)S(1)} %get-tuple-element.178), channel_id=1, source_target_pairs={{0,4},{4,8},{8,12},{12,16},{16,20},{20,24},{24,28},{1,5},{5,9},{9,... | collective-permute-start | bytes 196616 | tf_op jit(solution)/shard_map/ppermute | solution.py:22
  9.4 1.9 %collective-permute-done = f32[16,2,512]{2,0,1:T(8,128)S(1)} collective-permute-done((f32[16,2,512]{2,0,1:T(8,128)S(1)}, f32[16,2,512]{2,0,1:T(8,128)S(1)}, u32[]{:S(2)}, u32[]{:S(2)}) %collective-permute-start) | collective-permute-done | bytes 65568 | tf_op jit(solution)/shard_map/ppermute | solution.py:22
  11.3 1.1 constant_dynamic-update-slice_fusion.3
  12.5 0.7 copy-done.8
  13.2 0.5 fusion.53
  15.4 2.7 %stack.75 = f32[16,16,12,128]{3,1,2,0:T(8,128)S(1)} concatenate(f32[16,1,12,128]{3,1,2,0:T(1,128)S(1)} %copy.666, f32[16,1,12,128]{3,1,2,0:T(1,128)S(1)} %copy.667, f32[16,1,12,128]{3,1,2,0:T(1,128)S(1)} %copy.668, f32[16,1,12,128]{3,1,2,0:T(1,128)S(1)} %copy.669, f32[16,1,12,128]{3,1,2,0:T(1,128)S(1)} %copy.670, f32[16,1,12,128]{3,1,2,0:T(1,128)S(1)} %copy.671, ...), dimensions={1} | concatenate | bytes 3145728 | tf_op jit(solution)/shard_map/stack | solution.py:67
  18.1 6.0 %fusion.2.a_ref = f32[16,16,12,512]{3,2,1,0:T(8,128)} fusion(f32[16,16,12,128]{3,1,2,0:T(8,128)S(1)} %stack.75, f32[512]{0:T(512)S(1)} %get-tuple-element.185, f32[512]{0:T(512)S(1)} %get-tuple-element.186, f32[512]{0:T(512)S(1)} %get-tuple-element.184, f32[512]{0:T(512)S(1)} %get-tuple-element.183, s32[512]{0:T(512)S(1)} %add_select_fusion, ...), kind=kOutput, calls=%fused_computation.4 | convolution fusion | flops 1208549376 | bytes 7875072 | tf_op jit(solution)/shard_map/pbkn,nj->pbkj/dot_general | solution.py:68
  24.0 0.7 broadcast_in_dim.55.w_ref
  24.7 8.4 %shard_map.118 = f32[128,2048]{1,0:T(8,128)} custom-call(f32[4,16,256]{2,1,0:T(8,128)} %broadcast_in_dim.55.w_ref, bf16[16,128,8192]{2,1,0:T(8,128)(2,1)} %cov_ref.15, f32[16,16,12,512]{3,2,1,0:T(8,128)} %fusion.2.a_ref), custom_call_target="tpu_custom_call" | custom-call | flops 41943040 | bytes 11010048 | tf_op jit(solution)/shard_map/pallas_call | solution.py:172
  33.2 1.1 dynamic-slice_bitcast_fusion.3
  34.4 8.5 %shard_map.119 = f32[128,2048]{1,0:T(8,128)} custom-call(f32[4,16,256]{2,1,0:T(8,128)} %broadcast_in_dim.55.w_ref, bf16[16,128,8192]{2,1,0:T(8,128)(2,1)} %cov_ref.15, f32[16,16,12,512]{3,2,1,0:T(8,128)} %fusion.2.a_ref), custom_call_target="tpu_custom_call" | custom-call | flops 41943040 | bytes 11010048 | tf_op jit(solution)/shard_map/pallas_call | solution.py:172
  42.9 1.9 %dynamic-slice_bitcast_fusion.2 = f32[64,2048]{1,0:T(8,128)} fusion(f32[2,64,2048]{2,1,0:T(8,128)} %bitcast.67, s32[]{:T(128)S(6)} %select_n.158), kind=kLoop, calls=%fused_computation.35 | loop fusion | bytes 1048580 | tf_op jit(solution)/shard_map/jit(dynamic_index_in_dim)/squeeze | solution.py:100
  44.8 0.5 collective-permute-start.4
  45.3 2.0 %collective-permute-start.3 = (f32[64,2048]{1,0:T(8,128)S(1)}, f32[64,2048]{1,0:T(8,128)}, u32[]{:S(2)}, u32[]{:S(2)}) collective-permute-start(f32[64,2048]{1,0:T(8,128)S(1)} %bitcast_add_fusion.3), channel_id=1, source_target_pairs={{0,2},{1,3},{2,0},{3,1},{4,6},{5,7},{6,4},{7,5},{8,10},{9,11},{10,... | collective-permute-start | bytes 1572872 | tf_op jit(solution)/shard_map/ppermute | solution.py:258
  47.3 8.4 %shard_map.120 = f32[128,2048]{1,0:T(8,128)} custom-call(f32[4,16,256]{2,1,0:T(8,128)} %broadcast_in_dim.55.w_ref, bf16[16,128,8192]{2,1,0:T(8,128)(2,1)} %cov_ref.15, f32[16,16,12,512]{3,2,1,0:T(8,128)} %fusion.2.a_ref), custom_call_target="tpu_custom_call" | custom-call | flops 41943040 | bytes 11010048 | tf_op jit(solution)/shard_map/pallas_call | solution.py:172
  55.7 0.8 copy-done.14
  56.5 3.0 %collective-permute-done.3 = f32[64,2048]{1,0:T(8,128)} collective-permute-done((f32[64,2048]{1,0:T(8,128)S(1)}, f32[64,2048]{1,0:T(8,128)}, u32[]{:S(2)}, u32[]{:S(2)}) %collective-permute-start.3) | collective-permute-done | bytes 524320 | tf_op jit(solution)/shard_map/ppermute | solution.py:258
  59.5 1.1 bitcast_add_fusion.2
  60.6 1.1 add.328
  61.8 0.8 dynamic-slice_bitcast_fusion.1
  62.6 0.5 collective-permute-start.5
  63.1 1.7 %collective-permute-start.6 = (f32[64,2048]{1,0:T(8,128)S(1)}, f32[64,2048]{1,0:T(8,128)}, u32[]{:S(2)}, u32[]{:S(2)}) collective-permute-start(f32[64,2048]{1,0:T(8,128)S(1)} %bitcast_add_fusion.2), channel_id=1, source_target_pairs={{0,2},{1,3},{2,0},{3,1},{4,6},{5,7},{6,4},{7,5},{8,10},{9,11},{10,... | collective-permute-start | bytes 1572872 | tf_op jit(solution)/shard_map/ppermute | solution.py:258
  64.8 8.4 %shard_map.121 = f32[128,2048]{1,0:T(8,128)} custom-call(f32[4,16,256]{2,1,0:T(8,128)} %broadcast_in_dim.55.w_ref, bf16[16,128,8192]{2,1,0:T(8,128)(2,1)} %cov_ref.15, f32[16,16,12,512]{3,2,1,0:T(8,128)} %fusion.2.a_ref), custom_call_target="tpu_custom_call" | custom-call | flops 41943040 | bytes 11010048 | tf_op jit(solution)/shard_map/pallas_call | solution.py:172
  73.3 3.7 %collective-permute-done.6 = f32[64,2048]{1,0:T(8,128)} collective-permute-done((f32[64,2048]{1,0:T(8,128)S(1)}, f32[64,2048]{1,0:T(8,128)}, u32[]{:S(2)}, u32[]{:S(2)}) %collective-permute-start.6) | collective-permute-done | bytes 524320 | tf_op jit(solution)/shard_map/ppermute | solution.py:258
  77.0 1.9 %bitcast_add_fusion.1 = f32[64,2048]{1,0:T(8,128)} fusion(f32[64,2048]{1,0:T(8,128)} %collective-permute-done.7, f32[2,64,2048]{2,1,0:T(8,128)S(1)} %bitcast.66, s32[]{:T(128)S(6)} %select_n.157), kind=kLoop, calls=%fused_computation.30 | loop fusion | flops 131072 | bytes 1572868 | tf_op jit(solution)/shard_map/add | solution.py:101
  78.9 1.1 add.331
  80.0 0.8 dynamic-slice_bitcast_fusion
  80.9 0.5 collective-permute-start.8
  81.4 1.7 %collective-permute-start.9 = (f32[64,2048]{1,0:T(8,128)}, f32[64,2048]{1,0:T(8,128)}, u32[]{:S(2)}, u32[]{:S(2)}) collective-permute-start(f32[64,2048]{1,0:T(8,128)} %bitcast_add_fusion.1), channel_id=1, source_target_pairs={{0,2},{1,3},{2,0},{3,1},{4,6},{5,7},{6,4},{7,5},{8,10},{9,11},{10,... | collective-permute-start | bytes 1572872 | tf_op jit(solution)/shard_map/ppermute | solution.py:258
  83.1 1.1 broadcast_select_fusion.7
  84.3 1.0 pad_maximum_fusion.1.t_ref
  85.3 12.0 %shard_map.122 = f32[16,4,12,512]{3,2,1,0:T(8,128)} custom-call(f32[4,16,256]{2,1,0:T(8,128)} %broadcast_in_dim.55.w_ref, bf16[16,128,8192]{2,1,0:T(8,128)(2,1)} %cov_ref.15, f32[128,2048]{1,0:T(8,128)} %pad_maximum_fusion.1.t_ref, f32[128,8192]{1,0:T(8,128)} %y_ref.7, s32[128,8192]{1,0:T(8,128)} %g_ref.7), custom_call_target="tpu_custom_call" | custom-call | flops 41943040 | bytes 13107200 | tf_op jit(solution)/shard_map/pallas_call | solution.py:195
  97.3 0.7 fusion.20
  98.1 1.1 bitcast_add_fusion
  99.2 1.3 add.333
  100.5 0.4 collective-permute-start.12
  100.9 1.1 broadcast_select_fusion.5
  102.0 1.0 pad_maximum_fusion.2.t_ref
  103.0 11.4 %shard_map.123 = f32[16,4,12,512]{3,2,1,0:T(8,128)} custom-call(f32[4,16,256]{2,1,0:T(8,128)} %broadcast_in_dim.55.w_ref, bf16[16,128,8192]{2,1,0:T(8,128)(2,1)} %cov_ref.15, f32[128,2048]{1,0:T(8,128)} %pad_maximum_fusion.2.t_ref, f32[128,8192]{1,0:T(8,128)} %y_ref.7, s32[128,8192]{1,0:T(8,128)} %g_ref.7), custom_call_target="tpu_custom_call" | custom-call | flops 41943040 | bytes 13107200 | tf_op jit(solution)/shard_map/pallas_call | solution.py:195
  114.4 0.7 fusion.19
  115.2 1.1 add.335
  116.6 1.0 pad_maximum_fusion.3.t_ref
  117.6 11.4 %shard_map.124 = f32[16,4,12,512]{3,2,1,0:T(8,128)} custom-call(f32[4,16,256]{2,1,0:T(8,128)} %broadcast_in_dim.55.w_ref, bf16[16,128,8192]{2,1,0:T(8,128)(2,1)} %cov_ref.15, f32[128,2048]{1,0:T(8,128)} %pad_maximum_fusion.3.t_ref, f32[128,8192]{1,0:T(8,128)} %y_ref.7, s32[128,8192]{1,0:T(8,128)} %g_ref.7), custom_call_target="tpu_custom_call" | custom-call | flops 41943040 | bytes 13107200 | tf_op jit(solution)/shard_map/pallas_call | solution.py:195
  129.1 0.7 fusion.18
  129.9 0.8 fusion.17
  130.7 1.0 pad_maximum_fusion.4.t_ref
  131.7 11.5 %shard_map.125 = f32[16,4,12,512]{3,2,1,0:T(8,128)} custom-call(f32[4,16,256]{2,1,0:T(8,128)} %broadcast_in_dim.55.w_ref, bf16[16,128,8192]{2,1,0:T(8,128)(2,1)} %cov_ref.15, f32[128,2048]{1,0:T(8,128)} %pad_maximum_fusion.4.t_ref, f32[128,8192]{1,0:T(8,128)} %y_ref.7, s32[128,8192]{1,0:T(8,128)} %g_ref.7), custom_call_target="tpu_custom_call" | custom-call | flops 41943040 | bytes 13107200 | tf_op jit(solution)/shard_map/pallas_call | solution.py:195
  143.3 3.7 %pad_maximum_fusion = f32[16,16,12,512]{3,2,1,0:T(8,128)S(1)} fusion(f32[16,4,12,512]{3,2,1,0:T(8,128)} %shard_map.125, f32[16,4,12,512]{3,2,1,0:T(8,128)} %shard_map.124, f32[16,4,12,512]{3,2,1,0:T(8,128)} %shard_map.123, f32[16,4,12,512]{3,2,1,0:T(8,128)S(1)} %copy-done), kind=kLoop, calls=%fused_computation | loop fusion | flops 4718592 | bytes 12582912 | tf_op jit(solution)/shard_map/concatenate | solution.py:282
  147.0 6.0 %fusion.4 = f32[16,12,16,128]{3,2,1,0:T(8,128)S(1)} fusion(f32[16,16,12,512]{3,2,1,0:T(8,128)S(1)} %pad_maximum_fusion, f32[512]{0:T(512)S(1)} %get-tuple-element.185, f32[512]{0:T(512)S(1)} %get-tuple-element.186, f32[512]{0:T(512)S(1)} %get-tuple-element.184, f32[512]{0:T(512)S(1)} %get-tuple-element.183, s32[512]{0:T(512)S(1)} %add_select_fusion, ...), kind=kOutput, calls=%fused_computation.6 | convolution fusion | flops 1208549376 | bytes 7875072 | tf_op jit(solution)/shard_map/pbkj,nj->pkbn/dot_general | solution.py:75
  153.0 1.4 fusion.89
  154.3 1.1 pad_add_fusion
  155.5 0.5 reshape.225
  156.5 4.5 %collective-permute-start.14 = (f32[16,2,512]{2,0,1:T(8,128)S(1)}, f32[16,2,512]{2,0,1:T(8,128)S(1)}, u32[]{:S(2)}, u32[]{:S(2)}) collective-permute-start(f32[16,2,512]{2,0,1:T(8,128)S(1)} %get-tuple-element.156), channel_id=1, source_target_pairs={{0,4},{4,8},{8,12},{12,16},{16,20},{20,24},{24,28},{1,5},{5,9},{9,... | collective-permute-start | bytes 196616 | tf_op jit(solution)/shard_map/ppermute | solution.py:31
  161.1 1.4 collective-permute-start.15
  162.6 3.1 %subtract_multiply_fusion = (f32[32,8192]{1,0:T(8,128)}, f32[32,8192]{1,0:T(8,128)}) fusion(f32[128,8192]{1,0:T(8,128)} %y_ref.7, s32[]{:T(128)S(6)} %select_n.161, s32[128,8192]{1,0:T(8,128)} %g_ref.7, f32[32,2048]{1,0:T(8,128)S(1)} %copy-done.13, f32[32,2048]{1,0:T(8,128)S(1)} %copy-done.12, f32[32,2048]{1,0:T(8,128)S(1)} %copy-done.11, ...), kind=kLoop, calls=%fused_computation.20 | loop fusion | flops 1572864 | bytes 5242884 | tf_op jit(solution)/shard_map/mul | solution.py:281
  165.7 3.0 %collective-permute-done.15 = f32[16,2,512]{2,0,1:T(8,128)S(1)} collective-permute-done((f32[16,2,512]{2,0,1:T(8,128)S(1)}, f32[16,2,512]{2,0,1:T(8,128)S(1)}, u32[]{:S(2)}, u32[]{:S(2)}) %collective-permute-start.15) | collective-permute-done | bytes 65568 | tf_op jit(solution)/shard_map/ppermute | solution.py:31
  168.8 0.8 divide_subtract_fusion
  169.6 0.9 copy.696
  170.4 0.9 copy.697
  171.3 0.9 copy.698
  172.1 0.9 copy.695
  (82 shorter events, 3.0 us)
Async XLA Ops:
  1.7 0.7 copy-start.6
  2.5 10.0 %collective-permute-start.1 = (f32[16,2,512]{2,0,1:T(8,128)S(1)}, f32[16,2,512]{2,0,1:T(8,128)S(1)}, u32[]{:S(2)}, u32[]{:S(2)}) collective-permute-start(f32[16,2,512]{2,0,1:T(8,128)S(1)} %get-tuple-element.177), channel_id=1, source_target_pairs={{4,0},{8,4},{12,8},{16,12},{20,16},{24,20},{28,24},{5,1},{9,5},{13... | collective-permute-start | bytes 196616 | tf_op jit(solution)/shard_map/ppermute | solution.py:23
  3.8 7.5 %collective-permute-start = (f32[16,2,512]{2,0,1:T(8,128)S(1)}, f32[16,2,512]{2,0,1:T(8,128)S(1)}, u32[]{:S(2)}, u32[]{:S(2)}) collective-permute-start(f32[16,2,512]{2,0,1:T(8,128)S(1)} %get-tuple-element.178), channel_id=1, source_target_pairs={{0,4},{4,8},{8,12},{12,16},{16,20},{20,24},{24,28},{1,5},{5,9},{9,... | collective-permute-start | bytes 196616 | tf_op jit(solution)/shard_map/ppermute | solution.py:22
  12.4 0.7 copy-start.8
  34.3 8.6 %collective-permute-start.2 = (f32[64,2048]{1,0:T(8,128)S(1)}, f32[64,2048]{1,0:T(8,128)S(1)}, u32[]{:S(2)}, u32[]{:S(2)}) collective-permute-start(f32[64,2048]{1,0:T(8,128)S(1)} %dynamic-slice_bitcast_fusion.3), channel_id=1, source_target_pairs={{0,1},{1,0},{2,3},{3,2},{4,5},{5,4},{6,7},{7,6},{8,9},{9,8},{10,11... | collective-permute-start | bytes 1572872 | tf_op jit(solution)/shard_map/ppermute | solution.py:258
  34.3 10.9 %copy-start.1 = (f32[128,2048]{1,0:T(8,128)S(1)}, f32[128,2048]{1,0:T(8,128)}, u32[]{:S(2)}) copy-start(f32[128,2048]{1,0:T(8,128)} %shard_map.118) | copy-start | bytes 3145732
  44.8 10.9 %collective-permute-start.4 = (f32[64,2048]{1,0:T(8,128)}, f32[64,2048]{1,0:T(8,128)S(1)}, u32[]{:S(2)}, u32[]{:S(2)}) collective-permute-start(f32[64,2048]{1,0:T(8,128)} %dynamic-slice_bitcast_fusion.2), channel_id=1, source_target_pairs={{0,1},{1,0},{2,3},{3,2},{4,5},{5,4},{6,7},{7,6},{8,9},{9,8},{10,11... | collective-permute-start | bytes 1572872 | tf_op jit(solution)/shard_map/ppermute | solution.py:258
  45.3 14.2 %copy-start.4 = (f32[128,2048]{1,0:T(8,128)S(1)}, f32[128,2048]{1,0:T(8,128)}, u32[]{:S(2)}) copy-start(f32[128,2048]{1,0:T(8,128)} %shard_map.119) | copy-start | bytes 3145732
  45.3 14.2 %collective-permute-start.3 = (f32[64,2048]{1,0:T(8,128)S(1)}, f32[64,2048]{1,0:T(8,128)}, u32[]{:S(2)}, u32[]{:S(2)}) collective-permute-start(f32[64,2048]{1,0:T(8,128)S(1)} %bitcast_add_fusion.3), channel_id=1, source_target_pairs={{0,2},{1,3},{2,0},{3,1},{4,6},{5,7},{6,4},{7,5},{8,10},{9,11},{10,... | collective-permute-start | bytes 1572872 | tf_op jit(solution)/shard_map/ppermute | solution.py:258
  55.7 6.0 %copy-start.3 = (f32[128,2048]{1,0:T(8,128)S(1)}, f32[128,2048]{1,0:T(8,128)}, u32[]{:S(2)}) copy-start(f32[128,2048]{1,0:T(8,128)} %shard_map.120) | copy-start | bytes 3145732
  55.7 0.8 copy-start.14
  62.6 10.7 %collective-permute-start.7 = (f32[64,2048]{1,0:T(8,128)}, f32[64,2048]{1,0:T(8,128)}, u32[]{:S(2)}, u32[]{:S(2)}) collective-permute-start(f32[64,2048]{1,0:T(8,128)} %dynamic-slice_bitcast_fusion.1), channel_id=1, source_target_pairs={{0,1},{1,0},{2,3},{3,2},{4,5},{5,4},{6,7},{7,6},{8,9},{9,8},{10,11... | collective-permute-start | bytes 1572872 | tf_op jit(solution)/shard_map/ppermute | solution.py:258
  62.6 10.7 %collective-permute-start.5 = (f32[64,2048]{1,0:T(8,128)S(1)}, f32[64,2048]{1,0:T(8,128)}, u32[]{:S(2)}, u32[]{:S(2)}) collective-permute-start(f32[64,2048]{1,0:T(8,128)S(1)} %add.328), channel_id=1, source_target_pairs={{0,1},{1,0},{2,3},{3,2},{4,5},{5,4},{6,7},{7,6},{8,9},{9,8},{10,11... | collective-permute-start | bytes 1572872 | tf_op jit(solution)/shard_map/ppermute | solution.py:258
  63.1 13.9 %collective-permute-start.6 = (f32[64,2048]{1,0:T(8,128)S(1)}, f32[64,2048]{1,0:T(8,128)}, u32[]{:S(2)}, u32[]{:S(2)}) collective-permute-start(f32[64,2048]{1,0:T(8,128)S(1)} %bitcast_add_fusion.2), channel_id=1, source_target_pairs={{0,2},{1,3},{2,0},{3,1},{4,6},{5,7},{6,4},{7,5},{8,10},{9,11},{10,... | collective-permute-start | bytes 1572872 | tf_op jit(solution)/shard_map/ppermute | solution.py:258
  73.3 6.8 %copy-start.2 = (f32[128,2048]{1,0:T(8,128)S(1)}, f32[128,2048]{1,0:T(8,128)}, u32[]{:S(2)}) copy-start(f32[128,2048]{1,0:T(8,128)} %shard_map.121) | copy-start | bytes 3145732
  80.9 17.2 %collective-permute-start.10 = (f32[64,2048]{1,0:T(8,128)}, f32[64,2048]{1,0:T(8,128)}, u32[]{:S(2)}, u32[]{:S(2)}) collective-permute-start(f32[64,2048]{1,0:T(8,128)} %dynamic-slice_bitcast_fusion), channel_id=1, source_target_pairs={{0,1},{1,0},{2,3},{3,2},{4,5},{5,4},{6,7},{7,6},{8,9},{9,8},{10,11... | collective-permute-start | bytes 1572872 | tf_op jit(solution)/shard_map/ppermute | solution.py:258
  80.9 17.2 %collective-permute-start.8 = (f32[64,2048]{1,0:T(8,128)S(1)}, f32[64,2048]{1,0:T(8,128)}, u32[]{:S(2)}, u32[]{:S(2)}) collective-permute-start(f32[64,2048]{1,0:T(8,128)S(1)} %add.331), channel_id=1, source_target_pairs={{0,1},{1,0},{2,3},{3,2},{4,5},{5,4},{6,7},{7,6},{8,9},{9,8},{10,11... | collective-permute-start | bytes 1572872 | tf_op jit(solution)/shard_map/ppermute | solution.py:258
  81.4 16.7 %collective-permute-start.9 = (f32[64,2048]{1,0:T(8,128)}, f32[64,2048]{1,0:T(8,128)}, u32[]{:S(2)}, u32[]{:S(2)}) collective-permute-start(f32[64,2048]{1,0:T(8,128)} %bitcast_add_fusion.1), channel_id=1, source_target_pairs={{0,2},{1,3},{2,0},{3,1},{4,6},{5,7},{6,4},{7,5},{8,10},{9,11},{10,... | collective-permute-start | bytes 1572872 | tf_op jit(solution)/shard_map/ppermute | solution.py:258
  100.4 14.7 %collective-permute-start.11 = (f32[64,2048]{1,0:T(8,128)S(1)}, f32[64,2048]{1,0:T(8,128)S(1)}, u32[]{:S(2)}, u32[]{:S(2)}) collective-permute-start(f32[64,2048]{1,0:T(8,128)S(1)} %add.333), channel_id=1, source_target_pairs={{0,1},{1,0},{2,3},{3,2},{4,5},{5,4},{6,7},{7,6},{8,9},{9,8},{10,11... | collective-permute-start | bytes 1572872 | tf_op jit(solution)/shard_map/ppermute | solution.py:258
  100.5 14.7 %collective-permute-start.12 = (f32[64,2048]{1,0:T(8,128)S(1)}, f32[64,2048]{1,0:T(8,128)}, u32[]{:S(2)}, u32[]{:S(2)}) collective-permute-start(f32[64,2048]{1,0:T(8,128)S(1)} %bitcast_add_fusion), channel_id=1, source_target_pairs={{0,2},{1,3},{2,0},{3,1},{4,6},{5,7},{6,4},{7,5},{8,10},{9,11},{10,... | collective-permute-start | bytes 1572872 | tf_op jit(solution)/shard_map/ppermute | solution.py:258
  116.3 13.5 %collective-permute-start.13 = (f32[64,2048]{1,0:T(8,128)S(1)}, f32[64,2048]{1,0:T(8,128)S(1)}, u32[]{:S(2)}, u32[]{:S(2)}) collective-permute-start(f32[64,2048]{1,0:T(8,128)S(1)} %add.335), channel_id=1, source_target_pairs={{0,1},{1,0},{2,3},{3,2},{4,5},{5,4},{6,7},{7,6},{8,9},{9,8},{10,11... | collective-permute-start | bytes 1572872 | tf_op jit(solution)/shard_map/ppermute | solution.py:258
  131.7 11.5 %copy-start = (f32[16,4,12,512]{3,2,1,0:T(8,128)S(1)}, f32[16,4,12,512]{3,2,1,0:T(8,128)}, u32[]{:S(2)}) copy-start(f32[16,4,12,512]{3,2,1,0:T(8,128)} %shard_map.122) | copy-start | bytes 4718596
  156.0 6.6 %copy-start.10 = (f32[32,2048]{1,0:T(8,128)S(1)}, f32[32,2048]{1,0:T(8,128)}, u32[]{:S(2)}) copy-start(f32[32,2048]{1,0:T(8,128)} %fusion.20) | copy-start | bytes 786436
  156.0 6.6 %copy-start.11 = (f32[32,2048]{1,0:T(8,128)S(1)}, f32[32,2048]{1,0:T(8,128)}, u32[]{:S(2)}) copy-start(f32[32,2048]{1,0:T(8,128)} %fusion.19) | copy-start | bytes 786436
  156.0 6.6 %copy-start.12 = (f32[32,2048]{1,0:T(8,128)S(1)}, f32[32,2048]{1,0:T(8,128)}, u32[]{:S(2)}) copy-start(f32[32,2048]{1,0:T(8,128)} %fusion.18) | copy-start | bytes 786436
  156.0 6.6 %copy-start.13 = (f32[32,2048]{1,0:T(8,128)S(1)}, f32[32,2048]{1,0:T(8,128)}, u32[]{:S(2)}) copy-start(f32[32,2048]{1,0:T(8,128)} %fusion.17) | copy-start | bytes 786436
  156.5 9.2 %collective-permute-start.14 = (f32[16,2,512]{2,0,1:T(8,128)S(1)}, f32[16,2,512]{2,0,1:T(8,128)S(1)}, u32[]{:S(2)}, u32[]{:S(2)}) collective-permute-start(f32[16,2,512]{2,0,1:T(8,128)S(1)} %get-tuple-element.156), channel_id=1, source_target_pairs={{0,4},{4,8},{8,12},{12,16},{16,20},{20,24},{24,28},{1,5},{5,9},{9,... | collective-permute-start | bytes 196616 | tf_op jit(solution)/shard_map/ppermute | solution.py:31
  161.1 7.7 %copy-start.5 = (f32[16,8,512]{2,1,0:T(8,128)S(1)}, f32[16,8,512]{2,1,0:T(8,128)}, u32[]{:S(2)}) copy-start(f32[16,8,512]{2,1,0:T(8,128)} %param.10) | copy-start | bytes 786436
  161.1 7.7 %copy-start.7 = (f32[16,8,512]{2,0,1:T(8,128)S(1)}, f32[16,8,512]{2,0,1:T(8,128)}, u32[]{:S(2)}) copy-start(f32[16,8,512]{2,0,1:T(8,128)} %copy-done.6) | copy-start | bytes 786436
  161.1 7.7 %copy-start.9 = (f32[16,10,512]{2,0,1:T(8,128)S(1)}, f32[16,10,512]{2,0,1:T(8,128)}, u32[]{:S(2)}) copy-start(f32[16,10,512]{2,0,1:T(8,128)} %copy-done.8) | copy-start | bytes 983044
  161.1 7.7 %copy-start.15 = (f32[16,8,512]{2,1,0:T(8,128)S(1)}, f32[16,8,512]{2,1,0:T(8,128)}, u32[]{:S(2)}) copy-start(f32[16,8,512]{2,1,0:T(8,128)} %param.11) | copy-start | bytes 786436
  161.1 7.7 %copy-start.16 = (f32[16,8,512]{2,1,0:T(8,128)S(1)}, f32[16,8,512]{2,1,0:T(8,128)}, u32[]{:S(2)}) copy-start(f32[16,8,512]{2,1,0:T(8,128)} %param.12) | copy-start | bytes 786436
  161.1 7.7 %copy-start.17 = (f32[16]{0:T(128)S(1)}, f32[16]{0:T(128)}, u32[]{:S(2)}) copy-start(f32[16]{0:T(128)} %param.13) | copy-start | bytes 196
  161.1 7.6 %collective-permute-start.15 = (f32[16,2,512]{2,0,1:T(8,128)S(1)}, f32[16,2,512]{2,0,1:T(8,128)S(1)}, u32[]{:S(2)}, u32[]{:S(2)}) collective-permute-start(f32[16,2,512]{2,0,1:T(8,128)S(1)} %get-tuple-element.157), channel_id=1, source_target_pairs={{4,0},{8,4},{12,8},{16,12},{20,16},{24,20},{28,24},{5,1},{9,5},{13... | collective-permute-start | bytes 196616 | tf_op jit(solution)/shard_map/ppermute | solution.py:31

commit v5 on v4

--- a/solution.py
+++ b/solution.py
@@ -116,9 +116,18 @@
     return [(bit, fn, [(i, i ^ bit) for i in range(n)]) for bit, fn in steps]
 
 
-def fit_kernel(w_ref, cov_ref, a_ref, o_ref):
+def fit_kernel(w_ref, cov_ref, a_ref, h_ref, o_ref):
     npred = cov_ref.shape[0]
     nint = cov_ref.shape[1] // H
+    count = a_ref.shape[2]
+
+    def row(p, r, cols):
+        if r < 2:
+            return h_ref[p, 0, pl.ds(r, 1), cols]
+        if r < count + 2:
+            return a_ref[p, 0, pl.ds(r - 2, 1), cols]
+        return h_ref[p, 0, pl.ds(r - count, 1), cols]
+
     for s in range(TN // L):
         cols = pl.ds(s * L, L)
         w = [w_ref[d] for d in range(4)]
@@ -126,16 +135,17 @@
             rows = pl.ds(m * H, H)
 
             def body(p, acc):
-                surf = w[0] * a_ref[p, 0, pl.ds(m + 1, 1), cols]
+                surf = w[0] * row(p, m + 1, cols)
                 for d in range(1, 4):
-                    surf = surf + w[d] * a_ref[p, 0, pl.ds(m + 1 + d, 1), cols]
+                    surf = surf + w[d] * row(p, m + 1 + d, cols)
                 return acc + cov_ref[p, rows, cols].astype(jnp.float32) * surf
 
             acc = lax.fori_loop(0, npred, body, jnp.zeros((H, L), jnp.float32), unroll=True)
             o_ref[rows, cols] = acc
 
 
-def back_kernel(w_ref, cov_ref, t_ref, y_ref, g_ref, o_ref, rw_ref):
+def back_kernel(w_ref, cov_ref, t_ref, y_ref, g_ref, *rest):
+    o_ref, rw_ref = rest[-2], rest[-1]
     npred = cov_ref.shape[0]
     nint = cov_ref.shape[1] // H
     for s in range(TN // L):
@@ -165,9 +175,10 @@
         lax.fori_loop(0, npred, body, 0)
 
 
-def fit_chunk(wl, cov, along, chunk, width):
+def fit_chunk(wl, cov, along, halo, chunk, width):
     npred, rows, _ = cov.shape
-    nrow = along.shape[2]
+    count = along.shape[2]
+    nh = halo.shape[2]
     off = chunk * (width // TN)
     return pl.pallas_call(
         fit_kernel,
@@ -175,7 +186,8 @@
         in_specs=[
             pl.BlockSpec((4, H, L), lambda j: (0, 0, 0)),
             pl.BlockSpec((npred, rows, TN), lambda j: (0, 0, j + off)),
-            pl.BlockSpec((npred, 1, nrow, TN), lambda j: (0, j + off, 0, 0)),
+            pl.BlockSpec((npred, 1, count, TN), lambda j: (0, j + off, 0, 0)),
+            pl.BlockSpec((npred, 1, nh, TN), lambda j: (0, j + off, 0, 0)),
         ],
         out_specs=pl.BlockSpec((rows, TN), lambda j: (0, j)),
         out_shape=jax.ShapeDtypeStruct((rows, width), jnp.float32),
@@ -183,35 +195,43 @@
         cost_estimate=pl.CostEstimate(
             flops=10 * npred * rows * width,
             transcendentals=0,
-            bytes_accessed=2 * npred * rows * width + 4 * npred * nrow * width + 4 * rows * width,
+            bytes_accessed=2 * npred * rows * width + 4 * npred * (count + nh) * width + 4 * rows * width,
         ),
-    )(wl, cov, along)
-
-
-def back_chunk(wl, cov, total, target, land, chunk, nrow):
-    npred, rows, _ = cov.shape
+    )(wl, cov, along, halo)
+
+
+def back_chunk(wl, cov, total, target, land, chunk, nrow, buf):
+    npred, rows, ny = cov.shape
     width = total.shape[1]
     off = chunk * (width // TN)
+    in_specs = [
+        pl.BlockSpec((4, H, L), lambda j: (0, 0, 0)),
+        pl.BlockSpec((npred, rows, TN), lambda j: (0, 0, j + off)),
+        pl.BlockSpec((rows, TN), lambda j: (0, j)),
+        pl.BlockSpec((rows, TN), lambda j: (0, j + off)),
+        pl.BlockSpec((rows, TN), lambda j: (0, j + off)),
+    ]
+    args = [wl, cov, total, target, land]
+    aliases = {}
+    if buf is not None:
+        in_specs.append(pl.BlockSpec(memory_space=pl.ANY))
+        args.append(buf)
+        aliases = {len(args) - 1: 0}
     return pl.pallas_call(
         back_kernel,
         grid=(width // TN,),
-        in_specs=[
-            pl.BlockSpec((4, H, L), lambda j: (0, 0, 0)),
-            pl.BlockSpec((npred, rows, TN), lambda j: (0, 0, j + off)),
-            pl.BlockSpec((rows, TN), lambda j: (0, j)),
-            pl.BlockSpec((rows, TN), lambda j: (0, j + off)),
-            pl.BlockSpec((rows, TN), lambda j: (0, j + off)),
-        ],
-        out_specs=pl.BlockSpec((npred, 1, nrow, TN), lambda j: (0, j, 0, 0)),
-        out_shape=jax.ShapeDtypeStruct((npred, width // TN, nrow, TN), jnp.float32),
+        in_specs=in_specs,
+        out_specs=pl.BlockSpec((npred, 1, nrow, TN), lambda j: (0, j + off, 0, 0)),
+        out_shape=jax.ShapeDtypeStruct((npred, ny // TN, nrow, TN), jnp.float32),
         scratch_shapes=[pltpu.VMEM((4, rows, L), jnp.float32)],
+        input_output_aliases=aliases,
         compiler_params=pltpu.CompilerParams(dimension_semantics=("arbitrary",)),
         cost_estimate=pl.CostEstimate(
             flops=10 * npred * rows * width,
             transcendentals=0,
             bytes_accessed=2 * npred * rows * width + 12 * rows * width + 4 * npred * nrow * width,
         ),
-    )(wl, cov, total, target, land)
+    )(*args)
 
 
 def penalty(padded, count):
@@ -235,8 +255,14 @@
     share = rows // lax.axis_size("pred")
     start = lax.axis_index("pred") * share
     wl = jnp.broadcast_to(weight_table(H)[:, :, None], (4, H, L))
-    padded = extended(coefs, (("tile", 1),), 2)
-    along = banded_along(padded, ny)
+    peers = lax.axis_size("tile")
+    up = [(i, i + 1) for i in range(peers - 1)]
+    down = [(j, i) for i, j in up]
+    before = lax.ppermute(coefs[:, count - 2 :], "tile", up)
+    after = lax.ppermute(coefs[:, :2], "tile", down)
+    padded = jnp.concatenate([before, coefs, after], axis=1)
+    along = banded_along(coefs, ny)
+    halo_along = banded_along(jnp.concatenate([before, after], axis=1), ny)
     nrow = padded.shape[1]
     target_blk = lax.dynamic_slice_in_dim(target, start, share, 0)
     land_blk = lax.dynamic_slice_in_dim(land, start, share, 0).astype(jnp.float32)
@@ -245,8 +271,8 @@
     nsteps = len(steps)
     state = [None] * CHUNKS
     fitted_parts = [None] * CHUNKS
-    back_parts = [None] * CHUNKS
-    state[0] = fit_chunk(wl, covariates, along, 0, width)
+    back = None
+    state[0] = fit_chunk(wl, covariates, along, halo_along, 0, width)
     next_back = 0
     for s in range(1, CHUNKS + nsteps + 1):
         pending = []
@@ -258,10 +284,10 @@
                 pending.append((c, finish, lax.ppermute(send, "pred", pairs)))
         outs = []
         if s < CHUNKS:
-            outs.append(("fit", s, fit_chunk(wl, covariates, along, s, width)))
+            outs.append(("fit", s, fit_chunk(wl, covariates, along, halo_along, s, width)))
         if next_back < CHUNKS and next_back + nsteps + 1 <= s:
             c = next_back
-            outs.append(("back", c, back_chunk(wl, covariates, state[c], target, land, c, nrow)))
+            outs.append(("back", c, back_chunk(wl, covariates, state[c], target, land, c, nrow, back)))
             next_back += 1
         recvs = [r for _, _, r in pending]
         if outs:
@@ -270,16 +296,15 @@
                 if kind == "fit":
                     state[c] = v
                 else:
-                    back_parts[c] = v
+                    back = v
         for (c, finish, _), r in zip(pending, recvs):
             state[c] = finish(r)
     for c in range(CHUNKS):
-        if back_parts[c] is None:
-            back_parts[c] = back_chunk(wl, covariates, state[c], target, land, c, nrow)
+        if c >= next_back:
+            back = back_chunk(wl, covariates, state[c], target, land, c, nrow, back)
         fitted_parts[c] = lax.dynamic_slice_in_dim(state[c], start, share, 0)
     fitted = jnp.concatenate(fitted_parts, axis=1)
     residual = land_blk * (target_blk - fitted)
-    back = jnp.concatenate(back_parts, axis=1)
     grad_pad = -(1.0 / H) * banded_data(back, knots)
     inner = grad_pad[:, 2 : count + 2]
     from_below = from_behind(grad_pad[:, count + 2 :], "tile", 1)

time: 174 us -> 180 us (1.034)
  local copies, waits for them, and re-layouts: 20.2 us -> 31.3 us
  waiting for transfers between devices: 11.7 us -> 7.76 us
  other arithmetic: 27.4 us -> 24.4 us
  matrix products: 11.9 us -> 14.7 us
    unnamed x42 -> x64, local copies, waits for them, and re-layouts: 6.85 us -> 18 us
    another operation x18 -> x2, local copies, waits for them, and re-layouts: 4.77 us -> 0.86 us  [banded_along(): jnp.stack([cpad[..., per_block * b:per_block * b + window] for b in range...]
    dot_general x1, matrix products: 5.95 us -> 9.69 us  [banded_data(): jnp.einsum('pbkj,nj->pkbn', back4, block_basis(window), precision=lax.Pre...]
    concatenate x1 -> x3, other arithmetic: 3.74 us -> 0.62 us  [local(): halo_along = banded_along(jnp.concatenate([before, after], axis=1), ny)]
    dot_general x0 -> x1, local copies, waits for them, and re-layouts: none -> 2.76 us  [banded_along(): jnp.einsum('pbkn,nj->pbkj', cwin, block_basis(window), precision=lax.Prec...]
    ppermute x2, waiting for transfers between devices: 1.91 us -> 0.01 us  [the longest x1 0.01 us: local(): before = lax.ppermute(coefs[:, count - 2:], 'tile', up)]
    dot_general x1 -> x2, matrix products: 5.96 us -> 5.03 us  [banded_along(): jnp.einsum('pbkn,nj->pbkj', cwin, block_basis(window), precision=lax.Prec...]
  transfers between devices with their start and end apart: 16 -> 16, of which waited for: 4 -> 3; matrix products, arithmetic and copies ran while one was open for 7% -> 17% of each run, Pallas kernels for 35% -> 34%
where the time goes in v5:
time: 180 us; the launch traced here: 178 us
  Pallas kernels  79.9 us (44%)
  local copies, waits for them, and re-layouts  31.3 us (17%)
  other arithmetic  24.4 us (14%)
  starting transfers between devices  19.2 us (11%)
  matrix products  14.7 us (8%)
  waiting for transfers between devices  7.76 us (4%)
    pallas_call x4, Pallas kernels, back_chunk(): pl.pallas_call(back_kernel, grid=(width // TN,), in_specs=in_specs, out_s...  46.1 us
    pallas_call x4, Pallas kernels, fit_chunk(): pl.pallas_call(fit_kernel, grid=(width // TN,), in_specs=[pl.BlockSpec((4...  33.8 us
    unnamed x64, local copies, waits for them, and re-layouts  18 us
    dot_general x1, matrix products, banded_data(): jnp.einsum('pbkj,nj->pkbn', back4, block_basis(window), precision=lax.Pre...  9.69 us
    concatenate x8, other arithmetic, finish(): return jnp.concatenate([first, second], axis=0)  7.15 us
    ppermute x12, starting transfers between devices, local(): pending.append((c, finish, lax.ppermute(send, 'pred', pairs)))  7.05 us
    ppermute x2, starting transfers between devices, from_behind(): return lax.ppermute(block, axis, route)  5.97 us
    ppermute x12, waiting for transfers between devices, local(): pending.append((c, finish, lax.ppermute(send, 'pred', pairs)))  5.5 us
  transfers between devices with their start and end apart: 16, of which 3 were waited for; matrix products, arithmetic and copies ran while one was open for 17% of the time, Pallas kernels for 34%

profile of v5, /device:TPU:0, one launch (start us, length us, event | category | flops | bytes accessed | tf_op | source)
XLA Modules:
  0.0 178.4 jit_solution(6808454277399226792)
XLA Ops:
  0.6 1.1 fusion.124
  1.8 4.8 %collective-permute-start = (f32[16,2,512]{2,1,0:T(2,128)S(1)}, f32[16,2,512]{2,1,0:T(2,128)S(1)}, u32[]{:S(2)}, u32[]{:S(2)}) collective-permute-start(f32[16,2,512]{2,1,0:T(2,128)S(1)} %get-tuple-element.71), channel_id=1, source_target_pairs={{0,4},{4,8},{8,12},{12,16},{16,20},{20,24},{24,28},{1,5},{5,9},{9,... | collective-permute-start | bytes 196616 | tf_op jit(solution)/shard_map/ppermute | solution.py:261
  6.6 1.3 collective-permute-start.1
  8.0 0.9 fusion.63
  9.0 1.0 bitcast_dynamic-update-slice_fusion.11
  10.0 1.0 bitcast_dynamic-update-slice_fusion.10
  10.9 1.0 bitcast_dynamic-update-slice_fusion.9
  11.9 1.0 bitcast_dynamic-update-slice_fusion.8
  12.9 1.0 bitcast_dynamic-update-slice_fusion.7
  13.9 1.0 bitcast_dynamic-update-slice_fusion.6
  14.9 1.0 bitcast_dynamic-update-slice_fusion.5
  15.9 1.0 bitcast_dynamic-update-slice_fusion.4
  16.9 1.0 bitcast_dynamic-update-slice_fusion.3
  17.9 1.0 bitcast_dynamic-update-slice_fusion.2
  18.9 1.0 bitcast_dynamic-update-slice_fusion.1
  19.9 1.0 bitcast_dynamic-update-slice_fusion
  21.1 3.9 %fusion.26.a_ref = f32[16,16,8,512]{3,2,1,0:T(8,128)} fusion(f32[16,16,8,128]{3,2,1,0:T(8,128)S(1)} %fusion.69, f32[512]{0:T(512)S(1)} %get-tuple-element.91, f32[512]{0:T(512)S(1)} %get-tuple-element.92, f32[512]{0:T(512)S(1)} %get-tuple-element.90, f32[512]{0:T(512)S(1)} %get-tuple-element.89, s32[512]{0:T(512)S(1)} %add_select_fusion, ...), kind=kOutput, calls=%fused_computation.90 | convolution fusion | flops 805896192 | bytes 5253632 | tf_op jit(solution)/shard_map/pbkn,nj->pbkj/dot_general | solution.py:68
  25.8 0.8 stack.143
  26.6 1.1 fusion.24
  27.7 2.8 %copy.57.h_ref = f32[16,16,4,512]{3,2,1,0:T(4,128)} copy(f32[16,16,4,512]{3,1,2,0:T(8,128)S(1)} %fusion.24) | data formatting | bytes 4194304 | tf_op jit(solution)/shard_map/pbkn,nj->pbkj/dot_general | solution.py:68
  31.2 8.4 %shard_map.118 = f32[128,2048]{1,0:T(8,128)} custom-call(f32[4,16,256]{2,1,0:T(8,128)} %broadcast_in_dim.77.w_ref, bf16[16,128,8192]{2,1,0:T(8,128)(2,1)} %cov_ref.15, f32[16,16,8,512]{3,2,1,0:T(8,128)} %fusion.26.a_ref, f32[16,16,4,512]{3,2,1,0:T(4,128)} %copy.57.h_ref), custom_call_target="tpu_custom_call" | custom-call | flops 41943040 | bytes 11010048 | tf_op jit(solution)/shard_map/pallas_call | solution.py:183
  39.6 1.1 dynamic-slice_bitcast_fusion.3
  40.8 8.5 %shard_map.119 = f32[128,2048]{1,0:T(8,128)} custom-call(f32[4,16,256]{2,1,0:T(8,128)} %broadcast_in_dim.77.w_ref, bf16[16,128,8192]{2,1,0:T(8,128)(2,1)} %cov_ref.15, f32[16,16,8,512]{3,2,1,0:T(8,128)} %fusion.26.a_ref, f32[16,16,4,512]{3,2,1,0:T(4,128)} %copy.57.h_ref), custom_call_target="tpu_custom_call" | custom-call | flops 41943040 | bytes 11010048 | tf_op jit(solution)/shard_map/pallas_call | solution.py:183
  49.3 1.9 %dynamic-slice_bitcast_fusion.2 = f32[64,2048]{1,0:T(8,128)} fusion(f32[2,64,2048]{2,1,0:T(8,128)} %bitcast.131, s32[]{:T(128)S(6)} %select_n.177), kind=kLoop, calls=%fused_computation.28 | loop fusion | bytes 1048580 | tf_op jit(solution)/shard_map/jit(dynamic_index_in_dim)/squeeze | solution.py:100
  51.8 1.6 collective-permute-start.3
  53.3 8.5 %shard_map.120 = f32[128,2048]{1,0:T(8,128)} custom-call(f32[4,16,256]{2,1,0:T(8,128)} %broadcast_in_dim.77.w_ref, bf16[16,128,8192]{2,1,0:T(8,128)(2,1)} %cov_ref.15, f32[16,16,8,512]{3,2,1,0:T(8,128)} %fusion.26.a_ref, f32[16,16,4,512]{3,2,1,0:T(4,128)} %copy.57.h_ref), custom_call_target="tpu_custom_call" | custom-call | flops 41943040 | bytes 11010048 | tf_op jit(solution)/shard_map/pallas_call | solution.py:183
  61.9 0.8 copy-done.14
  62.7 3.1 %collective-permute-done.3 = f32[64,2048]{1,0:T(8,128)} collective-permute-done((f32[64,2048]{1,0:T(8,128)S(1)}, f32[64,2048]{1,0:T(8,128)}, u32[]{:S(2)}, u32[]{:S(2)}) %collective-permute-start.3) | collective-permute-done | bytes 524320 | tf_op jit(solution)/shard_map/ppermute | solution.py:284
  65.8 1.1 bitcast_add_fusion.2
  66.9 1.3 add.352
  68.2 0.8 dynamic-slice_bitcast_fusion.1
  69.5 1.5 collective-permute-start.6
  71.7 8.4 %shard_map.121 = f32[128,2048]{1,0:T(8,128)} custom-call(f32[4,16,256]{2,1,0:T(8,128)} %broadcast_in_dim.77.w_ref, bf16[16,128,8192]{2,1,0:T(8,128)(2,1)} %cov_ref.15, f32[16,16,8,512]{3,2,1,0:T(8,128)} %fusion.26.a_ref, f32[16,16,4,512]{3,2,1,0:T(4,128)} %copy.57.h_ref), custom_call_target="tpu_custom_call" | custom-call | flops 41943040 | bytes 11010048 | tf_op jit(solution)/shard_map/pallas_call | solution.py:183
  80.1 1.0 constant_dynamic-update-slice_fusion
  81.1 2.4 %collective-permute-done.6 = f32[64,2048]{1,0:T(8,128)} collective-permute-done((f32[64,2048]{1,0:T(8,128)S(1)}, f32[64,2048]{1,0:T(8,128)}, u32[]{:S(2)}, u32[]{:S(2)}) %collective-permute-start.6) | collective-permute-done | bytes 524320 | tf_op jit(solution)/shard_map/ppermute | solution.py:284
  83.5 1.9 %bitcast_add_fusion.1 = f32[64,2048]{1,0:T(8,128)} fusion(f32[64,2048]{1,0:T(8,128)} %collective-permute-done.7, f32[2,64,2048]{2,1,0:T(8,128)S(1)} %bitcast.130, s32[]{:T(128)S(6)} %select_n.176), kind=kLoop, calls=%fused_computation.23 | loop fusion | flops 131072 | bytes 1572868 | tf_op jit(solution)/shard_map/add | solution.py:101
  85.4 1.1 add.355
  86.5 0.8 dynamic-slice_bitcast_fusion
  87.8 1.5 collective-permute-start.9
  89.3 1.1 broadcast_select_fusion.7
  90.5 1.0 pad_maximum_fusion.t_ref
  91.5 12.0 %shard_map.122.rest_0_ = f32[16,16,12,512]{3,2,1,0:T(8,128)} custom-call(f32[4,16,256]{2,1,0:T(8,128)} %broadcast_in_dim.77.w_ref, bf16[16,128,8192]{2,1,0:T(8,128)(2,1)} %cov_ref.15, f32[128,2048]{1,0:T(8,128)} %pad_maximum_fusion.t_ref, f32[128,8192]{1,0:T(8,128)} %y_ref.7, s32[128,8192]{1,0:T(8,128)} %g_ref.7), custom_call_target="tpu_custom_call" | custom-call | flops 41943040 | bytes 13107200 | tf_op jit(solution)/shard_map/pallas_call | solution.py:220
  104.3 1.1 bitcast_add_fusion
  105.4 1.3 add.357
  107.3 1.1 broadcast_select_fusion.5
  108.4 1.0 pad_maximum_fusion.1.t_ref
  109.5 11.3 %shard_map.123.rest_0_ = f32[16,16,12,512]{3,2,1,0:T(8,128)} custom-call(f32[4,16,256]{2,1,0:T(8,128)} %broadcast_in_dim.77.w_ref, bf16[16,128,8192]{2,1,0:T(8,128)(2,1)} %cov_ref.15, f32[128,2048]{1,0:T(8,128)} %pad_maximum_fusion.1.t_ref, f32[128,8192]{1,0:T(8,128)} %y_ref.7, s32[128,8192]{1,0:T(8,128)} %g_ref.7, ...), custom_call_target="tpu_custom_call", output_to_operand_aliasing={{}: (5, {})} | custom-call | flops 41943040 | bytes 13107200 | tf_op jit(solution)/shard_map/pallas_call | solution.py:220
  121.6 1.1 add.359
  123.0 1.0 pad_maximum_fusion.2.t_ref
  124.0 11.4 %shard_map.124.rest_0_ = f32[16,16,12,512]{3,2,1,0:T(8,128)} custom-call(f32[4,16,256]{2,1,0:T(8,128)} %broadcast_in_dim.77.w_ref, bf16[16,128,8192]{2,1,0:T(8,128)(2,1)} %cov_ref.15, f32[128,2048]{1,0:T(8,128)} %pad_maximum_fusion.2.t_ref, f32[128,8192]{1,0:T(8,128)} %y_ref.7, s32[128,8192]{1,0:T(8,128)} %g_ref.7, ...), custom_call_target="tpu_custom_call", output_to_operand_aliasing={{}: (5, {})} | custom-call | flops 41943040 | bytes 13107200 | tf_op jit(solution)/shard_map/pallas_call | solution.py:220
  137.0 1.0 pad_maximum_fusion.3.t_ref
  138.1 11.4 %shard_map.125 = f32[16,16,12,512]{3,2,1,0:T(8,128)} custom-call(f32[4,16,256]{2,1,0:T(8,128)} %broadcast_in_dim.77.w_ref, bf16[16,128,8192]{2,1,0:T(8,128)(2,1)} %cov_ref.15, f32[128,2048]{1,0:T(8,128)} %pad_maximum_fusion.3.t_ref, f32[128,8192]{1,0:T(8,128)} %y_ref.7, s32[128,8192]{1,0:T(8,128)} %g_ref.7, ...), custom_call_target="tpu_custom_call", output_to_operand_aliasing={{}: (5, {})} | custom-call | flops 41943040 | bytes 13107200 | tf_op jit(solution)/shard_map/pallas_call | solution.py:220
  149.5 9.7 %fusion.2 = f32[16,12,16,128]{3,2,1,0:T(8,128)S(1)} fusion(f32[16,16,12,512]{3,2,1,0:T(8,128)} %shard_map.125, f32[512]{0:T(512)S(1)} %get-tuple-element.91, f32[512]{0:T(512)S(1)} %get-tuple-element.92, f32[512]{0:T(512)S(1)} %copy-done.18, f32[512]{0:T(512)S(1)} %get-tuple-element.89, s32[512]{0:T(512)S(1)} %add_select_fusion, s32[128]{0:T(128)S(1)} %copy-done.20), kind=kOutput, calls=%fused_computation.3 | convolution fusion | flops 1208549376 | bytes 7875072 | tf_op jit(solution)/shard_map/pbkj,nj->pkbn/dot_general | solution.py:75
  159.2 1.4 fusion.122
  160.5 1.1 pad_add_fusion
  162.7 4.5 %collective-permute-start.14 = (f32[16,2,512]{2,0,1:T(8,128)S(1)}, f32[16,2,512]{2,0,1:T(8,128)S(1)}, u32[]{:S(2)}, u32[]{:S(2)}) collective-permute-start(f32[16,2,512]{2,0,1:T(8,128)S(1)} %get-tuple-element.66), channel_id=1, source_target_pairs={{0,4},{4,8},{8,12},{12,16},{16,20},{20,24},{24,28},{1,5},{5,9},{9,... | collective-permute-start | bytes 196616 | tf_op jit(solution)/shard_map/ppermute | solution.py:31
  167.4 1.4 collective-permute-start.15
  168.8 3.1 %subtract_multiply_fusion = (f32[32,8192]{1,0:T(8,128)}, f32[32,8192]{1,0:T(8,128)}) fusion(f32[128,8192]{1,0:T(8,128)} %y_ref.7, s32[]{:T(128)S(6)} %select_n.180, s32[128,8192]{1,0:T(8,128)} %g_ref.7, f32[32,2048]{1,0:T(8,128)S(1)} %copy-done.13, f32[32,2048]{1,0:T(8,128)S(1)} %copy-done.12, f32[32,2048]{1,0:T(8,128)S(1)} %copy-done.11, ...), kind=kLoop, calls=%fused_computation.17 | loop fusion | flops 1572864 | bytes 5242884 | tf_op jit(solution)/shard_map/mul | solution.py:307
  171.9 2.2 %collective-permute-done.15 = f32[16,2,512]{2,0,1:T(8,128)S(1)} collective-permute-done((f32[16,2,512]{2,0,1:T(8,128)S(1)}, f32[16,2,512]{2,0,1:T(8,128)S(1)}, u32[]{:S(2)}, u32[]{:S(2)}) %collective-permute-start.15) | collective-permute-done | bytes 65568 | tf_op jit(solution)/shard_map/ppermute | solution.py:31
  174.2 0.8 divide_subtract_fusion
  175.0 0.9 copy.73
  175.8 0.9 copy.74
  176.7 0.9 copy.75
  177.5 0.9 copy.72
  (93 shorter events, 9.2 us)
Async XLA Ops:
  0.6 20.2 %copy-start = (f32[16,8,512]{2,1,0:T(8,128)S(1)}, f32[16,8,512]{2,1,0:T(8,128)}, u32[]{:S(2)}) copy-start(f32[16,8,512]{2,1,0:T(8,128)} %param.10) | copy-start | bytes 786436
  1.8 23.3 %collective-permute-start = (f32[16,2,512]{2,1,0:T(2,128)S(1)}, f32[16,2,512]{2,1,0:T(2,128)S(1)}, u32[]{:S(2)}, u32[]{:S(2)}) collective-permute-start(f32[16,2,512]{2,1,0:T(2,128)S(1)} %get-tuple-element.71), channel_id=1, source_target_pairs={{0,4},{4,8},{8,12},{12,16},{16,20},{20,24},{24,28},{1,5},{5,9},{9,... | collective-permute-start | bytes 196616 | tf_op jit(solution)/shard_map/ppermute | solution.py:261
  6.6 18.4 %collective-permute-start.1 = (f32[16,2,512]{2,1,0:T(2,128)S(1)}, f32[16,2,512]{2,1,0:T(2,128)S(1)}, u32[]{:S(2)}, u32[]{:S(2)}) collective-permute-start(f32[16,2,512]{2,1,0:T(2,128)S(1)} %get-tuple-element.72), channel_id=1, source_target_pairs={{4,0},{8,4},{12,8},{16,12},{20,16},{24,20},{28,24},{5,1},{9,5},{13... | collective-permute-start | bytes 196616 | tf_op jit(solution)/shard_map/ppermute | solution.py:262
  8.0 18.7 %copy-start.19 = (s32[128]{0:T(128)}, s32[128]{0:T(128)S(1)}, u32[]{:S(2)}) copy-start(s32[128]{0:T(128)S(1)} %iota_add_fusion) | copy-start | bytes 1540
  8.0 18.6 %copy-start.17 = (f32[512]{0:T(512)}, f32[512]{0:T(512)S(1)}, u32[]{:S(2)}) copy-start(f32[512]{0:T(512)S(1)} %get-tuple-element.90) | copy-start | bytes 6148
  40.7 8.6 %collective-permute-start.2 = (f32[64,2048]{1,0:T(8,128)S(1)}, f32[64,2048]{1,0:T(8,128)S(1)}, u32[]{:S(2)}, u32[]{:S(2)}) collective-permute-start(f32[64,2048]{1,0:T(8,128)S(1)} %dynamic-slice_bitcast_fusion.3), channel_id=1, source_target_pairs={{0,1},{1,0},{2,3},{3,2},{4,5},{5,4},{6,7},{7,6},{8,9},{9,8},{10,11... | collective-permute-start | bytes 1572872 | tf_op jit(solution)/shard_map/ppermute | solution.py:284
  40.8 10.9 %copy-start.1 = (f32[128,2048]{1,0:T(8,128)S(1)}, f32[128,2048]{1,0:T(8,128)}, u32[]{:S(2)}) copy-start(f32[128,2048]{1,0:T(8,128)} %shard_map.118) | copy-start | bytes 3145732
  51.2 10.6 %collective-permute-start.4 = (f32[64,2048]{1,0:T(8,128)}, f32[64,2048]{1,0:T(8,128)S(1)}, u32[]{:S(2)}, u32[]{:S(2)}) collective-permute-start(f32[64,2048]{1,0:T(8,128)} %dynamic-slice_bitcast_fusion.2), channel_id=1, source_target_pairs={{0,1},{1,0},{2,3},{3,2},{4,5},{5,4},{6,7},{7,6},{8,9},{9,8},{10,11... | collective-permute-start | bytes 1572872 | tf_op jit(solution)/shard_map/ppermute | solution.py:284
  51.7 10.1 %copy-start.5 = (f32[64,2048]{1,0:T(8,128)}, f32[64,2048]{1,0:T(8,128)S(1)}, u32[]{:S(2)}) copy-start(f32[64,2048]{1,0:T(8,128)S(1)} %bitcast_add_fusion.3) | copy-start | bytes 1572868
  51.8 14.0 %collective-permute-start.3 = (f32[64,2048]{1,0:T(8,128)S(1)}, f32[64,2048]{1,0:T(8,128)}, u32[]{:S(2)}, u32[]{:S(2)}) collective-permute-start(f32[64,2048]{1,0:T(8,128)S(1)} %bitcast_add_fusion.3), channel_id=1, source_target_pairs={{0,2},{1,3},{2,0},{3,1},{4,6},{5,7},{6,4},{7,5},{8,10},{9,11},{10,... | collective-permute-start | bytes 1572872 | tf_op jit(solution)/shard_map/ppermute | solution.py:284
  53.3 12.5 %copy-start.4 = (f32[128,2048]{1,0:T(8,128)S(1)}, f32[128,2048]{1,0:T(8,128)}, u32[]{:S(2)}) copy-start(f32[128,2048]{1,0:T(8,128)} %shard_map.119) | copy-start | bytes 3145732
  61.8 6.3 %copy-start.3 = (f32[128,2048]{1,0:T(8,128)S(1)}, f32[128,2048]{1,0:T(8,128)}, u32[]{:S(2)}) copy-start(f32[128,2048]{1,0:T(8,128)} %shard_map.120) | copy-start | bytes 3145732
  61.8 0.8 copy-start.14
  69.0 12.1 %collective-permute-start.7 = (f32[64,2048]{1,0:T(8,128)}, f32[64,2048]{1,0:T(8,128)}, u32[]{:S(2)}, u32[]{:S(2)}) collective-permute-start(f32[64,2048]{1,0:T(8,128)} %dynamic-slice_bitcast_fusion.1), channel_id=1, source_target_pairs={{0,1},{1,0},{2,3},{3,2},{4,5},{5,4},{6,7},{7,6},{8,9},{9,8},{10,11... | collective-permute-start | bytes 1572872 | tf_op jit(solution)/shard_map/ppermute | solution.py:284
  69.0 12.1 %collective-permute-start.5 = (f32[64,2048]{1,0:T(8,128)S(1)}, f32[64,2048]{1,0:T(8,128)}, u32[]{:S(2)}, u32[]{:S(2)}) collective-permute-start(f32[64,2048]{1,0:T(8,128)S(1)} %add.352), channel_id=1, source_target_pairs={{0,1},{1,0},{2,3},{3,2},{4,5},{5,4},{6,7},{7,6},{8,9},{9,8},{10,11... | collective-permute-start | bytes 1572872 | tf_op jit(solution)/shard_map/ppermute | solution.py:284
  69.5 13.9 %collective-permute-start.6 = (f32[64,2048]{1,0:T(8,128)S(1)}, f32[64,2048]{1,0:T(8,128)}, u32[]{:S(2)}, u32[]{:S(2)}) collective-permute-start(f32[64,2048]{1,0:T(8,128)S(1)} %bitcast_add_fusion.2), channel_id=1, source_target_pairs={{0,2},{1,3},{2,0},{3,1},{4,6},{5,7},{6,4},{7,5},{8,10},{9,11},{10,... | collective-permute-start | bytes 1572872 | tf_op jit(solution)/shard_map/ppermute | solution.py:284
  80.1 6.4 %copy-start.2 = (f32[128,2048]{1,0:T(8,128)S(1)}, f32[128,2048]{1,0:T(8,128)}, u32[]{:S(2)}) copy-start(f32[128,2048]{1,0:T(8,128)} %shard_map.121) | copy-start | bytes 3145732
  81.1 6.8 %copy-start.6 = (f32[16,10,512]{2,0,1:T(8,128)}, f32[16,10,512]{2,0,1:T(8,128)S(1)}, u32[]{:S(2)}) copy-start(f32[16,10,512]{2,0,1:T(8,128)S(1)} %copy_dynamic-update-slice_fusion) | copy-start | bytes 983044
  87.3 16.9 %collective-permute-start.10 = (f32[64,2048]{1,0:T(8,128)}, f32[64,2048]{1,0:T(8,128)}, u32[]{:S(2)}, u32[]{:S(2)}) collective-permute-start(f32[64,2048]{1,0:T(8,128)} %dynamic-slice_bitcast_fusion), channel_id=1, source_target_pairs={{0,1},{1,0},{2,3},{3,2},{4,5},{5,4},{6,7},{7,6},{8,9},{9,8},{10,11... | collective-permute-start | bytes 1572872 | tf_op jit(solution)/shard_map/ppermute | solution.py:284
  87.3 16.9 %collective-permute-start.8 = (f32[64,2048]{1,0:T(8,128)S(1)}, f32[64,2048]{1,0:T(8,128)}, u32[]{:S(2)}, u32[]{:S(2)}) collective-permute-start(f32[64,2048]{1,0:T(8,128)S(1)} %add.355), channel_id=1, source_target_pairs={{0,1},{1,0},{2,3},{3,2},{4,5},{5,4},{6,7},{7,6},{8,9},{9,8},{10,11... | collective-permute-start | bytes 1572872 | tf_op jit(solution)/shard_map/ppermute | solution.py:284
  87.8 16.4 %collective-permute-start.9 = (f32[64,2048]{1,0:T(8,128)}, f32[64,2048]{1,0:T(8,128)}, u32[]{:S(2)}, u32[]{:S(2)}) collective-permute-start(f32[64,2048]{1,0:T(8,128)} %bitcast_add_fusion.1), channel_id=1, source_target_pairs={{0,2},{1,3},{2,0},{3,1},{4,6},{5,7},{6,4},{7,5},{8,10},{9,11},{10,... | collective-permute-start | bytes 1572872 | tf_op jit(solution)/shard_map/ppermute | solution.py:284
  106.6 14.9 %collective-permute-start.11 = (f32[64,2048]{1,0:T(8,128)S(1)}, f32[64,2048]{1,0:T(8,128)S(1)}, u32[]{:S(2)}, u32[]{:S(2)}) collective-permute-start(f32[64,2048]{1,0:T(8,128)S(1)} %add.357), channel_id=1, source_target_pairs={{0,1},{1,0},{2,3},{3,2},{4,5},{5,4},{6,7},{7,6},{8,9},{9,8},{10,11... | collective-permute-start | bytes 1572872 | tf_op jit(solution)/shard_map/ppermute | solution.py:284
  106.7 14.8 %collective-permute-start.12 = (f32[64,2048]{1,0:T(8,128)S(1)}, f32[64,2048]{1,0:T(8,128)}, u32[]{:S(2)}, u32[]{:S(2)}) collective-permute-start(f32[64,2048]{1,0:T(8,128)S(1)} %bitcast_add_fusion), channel_id=1, source_target_pairs={{0,2},{1,3},{2,0},{3,1},{4,6},{5,7},{6,4},{7,5},{8,10},{9,11},{10,... | collective-permute-start | bytes 1572872 | tf_op jit(solution)/shard_map/ppermute | solution.py:284
  122.7 13.5 %collective-permute-start.13 = (f32[64,2048]{1,0:T(8,128)S(1)}, f32[64,2048]{1,0:T(8,128)S(1)}, u32[]{:S(2)}, u32[]{:S(2)}) collective-permute-start(f32[64,2048]{1,0:T(8,128)S(1)} %add.359), channel_id=1, source_target_pairs={{0,1},{1,0},{2,3},{3,2},{4,5},{5,4},{6,7},{7,6},{8,9},{9,8},{10,11... | collective-permute-start | bytes 1572872 | tf_op jit(solution)/shard_map/ppermute | solution.py:284
  138.1 11.4 %copy-start.18 = (f32[512]{0:T(512)S(1)}, f32[512]{0:T(512)}, u32[]{:S(2)}) copy-start(f32[512]{0:T(512)} %copy-done.17) | copy-start | bytes 6148
  138.1 11.4 %copy-start.20 = (s32[128]{0:T(128)S(1)}, s32[128]{0:T(128)}, u32[]{:S(2)}) copy-start(s32[128]{0:T(128)} %copy-done.19) | copy-start | bytes 1540
  161.7 7.1 %copy-start.10 = (f32[32,2048]{1,0:T(8,128)S(1)}, f32[32,2048]{1,0:T(8,128)}, u32[]{:S(2)}) copy-start(f32[32,2048]{1,0:T(8,128)} %fusion.18) | copy-start | bytes 786436
  162.2 6.6 %copy-start.11 = (f32[32,2048]{1,0:T(8,128)S(1)}, f32[32,2048]{1,0:T(8,128)}, u32[]{:S(2)}) copy-start(f32[32,2048]{1,0:T(8,128)} %fusion.17) | copy-start | bytes 786436
  162.2 6.6 %copy-start.12 = (f32[32,2048]{1,0:T(8,128)S(1)}, f32[32,2048]{1,0:T(8,128)}, u32[]{:S(2)}) copy-start(f32[32,2048]{1,0:T(8,128)} %fusion.16) | copy-start | bytes 786436
  162.2 6.6 %copy-start.13 = (f32[32,2048]{1,0:T(8,128)S(1)}, f32[32,2048]{1,0:T(8,128)}, u32[]{:S(2)}) copy-start(f32[32,2048]{1,0:T(8,128)} %fusion.15) | copy-start | bytes 786436
  162.7 9.2 %collective-permute-start.14 = (f32[16,2,512]{2,0,1:T(8,128)S(1)}, f32[16,2,512]{2,0,1:T(8,128)S(1)}, u32[]{:S(2)}, u32[]{:S(2)}) collective-permute-start(f32[16,2,512]{2,0,1:T(8,128)S(1)} %get-tuple-element.66), channel_id=1, source_target_pairs={{0,4},{4,8},{8,12},{12,16},{16,20},{20,24},{24,28},{1,5},{5,9},{9,... | collective-permute-start | bytes 196616 | tf_op jit(solution)/shard_map/ppermute | solution.py:31
  167.3 6.9 %copy-start.7 = (f32[16,10,512]{2,0,1:T(8,128)S(1)}, f32[16,10,512]{2,0,1:T(8,128)}, u32[]{:S(2)}) copy-start(f32[16,10,512]{2,0,1:T(8,128)} %copy-done.6) | copy-start | bytes 983044
  167.3 6.9 %copy-start.8 = (f32[16,10,512]{2,0,1:T(8,128)S(1)}, f32[16,10,512]{2,0,1:T(8,128)}, u32[]{:S(2)}) copy-start(f32[16,10,512]{2,0,1:T(8,128)} %get-tuple-element.68) | copy-start | bytes 983044
  167.3 6.9 %copy-start.9 = (f32[16,8,512]{2,0,1:T(8,128)S(1)}, f32[16,8,512]{2,0,1:T(8,128)}, u32[]{:S(2)}) copy-start(f32[16,8,512]{2,0,1:T(8,128)} %get-tuple-element.70) | copy-start | bytes 786436
  167.3 6.9 %copy-start.15 = (f32[16,8,512]{2,1,0:T(8,128)S(1)}, f32[16,8,512]{2,1,0:T(8,128)}, u32[]{:S(2)}) copy-start(f32[16,8,512]{2,1,0:T(8,128)} %param.11) | copy-start | bytes 786436
  167.3 6.9 %copy-start.16 = (f32[16,8,512]{2,1,0:T(8,128)S(1)}, f32[16,8,512]{2,1,0:T(8,128)}, u32[]{:S(2)}) copy-start(f32[16,8,512]{2,1,0:T(8,128)} %param.12) | copy-start | bytes 786436
  167.4 6.9 %copy-start.21 = (f32[16]{0:T(128)S(1)}, f32[16]{0:T(128)}, u32[]{:S(2)}) copy-start(f32[16]{0:T(128)} %param.13) | copy-start | bytes 196
  167.4 6.8 %collective-permute-start.15 = (f32[16,2,512]{2,0,1:T(8,128)S(1)}, f32[16,2,512]{2,0,1:T(8,128)S(1)}, u32[]{:S(2)}, u32[]{:S(2)}) collective-permute-start(f32[16,2,512]{2,0,1:T(8,128)S(1)} %get-tuple-element.67), channel_id=1, source_target_pairs={{4,0},{8,4},{12,8},{16,12},{20,16},{24,20},{28,24},{5,1},{9,5},{13... | collective-permute-start | bytes 196616 | tf_op jit(solution)/shard_map/ppermute | solution.py:31

commit v6 on v4

--- a/solution.py
+++ b/solution.py
@@ -104,7 +104,7 @@
         def swap(cur):
             return cur, lambda recv: cur + recv
         steps.append((bit, swap))
-    for bit in reversed(bits[:-1]):
+    for bit in reversed(bits[1:-1]):
         def double(cur, bit=bit):
             mine = (idx // bit) % 2
             def finish(other):
@@ -113,6 +113,10 @@
                 return jnp.concatenate([first, second], axis=0)
             return cur, finish
         steps.append((bit, double))
+    if len(bits) > 1:
+        def last(cur):
+            return cur, lambda other: (cur, other)
+        steps.append((1, last))
     return [(bit, fn, [(i, i ^ bit) for i in range(n)]) for bit, fn in steps]
 
 
@@ -135,14 +139,18 @@
             o_ref[rows, cols] = acc
 
 
-def back_kernel(w_ref, cov_ref, t_ref, y_ref, g_ref, o_ref, rw_ref):
+def back_kernel(b_ref, w_ref, cov_ref, t_ref, u_ref, y_ref, g_ref, o_ref, rw_ref):
     npred = cov_ref.shape[0]
     nint = cov_ref.shape[1] // H
+    mine = b_ref[0]
     for s in range(TN // L):
         cols = pl.ds(s * L, L)
         for m in range(nint):
             rows = pl.ds(m * H, H)
-            resid = g_ref[rows, cols].astype(jnp.float32) * (y_ref[rows, cols] - t_ref[rows, cols])
+            inner = pl.ds((m % (nint // 2)) * H, H)
+            side = m // (nint // 2)
+            total = jnp.where(mine == side, t_ref[inner, cols], u_ref[inner, cols])
+            resid = g_ref[rows, cols].astype(jnp.float32) * (y_ref[rows, cols] - total)
             for d in range(4):
                 rw_ref[d, rows, :] = w_ref[d] * resid
 
@@ -188,17 +196,20 @@
     )(wl, cov, along)
 
 
-def back_chunk(wl, cov, total, target, land, chunk, nrow):
+def back_chunk(wl, cov, halves, target, land, chunk, nrow):
     npred, rows, _ = cov.shape
-    width = total.shape[1]
+    cur, other, mine = halves
+    width = cur.shape[1]
     off = chunk * (width // TN)
     return pl.pallas_call(
         back_kernel,
         grid=(width // TN,),
         in_specs=[
+            pl.BlockSpec(memory_space=pltpu.SMEM),
             pl.BlockSpec((4, H, L), lambda j: (0, 0, 0)),
             pl.BlockSpec((npred, rows, TN), lambda j: (0, 0, j + off)),
-            pl.BlockSpec((rows, TN), lambda j: (0, j)),
+            pl.BlockSpec((rows // 2, TN), lambda j: (0, j)),
+            pl.BlockSpec((rows // 2, TN), lambda j: (0, j)),
             pl.BlockSpec((rows, TN), lambda j: (0, j + off)),
             pl.BlockSpec((rows, TN), lambda j: (0, j + off)),
         ],
@@ -211,7 +222,7 @@
             transcendentals=0,
             bytes_accessed=2 * npred * rows * width + 12 * rows * width + 4 * npred * nrow * width,
         ),
-    )(wl, cov, total, target, land)
+    )(mine, wl, cov, cur, other, target, land)
 
 
 def penalty(padded, count):
@@ -242,6 +253,12 @@
     land_blk = lax.dynamic_slice_in_dim(land, start, share, 0).astype(jnp.float32)
     width = ny // CHUNKS
     steps = reduce_steps(jnp.zeros((rows, width), jnp.float32), "pred")
+    bit0 = lax.axis_index("pred") % 2
+    bits_arr = jnp.reshape(bit0, (1,)).astype(jnp.int32)
+
+    def attach(halves):
+        return (halves[0], halves[1], bits_arr)
+
     nsteps = len(steps)
     state = [None] * CHUNKS
     fitted_parts = [None] * CHUNKS
@@ -261,6 +278,7 @@
             outs.append(("fit", s, fit_chunk(wl, covariates, along, s, width)))
         if next_back < CHUNKS and next_back + nsteps + 1 <= s:
             c = next_back
+            state[c] = attach(state[c])
             outs.append(("back", c, back_chunk(wl, covariates, state[c], target, land, c, nrow)))
             next_back += 1
         recvs = [r for _, _, r in pending]
@@ -275,8 +293,13 @@
             state[c] = finish(r)
     for c in range(CHUNKS):
         if back_parts[c] is None:
+            state[c] = attach(state[c])
             back_parts[c] = back_chunk(wl, covariates, state[c], target, land, c, nrow)
-        fitted_parts[c] = lax.dynamic_slice_in_dim(state[c], start, share, 0)
+        cur, other, _ = state[c]
+        half = rows // 2
+        side = start // half
+        picked = jnp.where(bit0 == side, cur, other)
+        fitted_parts[c] = lax.dynamic_slice_in_dim(picked, start - side * half, share, 0)
     fitted = jnp.concatenate(fitted_parts, axis=1)
     residual = land_blk * (target_blk - fitted)
     back = jnp.concatenate(back_parts, axis=1)

time: 174 us -> 172 us (0.989)
  other arithmetic: 27.4 us -> 22.4 us
  waiting for transfers between devices: 11.7 us -> 13.8 us
    concatenate x8 -> x0, other arithmetic: 7.15 us -> none  [finish(): return jnp.concatenate([first, second], axis=0)]
    select_n x4, other arithmetic: 2.44 us -> 5.03 us  [local(): picked = jnp.where(bit0 == side, cur, other)]
    ppermute x12, waiting for transfers between devices: 6.76 us -> 8.84 us  [local(): pending.append((c, finish, lax.ppermute(send, 'pred', pairs)))]
    unnamed x42 -> x66, local copies, waits for them, and re-layouts: 6.85 us -> 6.89 us
  transfers between devices with their start and end apart: 16 -> 16, of which waited for: 4 -> 5; matrix products, arithmetic and copies ran while one was open for 7% -> 5% of each run, Pallas kernels for 35% -> 35%
where the time goes in v6:
time: 172 us; the launch traced here: 171 us
  Pallas kernels  80.2 us (47%)
  other arithmetic  22.4 us (13%)
  starting transfers between devices  21.2 us (12%)
  local copies, waits for them, and re-layouts  20.4 us (12%)
  waiting for transfers between devices  13.8 us (8%)
  matrix products  11.9 us (7%)
    pallas_call x4, Pallas kernels, back_chunk(): pl.pallas_call(back_kernel, grid=(width // TN,), in_specs=[pl.BlockSpec(m...  46.3 us
    pallas_call x4, Pallas kernels, fit_chunk(): pl.pallas_call(fit_kernel, grid=(width // TN,), in_specs=[pl.BlockSpec((4...  33.9 us
    ppermute x12, waiting for transfers between devices, local(): pending.append((c, finish, lax.ppermute(send, 'pred', pairs)))  8.84 us
    ppermute x12, starting transfers between devices, local(): pending.append((c, finish, lax.ppermute(send, 'pred', pairs)))  8.67 us
    unnamed x66, local copies, waits for them, and re-layouts  6.89 us
    dot_general x1, matrix products, banded_data(): jnp.einsum('pbkj,nj->pkbn', back4, block_basis(window), precision=lax.Pre...  5.96 us
    dot_general x1, matrix products, banded_along(): jnp.einsum('pbkn,nj->pbkj', cwin, block_basis(window), precision=lax.Prec...  5.94 us
    ppermute x2, starting transfers between devices, from_behind(): return lax.ppermute(block, axis, route)  5.75 us
  transfers between devices with their start and end apart: 16, of which 5 were waited for; matrix products, arithmetic and copies ran while one was open for 5% of the time, Pallas kernels for 35%

profile of v6, /device:TPU:0, one launch (start us, length us, event | category | flops | bytes accessed | tf_op | source)
XLA Modules:
  0.0 171.2 jit_solution(10157256291027604561)
XLA Ops:
  0.6 1.1 copy.663
  1.8 0.7 copy-done.14
  2.5 1.3 collective-permute-start.1
  3.8 5.5 %collective-permute-start = (f32[16,2,512]{2,0,1:T(8,128)S(1)}, f32[16,2,512]{2,0,1:T(8,128)S(1)}, u32[]{:S(2)}, u32[]{:S(2)}) collective-permute-start(f32[16,2,512]{2,0,1:T(8,128)S(1)} %get-tuple-element.170), channel_id=1, source_target_pairs={{0,4},{4,8},{8,12},{12,16},{16,20},{20,24},{24,28},{1,5},{5,9},{9,... | collective-permute-start | bytes 196616 | tf_op jit(solution)/shard_map/ppermute | solution.py:22
  9.4 1.9 %collective-permute-done = f32[16,2,512]{2,0,1:T(8,128)S(1)} collective-permute-done((f32[16,2,512]{2,0,1:T(8,128)S(1)}, f32[16,2,512]{2,0,1:T(8,128)S(1)}, u32[]{:S(2)}, u32[]{:S(2)}) %collective-permute-start) | collective-permute-done | bytes 65568 | tf_op jit(solution)/shard_map/ppermute | solution.py:22
  11.3 1.1 constant_dynamic-update-slice_fusion.3
  12.4 0.7 copy-done.20
  13.1 0.5 fusion.49
  13.6 0.1 copy.681
  13.7 0.1 copy.679
  14.0 0.1 copy.677
  15.4 2.7 %stack.75 = f32[16,16,12,128]{3,1,2,0:T(8,128)S(1)} concatenate(f32[16,1,12,128]{3,1,2,0:T(1,128)S(1)} %copy.666, f32[16,1,12,128]{3,1,2,0:T(1,128)S(1)} %copy.667, f32[16,1,12,128]{3,1,2,0:T(1,128)S(1)} %copy.668, f32[16,1,12,128]{3,1,2,0:T(1,128)S(1)} %copy.669, f32[16,1,12,128]{3,1,2,0:T(1,128)S(1)} %copy.670, f32[16,1,12,128]{3,1,2,0:T(1,128)S(1)} %copy.671, ...), dimensions={1} | concatenate | bytes 3145728 | tf_op jit(solution)/shard_map/stack | solution.py:67
  18.0 5.9 %fusion.2.a_ref = f32[16,16,12,512]{3,2,1,0:T(8,128)} fusion(f32[16,16,12,128]{3,1,2,0:T(8,128)S(1)} %stack.75, f32[512]{0:T(512)S(1)} %get-tuple-element.177, f32[512]{0:T(512)S(1)} %get-tuple-element.178, f32[512]{0:T(512)S(1)} %get-tuple-element.176, f32[512]{0:T(512)S(1)} %get-tuple-element.175, s32[512]{0:T(512)S(1)} %add_select_fusion, ...), kind=kOutput, calls=%fused_computation.4 | convolution fusion | flops 1208549376 | bytes 7875072 | tf_op jit(solution)/shard_map/pbkn,nj->pbkj/dot_general | solution.py:68
  24.0 0.7 broadcast_in_dim.55.w_ref
  24.7 8.4 %shard_map.118 = f32[128,2048]{1,0:T(8,128)} custom-call(f32[4,16,256]{2,1,0:T(8,128)} %broadcast_in_dim.55.w_ref, bf16[16,128,8192]{2,1,0:T(8,128)(2,1)} %cov_ref.15, f32[16,16,12,512]{3,2,1,0:T(8,128)} %fusion.2.a_ref), custom_call_target="tpu_custom_call" | custom-call | flops 41943040 | bytes 11010048 | tf_op jit(solution)/shard_map/pallas_call | solution.py:180
  33.1 1.1 dynamic-slice_bitcast_fusion.3
  34.3 8.5 %shard_map.119 = f32[128,2048]{1,0:T(8,128)} custom-call(f32[4,16,256]{2,1,0:T(8,128)} %broadcast_in_dim.55.w_ref, bf16[16,128,8192]{2,1,0:T(8,128)(2,1)} %cov_ref.15, f32[16,16,12,512]{3,2,1,0:T(8,128)} %fusion.2.a_ref), custom_call_target="tpu_custom_call" | custom-call | flops 41943040 | bytes 11010048 | tf_op jit(solution)/shard_map/pallas_call | solution.py:180
  42.8 1.9 %dynamic-slice_bitcast_fusion.2 = f32[64,2048]{1,0:T(8,128)} fusion(f32[2,64,2048]{2,1,0:T(8,128)} %bitcast.68, s32[]{:T(128)S(6)} %select_n.141), kind=kLoop, calls=%fused_computation.23 | loop fusion | bytes 1048580 | tf_op jit(solution)/shard_map/jit(dynamic_index_in_dim)/squeeze | solution.py:100
  44.7 0.5 collective-permute-start.4
  45.3 2.0 %collective-permute-start.3 = (f32[64,2048]{1,0:T(8,128)S(1)}, f32[64,2048]{1,0:T(8,128)}, u32[]{:S(2)}, u32[]{:S(2)}) collective-permute-start(f32[64,2048]{1,0:T(8,128)S(1)} %bitcast_add_fusion.3), channel_id=1, source_target_pairs={{0,2},{1,3},{2,0},{3,1},{4,6},{5,7},{6,4},{7,5},{8,10},{9,11},{10,... | collective-permute-start | bytes 1572872 | tf_op jit(solution)/shard_map/ppermute | solution.py:275
  47.2 8.4 %shard_map.120 = f32[128,2048]{1,0:T(8,128)} custom-call(f32[4,16,256]{2,1,0:T(8,128)} %broadcast_in_dim.55.w_ref, bf16[16,128,8192]{2,1,0:T(8,128)(2,1)} %cov_ref.15, f32[16,16,12,512]{3,2,1,0:T(8,128)} %fusion.2.a_ref), custom_call_target="tpu_custom_call" | custom-call | flops 41943040 | bytes 11010048 | tf_op jit(solution)/shard_map/pallas_call | solution.py:180
  55.7 3.8 %collective-permute-done.3 = f32[64,2048]{1,0:T(8,128)} collective-permute-done((f32[64,2048]{1,0:T(8,128)S(1)}, f32[64,2048]{1,0:T(8,128)}, u32[]{:S(2)}, u32[]{:S(2)}) %collective-permute-start.3) | collective-permute-done | bytes 524320 | tf_op jit(solution)/shard_map/ppermute | solution.py:275
  59.5 1.1 bitcast_add_fusion.2
  60.6 1.3 add.328.t_ref
  61.9 0.9 dynamic-slice_bitcast_fusion.1
  62.8 0.5 collective-permute-start.5
  63.3 1.7 %collective-permute-start.6 = (f32[64,2048]{1,0:T(8,128)S(1)}, f32[64,2048]{1,0:T(8,128)}, u32[]{:S(2)}, u32[]{:S(2)}) collective-permute-start(f32[64,2048]{1,0:T(8,128)S(1)} %bitcast_add_fusion.2), channel_id=1, source_target_pairs={{0,2},{1,3},{2,0},{3,1},{4,6},{5,7},{6,4},{7,5},{8,10},{9,11},{10,... | collective-permute-start | bytes 1572872 | tf_op jit(solution)/shard_map/ppermute | solution.py:275
  65.0 8.4 %shard_map.121 = f32[128,2048]{1,0:T(8,128)} custom-call(f32[4,16,256]{2,1,0:T(8,128)} %broadcast_in_dim.55.w_ref, bf16[16,128,8192]{2,1,0:T(8,128)(2,1)} %cov_ref.15, f32[16,16,12,512]{3,2,1,0:T(8,128)} %fusion.2.a_ref), custom_call_target="tpu_custom_call" | custom-call | flops 41943040 | bytes 11010048 | tf_op jit(solution)/shard_map/pallas_call | solution.py:180
  73.5 3.7 %collective-permute-done.6 = f32[64,2048]{1,0:T(8,128)} collective-permute-done((f32[64,2048]{1,0:T(8,128)S(1)}, f32[64,2048]{1,0:T(8,128)}, u32[]{:S(2)}, u32[]{:S(2)}) %collective-permute-start.6) | collective-permute-done | bytes 524320 | tf_op jit(solution)/shard_map/ppermute | solution.py:275
  77.2 1.1 bitcast_add_fusion.1
  78.3 1.1 add.331.t_ref
  79.4 0.9 dynamic-slice_bitcast_fusion
  80.3 0.5 collective-permute-start.8
  80.8 1.7 %collective-permute-start.9 = (f32[64,2048]{1,0:T(8,128)S(1)}, f32[64,2048]{1,0:T(8,128)}, u32[]{:S(2)}, u32[]{:S(2)}) collective-permute-start(f32[64,2048]{1,0:T(8,128)S(1)} %bitcast_add_fusion.1), channel_id=1, source_target_pairs={{0,2},{1,3},{2,0},{3,1},{4,6},{5,7},{6,4},{7,5},{8,10},{9,11},{10,... | collective-permute-start | bytes 1572872 | tf_op jit(solution)/shard_map/ppermute | solution.py:275
  82.6 11.5 %shard_map.122 = f32[16,4,12,512]{3,2,1,0:T(8,128)} custom-call(s32[1]{0:T(128)} %bitcast.29.b_ref, f32[4,16,256]{2,1,0:T(8,128)} %broadcast_in_dim.55.w_ref, bf16[16,128,8192]{2,1,0:T(8,128)(2,1)} %cov_ref.15, f32[64,2048]{1,0:T(8,128)} %copy-done.5, f32[64,2048]{1,0:T(8,128)} %collective-permute-done.5.u_ref, f32[128,8192]{1,0:T(8,128)} %y_ref.7, ...), custom_call_target="tpu_custom_call" | custom-call | flops 41943040 | bytes 13107200 | tf_op jit(solution)/shard_map/pallas_call | solution.py:204
  94.1 0.8 copy-done.26
  94.9 1.3 bitcast_add_fusion
  96.1 1.1 add.333.t_ref
  97.3 1.5 collective-permute-start.12
  98.9 11.6 %shard_map.123 = f32[16,4,12,512]{3,2,1,0:T(8,128)} custom-call(s32[1]{0:T(128)} %bitcast.29.b_ref, f32[4,16,256]{2,1,0:T(8,128)} %broadcast_in_dim.55.w_ref, bf16[16,128,8192]{2,1,0:T(8,128)(2,1)} %cov_ref.15, f32[64,2048]{1,0:T(8,128)} %copy-done.7, f32[64,2048]{1,0:T(8,128)} %copy-done.16, f32[128,8192]{1,0:T(8,128)} %y_ref.7, s32[128,8192]{1,0:T(8,128)} %g_ref.7), custom_call_target="tpu_custom_call" | custom-call | flops 41943040 | bytes 13107200 | tf_op jit(solution)/shard_map/pallas_call | solution.py:204
  110.5 1.3 collective-permute-done.12
  111.8 1.1 add.335.t_ref
  113.0 1.8 %dynamic-slice_select_fusion.3 = f32[32,2048]{1,0:T(8,128)} fusion(f32[64,2048]{1,0:T(8,128)} %collective-permute-done.5.u_ref, s32[]{:T(128)S(6)} %select_n.143, f32[64,2048]{1,0:T(8,128)S(1)} %copy-done.6, pred[]{:T(512)S(6)} %eq.39), kind=kLoop, calls=%fused_computation.52 | loop fusion | flops 65536 | bytes 786437 | tf_op jit(solution)/shard_map/jit(_where)/select_n | solution.py:301
  114.8 0.7 dynamic-slice_select_fusion.2
  115.5 11.6 %shard_map.124 = f32[16,4,12,512]{3,2,1,0:T(8,128)} custom-call(s32[1]{0:T(128)} %bitcast.29.b_ref, f32[4,16,256]{2,1,0:T(8,128)} %broadcast_in_dim.55.w_ref, bf16[16,128,8192]{2,1,0:T(8,128)(2,1)} %cov_ref.15, f32[64,2048]{1,0:T(8,128)} %copy-done.9, f32[64,2048]{1,0:T(8,128)} %copy-done.18, f32[128,8192]{1,0:T(8,128)} %y_ref.7, s32[128,8192]{1,0:T(8,128)} %g_ref.7), custom_call_target="tpu_custom_call" | custom-call | flops 41943040 | bytes 13107200 | tf_op jit(solution)/shard_map/pallas_call | solution.py:204
  127.1 1.7 dynamic-slice_select_fusion.1
  128.8 0.8 dynamic-slice_select_fusion
  129.7 11.7 %shard_map.125 = f32[16,4,12,512]{3,2,1,0:T(8,128)} custom-call(s32[1]{0:T(128)} %bitcast.29.b_ref, f32[4,16,256]{2,1,0:T(8,128)} %broadcast_in_dim.55.w_ref, bf16[16,128,8192]{2,1,0:T(8,128)(2,1)} %cov_ref.15, f32[64,2048]{1,0:T(8,128)} %copy-done.11, f32[64,2048]{1,0:T(8,128)} %copy-done.19, f32[128,8192]{1,0:T(8,128)} %y_ref.7, s32[128,8192]{1,0:T(8,128)} %g_ref.7), custom_call_target="tpu_custom_call" | custom-call | flops 41943040 | bytes 13107200 | tf_op jit(solution)/shard_map/pallas_call | solution.py:204
  141.4 4.0 %pad_maximum_fusion = f32[16,16,12,512]{3,2,1,0:T(8,128)S(1)} fusion(f32[16,4,12,512]{3,2,1,0:T(8,128)} %shard_map.125, f32[16,4,12,512]{3,2,1,0:T(8,128)} %shard_map.124, f32[16,4,12,512]{3,2,1,0:T(8,128)} %shard_map.123, f32[16,4,12,512]{3,2,1,0:T(8,128)S(1)} %copy-done), kind=kLoop, calls=%fused_computation | loop fusion | flops 4718592 | bytes 12582912 | tf_op jit(solution)/shard_map/concatenate | solution.py:305
  145.4 6.0 %fusion.4 = f32[16,12,16,128]{3,2,1,0:T(8,128)S(1)} fusion(f32[16,16,12,512]{3,2,1,0:T(8,128)S(1)} %pad_maximum_fusion, f32[512]{0:T(512)S(1)} %get-tuple-element.177, f32[512]{0:T(512)S(1)} %get-tuple-element.178, f32[512]{0:T(512)S(1)} %get-tuple-element.176, f32[512]{0:T(512)S(1)} %get-tuple-element.175, s32[512]{0:T(512)S(1)} %add_select_fusion, ...), kind=kOutput, calls=%fused_computation.6 | convolution fusion | flops 1208549376 | bytes 7875072 | tf_op jit(solution)/shard_map/pbkj,nj->pkbn/dot_general | solution.py:75
  151.3 1.4 fusion.85
  152.7 1.1 pad_add_fusion
  153.8 0.5 reshape.229
  154.4 0.2 slice.171
  154.6 0.3 copy_multiply_fusion
  154.9 4.3 %collective-permute-start.14 = (f32[16,2,512]{2,0,1:T(8,128)S(1)}, f32[16,2,512]{2,0,1:T(8,128)S(1)}, u32[]{:S(2)}, u32[]{:S(2)}) collective-permute-start(f32[16,2,512]{2,0,1:T(8,128)S(1)} %get-tuple-element.148), channel_id=1, source_target_pairs={{0,4},{4,8},{8,12},{12,16},{16,20},{20,24},{24,28},{1,5},{5,9},{9,... | collective-permute-start | bytes 196616 | tf_op jit(solution)/shard_map/ppermute | solution.py:31
  159.3 1.4 collective-permute-start.15
  160.8 3.1 %subtract_multiply_fusion = (f32[32,8192]{1,0:T(8,128)}, f32[32,8192]{1,0:T(8,128)}) fusion(f32[128,8192]{1,0:T(8,128)} %y_ref.7, s32[]{:T(128)S(6)} %select_n.147, s32[128,8192]{1,0:T(8,128)} %g_ref.7, f32[32,2048]{1,0:T(8,128)S(1)} %copy-done.25, f32[32,2048]{1,0:T(8,128)S(1)} %copy-done.24, f32[32,2048]{1,0:T(8,128)S(1)} %copy-done.23, ...), kind=kLoop, calls=%fused_computation.8 | loop fusion | flops 1572864 | bytes 5242884 | tf_op jit(solution)/shard_map/mul | solution.py:304
  163.9 3.1 %collective-permute-done.15 = f32[16,2,512]{2,0,1:T(8,128)S(1)} collective-permute-done((f32[16,2,512]{2,0,1:T(8,128)S(1)}, f32[16,2,512]{2,0,1:T(8,128)S(1)}, u32[]{:S(2)}, u32[]{:S(2)}) %collective-permute-start.15) | collective-permute-done | bytes 65568 | tf_op jit(solution)/shard_map/ppermute | solution.py:31
  167.0 0.8 divide_subtract_fusion
  167.8 0.9 copy.696
  168.6 0.9 copy.697
  169.5 0.9 copy.698
  170.3 0.9 copy.695
  (98 shorter events, 1.9 us)
Async XLA Ops:
  1.7 0.7 copy-start.14
  2.5 10.0 %collective-permute-start.1 = (f32[16,2,512]{2,0,1:T(8,128)S(1)}, f32[16,2,512]{2,0,1:T(8,128)S(1)}, u32[]{:S(2)}, u32[]{:S(2)}) collective-permute-start(f32[16,2,512]{2,0,1:T(8,128)S(1)} %get-tuple-element.169), channel_id=1, source_target_pairs={{4,0},{8,4},{12,8},{16,12},{20,16},{24,20},{28,24},{5,1},{9,5},{13... | collective-permute-start | bytes 196616 | tf_op jit(solution)/shard_map/ppermute | solution.py:23
  3.8 7.5 %collective-permute-start = (f32[16,2,512]{2,0,1:T(8,128)S(1)}, f32[16,2,512]{2,0,1:T(8,128)S(1)}, u32[]{:S(2)}, u32[]{:S(2)}) collective-permute-start(f32[16,2,512]{2,0,1:T(8,128)S(1)} %get-tuple-element.170), channel_id=1, source_target_pairs={{0,4},{4,8},{8,12},{12,16},{16,20},{20,24},{24,28},{1,5},{5,9},{9,... | collective-permute-start | bytes 196616 | tf_op jit(solution)/shard_map/ppermute | solution.py:22
  12.4 0.7 copy-start.20
  34.2 8.6 %collective-permute-start.2 = (f32[64,2048]{1,0:T(8,128)S(1)}, f32[64,2048]{1,0:T(8,128)S(1)}, u32[]{:S(2)}, u32[]{:S(2)}) collective-permute-start(f32[64,2048]{1,0:T(8,128)S(1)} %dynamic-slice_bitcast_fusion.3), channel_id=1, source_target_pairs={{0,1},{1,0},{2,3},{3,2},{4,5},{5,4},{6,7},{7,6},{8,9},{9,8},{10,11... | collective-permute-start | bytes 1572872 | tf_op jit(solution)/shard_map/ppermute | solution.py:275
  34.3 10.9 %copy-start.1 = (f32[128,2048]{1,0:T(8,128)S(1)}, f32[128,2048]{1,0:T(8,128)}, u32[]{:S(2)}) copy-start(f32[128,2048]{1,0:T(8,128)} %shard_map.118) | copy-start | bytes 3145732
  44.7 11.0 %collective-permute-start.4 = (f32[64,2048]{1,0:T(8,128)}, f32[64,2048]{1,0:T(8,128)}, u32[]{:S(2)}, u32[]{:S(2)}) collective-permute-start(f32[64,2048]{1,0:T(8,128)} %dynamic-slice_bitcast_fusion.2), channel_id=1, source_target_pairs={{0,1},{1,0},{2,3},{3,2},{4,5},{5,4},{6,7},{7,6},{8,9},{9,8},{10,11... | collective-permute-start | bytes 1572872 | tf_op jit(solution)/shard_map/ppermute | solution.py:275
  45.2 10.4 %copy-start.13 = (f32[64,2048]{1,0:T(8,128)}, f32[64,2048]{1,0:T(8,128)S(1)}, u32[]{:S(2)}) copy-start(f32[64,2048]{1,0:T(8,128)S(1)} %bitcast_add_fusion.3) | copy-start | bytes 1572868
  45.3 14.2 %copy-start.4 = (f32[128,2048]{1,0:T(8,128)S(1)}, f32[128,2048]{1,0:T(8,128)}, u32[]{:S(2)}) copy-start(f32[128,2048]{1,0:T(8,128)} %shard_map.119) | copy-start | bytes 3145732
  45.3 14.2 %collective-permute-start.3 = (f32[64,2048]{1,0:T(8,128)S(1)}, f32[64,2048]{1,0:T(8,128)}, u32[]{:S(2)}, u32[]{:S(2)}) collective-permute-start(f32[64,2048]{1,0:T(8,128)S(1)} %bitcast_add_fusion.3), channel_id=1, source_target_pairs={{0,2},{1,3},{2,0},{3,1},{4,6},{5,7},{6,4},{7,5},{8,10},{9,11},{10,... | collective-permute-start | bytes 1572872 | tf_op jit(solution)/shard_map/ppermute | solution.py:275
  55.7 6.2 %copy-start.3 = (f32[128,2048]{1,0:T(8,128)S(1)}, f32[128,2048]{1,0:T(8,128)}, u32[]{:S(2)}) copy-start(f32[128,2048]{1,0:T(8,128)} %shard_map.120) | copy-start | bytes 3145732
  61.8 11.6 %copy-start.5 = (f32[64,2048]{1,0:T(8,128)}, f32[64,2048]{1,0:T(8,128)S(1)}, u32[]{:S(2)}) copy-start(f32[64,2048]{1,0:T(8,128)S(1)} %add.328.t_ref) | copy-start | bytes 1572868
  62.8 10.7 %collective-permute-start.7 = (f32[64,2048]{1,0:T(8,128)}, f32[64,2048]{1,0:T(8,128)}, u32[]{:S(2)}, u32[]{:S(2)}) collective-permute-start(f32[64,2048]{1,0:T(8,128)} %dynamic-slice_bitcast_fusion.1), channel_id=1, source_target_pairs={{0,1},{1,0},{2,3},{3,2},{4,5},{5,4},{6,7},{7,6},{8,9},{9,8},{10,11... | collective-permute-start | bytes 1572872 | tf_op jit(solution)/shard_map/ppermute | solution.py:275
  62.8 10.7 %collective-permute-start.5 = (f32[64,2048]{1,0:T(8,128)S(1)}, f32[64,2048]{1,0:T(8,128)}, u32[]{:S(2)}, u32[]{:S(2)}) collective-permute-start(f32[64,2048]{1,0:T(8,128)S(1)} %add.328.t_ref), channel_id=1, source_target_pairs={{0,1},{1,0},{2,3},{3,2},{4,5},{5,4},{6,7},{7,6},{8,9},{9,8},{10,11... | collective-permute-start | bytes 1572872 | tf_op jit(solution)/shard_map/ppermute | solution.py:275
  63.3 13.9 %collective-permute-start.6 = (f32[64,2048]{1,0:T(8,128)S(1)}, f32[64,2048]{1,0:T(8,128)}, u32[]{:S(2)}, u32[]{:S(2)}) collective-permute-start(f32[64,2048]{1,0:T(8,128)S(1)} %bitcast_add_fusion.2), channel_id=1, source_target_pairs={{0,2},{1,3},{2,0},{3,1},{4,6},{5,7},{6,4},{7,5},{8,10},{9,11},{10,... | collective-permute-start | bytes 1572872 | tf_op jit(solution)/shard_map/ppermute | solution.py:275
  73.5 6.0 %copy-start.2 = (f32[128,2048]{1,0:T(8,128)S(1)}, f32[128,2048]{1,0:T(8,128)}, u32[]{:S(2)}) copy-start(f32[128,2048]{1,0:T(8,128)} %shard_map.121) | copy-start | bytes 3145732
  79.4 14.6 %copy-start.7 = (f32[64,2048]{1,0:T(8,128)}, f32[64,2048]{1,0:T(8,128)S(1)}, u32[]{:S(2)}) copy-start(f32[64,2048]{1,0:T(8,128)S(1)} %add.331.t_ref) | copy-start | bytes 1572868
  80.3 13.7 %collective-permute-start.10 = (f32[64,2048]{1,0:T(8,128)}, f32[64,2048]{1,0:T(8,128)S(1)}, u32[]{:S(2)}, u32[]{:S(2)}) collective-permute-start(f32[64,2048]{1,0:T(8,128)} %dynamic-slice_bitcast_fusion), channel_id=1, source_target_pairs={{0,1},{1,0},{2,3},{3,2},{4,5},{5,4},{6,7},{7,6},{8,9},{9,8},{10,11... | collective-permute-start | bytes 1572872 | tf_op jit(solution)/shard_map/ppermute | solution.py:275
  80.3 13.7 %collective-permute-start.8 = (f32[64,2048]{1,0:T(8,128)S(1)}, f32[64,2048]{1,0:T(8,128)S(1)}, u32[]{:S(2)}, u32[]{:S(2)}) collective-permute-start(f32[64,2048]{1,0:T(8,128)S(1)} %add.331.t_ref), channel_id=1, source_target_pairs={{0,1},{1,0},{2,3},{3,2},{4,5},{5,4},{6,7},{7,6},{8,9},{9,8},{10,11... | collective-permute-start | bytes 1572872 | tf_op jit(solution)/shard_map/ppermute | solution.py:275
  80.8 14.0 %collective-permute-start.9 = (f32[64,2048]{1,0:T(8,128)S(1)}, f32[64,2048]{1,0:T(8,128)}, u32[]{:S(2)}, u32[]{:S(2)}) collective-permute-start(f32[64,2048]{1,0:T(8,128)S(1)} %bitcast_add_fusion.1), channel_id=1, source_target_pairs={{0,2},{1,3},{2,0},{3,1},{4,6},{5,7},{6,4},{7,5},{8,10},{9,11},{10,... | collective-permute-start | bytes 1572872 | tf_op jit(solution)/shard_map/ppermute | solution.py:275
  94.1 0.8 copy-start.26
  94.9 4.0 %copy-start.16 = (f32[64,2048]{1,0:T(8,128)}, f32[64,2048]{1,0:T(8,128)S(1)}, u32[]{:S(2)}) copy-start(f32[64,2048]{1,0:T(8,128)S(1)} %collective-permute-done.8.u_ref) | copy-start | bytes 1572868
  97.2 13.2 %copy-start.9 = (f32[64,2048]{1,0:T(8,128)}, f32[64,2048]{1,0:T(8,128)S(1)}, u32[]{:S(2)}) copy-start(f32[64,2048]{1,0:T(8,128)S(1)} %add.333.t_ref) | copy-start | bytes 1572868
  97.3 13.2 %collective-permute-start.11 = (f32[64,2048]{1,0:T(8,128)S(1)}, f32[64,2048]{1,0:T(8,128)S(1)}, u32[]{:S(2)}, u32[]{:S(2)}) collective-permute-start(f32[64,2048]{1,0:T(8,128)S(1)} %add.333.t_ref), channel_id=1, source_target_pairs={{0,1},{1,0},{2,3},{3,2},{4,5},{5,4},{6,7},{7,6},{8,9},{9,8},{10,11... | collective-permute-start | bytes 1572872 | tf_op jit(solution)/shard_map/ppermute | solution.py:275
  97.3 14.4 %collective-permute-start.12 = (f32[64,2048]{1,0:T(8,128)S(1)}, f32[64,2048]{1,0:T(8,128)}, u32[]{:S(2)}, u32[]{:S(2)}) collective-permute-start(f32[64,2048]{1,0:T(8,128)S(1)} %bitcast_add_fusion), channel_id=1, source_target_pairs={{0,2},{1,3},{2,0},{3,1},{4,6},{5,7},{6,4},{7,5},{8,10},{9,11},{10,... | collective-permute-start | bytes 1572872 | tf_op jit(solution)/shard_map/ppermute | solution.py:275
  98.9 14.1 %copy-start.6 = (f32[64,2048]{1,0:T(8,128)S(1)}, f32[64,2048]{1,0:T(8,128)}, u32[]{:S(2)}) copy-start(f32[64,2048]{1,0:T(8,128)} %copy-done.5) | copy-start | bytes 1572868
  110.5 4.3 %copy-start.8 = (f32[64,2048]{1,0:T(8,128)S(1)}, f32[64,2048]{1,0:T(8,128)}, u32[]{:S(2)}) copy-start(f32[64,2048]{1,0:T(8,128)} %copy-done.7) | copy-start | bytes 1572868
  110.5 4.3 %copy-start.17 = (f32[64,2048]{1,0:T(8,128)S(1)}, f32[64,2048]{1,0:T(8,128)}, u32[]{:S(2)}) copy-start(f32[64,2048]{1,0:T(8,128)} %copy-done.16) | copy-start | bytes 1572868
  110.5 5.0 %copy-start.18 = (f32[64,2048]{1,0:T(8,128)}, f32[64,2048]{1,0:T(8,128)S(1)}, u32[]{:S(2)}) copy-start(f32[64,2048]{1,0:T(8,128)S(1)} %collective-permute-done.11.u_ref) | copy-start | bytes 1572868
  112.9 15.9 %copy-start.11 = (f32[64,2048]{1,0:T(8,128)}, f32[64,2048]{1,0:T(8,128)S(1)}, u32[]{:S(2)}) copy-start(f32[64,2048]{1,0:T(8,128)S(1)} %add.335.t_ref) | copy-start | bytes 1572868
  112.9 15.9 %collective-permute-start.13 = (f32[64,2048]{1,0:T(8,128)S(1)}, f32[64,2048]{1,0:T(8,128)S(1)}, u32[]{:S(2)}, u32[]{:S(2)}) collective-permute-start(f32[64,2048]{1,0:T(8,128)S(1)} %add.335.t_ref), channel_id=1, source_target_pairs={{0,1},{1,0},{2,3},{3,2},{4,5},{5,4},{6,7},{7,6},{8,9},{9,8},{10,11... | collective-permute-start | bytes 1572872 | tf_op jit(solution)/shard_map/ppermute | solution.py:275
  115.5 11.6 %copy-start.10 = (f32[64,2048]{1,0:T(8,128)S(1)}, f32[64,2048]{1,0:T(8,128)}, u32[]{:S(2)}) copy-start(f32[64,2048]{1,0:T(8,128)} %copy-done.9) | copy-start | bytes 1572868
  128.8 0.9 copy-start.19
  129.7 11.7 %copy-start = (f32[16,4,12,512]{3,2,1,0:T(8,128)S(1)}, f32[16,4,12,512]{3,2,1,0:T(8,128)}, u32[]{:S(2)}) copy-start(f32[16,4,12,512]{3,2,1,0:T(8,128)} %shard_map.122) | copy-start | bytes 4718596
  154.4 6.4 %copy-start.22 = (f32[32,2048]{1,0:T(8,128)S(1)}, f32[32,2048]{1,0:T(8,128)}, u32[]{:S(2)}) copy-start(f32[32,2048]{1,0:T(8,128)} %dynamic-slice_select_fusion.3) | copy-start | bytes 786436
  154.4 6.4 %copy-start.23 = (f32[32,2048]{1,0:T(8,128)S(1)}, f32[32,2048]{1,0:T(8,128)}, u32[]{:S(2)}) copy-start(f32[32,2048]{1,0:T(8,128)} %dynamic-slice_select_fusion.2) | copy-start | bytes 786436
  154.4 6.4 %copy-start.24 = (f32[32,2048]{1,0:T(8,128)S(1)}, f32[32,2048]{1,0:T(8,128)}, u32[]{:S(2)}) copy-start(f32[32,2048]{1,0:T(8,128)} %dynamic-slice_select_fusion.1) | copy-start | bytes 786436
  154.4 6.4 %copy-start.25 = (f32[32,2048]{1,0:T(8,128)S(1)}, f32[32,2048]{1,0:T(8,128)}, u32[]{:S(2)}) copy-start(f32[32,2048]{1,0:T(8,128)} %dynamic-slice_select_fusion) | copy-start | bytes 786436
  154.9 9.0 %collective-permute-start.14 = (f32[16,2,512]{2,0,1:T(8,128)S(1)}, f32[16,2,512]{2,0,1:T(8,128)S(1)}, u32[]{:S(2)}, u32[]{:S(2)}) collective-permute-start(f32[16,2,512]{2,0,1:T(8,128)S(1)} %get-tuple-element.148), channel_id=1, source_target_pairs={{0,4},{4,8},{8,12},{12,16},{16,20},{20,24},{24,28},{1,5},{5,9},{9,... | collective-permute-start | bytes 196616 | tf_op jit(solution)/shard_map/ppermute | solution.py:31
  159.2 7.7 %copy-start.12 = (f32[16,8,512]{2,1,0:T(8,128)S(1)}, f32[16,8,512]{2,1,0:T(8,128)}, u32[]{:S(2)}) copy-start(f32[16,8,512]{2,1,0:T(8,128)} %param.10) | copy-start | bytes 786436
  159.3 7.7 %copy-start.15 = (f32[16,8,512]{2,0,1:T(8,128)S(1)}, f32[16,8,512]{2,0,1:T(8,128)}, u32[]{:S(2)}) copy-start(f32[16,8,512]{2,0,1:T(8,128)} %copy-done.14) | copy-start | bytes 786436
  159.3 7.7 %copy-start.21 = (f32[16,10,512]{2,0,1:T(8,128)S(1)}, f32[16,10,512]{2,0,1:T(8,128)}, u32[]{:S(2)}) copy-start(f32[16,10,512]{2,0,1:T(8,128)} %copy-done.20) | copy-start | bytes 983044
  159.3 7.7 %copy-start.27 = (f32[16,8,512]{2,1,0:T(8,128)S(1)}, f32[16,8,512]{2,1,0:T(8,128)}, u32[]{:S(2)}) copy-start(f32[16,8,512]{2,1,0:T(8,128)} %param.11) | copy-start | bytes 786436
  159.3 7.7 %copy-start.28 = (f32[16,8,512]{2,1,0:T(8,128)S(1)}, f32[16,8,512]{2,1,0:T(8,128)}, u32[]{:S(2)}) copy-start(f32[16,8,512]{2,1,0:T(8,128)} %param.12) | copy-start | bytes 786436
  159.3 7.7 %copy-start.29 = (f32[16]{0:T(128)S(1)}, f32[16]{0:T(128)}, u32[]{:S(2)}) copy-start(f32[16]{0:T(128)} %param.13) | copy-start | bytes 196
  159.3 7.6 %collective-permute-start.15 = (f32[16,2,512]{2,0,1:T(8,128)S(1)}, f32[16,2,512]{2,0,1:T(8,128)S(1)}, u32[]{:S(2)}, u32[]{:S(2)}) collective-permute-start(f32[16,2,512]{2,0,1:T(8,128)S(1)} %get-tuple-element.149), channel_id=1, source_target_pairs={{4,0},{8,4},{12,8},{16,12},{20,16},{24,20},{28,24},{5,1},{9,5},{13... | collective-permute-start | bytes 196616 | tf_op jit(solution)/shard_map/ppermute | solution.py:31

commit v7 on v6

--- a/solution.py
+++ b/solution.py
@@ -170,7 +170,7 @@
                 o_ref[p, 0, pl.ds(r, 1), cols] = jnp.sum(accs[r], axis=0, keepdims=True)
             return carry
 
-        lax.fori_loop(0, npred, body, 0)
+        lax.fori_loop(0, npred, body, 0, unroll=2 if npred % 2 == 0 else 1)
 
 
 def fit_chunk(wl, cov, along, chunk, width):

time: 172 us -> 171 us (level)
  Pallas kernels: 80.2 us -> 78.3 us
    pallas_call x4, Pallas kernels: 46.3 us -> 44.5 us  [back_chunk(): pl.pallas_call(back_kernel, grid=(width // TN,), in_specs=[pl.BlockSpec(m...]
  transfers between devices with their start and end apart: 16 -> 16, of which waited for: 5 -> 6; matrix products, arithmetic and copies ran while one was open for 5% -> 5% of each run, Pallas kernels for 35% -> 34%
where the time goes in v7:
time: 171 us; the launch traced here: 170 us
  Pallas kernels  78.3 us (46%)
  other arithmetic  22 us (13%)
  starting transfers between devices  21.7 us (13%)
  local copies, waits for them, and re-layouts  20.4 us (12%)
  waiting for transfers between devices  14.5 us (8%)
  matrix products  11.9 us (7%)
    pallas_call x4, Pallas kernels, back_chunk(): pl.pallas_call(back_kernel, grid=(width // TN,), in_specs=[pl.BlockSpec(m...  44.5 us
    pallas_call x4, Pallas kernels, fit_chunk(): pl.pallas_call(fit_kernel, grid=(width // TN,), in_specs=[pl.BlockSpec((4...  33.9 us
    ppermute x12, waiting for transfers between devices, local(): pending.append((c, finish, lax.ppermute(send, 'pred', pairs)))  9.51 us
    ppermute x12, starting transfers between devices, local(): pending.append((c, finish, lax.ppermute(send, 'pred', pairs)))  8.94 us
    unnamed x66, local copies, waits for them, and re-layouts  6.89 us
    ppermute x2, starting transfers between devices, from_behind(): return lax.ppermute(block, axis, route)  5.97 us
    dot_general x1, matrix products, banded_data(): jnp.einsum('pbkj,nj->pkbn', back4, block_basis(window), precision=lax.Pre...  5.95 us
    dot_general x1, matrix products, banded_along(): jnp.einsum('pbkn,nj->pbkj', cwin, block_basis(window), precision=lax.Prec...  5.94 us
  transfers between devices with their start and end apart: 16, of which 6 were waited for; matrix products, arithmetic and copies ran while one was open for 5% of the time, Pallas kernels for 34%

profile of v7, /device:TPU:0, one launch (start us, length us, event | category | flops | bytes accessed | tf_op | source)
XLA Modules:
  0.0 170.1 jit_solution(8373503342274812679)
XLA Ops:
  0.6 1.1 copy.663
  1.8 0.7 copy-done.14
  2.5 1.3 collective-permute-start.1
  3.8 5.5 %collective-permute-start = (f32[16,2,512]{2,0,1:T(8,128)S(1)}, f32[16,2,512]{2,0,1:T(8,128)S(1)}, u32[]{:S(2)}, u32[]{:S(2)}) collective-permute-start(f32[16,2,512]{2,0,1:T(8,128)S(1)} %get-tuple-element.170), channel_id=1, source_target_pairs={{0,4},{4,8},{8,12},{12,16},{16,20},{20,24},{24,28},{1,5},{5,9},{9,... | collective-permute-start | bytes 196616 | tf_op jit(solution)/shard_map/ppermute | solution.py:22
  9.4 1.9 %collective-permute-done = f32[16,2,512]{2,0,1:T(8,128)S(1)} collective-permute-done((f32[16,2,512]{2,0,1:T(8,128)S(1)}, f32[16,2,512]{2,0,1:T(8,128)S(1)}, u32[]{:S(2)}, u32[]{:S(2)}) %collective-permute-start) | collective-permute-done | bytes 65568 | tf_op jit(solution)/shard_map/ppermute | solution.py:22
  11.3 1.1 constant_dynamic-update-slice_fusion.3
  12.4 0.7 copy-done.20
  13.1 0.5 fusion.49
  13.6 0.1 copy.681
  13.8 0.1 copy.680
  15.4 2.7 %stack.75 = f32[16,16,12,128]{3,1,2,0:T(8,128)S(1)} concatenate(f32[16,1,12,128]{3,1,2,0:T(1,128)S(1)} %copy.666, f32[16,1,12,128]{3,1,2,0:T(1,128)S(1)} %copy.667, f32[16,1,12,128]{3,1,2,0:T(1,128)S(1)} %copy.668, f32[16,1,12,128]{3,1,2,0:T(1,128)S(1)} %copy.669, f32[16,1,12,128]{3,1,2,0:T(1,128)S(1)} %copy.670, f32[16,1,12,128]{3,1,2,0:T(1,128)S(1)} %copy.671, ...), dimensions={1} | concatenate | bytes 3145728 | tf_op jit(solution)/shard_map/stack | solution.py:67
  18.0 5.9 %fusion.2.a_ref = f32[16,16,12,512]{3,2,1,0:T(8,128)} fusion(f32[16,16,12,128]{3,1,2,0:T(8,128)S(1)} %stack.75, f32[512]{0:T(512)S(1)} %get-tuple-element.177, f32[512]{0:T(512)S(1)} %get-tuple-element.178, f32[512]{0:T(512)S(1)} %get-tuple-element.176, f32[512]{0:T(512)S(1)} %get-tuple-element.175, s32[512]{0:T(512)S(1)} %add_select_fusion, ...), kind=kOutput, calls=%fused_computation.4 | convolution fusion | flops 1208549376 | bytes 7875072 | tf_op jit(solution)/shard_map/pbkn,nj->pbkj/dot_general | solution.py:68
  24.0 0.7 broadcast_in_dim.55.w_ref
  24.7 8.4 %shard_map.118 = f32[128,2048]{1,0:T(8,128)} custom-call(f32[4,16,256]{2,1,0:T(8,128)} %broadcast_in_dim.55.w_ref, bf16[16,128,8192]{2,1,0:T(8,128)(2,1)} %cov_ref.15, f32[16,16,12,512]{3,2,1,0:T(8,128)} %fusion.2.a_ref), custom_call_target="tpu_custom_call" | custom-call | flops 41943040 | bytes 11010048 | tf_op jit(solution)/shard_map/pallas_call | solution.py:180
  33.1 1.1 dynamic-slice_bitcast_fusion.3
  34.3 8.5 %shard_map.119 = f32[128,2048]{1,0:T(8,128)} custom-call(f32[4,16,256]{2,1,0:T(8,128)} %broadcast_in_dim.55.w_ref, bf16[16,128,8192]{2,1,0:T(8,128)(2,1)} %cov_ref.15, f32[16,16,12,512]{3,2,1,0:T(8,128)} %fusion.2.a_ref), custom_call_target="tpu_custom_call" | custom-call | flops 41943040 | bytes 11010048 | tf_op jit(solution)/shard_map/pallas_call | solution.py:180
  42.8 1.9 %dynamic-slice_bitcast_fusion.2 = f32[64,2048]{1,0:T(8,128)} fusion(f32[2,64,2048]{2,1,0:T(8,128)} %bitcast.68, s32[]{:T(128)S(6)} %select_n.141), kind=kLoop, calls=%fused_computation.23 | loop fusion | bytes 1048580 | tf_op jit(solution)/shard_map/jit(dynamic_index_in_dim)/squeeze | solution.py:100
  44.7 0.5 collective-permute-start.4
  45.3 2.0 %collective-permute-start.3 = (f32[64,2048]{1,0:T(8,128)S(1)}, f32[64,2048]{1,0:T(8,128)}, u32[]{:S(2)}, u32[]{:S(2)}) collective-permute-start(f32[64,2048]{1,0:T(8,128)S(1)} %bitcast_add_fusion.3), channel_id=1, source_target_pairs={{0,2},{1,3},{2,0},{3,1},{4,6},{5,7},{6,4},{7,5},{8,10},{9,11},{10,... | collective-permute-start | bytes 1572872 | tf_op jit(solution)/shard_map/ppermute | solution.py:275
  47.2 8.4 %shard_map.120 = f32[128,2048]{1,0:T(8,128)} custom-call(f32[4,16,256]{2,1,0:T(8,128)} %broadcast_in_dim.55.w_ref, bf16[16,128,8192]{2,1,0:T(8,128)(2,1)} %cov_ref.15, f32[16,16,12,512]{3,2,1,0:T(8,128)} %fusion.2.a_ref), custom_call_target="tpu_custom_call" | custom-call | flops 41943040 | bytes 11010048 | tf_op jit(solution)/shard_map/pallas_call | solution.py:180
  55.7 3.8 %collective-permute-done.3 = f32[64,2048]{1,0:T(8,128)} collective-permute-done((f32[64,2048]{1,0:T(8,128)S(1)}, f32[64,2048]{1,0:T(8,128)}, u32[]{:S(2)}, u32[]{:S(2)}) %collective-permute-start.3) | collective-permute-done | bytes 524320 | tf_op jit(solution)/shard_map/ppermute | solution.py:275
  59.5 1.1 bitcast_add_fusion.2
  60.6 1.3 add.328.t_ref
  61.9 0.9 dynamic-slice_bitcast_fusion.1
  62.8 0.5 collective-permute-start.5
  63.3 1.7 %collective-permute-start.6 = (f32[64,2048]{1,0:T(8,128)S(1)}, f32[64,2048]{1,0:T(8,128)}, u32[]{:S(2)}, u32[]{:S(2)}) collective-permute-start(f32[64,2048]{1,0:T(8,128)S(1)} %bitcast_add_fusion.2), channel_id=1, source_target_pairs={{0,2},{1,3},{2,0},{3,1},{4,6},{5,7},{6,4},{7,5},{8,10},{9,11},{10,... | collective-permute-start | bytes 1572872 | tf_op jit(solution)/shard_map/ppermute | solution.py:275
  65.0 8.4 %shard_map.121 = f32[128,2048]{1,0:T(8,128)} custom-call(f32[4,16,256]{2,1,0:T(8,128)} %broadcast_in_dim.55.w_ref, bf16[16,128,8192]{2,1,0:T(8,128)(2,1)} %cov_ref.15, f32[16,16,12,512]{3,2,1,0:T(8,128)} %fusion.2.a_ref), custom_call_target="tpu_custom_call" | custom-call | flops 41943040 | bytes 11010048 | tf_op jit(solution)/shard_map/pallas_call | solution.py:180
  73.5 3.7 %collective-permute-done.6 = f32[64,2048]{1,0:T(8,128)} collective-permute-done((f32[64,2048]{1,0:T(8,128)S(1)}, f32[64,2048]{1,0:T(8,128)}, u32[]{:S(2)}, u32[]{:S(2)}) %collective-permute-start.6) | collective-permute-done | bytes 524320 | tf_op jit(solution)/shard_map/ppermute | solution.py:275
  77.2 1.1 bitcast_add_fusion.1
  78.3 1.1 add.331.t_ref
  79.4 0.9 dynamic-slice_bitcast_fusion
  80.3 0.5 collective-permute-start.8
  80.8 1.7 %collective-permute-start.9 = (f32[64,2048]{1,0:T(8,128)S(1)}, f32[64,2048]{1,0:T(8,128)}, u32[]{:S(2)}, u32[]{:S(2)}) collective-permute-start(f32[64,2048]{1,0:T(8,128)S(1)} %bitcast_add_fusion.1), channel_id=1, source_target_pairs={{0,2},{1,3},{2,0},{3,1},{4,6},{5,7},{6,4},{7,5},{8,10},{9,11},{10,... | collective-permute-start | bytes 1572872 | tf_op jit(solution)/shard_map/ppermute | solution.py:275
  82.6 11.0 %shard_map.122 = f32[16,4,12,512]{3,2,1,0:T(8,128)} custom-call(s32[1]{0:T(128)} %bitcast.29.b_ref, f32[4,16,256]{2,1,0:T(8,128)} %broadcast_in_dim.55.w_ref, bf16[16,128,8192]{2,1,0:T(8,128)(2,1)} %cov_ref.15, f32[64,2048]{1,0:T(8,128)} %copy-done.5, f32[64,2048]{1,0:T(8,128)} %collective-permute-done.5.u_ref, f32[128,8192]{1,0:T(8,128)} %y_ref.7, ...), custom_call_target="tpu_custom_call" | custom-call | flops 41943040 | bytes 13107200 | tf_op jit(solution)/shard_map/pallas_call | solution.py:204
  93.6 0.8 copy-done.26
  94.3 0.4 collective-permute-done.9
  94.8 1.1 bitcast_add_fusion
  95.9 1.1 add.333.t_ref
  97.1 1.8 %collective-permute-start.12 = (f32[64,2048]{1,0:T(8,128)S(1)}, f32[64,2048]{1,0:T(8,128)}, u32[]{:S(2)}, u32[]{:S(2)}) collective-permute-start(f32[64,2048]{1,0:T(8,128)S(1)} %bitcast_add_fusion), channel_id=1, source_target_pairs={{0,2},{1,3},{2,0},{3,1},{4,6},{5,7},{6,4},{7,5},{8,10},{9,11},{10,... | collective-permute-start | bytes 1572872 | tf_op jit(solution)/shard_map/ppermute | solution.py:275
  98.9 11.1 %shard_map.123 = f32[16,4,12,512]{3,2,1,0:T(8,128)} custom-call(s32[1]{0:T(128)} %bitcast.29.b_ref, f32[4,16,256]{2,1,0:T(8,128)} %broadcast_in_dim.55.w_ref, bf16[16,128,8192]{2,1,0:T(8,128)(2,1)} %cov_ref.15, f32[64,2048]{1,0:T(8,128)} %copy-done.7, f32[64,2048]{1,0:T(8,128)} %copy-done.16, f32[128,8192]{1,0:T(8,128)} %y_ref.7, s32[128,8192]{1,0:T(8,128)} %g_ref.7), custom_call_target="tpu_custom_call" | custom-call | flops 41943040 | bytes 13107200 | tf_op jit(solution)/shard_map/pallas_call | solution.py:204
  110.0 1.5 collective-permute-done.12
  111.5 1.1 add.335.t_ref
  112.7 1.8 %dynamic-slice_select_fusion.3 = f32[32,2048]{1,0:T(8,128)} fusion(f32[64,2048]{1,0:T(8,128)} %collective-permute-done.5.u_ref, s32[]{:T(128)S(6)} %select_n.143, f32[64,2048]{1,0:T(8,128)S(1)} %copy-done.6, pred[]{:T(512)S(6)} %eq.39), kind=kLoop, calls=%fused_computation.52 | loop fusion | flops 65536 | bytes 786437 | tf_op jit(solution)/shard_map/jit(_where)/select_n | solution.py:301
  114.5 0.7 dynamic-slice_select_fusion.2
  115.3 11.1 %shard_map.124 = f32[16,4,12,512]{3,2,1,0:T(8,128)} custom-call(s32[1]{0:T(128)} %bitcast.29.b_ref, f32[4,16,256]{2,1,0:T(8,128)} %broadcast_in_dim.55.w_ref, bf16[16,128,8192]{2,1,0:T(8,128)(2,1)} %cov_ref.15, f32[64,2048]{1,0:T(8,128)} %copy-done.9, f32[64,2048]{1,0:T(8,128)} %copy-done.18, f32[128,8192]{1,0:T(8,128)} %y_ref.7, s32[128,8192]{1,0:T(8,128)} %g_ref.7), custom_call_target="tpu_custom_call" | custom-call | flops 41943040 | bytes 13107200 | tf_op jit(solution)/shard_map/pallas_call | solution.py:204
  126.4 1.7 dynamic-slice_select_fusion.1
  128.1 0.8 dynamic-slice_select_fusion
  128.9 11.3 %shard_map.125 = f32[16,4,12,512]{3,2,1,0:T(8,128)} custom-call(s32[1]{0:T(128)} %bitcast.29.b_ref, f32[4,16,256]{2,1,0:T(8,128)} %broadcast_in_dim.55.w_ref, bf16[16,128,8192]{2,1,0:T(8,128)(2,1)} %cov_ref.15, f32[64,2048]{1,0:T(8,128)} %copy-done.11, f32[64,2048]{1,0:T(8,128)} %copy-done.19, f32[128,8192]{1,0:T(8,128)} %y_ref.7, s32[128,8192]{1,0:T(8,128)} %g_ref.7), custom_call_target="tpu_custom_call" | custom-call | flops 41943040 | bytes 13107200 | tf_op jit(solution)/shard_map/pallas_call | solution.py:204
  140.3 3.7 %pad_maximum_fusion = f32[16,16,12,512]{3,2,1,0:T(8,128)S(1)} fusion(f32[16,4,12,512]{3,2,1,0:T(8,128)} %shard_map.125, f32[16,4,12,512]{3,2,1,0:T(8,128)} %shard_map.124, f32[16,4,12,512]{3,2,1,0:T(8,128)} %shard_map.123, f32[16,4,12,512]{3,2,1,0:T(8,128)S(1)} %copy-done), kind=kLoop, calls=%fused_computation | loop fusion | flops 4718592 | bytes 12582912 | tf_op jit(solution)/shard_map/concatenate | solution.py:305
  144.0 6.0 %fusion.4 = f32[16,12,16,128]{3,2,1,0:T(8,128)S(1)} fusion(f32[16,16,12,512]{3,2,1,0:T(8,128)S(1)} %pad_maximum_fusion, f32[512]{0:T(512)S(1)} %get-tuple-element.177, f32[512]{0:T(512)S(1)} %get-tuple-element.178, f32[512]{0:T(512)S(1)} %get-tuple-element.176, f32[512]{0:T(512)S(1)} %get-tuple-element.175, s32[512]{0:T(512)S(1)} %add_select_fusion, ...), kind=kOutput, calls=%fused_computation.6 | convolution fusion | flops 1208549376 | bytes 7875072 | tf_op jit(solution)/shard_map/pbkj,nj->pkbn/dot_general | solution.py:75
  150.0 1.4 fusion.85
  151.4 1.1 pad_add_fusion
  152.5 0.5 reshape.229
  153.1 0.2 slice.171
  153.3 0.3 copy_multiply_fusion
  153.6 4.5 %collective-permute-start.14 = (f32[16,2,512]{2,0,1:T(8,128)S(1)}, f32[16,2,512]{2,0,1:T(8,128)S(1)}, u32[]{:S(2)}, u32[]{:S(2)}) collective-permute-start(f32[16,2,512]{2,0,1:T(8,128)S(1)} %get-tuple-element.148), channel_id=1, source_target_pairs={{0,4},{4,8},{8,12},{12,16},{16,20},{20,24},{24,28},{1,5},{5,9},{9,... | collective-permute-start | bytes 196616 | tf_op jit(solution)/shard_map/ppermute | solution.py:31
  158.2 1.4 collective-permute-start.15
  159.7 3.1 %subtract_multiply_fusion = (f32[32,8192]{1,0:T(8,128)}, f32[32,8192]{1,0:T(8,128)}) fusion(f32[128,8192]{1,0:T(8,128)} %y_ref.7, s32[]{:T(128)S(6)} %select_n.147, s32[128,8192]{1,0:T(8,128)} %g_ref.7, f32[32,2048]{1,0:T(8,128)S(1)} %copy-done.25, f32[32,2048]{1,0:T(8,128)S(1)} %copy-done.24, f32[32,2048]{1,0:T(8,128)S(1)} %copy-done.23, ...), kind=kLoop, calls=%fused_computation.8 | loop fusion | flops 1572864 | bytes 5242884 | tf_op jit(solution)/shard_map/mul | solution.py:304
  162.8 3.0 %collective-permute-done.15 = f32[16,2,512]{2,0,1:T(8,128)S(1)} collective-permute-done((f32[16,2,512]{2,0,1:T(8,128)S(1)}, f32[16,2,512]{2,0,1:T(8,128)S(1)}, u32[]{:S(2)}, u32[]{:S(2)}) %collective-permute-start.15) | collective-permute-done | bytes 65568 | tf_op jit(solution)/shard_map/ppermute | solution.py:31
  165.9 0.8 divide_subtract_fusion
  166.6 0.9 copy.696
  167.5 0.9 copy.697
  168.3 0.9 copy.698
  169.2 0.9 copy.695
  (98 shorter events, 2.1 us)
Async XLA Ops:
  1.7 0.7 copy-start.14
  2.5 10.0 %collective-permute-start.1 = (f32[16,2,512]{2,0,1:T(8,128)S(1)}, f32[16,2,512]{2,0,1:T(8,128)S(1)}, u32[]{:S(2)}, u32[]{:S(2)}) collective-permute-start(f32[16,2,512]{2,0,1:T(8,128)S(1)} %get-tuple-element.169), channel_id=1, source_target_pairs={{4,0},{8,4},{12,8},{16,12},{20,16},{24,20},{28,24},{5,1},{9,5},{13... | collective-permute-start | bytes 196616 | tf_op jit(solution)/shard_map/ppermute | solution.py:23
  3.8 7.5 %collective-permute-start = (f32[16,2,512]{2,0,1:T(8,128)S(1)}, f32[16,2,512]{2,0,1:T(8,128)S(1)}, u32[]{:S(2)}, u32[]{:S(2)}) collective-permute-start(f32[16,2,512]{2,0,1:T(8,128)S(1)} %get-tuple-element.170), channel_id=1, source_target_pairs={{0,4},{4,8},{8,12},{12,16},{16,20},{20,24},{24,28},{1,5},{5,9},{9,... | collective-permute-start | bytes 196616 | tf_op jit(solution)/shard_map/ppermute | solution.py:22
  12.4 0.7 copy-start.20
  34.2 8.6 %collective-permute-start.2 = (f32[64,2048]{1,0:T(8,128)S(1)}, f32[64,2048]{1,0:T(8,128)S(1)}, u32[]{:S(2)}, u32[]{:S(2)}) collective-permute-start(f32[64,2048]{1,0:T(8,128)S(1)} %dynamic-slice_bitcast_fusion.3), channel_id=1, source_target_pairs={{0,1},{1,0},{2,3},{3,2},{4,5},{5,4},{6,7},{7,6},{8,9},{9,8},{10,11... | collective-permute-start | bytes 1572872 | tf_op jit(solution)/shard_map/ppermute | solution.py:275
  34.3 10.9 %copy-start.1 = (f32[128,2048]{1,0:T(8,128)S(1)}, f32[128,2048]{1,0:T(8,128)}, u32[]{:S(2)}) copy-start(f32[128,2048]{1,0:T(8,128)} %shard_map.118) | copy-start | bytes 3145732
  44.7 11.0 %collective-permute-start.4 = (f32[64,2048]{1,0:T(8,128)}, f32[64,2048]{1,0:T(8,128)}, u32[]{:S(2)}, u32[]{:S(2)}) collective-permute-start(f32[64,2048]{1,0:T(8,128)} %dynamic-slice_bitcast_fusion.2), channel_id=1, source_target_pairs={{0,1},{1,0},{2,3},{3,2},{4,5},{5,4},{6,7},{7,6},{8,9},{9,8},{10,11... | collective-permute-start | bytes 1572872 | tf_op jit(solution)/shard_map/ppermute | solution.py:275
  45.2 10.4 %copy-start.13 = (f32[64,2048]{1,0:T(8,128)}, f32[64,2048]{1,0:T(8,128)S(1)}, u32[]{:S(2)}) copy-start(f32[64,2048]{1,0:T(8,128)S(1)} %bitcast_add_fusion.3) | copy-start | bytes 1572868
  45.3 14.2 %copy-start.4 = (f32[128,2048]{1,0:T(8,128)S(1)}, f32[128,2048]{1,0:T(8,128)}, u32[]{:S(2)}) copy-start(f32[128,2048]{1,0:T(8,128)} %shard_map.119) | copy-start | bytes 3145732
  45.3 14.2 %collective-permute-start.3 = (f32[64,2048]{1,0:T(8,128)S(1)}, f32[64,2048]{1,0:T(8,128)}, u32[]{:S(2)}, u32[]{:S(2)}) collective-permute-start(f32[64,2048]{1,0:T(8,128)S(1)} %bitcast_add_fusion.3), channel_id=1, source_target_pairs={{0,2},{1,3},{2,0},{3,1},{4,6},{5,7},{6,4},{7,5},{8,10},{9,11},{10,... | collective-permute-start | bytes 1572872 | tf_op jit(solution)/shard_map/ppermute | solution.py:275
  55.7 6.2 %copy-start.3 = (f32[128,2048]{1,0:T(8,128)S(1)}, f32[128,2048]{1,0:T(8,128)}, u32[]{:S(2)}) copy-start(f32[128,2048]{1,0:T(8,128)} %shard_map.120) | copy-start | bytes 3145732
  61.8 11.6 %copy-start.5 = (f32[64,2048]{1,0:T(8,128)}, f32[64,2048]{1,0:T(8,128)S(1)}, u32[]{:S(2)}) copy-start(f32[64,2048]{1,0:T(8,128)S(1)} %add.328.t_ref) | copy-start | bytes 1572868
  62.8 10.7 %collective-permute-start.7 = (f32[64,2048]{1,0:T(8,128)}, f32[64,2048]{1,0:T(8,128)}, u32[]{:S(2)}, u32[]{:S(2)}) collective-permute-start(f32[64,2048]{1,0:T(8,128)} %dynamic-slice_bitcast_fusion.1), channel_id=1, source_target_pairs={{0,1},{1,0},{2,3},{3,2},{4,5},{5,4},{6,7},{7,6},{8,9},{9,8},{10,11... | collective-permute-start | bytes 1572872 | tf_op jit(solution)/shard_map/ppermute | solution.py:275
  62.8 10.7 %collective-permute-start.5 = (f32[64,2048]{1,0:T(8,128)S(1)}, f32[64,2048]{1,0:T(8,128)}, u32[]{:S(2)}, u32[]{:S(2)}) collective-permute-start(f32[64,2048]{1,0:T(8,128)S(1)} %add.328.t_ref), channel_id=1, source_target_pairs={{0,1},{1,0},{2,3},{3,2},{4,5},{5,4},{6,7},{7,6},{8,9},{9,8},{10,11... | collective-permute-start | bytes 1572872 | tf_op jit(solution)/shard_map/ppermute | solution.py:275
  63.3 13.9 %collective-permute-start.6 = (f32[64,2048]{1,0:T(8,128)S(1)}, f32[64,2048]{1,0:T(8,128)}, u32[]{:S(2)}, u32[]{:S(2)}) collective-permute-start(f32[64,2048]{1,0:T(8,128)S(1)} %bitcast_add_fusion.2), channel_id=1, source_target_pairs={{0,2},{1,3},{2,0},{3,1},{4,6},{5,7},{6,4},{7,5},{8,10},{9,11},{10,... | collective-permute-start | bytes 1572872 | tf_op jit(solution)/shard_map/ppermute | solution.py:275
  73.5 6.0 %copy-start.2 = (f32[128,2048]{1,0:T(8,128)S(1)}, f32[128,2048]{1,0:T(8,128)}, u32[]{:S(2)}) copy-start(f32[128,2048]{1,0:T(8,128)} %shard_map.121) | copy-start | bytes 3145732
  79.4 14.1 %copy-start.7 = (f32[64,2048]{1,0:T(8,128)}, f32[64,2048]{1,0:T(8,128)S(1)}, u32[]{:S(2)}) copy-start(f32[64,2048]{1,0:T(8,128)S(1)} %add.331.t_ref) | copy-start | bytes 1572868
  80.3 13.2 %collective-permute-start.10 = (f32[64,2048]{1,0:T(8,128)}, f32[64,2048]{1,0:T(8,128)S(1)}, u32[]{:S(2)}, u32[]{:S(2)}) collective-permute-start(f32[64,2048]{1,0:T(8,128)} %dynamic-slice_bitcast_fusion), channel_id=1, source_target_pairs={{0,1},{1,0},{2,3},{3,2},{4,5},{5,4},{6,7},{7,6},{8,9},{9,8},{10,11... | collective-permute-start | bytes 1572872 | tf_op jit(solution)/shard_map/ppermute | solution.py:275
  80.3 13.2 %collective-permute-start.8 = (f32[64,2048]{1,0:T(8,128)S(1)}, f32[64,2048]{1,0:T(8,128)S(1)}, u32[]{:S(2)}, u32[]{:S(2)}) collective-permute-start(f32[64,2048]{1,0:T(8,128)S(1)} %add.331.t_ref), channel_id=1, source_target_pairs={{0,1},{1,0},{2,3},{3,2},{4,5},{5,4},{6,7},{7,6},{8,9},{9,8},{10,11... | collective-permute-start | bytes 1572872 | tf_op jit(solution)/shard_map/ppermute | solution.py:275
  80.8 13.9 %collective-permute-start.9 = (f32[64,2048]{1,0:T(8,128)S(1)}, f32[64,2048]{1,0:T(8,128)}, u32[]{:S(2)}, u32[]{:S(2)}) collective-permute-start(f32[64,2048]{1,0:T(8,128)S(1)} %bitcast_add_fusion.1), channel_id=1, source_target_pairs={{0,2},{1,3},{2,0},{3,1},{4,6},{5,7},{6,4},{7,5},{8,10},{9,11},{10,... | collective-permute-start | bytes 1572872 | tf_op jit(solution)/shard_map/ppermute | solution.py:275
  93.6 0.8 copy-start.26
  94.3 4.5 %copy-start.16 = (f32[64,2048]{1,0:T(8,128)}, f32[64,2048]{1,0:T(8,128)S(1)}, u32[]{:S(2)}) copy-start(f32[64,2048]{1,0:T(8,128)S(1)} %collective-permute-done.8.u_ref) | copy-start | bytes 1572868
  97.0 13.0 %copy-start.9 = (f32[64,2048]{1,0:T(8,128)}, f32[64,2048]{1,0:T(8,128)S(1)}, u32[]{:S(2)}) copy-start(f32[64,2048]{1,0:T(8,128)S(1)} %add.333.t_ref) | copy-start | bytes 1572868
  97.0 13.0 %collective-permute-start.11 = (f32[64,2048]{1,0:T(8,128)S(1)}, f32[64,2048]{1,0:T(8,128)S(1)}, u32[]{:S(2)}, u32[]{:S(2)}) collective-permute-start(f32[64,2048]{1,0:T(8,128)S(1)} %add.333.t_ref), channel_id=1, source_target_pairs={{0,1},{1,0},{2,3},{3,2},{4,5},{5,4},{6,7},{7,6},{8,9},{9,8},{10,11... | collective-permute-start | bytes 1572872 | tf_op jit(solution)/shard_map/ppermute | solution.py:275
  97.1 14.4 %collective-permute-start.12 = (f32[64,2048]{1,0:T(8,128)S(1)}, f32[64,2048]{1,0:T(8,128)}, u32[]{:S(2)}, u32[]{:S(2)}) collective-permute-start(f32[64,2048]{1,0:T(8,128)S(1)} %bitcast_add_fusion), channel_id=1, source_target_pairs={{0,2},{1,3},{2,0},{3,1},{4,6},{5,7},{6,4},{7,5},{8,10},{9,11},{10,... | collective-permute-start | bytes 1572872 | tf_op jit(solution)/shard_map/ppermute | solution.py:275
  98.9 13.8 %copy-start.6 = (f32[64,2048]{1,0:T(8,128)S(1)}, f32[64,2048]{1,0:T(8,128)}, u32[]{:S(2)}) copy-start(f32[64,2048]{1,0:T(8,128)} %copy-done.5) | copy-start | bytes 1572868
  110.0 4.6 %copy-start.8 = (f32[64,2048]{1,0:T(8,128)S(1)}, f32[64,2048]{1,0:T(8,128)}, u32[]{:S(2)}) copy-start(f32[64,2048]{1,0:T(8,128)} %copy-done.7) | copy-start | bytes 1572868
  110.0 4.5 %copy-start.17 = (f32[64,2048]{1,0:T(8,128)S(1)}, f32[64,2048]{1,0:T(8,128)}, u32[]{:S(2)}) copy-start(f32[64,2048]{1,0:T(8,128)} %copy-done.16) | copy-start | bytes 1572868
  110.0 5.3 %copy-start.18 = (f32[64,2048]{1,0:T(8,128)}, f32[64,2048]{1,0:T(8,128)S(1)}, u32[]{:S(2)}) copy-start(f32[64,2048]{1,0:T(8,128)S(1)} %collective-permute-done.11.u_ref) | copy-start | bytes 1572868
  112.6 15.4 %copy-start.11 = (f32[64,2048]{1,0:T(8,128)}, f32[64,2048]{1,0:T(8,128)S(1)}, u32[]{:S(2)}) copy-start(f32[64,2048]{1,0:T(8,128)S(1)} %add.335.t_ref) | copy-start | bytes 1572868
  112.6 15.4 %collective-permute-start.13 = (f32[64,2048]{1,0:T(8,128)S(1)}, f32[64,2048]{1,0:T(8,128)S(1)}, u32[]{:S(2)}, u32[]{:S(2)}) collective-permute-start(f32[64,2048]{1,0:T(8,128)S(1)} %add.335.t_ref), channel_id=1, source_target_pairs={{0,1},{1,0},{2,3},{3,2},{4,5},{5,4},{6,7},{7,6},{8,9},{9,8},{10,11... | collective-permute-start | bytes 1572872 | tf_op jit(solution)/shard_map/ppermute | solution.py:275
  115.3 11.1 %copy-start.10 = (f32[64,2048]{1,0:T(8,128)S(1)}, f32[64,2048]{1,0:T(8,128)}, u32[]{:S(2)}) copy-start(f32[64,2048]{1,0:T(8,128)} %copy-done.9) | copy-start | bytes 1572868
  128.0 0.9 copy-start.19
  128.9 11.4 %copy-start = (f32[16,4,12,512]{3,2,1,0:T(8,128)S(1)}, f32[16,4,12,512]{3,2,1,0:T(8,128)}, u32[]{:S(2)}) copy-start(f32[16,4,12,512]{3,2,1,0:T(8,128)} %shard_map.122) | copy-start | bytes 4718596
  153.0 6.6 %copy-start.22 = (f32[32,2048]{1,0:T(8,128)S(1)}, f32[32,2048]{1,0:T(8,128)}, u32[]{:S(2)}) copy-start(f32[32,2048]{1,0:T(8,128)} %dynamic-slice_select_fusion.3) | copy-start | bytes 786436
  153.0 6.6 %copy-start.23 = (f32[32,2048]{1,0:T(8,128)S(1)}, f32[32,2048]{1,0:T(8,128)}, u32[]{:S(2)}) copy-start(f32[32,2048]{1,0:T(8,128)} %dynamic-slice_select_fusion.2) | copy-start | bytes 786436
  153.1 6.6 %copy-start.24 = (f32[32,2048]{1,0:T(8,128)S(1)}, f32[32,2048]{1,0:T(8,128)}, u32[]{:S(2)}) copy-start(f32[32,2048]{1,0:T(8,128)} %dynamic-slice_select_fusion.1) | copy-start | bytes 786436
  153.1 6.6 %copy-start.25 = (f32[32,2048]{1,0:T(8,128)S(1)}, f32[32,2048]{1,0:T(8,128)}, u32[]{:S(2)}) copy-start(f32[32,2048]{1,0:T(8,128)} %dynamic-slice_select_fusion) | copy-start | bytes 786436
  153.6 9.2 %collective-permute-start.14 = (f32[16,2,512]{2,0,1:T(8,128)S(1)}, f32[16,2,512]{2,0,1:T(8,128)S(1)}, u32[]{:S(2)}, u32[]{:S(2)}) collective-permute-start(f32[16,2,512]{2,0,1:T(8,128)S(1)} %get-tuple-element.148), channel_id=1, source_target_pairs={{0,4},{4,8},{8,12},{12,16},{16,20},{20,24},{24,28},{1,5},{5,9},{9,... | collective-permute-start | bytes 196616 | tf_op jit(solution)/shard_map/ppermute | solution.py:31
  158.1 7.7 %copy-start.12 = (f32[16,8,512]{2,1,0:T(8,128)S(1)}, f32[16,8,512]{2,1,0:T(8,128)}, u32[]{:S(2)}) copy-start(f32[16,8,512]{2,1,0:T(8,128)} %param.10) | copy-start | bytes 786436
  158.1 7.7 %copy-start.15 = (f32[16,8,512]{2,0,1:T(8,128)S(1)}, f32[16,8,512]{2,0,1:T(8,128)}, u32[]{:S(2)}) copy-start(f32[16,8,512]{2,0,1:T(8,128)} %copy-done.14) | copy-start | bytes 786436
  158.2 7.7 %copy-start.21 = (f32[16,10,512]{2,0,1:T(8,128)S(1)}, f32[16,10,512]{2,0,1:T(8,128)}, u32[]{:S(2)}) copy-start(f32[16,10,512]{2,0,1:T(8,128)} %copy-done.20) | copy-start | bytes 983044
  158.2 7.7 %copy-start.27 = (f32[16,8,512]{2,1,0:T(8,128)S(1)}, f32[16,8,512]{2,1,0:T(8,128)}, u32[]{:S(2)}) copy-start(f32[16,8,512]{2,1,0:T(8,128)} %param.11) | copy-start | bytes 786436
  158.2 7.7 %copy-start.28 = (f32[16,8,512]{2,1,0:T(8,128)S(1)}, f32[16,8,512]{2,1,0:T(8,128)}, u32[]{:S(2)}) copy-start(f32[16,8,512]{2,1,0:T(8,128)} %param.12) | copy-start | bytes 786436
  158.2 7.7 %copy-start.29 = (f32[16]{0:T(128)S(1)}, f32[16]{0:T(128)}, u32[]{:S(2)}) copy-start(f32[16]{0:T(128)} %param.13) | copy-start | bytes 196
  158.2 7.6 %collective-permute-start.15 = (f32[16,2,512]{2,0,1:T(8,128)S(1)}, f32[16,2,512]{2,0,1:T(8,128)S(1)}, u32[]{:S(2)}, u32[]{:S(2)}) collective-permute-start(f32[16,2,512]{2,0,1:T(8,128)S(1)} %get-tuple-element.149), channel_id=1, source_target_pairs={{4,0},{8,4},{12,8},{16,12},{20,16},{24,20},{28,24},{5,1},{9,5},{13... | collective-permute-start | bytes 196616 | tf_op jit(solution)/shard_map/ppermute | solution.py:31

commit v8 on v7

--- a/solution.py
+++ b/solution.py
@@ -68,11 +68,15 @@
     return jnp.einsum("pbkn,nj->pbkj", cwin, block_basis(window), precision=lax.Precision.HIGH)
 
 
-def banded_data(back4, knots):
-    npred, blocks, nrow, _ = back4.shape
+def banded_data(parts, knots):
+    npred, _, nrow, _ = parts[0].shape
     per_block = TN // H
     window = 4 * per_block
-    dwin = jnp.einsum("pbkj,nj->pkbn", back4, block_basis(window), precision=lax.Precision.HIGH)
+    basis = block_basis(window)
+    dwin = jnp.concatenate(
+        [jnp.einsum("pbkj,nj->pkbn", part, basis, precision=lax.Precision.HIGH) for part in parts], axis=2
+    )
+    blocks = dwin.shape[2]
     total = None
     for a in range(4):
         part = dwin[..., a * per_block : (a + 1) * per_block]
@@ -302,8 +306,7 @@
         fitted_parts[c] = lax.dynamic_slice_in_dim(picked, start - side * half, share, 0)
     fitted = jnp.concatenate(fitted_parts, axis=1)
     residual = land_blk * (target_blk - fitted)
-    back = jnp.concatenate(back_parts, axis=1)
-    grad_pad = -(1.0 / H) * banded_data(back, knots)
+    grad_pad = -(1.0 / H) * banded_data(back_parts, knots)
     inner = grad_pad[:, 2 : count + 2]
     from_below = from_behind(grad_pad[:, count + 2 :], "tile", 1)
     from_above = from_behind(grad_pad[:, :2], "tile", -1)

time: 171 us -> 171 us (level)
  matrix products: 11.9 us -> 15.2 us
  other arithmetic: 22 us -> 19.7 us
    concatenate x1, other arithmetic: 3.74 us -> 0.16 us  [banded_data(): jnp.concatenate([jnp.einsum('pbkj,nj->pkbn', part, basis, precision=lax.P...]
    dot_general x1 -> x4, matrix products: 5.95 us -> 9.17 us  [banded_data(): jnp.einsum('pbkj,nj->pkbn', part, basis, precision=lax.Precision.HIGH)]
    unnamed x66 -> x64, local copies, waits for them, and re-layouts: 6.89 us -> 6.86 us
  transfers between devices with their start and end apart: 16 -> 16, of which waited for: 6 -> 5; matrix products, arithmetic and copies ran while one was open for 5% -> 8% of each run, Pallas kernels for 34% -> 35%
where the time goes in v8:
time: 171 us; the launch traced here: 170 us
  Pallas kernels  78.2 us (46%)
  starting transfers between devices  21.6 us (13%)
  local copies, waits for them, and re-layouts  21.2 us (12%)
  other arithmetic  19.7 us (12%)
  matrix products  15.2 us (9%)
  waiting for transfers between devices  12.8 us (7%)
    pallas_call x4, Pallas kernels, back_chunk(): pl.pallas_call(back_kernel, grid=(width // TN,), in_specs=[pl.BlockSpec(m...  44.4 us
    pallas_call x4, Pallas kernels, fit_chunk(): pl.pallas_call(fit_kernel, grid=(width // TN,), in_specs=[pl.BlockSpec((4...  33.9 us
    dot_general x4, matrix products, banded_data(): jnp.einsum('pbkj,nj->pkbn', part, basis, precision=lax.Precision.HIGH)  9.17 us
    ppermute x12, starting transfers between devices, local(): pending.append((c, finish, lax.ppermute(send, 'pred', pairs)))  9.1 us
    ppermute x12, waiting for transfers between devices, local(): pending.append((c, finish, lax.ppermute(send, 'pred', pairs)))  7.93 us
    unnamed x64, local copies, waits for them, and re-layouts  6.86 us
    dot_general x1, matrix products, banded_along(): jnp.einsum('pbkn,nj->pbkj', cwin, block_basis(window), precision=lax.Prec...  6 us
    select_n x4, other arithmetic, local(): picked = jnp.where(bit0 == side, cur, other)  5.78 us
  transfers between devices with their start and end apart: 16, of which 5 were waited for; matrix products, arithmetic and copies ran while one was open for 8% of the time, Pallas kernels for 35%

profile of v8, /device:TPU:0, one launch (start us, length us, event | category | flops | bytes accessed | tf_op | source)
XLA Modules:
  0.0 170.0 jit_solution(5845913189607341703)
XLA Ops:
  0.6 1.1 copy.711
  1.8 0.7 copy-done.17
  2.5 1.3 collective-permute-start.1
  3.8 5.5 %collective-permute-start = (f32[16,2,512]{2,0,1:T(8,128)S(1)}, f32[16,2,512]{2,0,1:T(8,128)S(1)}, u32[]{:S(2)}, u32[]{:S(2)}) collective-permute-start(f32[16,2,512]{2,0,1:T(8,128)S(1)} %get-tuple-element.170), channel_id=1, source_target_pairs={{0,4},{4,8},{8,12},{12,16},{16,20},{20,24},{24,28},{1,5},{5,9},{9,... | collective-permute-start | bytes 196616 | tf_op jit(solution)/shard_map/ppermute | solution.py:22
  9.4 1.9 %collective-permute-done = f32[16,2,512]{2,0,1:T(8,128)S(1)} collective-permute-done((f32[16,2,512]{2,0,1:T(8,128)S(1)}, f32[16,2,512]{2,0,1:T(8,128)S(1)}, u32[]{:S(2)}, u32[]{:S(2)}) %collective-permute-start) | collective-permute-done | bytes 65568 | tf_op jit(solution)/shard_map/ppermute | solution.py:22
  11.3 1.1 constant_dynamic-update-slice_fusion.3
  12.5 0.7 copy-done.22
  13.1 0.5 fusion.45
  15.4 2.7 %stack.75 = f32[16,16,12,128]{3,1,2,0:T(8,128)S(1)} concatenate(f32[16,1,12,128]{3,1,2,0:T(1,128)S(1)} %copy.714, f32[16,1,12,128]{3,1,2,0:T(1,128)S(1)} %copy.715, f32[16,1,12,128]{3,1,2,0:T(1,128)S(1)} %copy.716, f32[16,1,12,128]{3,1,2,0:T(1,128)S(1)} %copy.717, f32[16,1,12,128]{3,1,2,0:T(1,128)S(1)} %copy.718, f32[16,1,12,128]{3,1,2,0:T(1,128)S(1)} %copy.719, ...), dimensions={1} | concatenate | bytes 3145728 | tf_op jit(solution)/shard_map/stack | solution.py:67
  18.1 6.0 %fusion.a_ref = f32[16,16,12,512]{3,2,1,0:T(8,128)} fusion(f32[16,16,12,128]{3,1,2,0:T(8,128)S(1)} %stack.75, f32[512]{0:T(512)S(1)} %get-tuple-element.177, f32[512]{0:T(512)S(1)} %get-tuple-element.178, f32[512]{0:T(512)S(1)} %get-tuple-element.176, f32[512]{0:T(512)S(1)} %get-tuple-element.175, s32[512]{0:T(512)S(1)} %add_select_fusion, ...), kind=kOutput, calls=%fused_computation | convolution fusion | flops 1208549376 | bytes 7875072 | tf_op jit(solution)/shard_map/pbkn,nj->pbkj/dot_general | solution.py:68
  24.1 0.7 broadcast_in_dim.79.w_ref
  24.7 8.4 %shard_map.118 = f32[128,2048]{1,0:T(8,128)} custom-call(f32[4,16,256]{2,1,0:T(8,128)} %broadcast_in_dim.79.w_ref, bf16[16,128,8192]{2,1,0:T(8,128)(2,1)} %cov_ref.15, f32[16,16,12,512]{3,2,1,0:T(8,128)} %fusion.a_ref), custom_call_target="tpu_custom_call" | custom-call | flops 41943040 | bytes 11010048 | tf_op jit(solution)/shard_map/pallas_call | solution.py:184
  33.2 1.1 dynamic-slice_bitcast_fusion.3
  34.4 8.5 %shard_map.119 = f32[128,2048]{1,0:T(8,128)} custom-call(f32[4,16,256]{2,1,0:T(8,128)} %broadcast_in_dim.79.w_ref, bf16[16,128,8192]{2,1,0:T(8,128)(2,1)} %cov_ref.15, f32[16,16,12,512]{3,2,1,0:T(8,128)} %fusion.a_ref), custom_call_target="tpu_custom_call" | custom-call | flops 41943040 | bytes 11010048 | tf_op jit(solution)/shard_map/pallas_call | solution.py:184
  42.9 1.9 %dynamic-slice_bitcast_fusion.2 = f32[64,2048]{1,0:T(8,128)} fusion(f32[2,64,2048]{2,1,0:T(8,128)} %bitcast.82, s32[]{:T(128)S(6)} %select_n.177), kind=kLoop, calls=%fused_computation.32 | loop fusion | bytes 1048580 | tf_op jit(solution)/shard_map/jit(dynamic_index_in_dim)/squeeze | solution.py:104
  44.8 0.5 collective-permute-start.4
  45.3 2.0 %collective-permute-start.3 = (f32[64,2048]{1,0:T(8,128)S(1)}, f32[64,2048]{1,0:T(8,128)}, u32[]{:S(2)}, u32[]{:S(2)}) collective-permute-start(f32[64,2048]{1,0:T(8,128)S(1)} %bitcast_add_fusion.3), channel_id=1, source_target_pairs={{0,2},{1,3},{2,0},{3,1},{4,6},{5,7},{6,4},{7,5},{8,10},{9,11},{10,... | collective-permute-start | bytes 1572872 | tf_op jit(solution)/shard_map/ppermute | solution.py:279
  47.3 8.4 %shard_map.120 = f32[128,2048]{1,0:T(8,128)} custom-call(f32[4,16,256]{2,1,0:T(8,128)} %broadcast_in_dim.79.w_ref, bf16[16,128,8192]{2,1,0:T(8,128)(2,1)} %cov_ref.15, f32[16,16,12,512]{3,2,1,0:T(8,128)} %fusion.a_ref), custom_call_target="tpu_custom_call" | custom-call | flops 41943040 | bytes 11010048 | tf_op jit(solution)/shard_map/pallas_call | solution.py:184
  55.7 0.8 copy-done.25
  56.5 3.0 %collective-permute-done.3 = f32[64,2048]{1,0:T(8,128)} collective-permute-done((f32[64,2048]{1,0:T(8,128)S(1)}, f32[64,2048]{1,0:T(8,128)}, u32[]{:S(2)}, u32[]{:S(2)}) %collective-permute-start.3) | collective-permute-done | bytes 524320 | tf_op jit(solution)/shard_map/ppermute | solution.py:279
  59.5 1.1 bitcast_add_fusion.2
  60.6 1.3 add.370.t_ref
  61.9 0.9 dynamic-slice_bitcast_fusion.1
  62.9 0.5 collective-permute-start.5
  63.4 1.7 %collective-permute-start.6 = (f32[64,2048]{1,0:T(8,128)S(1)}, f32[64,2048]{1,0:T(8,128)}, u32[]{:S(2)}, u32[]{:S(2)}) collective-permute-start(f32[64,2048]{1,0:T(8,128)S(1)} %bitcast_add_fusion.2), channel_id=1, source_target_pairs={{0,2},{1,3},{2,0},{3,1},{4,6},{5,7},{6,4},{7,5},{8,10},{9,11},{10,... | collective-permute-start | bytes 1572872 | tf_op jit(solution)/shard_map/ppermute | solution.py:279
  65.1 8.4 %shard_map.121 = f32[128,2048]{1,0:T(8,128)} custom-call(f32[4,16,256]{2,1,0:T(8,128)} %broadcast_in_dim.79.w_ref, bf16[16,128,8192]{2,1,0:T(8,128)(2,1)} %cov_ref.15, f32[16,16,12,512]{3,2,1,0:T(8,128)} %fusion.a_ref), custom_call_target="tpu_custom_call" | custom-call | flops 41943040 | bytes 11010048 | tf_op jit(solution)/shard_map/pallas_call | solution.py:184
  73.6 3.7 %collective-permute-done.6 = f32[64,2048]{1,0:T(8,128)} collective-permute-done((f32[64,2048]{1,0:T(8,128)S(1)}, f32[64,2048]{1,0:T(8,128)}, u32[]{:S(2)}, u32[]{:S(2)}) %collective-permute-start.6) | collective-permute-done | bytes 524320 | tf_op jit(solution)/shard_map/ppermute | solution.py:279
  77.3 1.1 bitcast_add_fusion.1
  78.4 1.1 add.373.t_ref
  79.6 0.9 dynamic-slice_bitcast_fusion
  80.5 0.5 collective-permute-start.8
  81.0 1.7 %collective-permute-start.9 = (f32[64,2048]{1,0:T(8,128)S(1)}, f32[64,2048]{1,0:T(8,128)}, u32[]{:S(2)}, u32[]{:S(2)}) collective-permute-start(f32[64,2048]{1,0:T(8,128)S(1)} %bitcast_add_fusion.1), channel_id=1, source_target_pairs={{0,2},{1,3},{2,0},{3,1},{4,6},{5,7},{6,4},{7,5},{8,10},{9,11},{10,... | collective-permute-start | bytes 1572872 | tf_op jit(solution)/shard_map/ppermute | solution.py:279
  82.7 11.0 %shard_map.122 = f32[16,4,12,512]{3,2,1,0:T(8,128)} custom-call(s32[1]{0:T(128)} %bitcast.29.b_ref, f32[4,16,256]{2,1,0:T(8,128)} %broadcast_in_dim.79.w_ref, bf16[16,128,8192]{2,1,0:T(8,128)(2,1)} %cov_ref.15, f32[64,2048]{1,0:T(8,128)} %copy-done.7, f32[64,2048]{1,0:T(8,128)} %collective-permute-done.5.u_ref, f32[128,8192]{1,0:T(8,128)} %y_ref.7, ...), custom_call_target="tpu_custom_call" | custom-call | flops 41943040 | bytes 13107200 | tf_op jit(solution)/shard_map/pallas_call | solution.py:208
  93.7 1.2 collective-permute-done.9
  94.9 1.9 %bitcast_add_fusion = f32[64,2048]{1,0:T(8,128)} fusion(f32[64,2048]{1,0:T(8,128)} %collective-permute-done.10, f32[2,64,2048]{2,1,0:T(8,128)S(1)} %bitcast.79, s32[]{:T(128)S(6)} %select_n.176), kind=kLoop, calls=%fused_computation.26 | loop fusion | flops 131072 | bytes 1572868 | tf_op jit(solution)/shard_map/add | solution.py:105
  96.8 1.1 add.375.t_ref
  98.0 1.8 %collective-permute-start.12 = (f32[64,2048]{1,0:T(8,128)}, f32[64,2048]{1,0:T(8,128)}, u32[]{:S(2)}, u32[]{:S(2)}) collective-permute-start(f32[64,2048]{1,0:T(8,128)} %bitcast_add_fusion), channel_id=1, source_target_pairs={{0,2},{1,3},{2,0},{3,1},{4,6},{5,7},{6,4},{7,5},{8,10},{9,11},{10,... | collective-permute-start | bytes 1572872 | tf_op jit(solution)/shard_map/ppermute | solution.py:279
  99.8 1.7 dynamic-slice_select_fusion.3
  101.5 11.1 %shard_map.123 = f32[16,4,12,512]{3,2,1,0:T(8,128)} custom-call(s32[1]{0:T(128)} %bitcast.29.b_ref, f32[4,16,256]{2,1,0:T(8,128)} %broadcast_in_dim.79.w_ref, bf16[16,128,8192]{2,1,0:T(8,128)(2,1)} %cov_ref.15, f32[64,2048]{1,0:T(8,128)} %copy-done.9, f32[64,2048]{1,0:T(8,128)} %copy-done.20, f32[128,8192]{1,0:T(8,128)} %y_ref.7, s32[128,8192]{1,0:T(8,128)} %g_ref.7), custom_call_target="tpu_custom_call" | custom-call | flops 41943040 | bytes 13107200 | tf_op jit(solution)/shard_map/pallas_call | solution.py:208
  112.6 2.5 %fusion.10 = f32[16,12,4,128]{3,0,1,2:T(8,128)} fusion(f32[16,4,12,512]{3,2,1,0:T(8,128)S(1)} %copy-done, f32[512]{0:T(512)S(1)} %get-tuple-element.177, f32[512]{0:T(512)S(1)} %get-tuple-element.178, f32[512]{0:T(512)S(1)} %get-tuple-element.176, f32[512]{0:T(512)S(1)} %get-tuple-element.175, s32[512]{0:T(512)S(1)} %add_select_fusion, s32[128]{0:T(128)S(1)} %iota_add_fusion), kind=kOutput, calls=%fused_computation.12 | convolution fusion | flops 302579712 | bytes 1976832 | tf_op jit(solution)/shard_map/pbkj,nj->pkbn/dot_general | solution.py:77
  115.1 1.3 add.377.t_ref
  116.4 0.2 collective-permute-start.13
  116.6 0.7 dynamic-slice_select_fusion.2
  117.3 11.2 %shard_map.124 = f32[16,4,12,512]{3,2,1,0:T(8,128)} custom-call(s32[1]{0:T(128)} %bitcast.29.b_ref, f32[4,16,256]{2,1,0:T(8,128)} %broadcast_in_dim.79.w_ref, bf16[16,128,8192]{2,1,0:T(8,128)(2,1)} %cov_ref.15, f32[64,2048]{1,0:T(8,128)} %copy-done.11, f32[64,2048]{1,0:T(8,128)} %collective-permute-done.11.u_ref, f32[128,8192]{1,0:T(8,128)} %y_ref.7, ...), custom_call_target="tpu_custom_call" | custom-call | flops 41943040 | bytes 13107200 | tf_op jit(solution)/shard_map/pallas_call | solution.py:208
  128.5 1.7 dynamic-slice_select_fusion.1
  130.2 1.7 %fusion.13 = f32[16,12,4,128]{3,0,1,2:T(8,128)S(1)} fusion(f32[16,4,12,512]{3,2,1,0:T(8,128)S(1)} %copy-done.1, f32[512]{0:T(512)S(1)} %get-tuple-element.177, f32[512]{0:T(512)S(1)} %get-tuple-element.178, f32[512]{0:T(512)S(1)} %get-tuple-element.176, f32[512]{0:T(512)S(1)} %get-tuple-element.175, s32[512]{0:T(512)S(1)} %add_select_fusion, ...), kind=kOutput, calls=%fused_computation.13 | convolution fusion | flops 302579712 | bytes 1976832 | tf_op jit(solution)/shard_map/pbkj,nj->pkbn/dot_general | solution.py:77
  131.9 1.7 dynamic-slice_select_fusion
  133.6 11.1 %shard_map.125 = f32[16,4,12,512]{3,2,1,0:T(8,128)} custom-call(s32[1]{0:T(128)} %bitcast.29.b_ref, f32[4,16,256]{2,1,0:T(8,128)} %broadcast_in_dim.79.w_ref, bf16[16,128,8192]{2,1,0:T(8,128)(2,1)} %cov_ref.15, f32[64,2048]{1,0:T(8,128)} %copy-done.13, f32[64,2048]{1,0:T(8,128)} %collective-permute-done.13.u_ref, f32[128,8192]{1,0:T(8,128)} %y_ref.7, ...), custom_call_target="tpu_custom_call" | custom-call | flops 41943040 | bytes 13107200 | tf_op jit(solution)/shard_map/pallas_call | solution.py:208
  144.7 1.7 %fusion.16 = f32[16,12,4,128]{3,0,1,2:T(8,128)S(1)} fusion(f32[16,4,12,512]{3,2,1,0:T(8,128)S(1)} %copy-done.2, f32[512]{0:T(512)S(1)} %get-tuple-element.177, f32[512]{0:T(512)S(1)} %get-tuple-element.178, f32[512]{0:T(512)S(1)} %get-tuple-element.176, f32[512]{0:T(512)S(1)} %get-tuple-element.175, s32[512]{0:T(512)S(1)} %add_select_fusion, ...), kind=kOutput, calls=%fused_computation.14 | convolution fusion | flops 302579712 | bytes 1976832 | tf_op jit(solution)/shard_map/pbkj,nj->pkbn/dot_general | solution.py:77
  146.5 3.3 %fusion.19 = f32[16,12,4,128]{3,0,1,2:T(8,128)S(1)} fusion(f32[16,4,12,512]{3,2,1,0:T(8,128)} %shard_map.125, f32[512]{0:T(512)S(1)} %get-tuple-element.177, f32[512]{0:T(512)S(1)} %get-tuple-element.178, f32[512]{0:T(512)S(1)} %get-tuple-element.176, f32[512]{0:T(512)S(1)} %get-tuple-element.175, s32[512]{0:T(512)S(1)} %add_select_fusion, ...), kind=kOutput, calls=%fused_computation.15 | convolution fusion | flops 302579712 | bytes 1976832 | tf_op jit(solution)/shard_map/pbkj,nj->pkbn/dot_general | solution.py:77
  150.0 1.4 fusion.96
  151.3 0.6 pad_add_fusion
  151.9 1.1 copy.738
  153.0 0.5 reshape.227
  153.5 0.2 slice_multiply_fusion
  153.7 4.3 %collective-permute-start.14 = (f32[16,2,512]{2,0,1:T(8,128)S(1)}, f32[16,2,512]{2,0,1:T(8,128)S(1)}, u32[]{:S(2)}, u32[]{:S(2)}) collective-permute-start(f32[16,2,512]{2,0,1:T(8,128)S(1)} %get-tuple-element.148), channel_id=1, source_target_pairs={{0,4},{4,8},{8,12},{12,16},{16,20},{20,24},{24,28},{1,5},{5,9},{9,... | collective-permute-start | bytes 196616 | tf_op jit(solution)/shard_map/ppermute | solution.py:31
  158.1 1.4 collective-permute-start.15
  159.6 3.2 %subtract_multiply_fusion = (f32[32,8192]{1,0:T(8,128)}, f32[32,8192]{1,0:T(8,128)}) fusion(f32[128,8192]{1,0:T(8,128)} %y_ref.7, s32[]{:T(128)S(6)} %select_n.183, s32[128,8192]{1,0:T(8,128)} %g_ref.7, f32[32,2048]{1,0:T(8,128)} %dynamic-slice_select_fusion, f32[32,2048]{1,0:T(8,128)} %dynamic-slice_select_fusion.1, ...), kind=kLoop, calls=%fused_computation.17 | loop fusion | flops 1572864 | bytes 5242884 | tf_op jit(solution)/shard_map/mul | solution.py:308
  162.8 2.9 %collective-permute-done.15 = f32[16,2,512]{2,0,1:T(8,128)S(1)} collective-permute-done((f32[16,2,512]{2,0,1:T(8,128)S(1)}, f32[16,2,512]{2,0,1:T(8,128)S(1)}, u32[]{:S(2)}, u32[]{:S(2)}) %collective-permute-start.15) | collective-permute-done | bytes 65568 | tf_op jit(solution)/shard_map/ppermute | solution.py:31
  165.8 0.8 divide_subtract_fusion
  166.5 0.9 copy.747
  167.4 0.9 copy.748
  168.3 0.9 copy.749
  169.1 0.9 copy.746
  (99 shorter events, 2.3 us)
Async XLA Ops:
  1.7 0.7 copy-start.17
  2.5 10.0 %collective-permute-start.1 = (f32[16,2,512]{2,0,1:T(8,128)S(1)}, f32[16,2,512]{2,0,1:T(8,128)S(1)}, u32[]{:S(2)}, u32[]{:S(2)}) collective-permute-start(f32[16,2,512]{2,0,1:T(8,128)S(1)} %get-tuple-element.169), channel_id=1, source_target_pairs={{4,0},{8,4},{12,8},{16,12},{20,16},{24,20},{28,24},{5,1},{9,5},{13... | collective-permute-start | bytes 196616 | tf_op jit(solution)/shard_map/ppermute | solution.py:23
  3.8 7.5 %collective-permute-start = (f32[16,2,512]{2,0,1:T(8,128)S(1)}, f32[16,2,512]{2,0,1:T(8,128)S(1)}, u32[]{:S(2)}, u32[]{:S(2)}) collective-permute-start(f32[16,2,512]{2,0,1:T(8,128)S(1)} %get-tuple-element.170), channel_id=1, source_target_pairs={{0,4},{4,8},{8,12},{12,16},{16,20},{20,24},{24,28},{1,5},{5,9},{9,... | collective-permute-start | bytes 196616 | tf_op jit(solution)/shard_map/ppermute | solution.py:22
  12.4 0.7 copy-start.22
  34.3 8.6 %collective-permute-start.2 = (f32[64,2048]{1,0:T(8,128)S(1)}, f32[64,2048]{1,0:T(8,128)S(1)}, u32[]{:S(2)}, u32[]{:S(2)}) collective-permute-start(f32[64,2048]{1,0:T(8,128)S(1)} %dynamic-slice_bitcast_fusion.3), channel_id=1, source_target_pairs={{0,1},{1,0},{2,3},{3,2},{4,5},{5,4},{6,7},{7,6},{8,9},{9,8},{10,11... | collective-permute-start | bytes 1572872 | tf_op jit(solution)/shard_map/ppermute | solution.py:279
  34.3 10.9 %copy-start.3 = (f32[128,2048]{1,0:T(8,128)S(1)}, f32[128,2048]{1,0:T(8,128)}, u32[]{:S(2)}) copy-start(f32[128,2048]{1,0:T(8,128)} %shard_map.118) | copy-start | bytes 3145732
  44.8 10.9 %collective-permute-start.4 = (f32[64,2048]{1,0:T(8,128)}, f32[64,2048]{1,0:T(8,128)S(1)}, u32[]{:S(2)}, u32[]{:S(2)}) collective-permute-start(f32[64,2048]{1,0:T(8,128)} %dynamic-slice_bitcast_fusion.2), channel_id=1, source_target_pairs={{0,1},{1,0},{2,3},{3,2},{4,5},{5,4},{6,7},{7,6},{8,9},{9,8},{10,11... | collective-permute-start | bytes 1572872 | tf_op jit(solution)/shard_map/ppermute | solution.py:279
  45.3 14.2 %copy-start.6 = (f32[128,2048]{1,0:T(8,128)S(1)}, f32[128,2048]{1,0:T(8,128)}, u32[]{:S(2)}) copy-start(f32[128,2048]{1,0:T(8,128)} %shard_map.119) | copy-start | bytes 3145732
  45.3 14.2 %collective-permute-start.3 = (f32[64,2048]{1,0:T(8,128)S(1)}, f32[64,2048]{1,0:T(8,128)}, u32[]{:S(2)}, u32[]{:S(2)}) collective-permute-start(f32[64,2048]{1,0:T(8,128)S(1)} %bitcast_add_fusion.3), channel_id=1, source_target_pairs={{0,2},{1,3},{2,0},{3,1},{4,6},{5,7},{6,4},{7,5},{8,10},{9,11},{10,... | collective-permute-start | bytes 1572872 | tf_op jit(solution)/shard_map/ppermute | solution.py:279
  55.7 6.2 %copy-start.5 = (f32[128,2048]{1,0:T(8,128)S(1)}, f32[128,2048]{1,0:T(8,128)}, u32[]{:S(2)}) copy-start(f32[128,2048]{1,0:T(8,128)} %shard_map.120) | copy-start | bytes 3145732
  55.7 0.8 copy-start.25
  60.6 12.9 %copy-start.15 = (f32[64,2048]{1,0:T(8,128)}, f32[64,2048]{1,0:T(8,128)S(1)}, u32[]{:S(2)}) copy-start(f32[64,2048]{1,0:T(8,128)S(1)} %bitcast_add_fusion.2) | copy-start | bytes 1572868
  61.9 11.6 %copy-start.7 = (f32[64,2048]{1,0:T(8,128)}, f32[64,2048]{1,0:T(8,128)S(1)}, u32[]{:S(2)}) copy-start(f32[64,2048]{1,0:T(8,128)S(1)} %add.370.t_ref) | copy-start | bytes 1572868
  62.9 10.7 %collective-permute-start.7 = (f32[64,2048]{1,0:T(8,128)}, f32[64,2048]{1,0:T(8,128)}, u32[]{:S(2)}, u32[]{:S(2)}) collective-permute-start(f32[64,2048]{1,0:T(8,128)} %dynamic-slice_bitcast_fusion.1), channel_id=1, source_target_pairs={{0,1},{1,0},{2,3},{3,2},{4,5},{5,4},{6,7},{7,6},{8,9},{9,8},{10,11... | collective-permute-start | bytes 1572872 | tf_op jit(solution)/shard_map/ppermute | solution.py:279
  62.9 10.7 %collective-permute-start.5 = (f32[64,2048]{1,0:T(8,128)S(1)}, f32[64,2048]{1,0:T(8,128)}, u32[]{:S(2)}, u32[]{:S(2)}) collective-permute-start(f32[64,2048]{1,0:T(8,128)S(1)} %add.370.t_ref), channel_id=1, source_target_pairs={{0,1},{1,0},{2,3},{3,2},{4,5},{5,4},{6,7},{7,6},{8,9},{9,8},{10,11... | collective-permute-start | bytes 1572872 | tf_op jit(solution)/shard_map/ppermute | solution.py:279
  63.4 13.9 %collective-permute-start.6 = (f32[64,2048]{1,0:T(8,128)S(1)}, f32[64,2048]{1,0:T(8,128)}, u32[]{:S(2)}, u32[]{:S(2)}) collective-permute-start(f32[64,2048]{1,0:T(8,128)S(1)} %bitcast_add_fusion.2), channel_id=1, source_target_pairs={{0,2},{1,3},{2,0},{3,1},{4,6},{5,7},{6,4},{7,5},{8,10},{9,11},{10,... | collective-permute-start | bytes 1572872 | tf_op jit(solution)/shard_map/ppermute | solution.py:279
  73.6 6.0 %copy-start.4 = (f32[128,2048]{1,0:T(8,128)S(1)}, f32[128,2048]{1,0:T(8,128)}, u32[]{:S(2)}) copy-start(f32[128,2048]{1,0:T(8,128)} %shard_map.121) | copy-start | bytes 3145732
  73.6 4.8 %copy-start.16 = (f32[64,2048]{1,0:T(8,128)S(1)}, f32[64,2048]{1,0:T(8,128)}, u32[]{:S(2)}) copy-start(f32[64,2048]{1,0:T(8,128)} %copy-done.15) | copy-start | bytes 1572868
  79.5 14.1 %copy-start.9 = (f32[64,2048]{1,0:T(8,128)}, f32[64,2048]{1,0:T(8,128)S(1)}, u32[]{:S(2)}) copy-start(f32[64,2048]{1,0:T(8,128)S(1)} %add.373.t_ref) | copy-start | bytes 1572868
  80.4 13.2 %collective-permute-start.10 = (f32[64,2048]{1,0:T(8,128)}, f32[64,2048]{1,0:T(8,128)}, u32[]{:S(2)}, u32[]{:S(2)}) collective-permute-start(f32[64,2048]{1,0:T(8,128)} %dynamic-slice_bitcast_fusion), channel_id=1, source_target_pairs={{0,1},{1,0},{2,3},{3,2},{4,5},{5,4},{6,7},{7,6},{8,9},{9,8},{10,11... | collective-permute-start | bytes 1572872 | tf_op jit(solution)/shard_map/ppermute | solution.py:279
  80.5 13.2 %collective-permute-start.8 = (f32[64,2048]{1,0:T(8,128)S(1)}, f32[64,2048]{1,0:T(8,128)S(1)}, u32[]{:S(2)}, u32[]{:S(2)}) collective-permute-start(f32[64,2048]{1,0:T(8,128)S(1)} %add.373.t_ref), channel_id=1, source_target_pairs={{0,1},{1,0},{2,3},{3,2},{4,5},{5,4},{6,7},{7,6},{8,9},{9,8},{10,11... | collective-permute-start | bytes 1572872 | tf_op jit(solution)/shard_map/ppermute | solution.py:279
  81.0 13.9 %collective-permute-start.9 = (f32[64,2048]{1,0:T(8,128)S(1)}, f32[64,2048]{1,0:T(8,128)}, u32[]{:S(2)}, u32[]{:S(2)}) collective-permute-start(f32[64,2048]{1,0:T(8,128)S(1)} %bitcast_add_fusion.1), channel_id=1, source_target_pairs={{0,2},{1,3},{2,0},{3,1},{4,6},{5,7},{6,4},{7,5},{8,10},{9,11},{10,... | collective-permute-start | bytes 1572872 | tf_op jit(solution)/shard_map/ppermute | solution.py:279
  93.7 6.1 %copy-start.8 = (f32[64,2048]{1,0:T(8,128)S(1)}, f32[64,2048]{1,0:T(8,128)}, u32[]{:S(2)}) copy-start(f32[64,2048]{1,0:T(8,128)} %copy-done.7) | copy-start | bytes 1572868
  93.7 4.2 %copy-start.20 = (f32[64,2048]{1,0:T(8,128)}, f32[64,2048]{1,0:T(8,128)S(1)}, u32[]{:S(2)}) copy-start(f32[64,2048]{1,0:T(8,128)S(1)} %collective-permute-done.8.u_ref) | copy-start | bytes 1572868
  97.9 14.7 %copy-start.11 = (f32[64,2048]{1,0:T(8,128)}, f32[64,2048]{1,0:T(8,128)S(1)}, u32[]{:S(2)}) copy-start(f32[64,2048]{1,0:T(8,128)S(1)} %add.375.t_ref) | copy-start | bytes 1572868
  97.9 17.2 %collective-permute-start.11 = (f32[64,2048]{1,0:T(8,128)S(1)}, f32[64,2048]{1,0:T(8,128)}, u32[]{:S(2)}, u32[]{:S(2)}) collective-permute-start(f32[64,2048]{1,0:T(8,128)S(1)} %add.375.t_ref), channel_id=1, source_target_pairs={{0,1},{1,0},{2,3},{3,2},{4,5},{5,4},{6,7},{7,6},{8,9},{9,8},{10,11... | collective-permute-start | bytes 1572872 | tf_op jit(solution)/shard_map/ppermute | solution.py:279
  98.0 17.1 %collective-permute-start.12 = (f32[64,2048]{1,0:T(8,128)}, f32[64,2048]{1,0:T(8,128)}, u32[]{:S(2)}, u32[]{:S(2)}) collective-permute-start(f32[64,2048]{1,0:T(8,128)} %bitcast_add_fusion), channel_id=1, source_target_pairs={{0,2},{1,3},{2,0},{3,1},{4,6},{5,7},{6,4},{7,5},{8,10},{9,11},{10,... | collective-permute-start | bytes 1572872 | tf_op jit(solution)/shard_map/ppermute | solution.py:279
  101.5 11.1 %copy-start = (f32[16,4,12,512]{3,2,1,0:T(8,128)S(1)}, f32[16,4,12,512]{3,2,1,0:T(8,128)}, u32[]{:S(2)}) copy-start(f32[16,4,12,512]{3,2,1,0:T(8,128)} %shard_map.122) | copy-start | bytes 4718596
  112.6 4.0 %copy-start.10 = (f32[64,2048]{1,0:T(8,128)S(1)}, f32[64,2048]{1,0:T(8,128)}, u32[]{:S(2)}) copy-start(f32[64,2048]{1,0:T(8,128)} %copy-done.9) | copy-start | bytes 1572868
  112.6 4.0 %copy-start.21 = (f32[64,2048]{1,0:T(8,128)S(1)}, f32[64,2048]{1,0:T(8,128)}, u32[]{:S(2)}) copy-start(f32[64,2048]{1,0:T(8,128)} %copy-done.20) | copy-start | bytes 1572868
  116.4 15.6 %copy-start.13 = (f32[64,2048]{1,0:T(8,128)}, f32[64,2048]{1,0:T(8,128)S(1)}, u32[]{:S(2)}) copy-start(f32[64,2048]{1,0:T(8,128)S(1)} %add.377.t_ref) | copy-start | bytes 1572868
  116.4 15.5 %collective-permute-start.13 = (f32[64,2048]{1,0:T(8,128)S(1)}, f32[64,2048]{1,0:T(8,128)}, u32[]{:S(2)}, u32[]{:S(2)}) collective-permute-start(f32[64,2048]{1,0:T(8,128)S(1)} %add.377.t_ref), channel_id=1, source_target_pairs={{0,1},{1,0},{2,3},{3,2},{4,5},{5,4},{6,7},{7,6},{8,9},{9,8},{10,11... | collective-permute-start | bytes 1572872 | tf_op jit(solution)/shard_map/ppermute | solution.py:279
  117.3 11.2 %copy-start.12 = (f32[64,2048]{1,0:T(8,128)S(1)}, f32[64,2048]{1,0:T(8,128)}, u32[]{:S(2)}) copy-start(f32[64,2048]{1,0:T(8,128)} %copy-done.11) | copy-start | bytes 1572868
  117.3 12.9 %copy-start.1 = (f32[16,4,12,512]{3,2,1,0:T(8,128)S(1)}, f32[16,4,12,512]{3,2,1,0:T(8,128)}, u32[]{:S(2)}) copy-start(f32[16,4,12,512]{3,2,1,0:T(8,128)} %shard_map.123) | copy-start | bytes 4718596
  133.6 11.1 %copy-start.2 = (f32[16,4,12,512]{3,2,1,0:T(8,128)S(1)}, f32[16,4,12,512]{3,2,1,0:T(8,128)}, u32[]{:S(2)}) copy-start(f32[16,4,12,512]{3,2,1,0:T(8,128)} %shard_map.124) | copy-start | bytes 4718596
  144.7 5.0 %copy-start.19 = (f32[16,12,4,128]{3,0,1,2:T(8,128)S(1)}, f32[16,12,4,128]{3,0,1,2:T(8,128)}, u32[]{:S(2)}) copy-start(f32[16,12,4,128]{3,0,1,2:T(8,128)} %fusion.10) | copy-start | bytes 1179652
  153.0 6.5 %copy-start.24 = (f32[32,2048]{1,0:T(8,128)S(1)}, f32[32,2048]{1,0:T(8,128)}, u32[]{:S(2)}) copy-start(f32[32,2048]{1,0:T(8,128)} %dynamic-slice_select_fusion.3) | copy-start | bytes 786436
  153.7 9.1 %collective-permute-start.14 = (f32[16,2,512]{2,0,1:T(8,128)S(1)}, f32[16,2,512]{2,0,1:T(8,128)S(1)}, u32[]{:S(2)}, u32[]{:S(2)}) collective-permute-start(f32[16,2,512]{2,0,1:T(8,128)S(1)} %get-tuple-element.148), channel_id=1, source_target_pairs={{0,4},{4,8},{8,12},{12,16},{16,20},{20,24},{24,28},{1,5},{5,9},{9,... | collective-permute-start | bytes 196616 | tf_op jit(solution)/shard_map/ppermute | solution.py:31
  158.0 7.7 %copy-start.14 = (f32[16,8,512]{2,1,0:T(8,128)S(1)}, f32[16,8,512]{2,1,0:T(8,128)}, u32[]{:S(2)}) copy-start(f32[16,8,512]{2,1,0:T(8,128)} %param.10) | copy-start | bytes 786436
  158.1 7.7 %copy-start.18 = (f32[16,8,512]{2,0,1:T(8,128)S(1)}, f32[16,8,512]{2,0,1:T(8,128)}, u32[]{:S(2)}) copy-start(f32[16,8,512]{2,0,1:T(8,128)} %copy-done.17) | copy-start | bytes 786436
  158.1 7.7 %copy-start.23 = (f32[16,10,512]{2,0,1:T(8,128)S(1)}, f32[16,10,512]{2,0,1:T(8,128)}, u32[]{:S(2)}) copy-start(f32[16,10,512]{2,0,1:T(8,128)} %copy-done.22) | copy-start | bytes 983044
  158.1 7.7 %copy-start.26 = (f32[16,8,512]{2,1,0:T(8,128)S(1)}, f32[16,8,512]{2,1,0:T(8,128)}, u32[]{:S(2)}) copy-start(f32[16,8,512]{2,1,0:T(8,128)} %param.11) | copy-start | bytes 786436
  158.1 7.7 %copy-start.27 = (f32[16,8,512]{2,1,0:T(8,128)S(1)}, f32[16,8,512]{2,1,0:T(8,128)}, u32[]{:S(2)}) copy-start(f32[16,8,512]{2,1,0:T(8,128)} %param.12) | copy-start | bytes 786436
  158.1 7.7 %copy-start.28 = (f32[16]{0:T(128)S(1)}, f32[16]{0:T(128)}, u32[]{:S(2)}) copy-start(f32[16]{0:T(128)} %param.13) | copy-start | bytes 196
  158.1 7.6 %collective-permute-start.15 = (f32[16,2,512]{2,0,1:T(8,128)S(1)}, f32[16,2,512]{2,0,1:T(8,128)S(1)}, u32[]{:S(2)}, u32[]{:S(2)}) collective-permute-start(f32[16,2,512]{2,0,1:T(8,128)S(1)} %get-tuple-element.149), channel_id=1, source_target_pairs={{4,0},{8,4},{12,8},{16,12},{20,16},{24,20},{28,24},{5,1},{9,5},{13... | collective-permute-start | bytes 196616 | tf_op jit(solution)/shard_map/ppermute | solution.py:31

commit v9 on v8

--- a/solution.py
+++ b/solution.py
@@ -177,10 +177,9 @@
         lax.fori_loop(0, npred, body, 0, unroll=2 if npred % 2 == 0 else 1)
 
 
-def fit_chunk(wl, cov, along, chunk, width):
+def fit_chunk(wl, cov, along, off, width):
     npred, rows, _ = cov.shape
     nrow = along.shape[2]
-    off = chunk * (width // TN)
     return pl.pallas_call(
         fit_kernel,
         grid=(width // TN,),
@@ -200,11 +199,10 @@
     )(wl, cov, along)
 
 
-def back_chunk(wl, cov, halves, target, land, chunk, nrow):
+def back_chunk(wl, cov, halves, target, land, off, nrow):
     npred, rows, _ = cov.shape
     cur, other, mine = halves
     width = cur.shape[1]
-    off = chunk * (width // TN)
     return pl.pallas_call(
         back_kernel,
         grid=(width // TN,),
@@ -255,7 +253,15 @@
     nrow = padded.shape[1]
     target_blk = lax.dynamic_slice_in_dim(target, start, share, 0)
     land_blk = lax.dynamic_slice_in_dim(land, start, share, 0).astype(jnp.float32)
-    width = ny // CHUNKS
+    blocks = ny // TN
+    base = blocks // CHUNKS
+    counts = [base] * CHUNKS
+    if base >= 2 and CHUNKS >= 2 and blocks == base * CHUNKS:
+        counts[0] -= 1
+        counts[-1] += 1
+    offs = [sum(counts[:c]) for c in range(CHUNKS)]
+    widths = [n * TN for n in counts]
+    width = widths[0]
     steps = reduce_steps(jnp.zeros((rows, width), jnp.float32), "pred")
     bit0 = lax.axis_index("pred") % 2
     bits_arr = jnp.reshape(bit0, (1,)).astype(jnp.int32)
@@ -267,7 +273,7 @@
     state = [None] * CHUNKS
     fitted_parts = [None] * CHUNKS
     back_parts = [None] * CHUNKS
-    state[0] = fit_chunk(wl, covariates, along, 0, width)
+    state[0] = fit_chunk(wl, covariates, along, offs[0], widths[0])
     next_back = 0
     for s in range(1, CHUNKS + nsteps + 1):
         pending = []
@@ -279,11 +285,11 @@
                 pending.append((c, finish, lax.ppermute(send, "pred", pairs)))
         outs = []
         if s < CHUNKS:
-            outs.append(("fit", s, fit_chunk(wl, covariates, along, s, width)))
+            outs.append(("fit", s, fit_chunk(wl, covariates, along, offs[s], widths[s])))
         if next_back < CHUNKS and next_back + nsteps + 1 <= s:
             c = next_back
             state[c] = attach(state[c])
-            outs.append(("back", c, back_chunk(wl, covariates, state[c], target, land, c, nrow)))
+            outs.append(("back", c, back_chunk(wl, covariates, state[c], target, land, offs[c], nrow)))
             next_back += 1
         recvs = [r for _, _, r in pending]
         if outs:
@@ -298,7 +304,7 @@
     for c in range(CHUNKS):
         if back_parts[c] is None:
             state[c] = attach(state[c])
-            back_parts[c] = back_chunk(wl, covariates, state[c], target, land, c, nrow)
+            back_parts[c] = back_chunk(wl, covariates, state[c], target, land, offs[c], nrow)
         cur, other, _ = state[c]
         half = rows // 2
         side = start // half

time: 171 us -> 169 us (0.988)
  waiting for transfers between devices: 12.8 us -> 10.5 us
  other arithmetic: 19.7 us -> 17.6 us
    ppermute x12, waiting for transfers between devices: 7.93 us -> 5.78 us  [local(): pending.append((c, finish, lax.ppermute(send, 'pred', pairs)))]
    unnamed x64 -> x70, local copies, waits for them, and re-layouts: 6.86 us -> 6.26 us
  transfers between devices with their start and end apart: 16 -> 16, of which waited for: 5 -> 5; matrix products, arithmetic and copies ran while one was open for 8% -> 11% of each run, Pallas kernels for 35% -> 35%
where the time goes in v9:
time: 169 us; the launch traced here: 168 us
  Pallas kernels  78.6 us (47%)
  local copies, waits for them, and re-layouts  21.6 us (13%)
  starting transfers between devices  21.3 us (13%)
  other arithmetic  17.6 us (10%)
  matrix products  16.7 us (10%)
  waiting for transfers between devices  10.5 us (6%)
    pallas_call x4, Pallas kernels, back_chunk(): pl.pallas_call(back_kernel, grid=(width // TN,), in_specs=[pl.BlockSpec(m...  44.6 us
    pallas_call x4, Pallas kernels, fit_chunk(): pl.pallas_call(fit_kernel, grid=(width // TN,), in_specs=[pl.BlockSpec((4...  34.1 us
    dot_general x4, matrix products, banded_data(): jnp.einsum('pbkj,nj->pkbn', part, basis, precision=lax.Precision.HIGH)  10.8 us
    ppermute x12, starting transfers between devices, local(): pending.append((c, finish, lax.ppermute(send, 'pred', pairs)))  8.76 us
    unnamed x70, local copies, waits for them, and re-layouts  6.26 us
    dot_general x1, matrix products, banded_along(): jnp.einsum('pbkn,nj->pbkj', cwin, block_basis(window), precision=lax.Prec...  5.94 us
    select_n x4, other arithmetic, local(): picked = jnp.where(bit0 == side, cur, other)  5.87 us
    ppermute x12, waiting for transfers between devices, local(): pending.append((c, finish, lax.ppermute(send, 'pred', pairs)))  5.78 us
  transfers between devices with their start and end apart: 16, of which 5 were waited for; matrix products, arithmetic and copies ran while one was open for 11% of the time, Pallas kernels for 35%

profile of v9, /device:TPU:0, one launch (start us, length us, event | category | flops | bytes accessed | tf_op | source)
XLA Modules:
  0.0 167.6 jit_solution(936842534779769858)
XLA Ops:
  0.6 1.1 copy.711
  1.8 1.3 collective-permute-start.1
  3.1 5.5 %collective-permute-start = (f32[16,2,512]{2,0,1:T(8,128)S(1)}, f32[16,2,512]{2,0,1:T(8,128)S(1)}, u32[]{:S(2)}, u32[]{:S(2)}) collective-permute-start(f32[16,2,512]{2,0,1:T(8,128)S(1)} %get-tuple-element.170), channel_id=1, source_target_pairs={{0,4},{4,8},{8,12},{12,16},{16,20},{20,24},{24,28},{1,5},{5,9},{9,... | collective-permute-start | bytes 196616 | tf_op jit(solution)/shard_map/ppermute | solution.py:22
  8.7 1.9 %collective-permute-done = f32[16,2,512]{2,0,1:T(8,128)S(1)} collective-permute-done((f32[16,2,512]{2,0,1:T(8,128)S(1)}, f32[16,2,512]{2,0,1:T(8,128)S(1)}, u32[]{:S(2)}, u32[]{:S(2)}) %collective-permute-start) | collective-permute-done | bytes 65568 | tf_op jit(solution)/shard_map/ppermute | solution.py:22
  10.6 1.1 constant_dynamic-update-slice_fusion.3
  11.8 0.7 copy-done.22
  12.5 0.7 copy-done.15
  13.2 0.5 fusion.45
  13.6 0.1 copy.729
  15.4 2.7 %stack.75 = f32[16,16,12,128]{3,1,2,0:T(8,128)S(1)} concatenate(f32[16,1,12,128]{3,1,2,0:T(1,128)S(1)} %copy.714, f32[16,1,12,128]{3,1,2,0:T(1,128)S(1)} %copy.715, f32[16,1,12,128]{3,1,2,0:T(1,128)S(1)} %copy.716, f32[16,1,12,128]{3,1,2,0:T(1,128)S(1)} %copy.717, f32[16,1,12,128]{3,1,2,0:T(1,128)S(1)} %copy.718, f32[16,1,12,128]{3,1,2,0:T(1,128)S(1)} %copy.719, ...), dimensions={1} | concatenate | bytes 3145728 | tf_op jit(solution)/shard_map/stack | solution.py:67
  18.1 5.9 %fusion.a_ref = f32[16,16,12,512]{3,2,1,0:T(8,128)} fusion(f32[16,16,12,128]{3,1,2,0:T(8,128)S(1)} %stack.75, f32[512]{0:T(512)S(1)} %get-tuple-element.177, f32[512]{0:T(512)S(1)} %get-tuple-element.178, f32[512]{0:T(512)S(1)} %get-tuple-element.176, f32[512]{0:T(512)S(1)} %get-tuple-element.175, s32[512]{0:T(512)S(1)} %add_select_fusion, ...), kind=kOutput, calls=%fused_computation | convolution fusion | flops 1208549376 | bytes 7875072 | tf_op jit(solution)/shard_map/pbkn,nj->pbkj/dot_general | solution.py:68
  24.0 0.7 broadcast_in_dim.79.w_ref
  24.7 6.9 %shard_map.118 = f32[128,1536]{1,0:T(8,128)} custom-call(f32[4,16,256]{2,1,0:T(8,128)} %broadcast_in_dim.79.w_ref, bf16[16,128,8192]{2,1,0:T(8,128)(2,1)} %cov_ref.15, f32[16,16,12,512]{3,2,1,0:T(8,128)} %fusion.a_ref), custom_call_target="tpu_custom_call" | custom-call | flops 31457280 | bytes 8257536 | tf_op jit(solution)/shard_map/pallas_call | solution.py:183
  31.7 1.0 dynamic-slice_bitcast_fusion.3
  32.8 8.5 %shard_map.119 = f32[128,2048]{1,0:T(8,128)} custom-call(f32[4,16,256]{2,1,0:T(8,128)} %broadcast_in_dim.79.w_ref, bf16[16,128,8192]{2,1,0:T(8,128)(2,1)} %cov_ref.15, f32[16,16,12,512]{3,2,1,0:T(8,128)} %fusion.a_ref), custom_call_target="tpu_custom_call" | custom-call | flops 41943040 | bytes 11010048 | tf_op jit(solution)/shard_map/pallas_call | solution.py:183
  41.3 1.9 %dynamic-slice_bitcast_fusion.2 = f32[64,2048]{1,0:T(8,128)} fusion(f32[2,64,2048]{2,1,0:T(8,128)} %bitcast.80, s32[]{:T(128)S(6)} %select_n.187), kind=kLoop, calls=%fused_computation.31 | loop fusion | bytes 1048580 | tf_op jit(solution)/shard_map/jit(dynamic_index_in_dim)/squeeze | solution.py:104
  43.2 0.5 collective-permute-start.4
  43.7 2.0 %collective-permute-start.3 = (f32[64,1536]{1,0:T(8,128)S(1)}, f32[64,1536]{1,0:T(8,128)}, u32[]{:S(2)}, u32[]{:S(2)}) collective-permute-start(f32[64,1536]{1,0:T(8,128)S(1)} %bitcast_add_fusion.3), channel_id=1, source_target_pairs={{0,2},{1,3},{2,0},{3,1},{4,6},{5,7},{6,4},{7,5},{8,10},{9,11},{10,... | collective-permute-start | bytes 1179656 | tf_op jit(solution)/shard_map/ppermute | solution.py:285
  45.7 8.4 %shard_map.120 = f32[128,2048]{1,0:T(8,128)} custom-call(f32[4,16,256]{2,1,0:T(8,128)} %broadcast_in_dim.79.w_ref, bf16[16,128,8192]{2,1,0:T(8,128)(2,1)} %cov_ref.15, f32[16,16,12,512]{3,2,1,0:T(8,128)} %fusion.a_ref), custom_call_target="tpu_custom_call" | custom-call | flops 41943040 | bytes 11010048 | tf_op jit(solution)/shard_map/pallas_call | solution.py:183
  54.1 1.0 collective-permute-done.3
  55.2 0.2 copy-done.4
  55.4 0.8 dynamic-slice_bitcast_fusion.1
  56.2 1.6 collective-permute-start.6
  57.8 1.1 add.372.t_ref
  58.9 0.3 collective-permute-start.5
  59.2 10.2 %shard_map.121 = f32[128,2560]{1,0:T(8,128)} custom-call(f32[4,16,256]{2,1,0:T(8,128)} %broadcast_in_dim.79.w_ref, bf16[16,128,8192]{2,1,0:T(8,128)(2,1)} %cov_ref.15, f32[16,16,12,512]{3,2,1,0:T(8,128)} %fusion.a_ref), custom_call_target="tpu_custom_call" | custom-call | flops 52428800 | bytes 13762560 | tf_op jit(solution)/shard_map/pallas_call | solution.py:183
  69.4 1.2 collective-permute-done.6
  70.5 2.0 %dynamic-slice_bitcast_fusion = f32[64,2560]{1,0:T(8,128)} fusion(f32[2,64,2560]{2,1,0:T(8,128)} %bitcast.76, s32[]{:T(128)S(6)} %select_n.187), kind=kLoop, calls=%fused_computation.19 | loop fusion | bytes 1310724 | tf_op jit(solution)/shard_map/jit(dynamic_index_in_dim)/squeeze | solution.py:104
  72.5 1.9 %bitcast_add_fusion.1 = f32[64,2048]{1,0:T(8,128)} fusion(f32[64,2048]{1,0:T(8,128)} %collective-permute-done.7, f32[2,64,2048]{2,1,0:T(8,128)S(1)} %bitcast.79, s32[]{:T(128)S(6)} %select_n.186), kind=kLoop, calls=%fused_computation.28 | loop fusion | flops 131072 | bytes 1572868 | tf_op jit(solution)/shard_map/add | solution.py:105
  74.5 0.6 collective-permute-start.8
  75.1 1.6 collective-permute-start.9
  76.7 9.0 %shard_map.122 = f32[16,3,12,512]{3,2,1,0:T(8,128)} custom-call(s32[1]{0:T(128)} %bitcast.29.b_ref, f32[4,16,256]{2,1,0:T(8,128)} %broadcast_in_dim.79.w_ref, bf16[16,128,8192]{2,1,0:T(8,128)(2,1)} %cov_ref.15, f32[64,1536]{1,0:T(8,128)} %copy-done.12, f32[64,1536]{1,0:T(8,128)} %copy-done.24, f32[128,8192]{1,0:T(8,128)} %y_ref.7, s32[128,8192]{1,0:T(8,128)} %g_ref.7), custom_call_target="tpu_custom_call" | custom-call | flops 31457280 | bytes 9830400 | tf_op jit(solution)/shard_map/pallas_call | solution.py:206
  85.7 3.6 %collective-permute-done.9 = f32[64,2048]{1,0:T(8,128)} collective-permute-done((f32[64,2048]{1,0:T(8,128)}, f32[64,2048]{1,0:T(8,128)}, u32[]{:S(2)}, u32[]{:S(2)}) %collective-permute-start.9) | collective-permute-done | bytes 524320 | tf_op jit(solution)/shard_map/ppermute | solution.py:285
  89.3 1.2 bitcast_add_fusion
  90.5 1.7 collective-permute-start.12
  92.1 1.3 add.377.t_ref
  93.5 1.7 %dynamic-slice_select_fusion.3 = f32[32,1536]{1,0:T(8,128)} fusion(f32[64,1536]{1,0:T(8,128)} %copy-done.24, s32[]{:T(128)S(6)} %select_n.189, f32[64,1536]{1,0:T(8,128)S(1)} %copy-done.13, pred[]{:T(512)S(6)} %eq.63), kind=kLoop, calls=%fused_computation.71 | loop fusion | flops 49152 | bytes 589829 | tf_op jit(solution)/shard_map/jit(_where)/select_n | solution.py:311
  95.2 11.1 %shard_map.123 = f32[16,4,12,512]{3,2,1,0:T(8,128)} custom-call(s32[1]{0:T(128)} %bitcast.29.b_ref, f32[4,16,256]{2,1,0:T(8,128)} %broadcast_in_dim.79.w_ref, bf16[16,128,8192]{2,1,0:T(8,128)(2,1)} %cov_ref.15, f32[64,2048]{1,0:T(8,128)} %copy-done.7, f32[64,2048]{1,0:T(8,128)} %copy-done.19, f32[128,8192]{1,0:T(8,128)} %y_ref.7, s32[128,8192]{1,0:T(8,128)} %g_ref.7), custom_call_target="tpu_custom_call" | custom-call | flops 41943040 | bytes 13107200 | tf_op jit(solution)/shard_map/pallas_call | solution.py:206
  106.3 2.8 %fusion.19 = f32[16,12,3,128]{3,0,1,2:T(8,128)} fusion(f32[16,3,12,512]{3,2,1,0:T(8,128)S(1)} %copy-done.3, f32[512]{0:T(512)S(1)} %get-tuple-element.177, f32[512]{0:T(512)S(1)} %get-tuple-element.178, f32[512]{0:T(512)} %copy-done.27, f32[512]{0:T(512)S(1)} %get-tuple-element.175, s32[512]{0:T(512)S(1)} %add_select_fusion, s32[128]{0:T(128)} %copy-done.29), kind=kOutput, calls=%fused_computation.15 | convolution fusion | flops 227082240 | bytes 1485312 | tf_op jit(solution)/shard_map/pbkj,nj->pkbn/dot_general | solution.py:77
  109.2 1.2 add.379.t_ref
  110.3 0.5 collective-permute-start.13
  110.8 0.7 dynamic-slice_select_fusion.2
  111.5 11.2 %shard_map.124 = f32[16,4,12,512]{3,2,1,0:T(8,128)} custom-call(s32[1]{0:T(128)} %bitcast.29.b_ref, f32[4,16,256]{2,1,0:T(8,128)} %broadcast_in_dim.79.w_ref, bf16[16,128,8192]{2,1,0:T(8,128)(2,1)} %cov_ref.15, f32[64,2048]{1,0:T(8,128)} %copy-done.9, f32[64,2048]{1,0:T(8,128)} %collective-permute-done.11.u_ref, f32[128,8192]{1,0:T(8,128)} %y_ref.7, ...), custom_call_target="tpu_custom_call" | custom-call | flops 41943040 | bytes 13107200 | tf_op jit(solution)/shard_map/pallas_call | solution.py:206
  122.8 1.7 %dynamic-slice_select_fusion.1 = f32[32,2048]{1,0:T(8,128)} fusion(f32[64,2048]{1,0:T(8,128)} %collective-permute-done.11.u_ref, s32[]{:T(128)S(6)} %select_n.189, f32[64,2048]{1,0:T(8,128)S(1)} %copy-done.10, pred[]{:T(512)S(6)} %eq.63), kind=kLoop, calls=%fused_computation.59 | loop fusion | flops 65536 | bytes 786437 | tf_op jit(solution)/shard_map/jit(_where)/select_n | solution.py:311
  124.4 2.4 %fusion.11 = f32[16,12,4,128]{3,0,1,2:T(8,128)S(1)} fusion(f32[16,4,12,512]{3,2,1,0:T(8,128)S(1)} %copy-done, f32[512]{0:T(512)S(1)} %get-tuple-element.177, f32[512]{0:T(512)S(1)} %get-tuple-element.178, f32[512]{0:T(512)} %copy-done.27, f32[512]{0:T(512)S(1)} %get-tuple-element.175, s32[512]{0:T(512)S(1)} %add_select_fusion, s32[128]{0:T(128)} %copy-done.29), kind=kOutput, calls=%fused_computation.11 | convolution fusion | flops 302579712 | bytes 1976832 | tf_op jit(solution)/shard_map/pbkj,nj->pkbn/dot_general | solution.py:77
  126.8 1.8 %dynamic-slice_select_fusion = f32[32,2560]{1,0:T(8,128)} fusion(f32[64,2560]{1,0:T(8,128)} %collective-permute-done.13.u_ref, s32[]{:T(128)S(6)} %select_n.189, f32[64,2560]{1,0:T(8,128)S(1)} %add.379.t_ref, pred[]{:T(512)S(6)} %eq.63), kind=kLoop, calls=%fused_computation.40 | loop fusion | flops 81920 | bytes 983045 | tf_op jit(solution)/shard_map/jit(_where)/select_n | solution.py:311
  128.6 13.2 %shard_map.125 = f32[16,5,12,512]{3,2,1,0:T(8,128)} custom-call(s32[1]{0:T(128)} %bitcast.29.b_ref, f32[4,16,256]{2,1,0:T(8,128)} %broadcast_in_dim.79.w_ref, bf16[16,128,8192]{2,1,0:T(8,128)(2,1)} %cov_ref.15, f32[64,2560]{1,0:T(8,128)} %copy-done.6, f32[64,2560]{1,0:T(8,128)} %collective-permute-done.13.u_ref, f32[128,8192]{1,0:T(8,128)} %y_ref.7, ...), custom_call_target="tpu_custom_call" | custom-call | flops 52428800 | bytes 16384000 | tf_op jit(solution)/shard_map/pallas_call | solution.py:206
  141.9 1.7 %fusion.14 = f32[16,12,4,128]{3,0,1,2:T(8,128)S(1)} fusion(f32[16,4,12,512]{3,2,1,0:T(8,128)S(1)} %copy-done.1, f32[512]{0:T(512)S(1)} %get-tuple-element.177, f32[512]{0:T(512)S(1)} %get-tuple-element.178, f32[512]{0:T(512)S(1)} %copy-done.28, f32[512]{0:T(512)S(1)} %get-tuple-element.175, s32[512]{0:T(512)S(1)} %add_select_fusion, s32[128]{0:T(128)S(1)} %copy-done.30), kind=kOutput, calls=%fused_computation.12 | convolution fusion | flops 302579712 | bytes 1976832 | tf_op jit(solution)/shard_map/pbkj,nj->pkbn/dot_general | solution.py:77
  143.6 3.9 %fusion.8 = f32[16,12,5,128]{3,0,1,2:T(8,128)S(1)} fusion(f32[16,5,12,512]{3,2,1,0:T(8,128)} %shard_map.125, f32[512]{0:T(512)S(1)} %get-tuple-element.177, f32[512]{0:T(512)S(1)} %get-tuple-element.178, f32[512]{0:T(512)S(1)} %copy-done.28, f32[512]{0:T(512)S(1)} %get-tuple-element.175, s32[512]{0:T(512)S(1)} %add_select_fusion, s32[128]{0:T(128)S(1)} %copy-done.30), kind=kOutput, calls=%fused_computation.10 | convolution fusion | flops 378077184 | bytes 2468352 | tf_op jit(solution)/shard_map/pbkj,nj->pkbn/dot_general | solution.py:77
  147.4 0.2 pad_maximum_fusion
  147.6 1.4 fusion.96
  149.0 0.6 pad_add_fusion
  149.6 1.1 copy.738
  150.7 0.5 reshape.227
  151.2 0.2 slice_multiply_fusion
  151.4 4.3 %collective-permute-start.14 = (f32[16,2,512]{2,0,1:T(8,128)S(1)}, f32[16,2,512]{2,0,1:T(8,128)S(1)}, u32[]{:S(2)}, u32[]{:S(2)}) collective-permute-start(f32[16,2,512]{2,0,1:T(8,128)S(1)} %get-tuple-element.148), channel_id=1, source_target_pairs={{0,4},{4,8},{8,12},{12,16},{16,20},{20,24},{24,28},{1,5},{5,9},{9,... | collective-permute-start | bytes 196616 | tf_op jit(solution)/shard_map/ppermute | solution.py:31
  155.8 1.4 collective-permute-start.15
  157.2 3.3 %subtract_multiply_fusion = (f32[32,8192]{1,0:T(8,128)}, f32[32,8192]{1,0:T(8,128)}) fusion(f32[128,8192]{1,0:T(8,128)} %y_ref.7, s32[]{:T(128)S(6)} %select_n.195, s32[128,8192]{1,0:T(8,128)} %g_ref.7, f32[32,2560]{1,0:T(8,128)} %dynamic-slice_select_fusion, f32[32,2048]{1,0:T(8,128)} %dynamic-slice_select_fusion.1, ...), kind=kLoop, calls=%fused_computation.17 | loop fusion | flops 1572864 | bytes 5242884 | tf_op jit(solution)/shard_map/mul | solution.py:314
  160.5 2.8 %collective-permute-done.15 = f32[16,2,512]{2,0,1:T(8,128)S(1)} collective-permute-done((f32[16,2,512]{2,0,1:T(8,128)S(1)}, f32[16,2,512]{2,0,1:T(8,128)S(1)}, u32[]{:S(2)}, u32[]{:S(2)}) %collective-permute-start.15) | collective-permute-done | bytes 65568 | tf_op jit(solution)/shard_map/ppermute | solution.py:31
  163.3 0.8 divide_subtract_fusion
  164.2 0.9 copy.747
  165.0 0.9 copy.748
  165.9 0.9 copy.749
  166.7 0.9 copy.746
  (105 shorter events, 2.1 us)
Async XLA Ops:
  1.8 10.0 %collective-permute-start.1 = (f32[16,2,512]{2,0,1:T(8,128)S(1)}, f32[16,2,512]{2,0,1:T(8,128)S(1)}, u32[]{:S(2)}, u32[]{:S(2)}) collective-permute-start(f32[16,2,512]{2,0,1:T(8,128)S(1)} %get-tuple-element.169), channel_id=1, source_target_pairs={{4,0},{8,4},{12,8},{16,12},{20,16},{24,20},{28,24},{5,1},{9,5},{13... | collective-permute-start | bytes 196616 | tf_op jit(solution)/shard_map/ppermute | solution.py:23
  3.1 7.5 %collective-permute-start = (f32[16,2,512]{2,0,1:T(8,128)S(1)}, f32[16,2,512]{2,0,1:T(8,128)S(1)}, u32[]{:S(2)}, u32[]{:S(2)}) collective-permute-start(f32[16,2,512]{2,0,1:T(8,128)S(1)} %get-tuple-element.170), channel_id=1, source_target_pairs={{0,4},{4,8},{8,12},{12,16},{16,20},{20,24},{24,28},{1,5},{5,9},{9,... | collective-permute-start | bytes 196616 | tf_op jit(solution)/shard_map/ppermute | solution.py:22
  8.6 9.5 %copy-start.27 = (f32[512]{0:T(512)}, f32[512]{0:T(512)S(1)}, u32[]{:S(2)}) copy-start(f32[512]{0:T(512)S(1)} %get-tuple-element.176) | copy-start | bytes 6148
  8.7 9.4 %copy-start.29 = (s32[128]{0:T(128)}, s32[128]{0:T(128)S(1)}, u32[]{:S(2)}) copy-start(s32[128]{0:T(128)S(1)} %iota_add_fusion) | copy-start | bytes 1540
  11.7 0.7 copy-start.22
  12.4 0.7 copy-start.15
  32.7 8.6 %collective-permute-start.2 = (f32[64,1536]{1,0:T(8,128)S(1)}, f32[64,1536]{1,0:T(8,128)S(1)}, u32[]{:S(2)}, u32[]{:S(2)}) collective-permute-start(f32[64,1536]{1,0:T(8,128)S(1)} %dynamic-slice_bitcast_fusion.3), channel_id=1, source_target_pairs={{0,1},{1,0},{2,3},{3,2},{4,5},{5,4},{6,7},{7,6},{8,9},{9,8},{10,11... | collective-permute-start | bytes 1179656 | tf_op jit(solution)/shard_map/ppermute | solution.py:285
  32.8 10.9 %copy-start.11 = (f32[128,1536]{1,0:T(8,128)S(1)}, f32[128,1536]{1,0:T(8,128)}, u32[]{:S(2)}) copy-start(f32[128,1536]{1,0:T(8,128)} %shard_map.118) | copy-start | bytes 2359300
  43.2 11.9 %collective-permute-start.4 = (f32[64,2048]{1,0:T(8,128)}, f32[64,2048]{1,0:T(8,128)S(1)}, u32[]{:S(2)}, u32[]{:S(2)}) collective-permute-start(f32[64,2048]{1,0:T(8,128)} %dynamic-slice_bitcast_fusion.2), channel_id=1, source_target_pairs={{0,1},{1,0},{2,3},{3,2},{4,5},{5,4},{6,7},{7,6},{8,9},{9,8},{10,11... | collective-permute-start | bytes 1572872 | tf_op jit(solution)/shard_map/ppermute | solution.py:285
  43.7 10.4 %copy-start.17 = (f32[64,1536]{1,0:T(8,128)}, f32[64,1536]{1,0:T(8,128)S(1)}, u32[]{:S(2)}) copy-start(f32[64,1536]{1,0:T(8,128)S(1)} %bitcast_add_fusion.3) | copy-start | bytes 1179652
  43.7 11.4 %copy-start.5 = (f32[128,2048]{1,0:T(8,128)S(1)}, f32[128,2048]{1,0:T(8,128)}, u32[]{:S(2)}) copy-start(f32[128,2048]{1,0:T(8,128)} %shard_map.119) | copy-start | bytes 3145732
  43.7 11.4 %collective-permute-start.3 = (f32[64,1536]{1,0:T(8,128)S(1)}, f32[64,1536]{1,0:T(8,128)}, u32[]{:S(2)}, u32[]{:S(2)}) collective-permute-start(f32[64,1536]{1,0:T(8,128)S(1)} %bitcast_add_fusion.3), channel_id=1, source_target_pairs={{0,2},{1,3},{2,0},{3,1},{4,6},{5,7},{6,4},{7,5},{8,10},{9,11},{10,... | collective-permute-start | bytes 1179656 | tf_op jit(solution)/shard_map/ppermute | solution.py:285
  54.1 1.2 copy-start.4
  55.1 2.7 %copy-start.18 = (f32[64,1536]{1,0:T(8,128)S(1)}, f32[64,1536]{1,0:T(8,128)}, u32[]{:S(2)}) copy-start(f32[64,1536]{1,0:T(8,128)} %copy-done.17) | copy-start | bytes 1179652
  56.2 13.2 %collective-permute-start.7 = (f32[64,2048]{1,0:T(8,128)}, f32[64,2048]{1,0:T(8,128)}, u32[]{:S(2)}, u32[]{:S(2)}) collective-permute-start(f32[64,2048]{1,0:T(8,128)} %dynamic-slice_bitcast_fusion.1), channel_id=1, source_target_pairs={{0,1},{1,0},{2,3},{3,2},{4,5},{5,4},{6,7},{7,6},{8,9},{9,8},{10,11... | collective-permute-start | bytes 1572872 | tf_op jit(solution)/shard_map/ppermute | solution.py:285
  56.2 14.3 %collective-permute-start.6 = (f32[64,2048]{1,0:T(8,128)S(1)}, f32[64,2048]{1,0:T(8,128)S(1)}, u32[]{:S(2)}, u32[]{:S(2)}) collective-permute-start(f32[64,2048]{1,0:T(8,128)S(1)} %bitcast_add_fusion.2), channel_id=1, source_target_pairs={{0,2},{1,3},{2,0},{3,1},{4,6},{5,7},{6,4},{7,5},{8,10},{9,11},{10,... | collective-permute-start | bytes 1572872 | tf_op jit(solution)/shard_map/ppermute | solution.py:285
  58.9 10.5 %copy-start.12 = (f32[64,1536]{1,0:T(8,128)}, f32[64,1536]{1,0:T(8,128)S(1)}, u32[]{:S(2)}) copy-start(f32[64,1536]{1,0:T(8,128)S(1)} %add.372.t_ref) | copy-start | bytes 1179652
  58.9 10.5 %collective-permute-start.5 = (f32[64,1536]{1,0:T(8,128)S(1)}, f32[64,1536]{1,0:T(8,128)S(1)}, u32[]{:S(2)}, u32[]{:S(2)}) collective-permute-start(f32[64,1536]{1,0:T(8,128)S(1)} %add.372.t_ref), channel_id=1, source_target_pairs={{0,1},{1,0},{2,3},{3,2},{4,5},{5,4},{6,7},{7,6},{8,9},{9,8},{10,11... | collective-permute-start | bytes 1179656 | tf_op jit(solution)/shard_map/ppermute | solution.py:285
  69.3 5.1 %copy-start.24 = (f32[64,1536]{1,0:T(8,128)}, f32[64,1536]{1,0:T(8,128)S(1)}, u32[]{:S(2)}) copy-start(f32[64,1536]{1,0:T(8,128)S(1)} %collective-permute-done.5.u_ref) | copy-start | bytes 1179652
  72.5 16.8 %collective-permute-start.10 = (f32[64,2560]{1,0:T(8,128)}, f32[64,2560]{1,0:T(8,128)}, u32[]{:S(2)}, u32[]{:S(2)}) collective-permute-start(f32[64,2560]{1,0:T(8,128)} %dynamic-slice_bitcast_fusion), channel_id=1, source_target_pairs={{0,1},{1,0},{2,3},{3,2},{4,5},{5,4},{6,7},{7,6},{8,9},{9,8},{10,11... | collective-permute-start | bytes 1966088 | tf_op jit(solution)/shard_map/ppermute | solution.py:285
  74.5 11.2 %copy-start.7 = (f32[64,2048]{1,0:T(8,128)}, f32[64,2048]{1,0:T(8,128)S(1)}, u32[]{:S(2)}) copy-start(f32[64,2048]{1,0:T(8,128)S(1)} %add.375.t_ref) | copy-start | bytes 1572868
  74.5 11.2 %collective-permute-start.8 = (f32[64,2048]{1,0:T(8,128)S(1)}, f32[64,2048]{1,0:T(8,128)S(1)}, u32[]{:S(2)}, u32[]{:S(2)}) collective-permute-start(f32[64,2048]{1,0:T(8,128)S(1)} %add.375.t_ref), channel_id=1, source_target_pairs={{0,1},{1,0},{2,3},{3,2},{4,5},{5,4},{6,7},{7,6},{8,9},{9,8},{10,11... | collective-permute-start | bytes 1572872 | tf_op jit(solution)/shard_map/ppermute | solution.py:285
  75.1 14.2 %collective-permute-start.9 = (f32[64,2048]{1,0:T(8,128)}, f32[64,2048]{1,0:T(8,128)}, u32[]{:S(2)}, u32[]{:S(2)}) collective-permute-start(f32[64,2048]{1,0:T(8,128)} %bitcast_add_fusion.1), channel_id=1, source_target_pairs={{0,2},{1,3},{2,0},{3,1},{4,6},{5,7},{6,4},{7,5},{8,10},{9,11},{10,... | collective-permute-start | bytes 1572872 | tf_op jit(solution)/shard_map/ppermute | solution.py:285
  76.7 12.6 %copy-start.2 = (f32[128,2560]{1,0:T(8,128)S(1)}, f32[128,2560]{1,0:T(8,128)}, u32[]{:S(2)}) copy-start(f32[128,2560]{1,0:T(8,128)} %shard_map.121) | copy-start | bytes 3932164
  85.7 7.8 %copy-start.13 = (f32[64,1536]{1,0:T(8,128)S(1)}, f32[64,1536]{1,0:T(8,128)}, u32[]{:S(2)}) copy-start(f32[64,1536]{1,0:T(8,128)} %copy-done.12) | copy-start | bytes 1179652
  85.7 3.6 %copy-start.19 = (f32[64,2048]{1,0:T(8,128)}, f32[64,2048]{1,0:T(8,128)S(1)}, u32[]{:S(2)}) copy-start(f32[64,2048]{1,0:T(8,128)S(1)} %collective-permute-done.8.u_ref) | copy-start | bytes 1572868
  90.5 18.7 %collective-permute-start.12 = (f32[64,2560]{1,0:T(8,128)S(1)}, f32[64,2560]{1,0:T(8,128)}, u32[]{:S(2)}, u32[]{:S(2)}) collective-permute-start(f32[64,2560]{1,0:T(8,128)S(1)} %bitcast_add_fusion), channel_id=1, source_target_pairs={{0,2},{1,3},{2,0},{3,1},{4,6},{5,7},{6,4},{7,5},{8,10},{9,11},{10,... | collective-permute-start | bytes 1966088 | tf_op jit(solution)/shard_map/ppermute | solution.py:285
  93.4 12.9 %copy-start.9 = (f32[64,2048]{1,0:T(8,128)}, f32[64,2048]{1,0:T(8,128)S(1)}, u32[]{:S(2)}) copy-start(f32[64,2048]{1,0:T(8,128)S(1)} %add.377.t_ref) | copy-start | bytes 1572868
  93.4 15.8 %collective-permute-start.11 = (f32[64,2048]{1,0:T(8,128)S(1)}, f32[64,2048]{1,0:T(8,128)}, u32[]{:S(2)}, u32[]{:S(2)}) collective-permute-start(f32[64,2048]{1,0:T(8,128)S(1)} %add.377.t_ref), channel_id=1, source_target_pairs={{0,1},{1,0},{2,3},{3,2},{4,5},{5,4},{6,7},{7,6},{8,9},{9,8},{10,11... | collective-permute-start | bytes 1572872 | tf_op jit(solution)/shard_map/ppermute | solution.py:285
  95.2 11.1 %copy-start.3 = (f32[16,3,12,512]{3,2,1,0:T(8,128)S(1)}, f32[16,3,12,512]{3,2,1,0:T(8,128)}, u32[]{:S(2)}) copy-start(f32[16,3,12,512]{3,2,1,0:T(8,128)} %shard_map.122) | copy-start | bytes 3538948
  106.3 4.5 %copy-start.8 = (f32[64,2048]{1,0:T(8,128)S(1)}, f32[64,2048]{1,0:T(8,128)}, u32[]{:S(2)}) copy-start(f32[64,2048]{1,0:T(8,128)} %copy-done.7) | copy-start | bytes 1572868
  106.3 4.5 %copy-start.20 = (f32[64,2048]{1,0:T(8,128)S(1)}, f32[64,2048]{1,0:T(8,128)}, u32[]{:S(2)}) copy-start(f32[64,2048]{1,0:T(8,128)} %copy-done.19) | copy-start | bytes 1572868
  110.3 16.5 %copy-start.6 = (f32[64,2560]{1,0:T(8,128)}, f32[64,2560]{1,0:T(8,128)S(1)}, u32[]{:S(2)}) copy-start(f32[64,2560]{1,0:T(8,128)S(1)} %add.379.t_ref) | copy-start | bytes 1966084
  110.3 16.5 %collective-permute-start.13 = (f32[64,2560]{1,0:T(8,128)S(1)}, f32[64,2560]{1,0:T(8,128)}, u32[]{:S(2)}, u32[]{:S(2)}) collective-permute-start(f32[64,2560]{1,0:T(8,128)S(1)} %add.379.t_ref), channel_id=1, source_target_pairs={{0,1},{1,0},{2,3},{3,2},{4,5},{5,4},{6,7},{7,6},{8,9},{9,8},{10,11... | collective-permute-start | bytes 1966088 | tf_op jit(solution)/shard_map/ppermute | solution.py:285
  111.5 11.2 %copy-start.10 = (f32[64,2048]{1,0:T(8,128)S(1)}, f32[64,2048]{1,0:T(8,128)}, u32[]{:S(2)}) copy-start(f32[64,2048]{1,0:T(8,128)} %copy-done.9) | copy-start | bytes 1572868
  111.5 12.9 %copy-start = (f32[16,4,12,512]{3,2,1,0:T(8,128)S(1)}, f32[16,4,12,512]{3,2,1,0:T(8,128)}, u32[]{:S(2)}) copy-start(f32[16,4,12,512]{3,2,1,0:T(8,128)} %shard_map.123) | copy-start | bytes 4718596
  128.6 13.2 %copy-start.1 = (f32[16,4,12,512]{3,2,1,0:T(8,128)S(1)}, f32[16,4,12,512]{3,2,1,0:T(8,128)}, u32[]{:S(2)}) copy-start(f32[16,4,12,512]{3,2,1,0:T(8,128)} %shard_map.124) | copy-start | bytes 4718596
  128.6 13.2 %copy-start.28 = (f32[512]{0:T(512)S(1)}, f32[512]{0:T(512)}, u32[]{:S(2)}) copy-start(f32[512]{0:T(512)} %copy-done.27) | copy-start | bytes 6148
  128.6 13.3 %copy-start.30 = (s32[128]{0:T(128)S(1)}, s32[128]{0:T(128)}, u32[]{:S(2)}) copy-start(s32[128]{0:T(128)} %copy-done.29) | copy-start | bytes 1540
  143.6 3.9 %copy-start.21 = (f32[16,12,3,128]{3,0,1,2:T(8,128)S(1)}, f32[16,12,3,128]{3,0,1,2:T(8,128)}, u32[]{:S(2)}) copy-start(f32[16,12,3,128]{3,0,1,2:T(8,128)} %fusion.19) | copy-start | bytes 884740
  151.4 9.1 %collective-permute-start.14 = (f32[16,2,512]{2,0,1:T(8,128)S(1)}, f32[16,2,512]{2,0,1:T(8,128)S(1)}, u32[]{:S(2)}, u32[]{:S(2)}) collective-permute-start(f32[16,2,512]{2,0,1:T(8,128)S(1)} %get-tuple-element.148), channel_id=1, source_target_pairs={{0,4},{4,8},{8,12},{12,16},{16,20},{20,24},{24,28},{1,5},{5,9},{9,... | collective-permute-start | bytes 196616 | tf_op jit(solution)/shard_map/ppermute | solution.py:31
  155.7 7.6 %copy-start.14 = (f32[16,8,512]{2,1,0:T(8,128)S(1)}, f32[16,8,512]{2,1,0:T(8,128)}, u32[]{:S(2)}) copy-start(f32[16,8,512]{2,1,0:T(8,128)} %param.10) | copy-start | bytes 786436
  155.7 7.6 %copy-start.16 = (f32[16,10,512]{2,0,1:T(8,128)S(1)}, f32[16,10,512]{2,0,1:T(8,128)}, u32[]{:S(2)}) copy-start(f32[16,10,512]{2,0,1:T(8,128)} %copy-done.15) | copy-start | bytes 983044
  155.7 7.6 %copy-start.23 = (f32[16,10,512]{2,0,1:T(8,128)S(1)}, f32[16,10,512]{2,0,1:T(8,128)}, u32[]{:S(2)}) copy-start(f32[16,10,512]{2,0,1:T(8,128)} %copy-done.22) | copy-start | bytes 983044
  155.7 7.6 %copy-start.25 = (f32[16,8,512]{2,1,0:T(8,128)S(1)}, f32[16,8,512]{2,1,0:T(8,128)}, u32[]{:S(2)}) copy-start(f32[16,8,512]{2,1,0:T(8,128)} %param.11) | copy-start | bytes 786436
  155.7 7.6 %copy-start.26 = (f32[16,8,512]{2,1,0:T(8,128)S(1)}, f32[16,8,512]{2,1,0:T(8,128)}, u32[]{:S(2)}) copy-start(f32[16,8,512]{2,1,0:T(8,128)} %param.12) | copy-start | bytes 786436
  155.8 7.6 %copy-start.31 = (f32[16]{0:T(128)S(1)}, f32[16]{0:T(128)}, u32[]{:S(2)}) copy-start(f32[16]{0:T(128)} %param.13) | copy-start | bytes 196
  155.8 7.5 %collective-permute-start.15 = (f32[16,2,512]{2,0,1:T(8,128)S(1)}, f32[16,2,512]{2,0,1:T(8,128)S(1)}, u32[]{:S(2)}, u32[]{:S(2)}) collective-permute-start(f32[16,2,512]{2,0,1:T(8,128)S(1)} %get-tuple-element.149), channel_id=1, source_target_pairs={{4,0},{8,4},{12,8},{16,12},{20,16},{24,20},{28,24},{5,1},{9,5},{13... | collective-permute-start | bytes 196616 | tf_op jit(solution)/shard_map/ppermute | solution.py:31

commit v10 on v9

--- a/solution.py
+++ b/solution.py
@@ -174,7 +174,7 @@
                 o_ref[p, 0, pl.ds(r, 1), cols] = jnp.sum(accs[r], axis=0, keepdims=True)
             return carry
 
-        lax.fori_loop(0, npred, body, 0, unroll=2 if npred % 2 == 0 else 1)
+        lax.fori_loop(0, npred, body, 0, unroll=4 if npred % 4 == 0 else 1)
 
 
 def fit_chunk(wl, cov, along, off, width):

time: 169 us -> 168 us (level)
  no operation moved by 1% of the time
where the time goes in v10:
time: 168 us; the launch traced here: 167 us
  Pallas kernels  77.6 us (46%)
  local copies, waits for them, and re-layouts  21.6 us (13%)
  starting transfers between devices  21.3 us (13%)
  other arithmetic  17.6 us (10%)
  matrix products  16.7 us (10%)
  waiting for transfers between devices  10.7 us (6%)
    pallas_call x4, Pallas kernels, back_chunk(): pl.pallas_call(back_kernel, grid=(width // TN,), in_specs=[pl.BlockSpec(m...  43.6 us
    pallas_call x4, Pallas kernels, fit_chunk(): pl.pallas_call(fit_kernel, grid=(width // TN,), in_specs=[pl.BlockSpec((4...  34.1 us
    dot_general x4, matrix products, banded_data(): jnp.einsum('pbkj,nj->pkbn', part, basis, precision=lax.Precision.HIGH)  10.8 us
    ppermute x12, starting transfers between devices, local(): pending.append((c, finish, lax.ppermute(send, 'pred', pairs)))  8.76 us
    unnamed x70, local copies, waits for them, and re-layouts  6.26 us
    ppermute x12, waiting for transfers between devices, local(): pending.append((c, finish, lax.ppermute(send, 'pred', pairs)))  5.96 us
    dot_general x1, matrix products, banded_along(): jnp.einsum('pbkn,nj->pbkj', cwin, block_basis(window), precision=lax.Prec...  5.94 us
    select_n x4, other arithmetic, local(): picked = jnp.where(bit0 == side, cur, other)  5.87 us
  transfers between devices with their start and end apart: 16, of which 5 were waited for; matrix products, arithmetic and copies ran while one was open for 11% of the time, Pallas kernels for 35%

profile of v10, /device:TPU:0, one launch (start us, length us, event | category | flops | bytes accessed | tf_op | source)
XLA Modules:
  0.0 166.8 jit_solution(3312395990519807387)
XLA Ops:
  0.6 1.1 copy.711
  1.8 1.3 collective-permute-start.1
  3.1 5.5 %collective-permute-start = (f32[16,2,512]{2,0,1:T(8,128)S(1)}, f32[16,2,512]{2,0,1:T(8,128)S(1)}, u32[]{:S(2)}, u32[]{:S(2)}) collective-permute-start(f32[16,2,512]{2,0,1:T(8,128)S(1)} %get-tuple-element.170), channel_id=1, source_target_pairs={{0,4},{4,8},{8,12},{12,16},{16,20},{20,24},{24,28},{1,5},{5,9},{9,... | collective-permute-start | bytes 196616 | tf_op jit(solution)/shard_map/ppermute | solution.py:22
  8.7 1.9 %collective-permute-done = f32[16,2,512]{2,0,1:T(8,128)S(1)} collective-permute-done((f32[16,2,512]{2,0,1:T(8,128)S(1)}, f32[16,2,512]{2,0,1:T(8,128)S(1)}, u32[]{:S(2)}, u32[]{:S(2)}) %collective-permute-start) | collective-permute-done | bytes 65568 | tf_op jit(solution)/shard_map/ppermute | solution.py:22
  10.6 1.1 constant_dynamic-update-slice_fusion.3
  11.8 0.7 copy-done.22
  12.5 0.7 copy-done.15
  13.2 0.5 fusion.45
  13.6 0.1 copy.729
  15.4 2.7 %stack.75 = f32[16,16,12,128]{3,1,2,0:T(8,128)S(1)} concatenate(f32[16,1,12,128]{3,1,2,0:T(1,128)S(1)} %copy.714, f32[16,1,12,128]{3,1,2,0:T(1,128)S(1)} %copy.715, f32[16,1,12,128]{3,1,2,0:T(1,128)S(1)} %copy.716, f32[16,1,12,128]{3,1,2,0:T(1,128)S(1)} %copy.717, f32[16,1,12,128]{3,1,2,0:T(1,128)S(1)} %copy.718, f32[16,1,12,128]{3,1,2,0:T(1,128)S(1)} %copy.719, ...), dimensions={1} | concatenate | bytes 3145728 | tf_op jit(solution)/shard_map/stack | solution.py:67
  18.1 5.9 %fusion.a_ref = f32[16,16,12,512]{3,2,1,0:T(8,128)} fusion(f32[16,16,12,128]{3,1,2,0:T(8,128)S(1)} %stack.75, f32[512]{0:T(512)S(1)} %get-tuple-element.177, f32[512]{0:T(512)S(1)} %get-tuple-element.178, f32[512]{0:T(512)S(1)} %get-tuple-element.176, f32[512]{0:T(512)S(1)} %get-tuple-element.175, s32[512]{0:T(512)S(1)} %add_select_fusion, ...), kind=kOutput, calls=%fused_computation | convolution fusion | flops 1208549376 | bytes 7875072 | tf_op jit(solution)/shard_map/pbkn,nj->pbkj/dot_general | solution.py:68
  24.0 0.7 broadcast_in_dim.79.w_ref
  24.7 6.9 %shard_map.118 = f32[128,1536]{1,0:T(8,128)} custom-call(f32[4,16,256]{2,1,0:T(8,128)} %broadcast_in_dim.79.w_ref, bf16[16,128,8192]{2,1,0:T(8,128)(2,1)} %cov_ref.15, f32[16,16,12,512]{3,2,1,0:T(8,128)} %fusion.a_ref), custom_call_target="tpu_custom_call" | custom-call | flops 31457280 | bytes 8257536 | tf_op jit(solution)/shard_map/pallas_call | solution.py:183
  31.7 1.0 dynamic-slice_bitcast_fusion.3
  32.8 8.5 %shard_map.119 = f32[128,2048]{1,0:T(8,128)} custom-call(f32[4,16,256]{2,1,0:T(8,128)} %broadcast_in_dim.79.w_ref, bf16[16,128,8192]{2,1,0:T(8,128)(2,1)} %cov_ref.15, f32[16,16,12,512]{3,2,1,0:T(8,128)} %fusion.a_ref), custom_call_target="tpu_custom_call" | custom-call | flops 41943040 | bytes 11010048 | tf_op jit(solution)/shard_map/pallas_call | solution.py:183
  41.3 1.9 %dynamic-slice_bitcast_fusion.2 = f32[64,2048]{1,0:T(8,128)} fusion(f32[2,64,2048]{2,1,0:T(8,128)} %bitcast.80, s32[]{:T(128)S(6)} %select_n.187), kind=kLoop, calls=%fused_computation.31 | loop fusion | bytes 1048580 | tf_op jit(solution)/shard_map/jit(dynamic_index_in_dim)/squeeze | solution.py:104
  43.2 0.5 collective-permute-start.4
  43.7 2.0 %collective-permute-start.3 = (f32[64,1536]{1,0:T(8,128)S(1)}, f32[64,1536]{1,0:T(8,128)}, u32[]{:S(2)}, u32[]{:S(2)}) collective-permute-start(f32[64,1536]{1,0:T(8,128)S(1)} %bitcast_add_fusion.3), channel_id=1, source_target_pairs={{0,2},{1,3},{2,0},{3,1},{4,6},{5,7},{6,4},{7,5},{8,10},{9,11},{10,... | collective-permute-start | bytes 1179656 | tf_op jit(solution)/shard_map/ppermute | solution.py:285
  45.7 8.4 %shard_map.120 = f32[128,2048]{1,0:T(8,128)} custom-call(f32[4,16,256]{2,1,0:T(8,128)} %broadcast_in_dim.79.w_ref, bf16[16,128,8192]{2,1,0:T(8,128)(2,1)} %cov_ref.15, f32[16,16,12,512]{3,2,1,0:T(8,128)} %fusion.a_ref), custom_call_target="tpu_custom_call" | custom-call | flops 41943040 | bytes 11010048 | tf_op jit(solution)/shard_map/pallas_call | solution.py:183
  54.1 1.0 collective-permute-done.3
  55.2 0.2 copy-done.4
  55.4 0.8 dynamic-slice_bitcast_fusion.1
  56.2 1.6 collective-permute-start.6
  57.8 1.1 add.372.t_ref
  58.9 0.3 collective-permute-start.5
  59.2 10.2 %shard_map.121 = f32[128,2560]{1,0:T(8,128)} custom-call(f32[4,16,256]{2,1,0:T(8,128)} %broadcast_in_dim.79.w_ref, bf16[16,128,8192]{2,1,0:T(8,128)(2,1)} %cov_ref.15, f32[16,16,12,512]{3,2,1,0:T(8,128)} %fusion.a_ref), custom_call_target="tpu_custom_call" | custom-call | flops 52428800 | bytes 13762560 | tf_op jit(solution)/shard_map/pallas_call | solution.py:183
  69.4 1.2 collective-permute-done.6
  70.5 2.0 %dynamic-slice_bitcast_fusion = f32[64,2560]{1,0:T(8,128)} fusion(f32[2,64,2560]{2,1,0:T(8,128)} %bitcast.76, s32[]{:T(128)S(6)} %select_n.187), kind=kLoop, calls=%fused_computation.19 | loop fusion | bytes 1310724 | tf_op jit(solution)/shard_map/jit(dynamic_index_in_dim)/squeeze | solution.py:104
  72.5 1.9 %bitcast_add_fusion.1 = f32[64,2048]{1,0:T(8,128)} fusion(f32[64,2048]{1,0:T(8,128)} %collective-permute-done.7, f32[2,64,2048]{2,1,0:T(8,128)S(1)} %bitcast.79, s32[]{:T(128)S(6)} %select_n.186), kind=kLoop, calls=%fused_computation.28 | loop fusion | flops 131072 | bytes 1572868 | tf_op jit(solution)/shard_map/add | solution.py:105
  74.5 0.6 collective-permute-start.8
  75.1 1.6 collective-permute-start.9
  76.7 8.8 %shard_map.122 = f32[16,3,12,512]{3,2,1,0:T(8,128)} custom-call(s32[1]{0:T(128)} %bitcast.29.b_ref, f32[4,16,256]{2,1,0:T(8,128)} %broadcast_in_dim.79.w_ref, bf16[16,128,8192]{2,1,0:T(8,128)(2,1)} %cov_ref.15, f32[64,1536]{1,0:T(8,128)} %copy-done.12, f32[64,1536]{1,0:T(8,128)} %copy-done.24, f32[128,8192]{1,0:T(8,128)} %y_ref.7, s32[128,8192]{1,0:T(8,128)} %g_ref.7), custom_call_target="tpu_custom_call" | custom-call | flops 31457280 | bytes 9830400 | tf_op jit(solution)/shard_map/pallas_call | solution.py:206
  85.5 3.8 %collective-permute-done.9 = f32[64,2048]{1,0:T(8,128)} collective-permute-done((f32[64,2048]{1,0:T(8,128)}, f32[64,2048]{1,0:T(8,128)}, u32[]{:S(2)}, u32[]{:S(2)}) %collective-permute-start.9) | collective-permute-done | bytes 524320 | tf_op jit(solution)/shard_map/ppermute | solution.py:285
  89.3 1.2 bitcast_add_fusion
  90.5 1.7 %collective-permute-start.12 = (f32[64,2560]{1,0:T(8,128)S(1)}, f32[64,2560]{1,0:T(8,128)}, u32[]{:S(2)}, u32[]{:S(2)}) collective-permute-start(f32[64,2560]{1,0:T(8,128)S(1)} %bitcast_add_fusion), channel_id=1, source_target_pairs={{0,2},{1,3},{2,0},{3,1},{4,6},{5,7},{6,4},{7,5},{8,10},{9,11},{10,... | collective-permute-start | bytes 1966088 | tf_op jit(solution)/shard_map/ppermute | solution.py:285
  92.1 1.3 add.377.t_ref
  93.5 1.7 %dynamic-slice_select_fusion.3 = f32[32,1536]{1,0:T(8,128)} fusion(f32[64,1536]{1,0:T(8,128)} %copy-done.24, s32[]{:T(128)S(6)} %select_n.189, f32[64,1536]{1,0:T(8,128)S(1)} %copy-done.13, pred[]{:T(512)S(6)} %eq.63), kind=kLoop, calls=%fused_computation.71 | loop fusion | flops 49152 | bytes 589829 | tf_op jit(solution)/shard_map/jit(_where)/select_n | solution.py:311
  95.2 10.9 %shard_map.123 = f32[16,4,12,512]{3,2,1,0:T(8,128)} custom-call(s32[1]{0:T(128)} %bitcast.29.b_ref, f32[4,16,256]{2,1,0:T(8,128)} %broadcast_in_dim.79.w_ref, bf16[16,128,8192]{2,1,0:T(8,128)(2,1)} %cov_ref.15, f32[64,2048]{1,0:T(8,128)} %copy-done.7, f32[64,2048]{1,0:T(8,128)} %copy-done.19, f32[128,8192]{1,0:T(8,128)} %y_ref.7, s32[128,8192]{1,0:T(8,128)} %g_ref.7), custom_call_target="tpu_custom_call" | custom-call | flops 41943040 | bytes 13107200 | tf_op jit(solution)/shard_map/pallas_call | solution.py:206
  106.1 2.8 %fusion.19 = f32[16,12,3,128]{3,0,1,2:T(8,128)} fusion(f32[16,3,12,512]{3,2,1,0:T(8,128)S(1)} %copy-done.3, f32[512]{0:T(512)S(1)} %get-tuple-element.177, f32[512]{0:T(512)S(1)} %get-tuple-element.178, f32[512]{0:T(512)} %copy-done.27, f32[512]{0:T(512)S(1)} %get-tuple-element.175, s32[512]{0:T(512)S(1)} %add_select_fusion, s32[128]{0:T(128)} %copy-done.29), kind=kOutput, calls=%fused_computation.15 | convolution fusion | flops 227082240 | bytes 1485312 | tf_op jit(solution)/shard_map/pbkj,nj->pkbn/dot_general | solution.py:77
  108.9 1.2 add.379.t_ref
  110.1 0.5 collective-permute-start.13
  110.6 0.7 dynamic-slice_select_fusion.2
  111.3 11.0 %shard_map.124 = f32[16,4,12,512]{3,2,1,0:T(8,128)} custom-call(s32[1]{0:T(128)} %bitcast.29.b_ref, f32[4,16,256]{2,1,0:T(8,128)} %broadcast_in_dim.79.w_ref, bf16[16,128,8192]{2,1,0:T(8,128)(2,1)} %cov_ref.15, f32[64,2048]{1,0:T(8,128)} %copy-done.9, f32[64,2048]{1,0:T(8,128)} %collective-permute-done.11.u_ref, f32[128,8192]{1,0:T(8,128)} %y_ref.7, ...), custom_call_target="tpu_custom_call" | custom-call | flops 41943040 | bytes 13107200 | tf_op jit(solution)/shard_map/pallas_call | solution.py:206
  122.3 1.7 %dynamic-slice_select_fusion.1 = f32[32,2048]{1,0:T(8,128)} fusion(f32[64,2048]{1,0:T(8,128)} %collective-permute-done.11.u_ref, s32[]{:T(128)S(6)} %select_n.189, f32[64,2048]{1,0:T(8,128)S(1)} %copy-done.10, pred[]{:T(512)S(6)} %eq.63), kind=kLoop, calls=%fused_computation.59 | loop fusion | flops 65536 | bytes 786437 | tf_op jit(solution)/shard_map/jit(_where)/select_n | solution.py:311
  124.0 2.4 %fusion.11 = f32[16,12,4,128]{3,0,1,2:T(8,128)S(1)} fusion(f32[16,4,12,512]{3,2,1,0:T(8,128)S(1)} %copy-done, f32[512]{0:T(512)S(1)} %get-tuple-element.177, f32[512]{0:T(512)S(1)} %get-tuple-element.178, f32[512]{0:T(512)} %copy-done.27, f32[512]{0:T(512)S(1)} %get-tuple-element.175, s32[512]{0:T(512)S(1)} %add_select_fusion, s32[128]{0:T(128)} %copy-done.29), kind=kOutput, calls=%fused_computation.11 | convolution fusion | flops 302579712 | bytes 1976832 | tf_op jit(solution)/shard_map/pbkj,nj->pkbn/dot_general | solution.py:77
  126.3 1.8 %dynamic-slice_select_fusion = f32[32,2560]{1,0:T(8,128)} fusion(f32[64,2560]{1,0:T(8,128)} %collective-permute-done.13.u_ref, s32[]{:T(128)S(6)} %select_n.189, f32[64,2560]{1,0:T(8,128)S(1)} %add.379.t_ref, pred[]{:T(512)S(6)} %eq.63), kind=kLoop, calls=%fused_computation.40 | loop fusion | flops 81920 | bytes 983045 | tf_op jit(solution)/shard_map/jit(_where)/select_n | solution.py:311
  128.1 12.9 %shard_map.125 = f32[16,5,12,512]{3,2,1,0:T(8,128)} custom-call(s32[1]{0:T(128)} %bitcast.29.b_ref, f32[4,16,256]{2,1,0:T(8,128)} %broadcast_in_dim.79.w_ref, bf16[16,128,8192]{2,1,0:T(8,128)(2,1)} %cov_ref.15, f32[64,2560]{1,0:T(8,128)} %copy-done.6, f32[64,2560]{1,0:T(8,128)} %collective-permute-done.13.u_ref, f32[128,8192]{1,0:T(8,128)} %y_ref.7, ...), custom_call_target="tpu_custom_call" | custom-call | flops 52428800 | bytes 16384000 | tf_op jit(solution)/shard_map/pallas_call | solution.py:206
  141.1 1.7 %fusion.14 = f32[16,12,4,128]{3,0,1,2:T(8,128)S(1)} fusion(f32[16,4,12,512]{3,2,1,0:T(8,128)S(1)} %copy-done.1, f32[512]{0:T(512)S(1)} %get-tuple-element.177, f32[512]{0:T(512)S(1)} %get-tuple-element.178, f32[512]{0:T(512)S(1)} %copy-done.28, f32[512]{0:T(512)S(1)} %get-tuple-element.175, s32[512]{0:T(512)S(1)} %add_select_fusion, s32[128]{0:T(128)S(1)} %copy-done.30), kind=kOutput, calls=%fused_computation.12 | convolution fusion | flops 302579712 | bytes 1976832 | tf_op jit(solution)/shard_map/pbkj,nj->pkbn/dot_general | solution.py:77
  142.8 3.9 %fusion.8 = f32[16,12,5,128]{3,0,1,2:T(8,128)S(1)} fusion(f32[16,5,12,512]{3,2,1,0:T(8,128)} %shard_map.125, f32[512]{0:T(512)S(1)} %get-tuple-element.177, f32[512]{0:T(512)S(1)} %get-tuple-element.178, f32[512]{0:T(512)S(1)} %copy-done.28, f32[512]{0:T(512)S(1)} %get-tuple-element.175, s32[512]{0:T(512)S(1)} %add_select_fusion, s32[128]{0:T(128)S(1)} %copy-done.30), kind=kOutput, calls=%fused_computation.10 | convolution fusion | flops 378077184 | bytes 2468352 | tf_op jit(solution)/shard_map/pbkj,nj->pkbn/dot_general | solution.py:77
  146.7 0.2 pad_maximum_fusion
  146.8 1.4 fusion.96
  148.2 0.6 pad_add_fusion
  148.8 1.1 copy.738
  149.9 0.5 reshape.227
  150.4 0.2 slice_multiply_fusion
  150.6 4.3 %collective-permute-start.14 = (f32[16,2,512]{2,0,1:T(8,128)S(1)}, f32[16,2,512]{2,0,1:T(8,128)S(1)}, u32[]{:S(2)}, u32[]{:S(2)}) collective-permute-start(f32[16,2,512]{2,0,1:T(8,128)S(1)} %get-tuple-element.148), channel_id=1, source_target_pairs={{0,4},{4,8},{8,12},{12,16},{16,20},{20,24},{24,28},{1,5},{5,9},{9,... | collective-permute-start | bytes 196616 | tf_op jit(solution)/shard_map/ppermute | solution.py:31
  155.0 1.4 collective-permute-start.15
  156.4 3.3 %subtract_multiply_fusion = (f32[32,8192]{1,0:T(8,128)}, f32[32,8192]{1,0:T(8,128)}) fusion(f32[128,8192]{1,0:T(8,128)} %y_ref.7, s32[]{:T(128)S(6)} %select_n.195, s32[128,8192]{1,0:T(8,128)} %g_ref.7, f32[32,2560]{1,0:T(8,128)} %dynamic-slice_select_fusion, f32[32,2048]{1,0:T(8,128)} %dynamic-slice_select_fusion.1, ...), kind=kLoop, calls=%fused_computation.17 | loop fusion | flops 1572864 | bytes 5242884 | tf_op jit(solution)/shard_map/mul | solution.py:314
  159.7 2.8 %collective-permute-done.15 = f32[16,2,512]{2,0,1:T(8,128)S(1)} collective-permute-done((f32[16,2,512]{2,0,1:T(8,128)S(1)}, f32[16,2,512]{2,0,1:T(8,128)S(1)}, u32[]{:S(2)}, u32[]{:S(2)}) %collective-permute-start.15) | collective-permute-done | bytes 65568 | tf_op jit(solution)/shard_map/ppermute | solution.py:31
  162.6 0.8 divide_subtract_fusion
  163.4 0.9 copy.747
  164.2 0.9 copy.748
  165.1 0.9 copy.749
  165.9 0.9 copy.746
  (105 shorter events, 2.1 us)
Async XLA Ops:
  1.8 10.0 %collective-permute-start.1 = (f32[16,2,512]{2,0,1:T(8,128)S(1)}, f32[16,2,512]{2,0,1:T(8,128)S(1)}, u32[]{:S(2)}, u32[]{:S(2)}) collective-permute-start(f32[16,2,512]{2,0,1:T(8,128)S(1)} %get-tuple-element.169), channel_id=1, source_target_pairs={{4,0},{8,4},{12,8},{16,12},{20,16},{24,20},{28,24},{5,1},{9,5},{13... | collective-permute-start | bytes 196616 | tf_op jit(solution)/shard_map/ppermute | solution.py:23
  3.1 7.5 %collective-permute-start = (f32[16,2,512]{2,0,1:T(8,128)S(1)}, f32[16,2,512]{2,0,1:T(8,128)S(1)}, u32[]{:S(2)}, u32[]{:S(2)}) collective-permute-start(f32[16,2,512]{2,0,1:T(8,128)S(1)} %get-tuple-element.170), channel_id=1, source_target_pairs={{0,4},{4,8},{8,12},{12,16},{16,20},{20,24},{24,28},{1,5},{5,9},{9,... | collective-permute-start | bytes 196616 | tf_op jit(solution)/shard_map/ppermute | solution.py:22
  8.6 9.5 %copy-start.27 = (f32[512]{0:T(512)}, f32[512]{0:T(512)S(1)}, u32[]{:S(2)}) copy-start(f32[512]{0:T(512)S(1)} %get-tuple-element.176) | copy-start | bytes 6148
  8.7 9.4 %copy-start.29 = (s32[128]{0:T(128)}, s32[128]{0:T(128)S(1)}, u32[]{:S(2)}) copy-start(s32[128]{0:T(128)S(1)} %iota_add_fusion) | copy-start | bytes 1540
  11.7 0.7 copy-start.22
  12.4 0.7 copy-start.15
  32.7 8.6 %collective-permute-start.2 = (f32[64,1536]{1,0:T(8,128)S(1)}, f32[64,1536]{1,0:T(8,128)S(1)}, u32[]{:S(2)}, u32[]{:S(2)}) collective-permute-start(f32[64,1536]{1,0:T(8,128)S(1)} %dynamic-slice_bitcast_fusion.3), channel_id=1, source_target_pairs={{0,1},{1,0},{2,3},{3,2},{4,5},{5,4},{6,7},{7,6},{8,9},{9,8},{10,11... | collective-permute-start | bytes 1179656 | tf_op jit(solution)/shard_map/ppermute | solution.py:285
  32.8 10.9 %copy-start.11 = (f32[128,1536]{1,0:T(8,128)S(1)}, f32[128,1536]{1,0:T(8,128)}, u32[]{:S(2)}) copy-start(f32[128,1536]{1,0:T(8,128)} %shard_map.118) | copy-start | bytes 2359300
  43.2 11.9 %collective-permute-start.4 = (f32[64,2048]{1,0:T(8,128)}, f32[64,2048]{1,0:T(8,128)S(1)}, u32[]{:S(2)}, u32[]{:S(2)}) collective-permute-start(f32[64,2048]{1,0:T(8,128)} %dynamic-slice_bitcast_fusion.2), channel_id=1, source_target_pairs={{0,1},{1,0},{2,3},{3,2},{4,5},{5,4},{6,7},{7,6},{8,9},{9,8},{10,11... | collective-permute-start | bytes 1572872 | tf_op jit(solution)/shard_map/ppermute | solution.py:285
  43.7 10.4 %copy-start.17 = (f32[64,1536]{1,0:T(8,128)}, f32[64,1536]{1,0:T(8,128)S(1)}, u32[]{:S(2)}) copy-start(f32[64,1536]{1,0:T(8,128)S(1)} %bitcast_add_fusion.3) | copy-start | bytes 1179652
  43.7 11.4 %copy-start.5 = (f32[128,2048]{1,0:T(8,128)S(1)}, f32[128,2048]{1,0:T(8,128)}, u32[]{:S(2)}) copy-start(f32[128,2048]{1,0:T(8,128)} %shard_map.119) | copy-start | bytes 3145732
  43.7 11.4 %collective-permute-start.3 = (f32[64,1536]{1,0:T(8,128)S(1)}, f32[64,1536]{1,0:T(8,128)}, u32[]{:S(2)}, u32[]{:S(2)}) collective-permute-start(f32[64,1536]{1,0:T(8,128)S(1)} %bitcast_add_fusion.3), channel_id=1, source_target_pairs={{0,2},{1,3},{2,0},{3,1},{4,6},{5,7},{6,4},{7,5},{8,10},{9,11},{10,... | collective-permute-start | bytes 1179656 | tf_op jit(solution)/shard_map/ppermute | solution.py:285
  54.1 1.2 copy-start.4
  55.1 2.7 %copy-start.18 = (f32[64,1536]{1,0:T(8,128)S(1)}, f32[64,1536]{1,0:T(8,128)}, u32[]{:S(2)}) copy-start(f32[64,1536]{1,0:T(8,128)} %copy-done.17) | copy-start | bytes 1179652
  56.2 13.2 %collective-permute-start.7 = (f32[64,2048]{1,0:T(8,128)}, f32[64,2048]{1,0:T(8,128)}, u32[]{:S(2)}, u32[]{:S(2)}) collective-permute-start(f32[64,2048]{1,0:T(8,128)} %dynamic-slice_bitcast_fusion.1), channel_id=1, source_target_pairs={{0,1},{1,0},{2,3},{3,2},{4,5},{5,4},{6,7},{7,6},{8,9},{9,8},{10,11... | collective-permute-start | bytes 1572872 | tf_op jit(solution)/shard_map/ppermute | solution.py:285
  56.2 14.3 %collective-permute-start.6 = (f32[64,2048]{1,0:T(8,128)S(1)}, f32[64,2048]{1,0:T(8,128)S(1)}, u32[]{:S(2)}, u32[]{:S(2)}) collective-permute-start(f32[64,2048]{1,0:T(8,128)S(1)} %bitcast_add_fusion.2), channel_id=1, source_target_pairs={{0,2},{1,3},{2,0},{3,1},{4,6},{5,7},{6,4},{7,5},{8,10},{9,11},{10,... | collective-permute-start | bytes 1572872 | tf_op jit(solution)/shard_map/ppermute | solution.py:285
  58.9 10.5 %copy-start.12 = (f32[64,1536]{1,0:T(8,128)}, f32[64,1536]{1,0:T(8,128)S(1)}, u32[]{:S(2)}) copy-start(f32[64,1536]{1,0:T(8,128)S(1)} %add.372.t_ref) | copy-start | bytes 1179652
  58.9 10.5 %collective-permute-start.5 = (f32[64,1536]{1,0:T(8,128)S(1)}, f32[64,1536]{1,0:T(8,128)S(1)}, u32[]{:S(2)}, u32[]{:S(2)}) collective-permute-start(f32[64,1536]{1,0:T(8,128)S(1)} %add.372.t_ref), channel_id=1, source_target_pairs={{0,1},{1,0},{2,3},{3,2},{4,5},{5,4},{6,7},{7,6},{8,9},{9,8},{10,11... | collective-permute-start | bytes 1179656 | tf_op jit(solution)/shard_map/ppermute | solution.py:285
  69.3 5.1 %copy-start.24 = (f32[64,1536]{1,0:T(8,128)}, f32[64,1536]{1,0:T(8,128)S(1)}, u32[]{:S(2)}) copy-start(f32[64,1536]{1,0:T(8,128)S(1)} %collective-permute-done.5.u_ref) | copy-start | bytes 1179652
  72.5 16.8 %collective-permute-start.10 = (f32[64,2560]{1,0:T(8,128)}, f32[64,2560]{1,0:T(8,128)}, u32[]{:S(2)}, u32[]{:S(2)}) collective-permute-start(f32[64,2560]{1,0:T(8,128)} %dynamic-slice_bitcast_fusion), channel_id=1, source_target_pairs={{0,1},{1,0},{2,3},{3,2},{4,5},{5,4},{6,7},{7,6},{8,9},{9,8},{10,11... | collective-permute-start | bytes 1966088 | tf_op jit(solution)/shard_map/ppermute | solution.py:285
  74.5 11.0 %copy-start.7 = (f32[64,2048]{1,0:T(8,128)}, f32[64,2048]{1,0:T(8,128)S(1)}, u32[]{:S(2)}) copy-start(f32[64,2048]{1,0:T(8,128)S(1)} %add.375.t_ref) | copy-start | bytes 1572868
  74.5 11.0 %collective-permute-start.8 = (f32[64,2048]{1,0:T(8,128)S(1)}, f32[64,2048]{1,0:T(8,128)S(1)}, u32[]{:S(2)}, u32[]{:S(2)}) collective-permute-start(f32[64,2048]{1,0:T(8,128)S(1)} %add.375.t_ref), channel_id=1, source_target_pairs={{0,1},{1,0},{2,3},{3,2},{4,5},{5,4},{6,7},{7,6},{8,9},{9,8},{10,11... | collective-permute-start | bytes 1572872 | tf_op jit(solution)/shard_map/ppermute | solution.py:285
  75.1 14.2 %collective-permute-start.9 = (f32[64,2048]{1,0:T(8,128)}, f32[64,2048]{1,0:T(8,128)}, u32[]{:S(2)}, u32[]{:S(2)}) collective-permute-start(f32[64,2048]{1,0:T(8,128)} %bitcast_add_fusion.1), channel_id=1, source_target_pairs={{0,2},{1,3},{2,0},{3,1},{4,6},{5,7},{6,4},{7,5},{8,10},{9,11},{10,... | collective-permute-start | bytes 1572872 | tf_op jit(solution)/shard_map/ppermute | solution.py:285
  76.7 12.6 %copy-start.2 = (f32[128,2560]{1,0:T(8,128)S(1)}, f32[128,2560]{1,0:T(8,128)}, u32[]{:S(2)}) copy-start(f32[128,2560]{1,0:T(8,128)} %shard_map.121) | copy-start | bytes 3932164
  85.5 8.0 %copy-start.13 = (f32[64,1536]{1,0:T(8,128)S(1)}, f32[64,1536]{1,0:T(8,128)}, u32[]{:S(2)}) copy-start(f32[64,1536]{1,0:T(8,128)} %copy-done.12) | copy-start | bytes 1179652
  85.5 3.8 %copy-start.19 = (f32[64,2048]{1,0:T(8,128)}, f32[64,2048]{1,0:T(8,128)S(1)}, u32[]{:S(2)}) copy-start(f32[64,2048]{1,0:T(8,128)S(1)} %collective-permute-done.8.u_ref) | copy-start | bytes 1572868
  90.5 18.5 %collective-permute-start.12 = (f32[64,2560]{1,0:T(8,128)S(1)}, f32[64,2560]{1,0:T(8,128)}, u32[]{:S(2)}, u32[]{:S(2)}) collective-permute-start(f32[64,2560]{1,0:T(8,128)S(1)} %bitcast_add_fusion), channel_id=1, source_target_pairs={{0,2},{1,3},{2,0},{3,1},{4,6},{5,7},{6,4},{7,5},{8,10},{9,11},{10,... | collective-permute-start | bytes 1966088 | tf_op jit(solution)/shard_map/ppermute | solution.py:285
  93.4 12.7 %copy-start.9 = (f32[64,2048]{1,0:T(8,128)}, f32[64,2048]{1,0:T(8,128)S(1)}, u32[]{:S(2)}) copy-start(f32[64,2048]{1,0:T(8,128)S(1)} %add.377.t_ref) | copy-start | bytes 1572868
  93.4 15.5 %collective-permute-start.11 = (f32[64,2048]{1,0:T(8,128)S(1)}, f32[64,2048]{1,0:T(8,128)}, u32[]{:S(2)}, u32[]{:S(2)}) collective-permute-start(f32[64,2048]{1,0:T(8,128)S(1)} %add.377.t_ref), channel_id=1, source_target_pairs={{0,1},{1,0},{2,3},{3,2},{4,5},{5,4},{6,7},{7,6},{8,9},{9,8},{10,11... | collective-permute-start | bytes 1572872 | tf_op jit(solution)/shard_map/ppermute | solution.py:285
  95.2 10.9 %copy-start.3 = (f32[16,3,12,512]{3,2,1,0:T(8,128)S(1)}, f32[16,3,12,512]{3,2,1,0:T(8,128)}, u32[]{:S(2)}) copy-start(f32[16,3,12,512]{3,2,1,0:T(8,128)} %shard_map.122) | copy-start | bytes 3538948
  106.1 4.5 %copy-start.8 = (f32[64,2048]{1,0:T(8,128)S(1)}, f32[64,2048]{1,0:T(8,128)}, u32[]{:S(2)}) copy-start(f32[64,2048]{1,0:T(8,128)} %copy-done.7) | copy-start | bytes 1572868
  106.1 4.5 %copy-start.20 = (f32[64,2048]{1,0:T(8,128)S(1)}, f32[64,2048]{1,0:T(8,128)}, u32[]{:S(2)}) copy-start(f32[64,2048]{1,0:T(8,128)} %copy-done.19) | copy-start | bytes 1572868
  110.1 16.2 %copy-start.6 = (f32[64,2560]{1,0:T(8,128)}, f32[64,2560]{1,0:T(8,128)S(1)}, u32[]{:S(2)}) copy-start(f32[64,2560]{1,0:T(8,128)S(1)} %add.379.t_ref) | copy-start | bytes 1966084
  110.1 16.2 %collective-permute-start.13 = (f32[64,2560]{1,0:T(8,128)S(1)}, f32[64,2560]{1,0:T(8,128)}, u32[]{:S(2)}, u32[]{:S(2)}) collective-permute-start(f32[64,2560]{1,0:T(8,128)S(1)} %add.379.t_ref), channel_id=1, source_target_pairs={{0,1},{1,0},{2,3},{3,2},{4,5},{5,4},{6,7},{7,6},{8,9},{9,8},{10,11... | collective-permute-start | bytes 1966088 | tf_op jit(solution)/shard_map/ppermute | solution.py:285
  111.3 11.0 %copy-start.10 = (f32[64,2048]{1,0:T(8,128)S(1)}, f32[64,2048]{1,0:T(8,128)}, u32[]{:S(2)}) copy-start(f32[64,2048]{1,0:T(8,128)} %copy-done.9) | copy-start | bytes 1572868
  111.3 12.7 %copy-start = (f32[16,4,12,512]{3,2,1,0:T(8,128)S(1)}, f32[16,4,12,512]{3,2,1,0:T(8,128)}, u32[]{:S(2)}) copy-start(f32[16,4,12,512]{3,2,1,0:T(8,128)} %shard_map.123) | copy-start | bytes 4718596
  128.1 12.9 %copy-start.1 = (f32[16,4,12,512]{3,2,1,0:T(8,128)S(1)}, f32[16,4,12,512]{3,2,1,0:T(8,128)}, u32[]{:S(2)}) copy-start(f32[16,4,12,512]{3,2,1,0:T(8,128)} %shard_map.124) | copy-start | bytes 4718596
  128.1 12.9 %copy-start.28 = (f32[512]{0:T(512)S(1)}, f32[512]{0:T(512)}, u32[]{:S(2)}) copy-start(f32[512]{0:T(512)} %copy-done.27) | copy-start | bytes 6148
  128.1 12.9 %copy-start.30 = (s32[128]{0:T(128)S(1)}, s32[128]{0:T(128)}, u32[]{:S(2)}) copy-start(s32[128]{0:T(128)} %copy-done.29) | copy-start | bytes 1540
  142.8 3.9 %copy-start.21 = (f32[16,12,3,128]{3,0,1,2:T(8,128)S(1)}, f32[16,12,3,128]{3,0,1,2:T(8,128)}, u32[]{:S(2)}) copy-start(f32[16,12,3,128]{3,0,1,2:T(8,128)} %fusion.19) | copy-start | bytes 884740
  150.6 9.1 %collective-permute-start.14 = (f32[16,2,512]{2,0,1:T(8,128)S(1)}, f32[16,2,512]{2,0,1:T(8,128)S(1)}, u32[]{:S(2)}, u32[]{:S(2)}) collective-permute-start(f32[16,2,512]{2,0,1:T(8,128)S(1)} %get-tuple-element.148), channel_id=1, source_target_pairs={{0,4},{4,8},{8,12},{12,16},{16,20},{20,24},{24,28},{1,5},{5,9},{9,... | collective-permute-start | bytes 196616 | tf_op jit(solution)/shard_map/ppermute | solution.py:31
  154.9 7.6 %copy-start.14 = (f32[16,8,512]{2,1,0:T(8,128)S(1)}, f32[16,8,512]{2,1,0:T(8,128)}, u32[]{:S(2)}) copy-start(f32[16,8,512]{2,1,0:T(8,128)} %param.10) | copy-start | bytes 786436
  154.9 7.6 %copy-start.16 = (f32[16,10,512]{2,0,1:T(8,128)S(1)}, f32[16,10,512]{2,0,1:T(8,128)}, u32[]{:S(2)}) copy-start(f32[16,10,512]{2,0,1:T(8,128)} %copy-done.15) | copy-start | bytes 983044
  154.9 7.6 %copy-start.23 = (f32[16,10,512]{2,0,1:T(8,128)S(1)}, f32[16,10,512]{2,0,1:T(8,128)}, u32[]{:S(2)}) copy-start(f32[16,10,512]{2,0,1:T(8,128)} %copy-done.22) | copy-start | bytes 983044
  154.9 7.6 %copy-start.25 = (f32[16,8,512]{2,1,0:T(8,128)S(1)}, f32[16,8,512]{2,1,0:T(8,128)}, u32[]{:S(2)}) copy-start(f32[16,8,512]{2,1,0:T(8,128)} %param.11) | copy-start | bytes 786436
  154.9 7.6 %copy-start.26 = (f32[16,8,512]{2,1,0:T(8,128)S(1)}, f32[16,8,512]{2,1,0:T(8,128)}, u32[]{:S(2)}) copy-start(f32[16,8,512]{2,1,0:T(8,128)} %param.12) | copy-start | bytes 786436
  155.0 7.6 %copy-start.31 = (f32[16]{0:T(128)S(1)}, f32[16]{0:T(128)}, u32[]{:S(2)}) copy-start(f32[16]{0:T(128)} %param.13) | copy-start | bytes 196
  155.0 7.5 %collective-permute-start.15 = (f32[16,2,512]{2,0,1:T(8,128)S(1)}, f32[16,2,512]{2,0,1:T(8,128)S(1)}, u32[]{:S(2)}, u32[]{:S(2)}) collective-permute-start(f32[16,2,512]{2,0,1:T(8,128)S(1)} %get-tuple-element.149), channel_id=1, source_target_pairs={{4,0},{8,4},{12,8},{16,12},{20,16},{24,20},{28,24},{5,1},{9,5},{13... | collective-permute-start | bytes 196616 | tf_op jit(solution)/shard_map/ppermute | solution.py:31

commit v11 on v10

--- a/solution.py
+++ b/solution.py
@@ -124,12 +124,17 @@
     return [(bit, fn, [(i, i ^ bit) for i in range(n)]) for bit, fn in steps]
 
 
-def fit_kernel(w_ref, cov_ref, a_ref, o_ref):
+def kernel_weights():
+    u = (lax.broadcasted_iota(jnp.int32, (H, L), 0).astype(jnp.float32) + 0.5) / H
+    return weights_of(u)
+
+
+def fit_kernel(cov_ref, a_ref, o_ref):
     npred = cov_ref.shape[0]
     nint = cov_ref.shape[1] // H
     for s in range(TN // L):
         cols = pl.ds(s * L, L)
-        w = [w_ref[d] for d in range(4)]
+        w = kernel_weights()
         for m in range(nint):
             rows = pl.ds(m * H, H)
 
@@ -143,10 +148,11 @@
             o_ref[rows, cols] = acc
 
 
-def back_kernel(b_ref, w_ref, cov_ref, t_ref, u_ref, y_ref, g_ref, o_ref, rw_ref):
+def back_kernel(b_ref, cov_ref, t_ref, u_ref, y_ref, g_ref, o_ref, rw_ref):
     npred = cov_ref.shape[0]
     nint = cov_ref.shape[1] // H
     mine = b_ref[0]
+    w = kernel_weights()
     for s in range(TN // L):
         cols = pl.ds(s * L, L)
         for m in range(nint):
@@ -156,7 +162,7 @@
             total = jnp.where(mine == side, t_ref[inner, cols], u_ref[inner, cols])
             resid = g_ref[rows, cols].astype(jnp.float32) * (y_ref[rows, cols] - total)
             for d in range(4):
-                rw_ref[d, rows, :] = w_ref[d] * resid
+                rw_ref[d, rows, :] = w[d] * resid
 
         def body(p, carry):
             o_ref[p, 0, pl.ds(0, 1), cols] = jnp.zeros((1, L), jnp.float32)
@@ -177,14 +183,13 @@
         lax.fori_loop(0, npred, body, 0, unroll=4 if npred % 4 == 0 else 1)
 
 
-def fit_chunk(wl, cov, along, off, width):
+def fit_chunk(cov, along, off, width):
     npred, rows, _ = cov.shape
     nrow = along.shape[2]
     return pl.pallas_call(
         fit_kernel,
         grid=(width // TN,),
         in_specs=[
-            pl.BlockSpec((4, H, L), lambda j: (0, 0, 0)),
             pl.BlockSpec((npred, rows, TN), lambda j: (0, 0, j + off)),
             pl.BlockSpec((npred, 1, nrow, TN), lambda j: (0, j + off, 0, 0)),
         ],
@@ -196,10 +201,10 @@
             transcendentals=0,
             bytes_accessed=2 * npred * rows * width + 4 * npred * nrow * width + 4 * rows * width,
         ),
-    )(wl, cov, along)
-
-
-def back_chunk(wl, cov, halves, target, land, off, nrow):
+    )(cov, along)
+
+
+def back_chunk(cov, halves, target, land, off, nrow):
     npred, rows, _ = cov.shape
     cur, other, mine = halves
     width = cur.shape[1]
@@ -208,7 +213,6 @@
         grid=(width // TN,),
         in_specs=[
             pl.BlockSpec(memory_space=pltpu.SMEM),
-            pl.BlockSpec((4, H, L), lambda j: (0, 0, 0)),
             pl.BlockSpec((npred, rows, TN), lambda j: (0, 0, j + off)),
             pl.BlockSpec((rows // 2, TN), lambda j: (0, j)),
             pl.BlockSpec((rows // 2, TN), lambda j: (0, j)),
@@ -224,7 +228,7 @@
             transcendentals=0,
             bytes_accessed=2 * npred * rows * width + 12 * rows * width + 4 * npred * nrow * width,
         ),
-    )(mine, wl, cov, cur, other, target, land)
+    )(mine, cov, cur, other, target, land)
 
 
 def penalty(padded, count):
@@ -247,7 +251,6 @@
     knots = coefs.shape[2]
     share = rows // lax.axis_size("pred")
     start = lax.axis_index("pred") * share
-    wl = jnp.broadcast_to(weight_table(H)[:, :, None], (4, H, L))
     padded = extended(coefs, (("tile", 1),), 2)
     along = banded_along(padded, ny)
     nrow = padded.shape[1]
@@ -273,7 +276,7 @@
     state = [None] * CHUNKS
     fitted_parts = [None] * CHUNKS
     back_parts = [None] * CHUNKS
-    state[0] = fit_chunk(wl, covariates, along, offs[0], widths[0])
+    state[0] = fit_chunk(covariates, along, offs[0], widths[0])
     next_back = 0
     for s in range(1, CHUNKS + nsteps + 1):
         pending = []
@@ -285,11 +288,11 @@
                 pending.append((c, finish, lax.ppermute(send, "pred", pairs)))
         outs = []
         if s < CHUNKS:
-            outs.append(("fit", s, fit_chunk(wl, covariates, along, offs[s], widths[s])))
+            outs.append(("fit", s, fit_chunk(covariates, along, offs[s], widths[s])))
         if next_back < CHUNKS and next_back + nsteps + 1 <= s:
             c = next_back
             state[c] = attach(state[c])
-            outs.append(("back", c, back_chunk(wl, covariates, state[c], target, land, offs[c], nrow)))
+            outs.append(("back", c, back_chunk(covariates, state[c], target, land, offs[c], nrow)))
             next_back += 1
         recvs = [r for _, _, r in pending]
         if outs:
@@ -304,7 +307,7 @@
     for c in range(CHUNKS):
         if back_parts[c] is None:
             state[c] = attach(state[c])
-            back_parts[c] = back_chunk(wl, covariates, state[c], target, land, offs[c], nrow)
+            back_parts[c] = back_chunk(covariates, state[c], target, land, offs[c], nrow)
         cur, other, _ = state[c]
         half = rows // 2
         side = start // half

time: 168 us -> 169 us (level)
  Pallas kernels: 77.6 us -> 81.3 us
  starting transfers between devices: 21.3 us -> 18.3 us
    pallas_call x4, Pallas kernels: 34.1 us -> 38 us  [fit_chunk(): pl.pallas_call(fit_kernel, grid=(width // TN,), in_specs=[pl.BlockSpec((n...]
    ppermute x12, starting transfers between devices: 8.76 us -> 5.78 us  [local(): pending.append((c, finish, lax.ppermute(send, 'pred', pairs)))]
  transfers between devices with their start and end apart: 16 -> 16, of which waited for: 5 -> 4; matrix products, arithmetic and copies ran while one was open for 11% -> 11% of each run, Pallas kernels for 35% -> 36%
where the time goes in v11:
time: 169 us; the launch traced here: 168 us
  Pallas kernels  81.3 us (48%)
  local copies, waits for them, and re-layouts  21.8 us (13%)
  starting transfers between devices  18.3 us (11%)
  other arithmetic  17.6 us (10%)
  matrix products  16.8 us (10%)
  waiting for transfers between devices  10.7 us (6%)
    pallas_call x4, Pallas kernels, back_chunk(): pl.pallas_call(back_kernel, grid=(width // TN,), in_specs=[pl.BlockSpec(m...  43.4 us
    pallas_call x4, Pallas kernels, fit_chunk(): pl.pallas_call(fit_kernel, grid=(width // TN,), in_specs=[pl.BlockSpec((n...  38 us
    dot_general x4, matrix products, banded_data(): jnp.einsum('pbkj,nj->pkbn', part, basis, precision=lax.Precision.HIGH)  10.8 us
    unnamed x70, local copies, waits for them, and re-layouts  7.23 us
    ppermute x12, waiting for transfers between devices, local(): pending.append((c, finish, lax.ppermute(send, 'pred', pairs)))  5.99 us
    dot_general x1, matrix products, banded_along(): jnp.einsum('pbkn,nj->pbkj', cwin, block_basis(window), precision=lax.Prec...  5.94 us
    select_n x4, other arithmetic, local(): picked = jnp.where(bit0 == side, cur, other)  5.86 us
    ppermute x12, starting transfers between devices, local(): pending.append((c, finish, lax.ppermute(send, 'pred', pairs)))  5.78 us
  transfers between devices with their start and end apart: 16, of which 4 were waited for; matrix products, arithmetic and copies ran while one was open for 11% of the time, Pallas kernels for 36%

profile of v11, /device:TPU:0, one launch (start us, length us, event | category | flops | bytes accessed | tf_op | source)
XLA Modules:
  0.0 167.9 jit_solution(8860357614492713307)
XLA Ops:
  0.6 1.1 copy.711
  1.8 1.3 collective-permute-start.1
  3.1 5.5 %collective-permute-start = (f32[16,2,512]{2,0,1:T(8,128)S(1)}, f32[16,2,512]{2,0,1:T(8,128)S(1)}, u32[]{:S(2)}, u32[]{:S(2)}) collective-permute-start(f32[16,2,512]{2,0,1:T(8,128)S(1)} %get-tuple-element.170), channel_id=1, source_target_pairs={{0,4},{4,8},{8,12},{12,16},{16,20},{20,24},{24,28},{1,5},{5,9},{9,... | collective-permute-start | bytes 196616 | tf_op jit(solution)/shard_map/ppermute | solution.py:22
  8.6 1.9 %collective-permute-done = f32[16,2,512]{2,0,1:T(8,128)S(1)} collective-permute-done((f32[16,2,512]{2,0,1:T(8,128)S(1)}, f32[16,2,512]{2,0,1:T(8,128)S(1)}, u32[]{:S(2)}, u32[]{:S(2)}) %collective-permute-start) | collective-permute-done | bytes 65568 | tf_op jit(solution)/shard_map/ppermute | solution.py:22
  10.6 1.1 constant_dynamic-update-slice_fusion.3
  11.8 0.7 copy-done.22
  12.5 0.7 copy-done.15
  13.2 0.5 fusion.45
  13.6 0.1 copy.729
  13.8 0.1 copy.727
  14.0 0.1 copy.726
  15.4 2.7 %stack.67 = f32[16,16,12,128]{3,1,2,0:T(8,128)S(1)} concatenate(f32[16,1,12,128]{3,1,2,0:T(1,128)S(1)} %copy.714, f32[16,1,12,128]{3,1,2,0:T(1,128)S(1)} %copy.715, f32[16,1,12,128]{3,1,2,0:T(1,128)S(1)} %copy.716, f32[16,1,12,128]{3,1,2,0:T(1,128)S(1)} %copy.717, f32[16,1,12,128]{3,1,2,0:T(1,128)S(1)} %copy.718, f32[16,1,12,128]{3,1,2,0:T(1,128)S(1)} %copy.719, ...), dimensions={1} | concatenate | bytes 3145728 | tf_op jit(solution)/shard_map/stack | solution.py:67
  18.1 5.9 %fusion.a_ref = f32[16,16,12,512]{3,2,1,0:T(8,128)} fusion(f32[16,16,12,128]{3,1,2,0:T(8,128)S(1)} %stack.67, f32[512]{0:T(512)S(1)} %get-tuple-element.177, f32[512]{0:T(512)S(1)} %get-tuple-element.178, f32[512]{0:T(512)S(1)} %get-tuple-element.176, f32[512]{0:T(512)S(1)} %get-tuple-element.175, s32[512]{0:T(512)S(1)} %add_select_fusion, ...), kind=kOutput, calls=%fused_computation | convolution fusion | flops 1208549376 | bytes 7875072 | tf_op jit(solution)/shard_map/pbkn,nj->pbkj/dot_general | solution.py:68
  24.0 7.7 %shard_map.118 = f32[128,1536]{1,0:T(8,128)} custom-call(bf16[16,128,8192]{2,1,0:T(8,128)(2,1)} %cov_ref.15, f32[16,16,12,512]{3,2,1,0:T(8,128)} %fusion.a_ref), custom_call_target="tpu_custom_call" | custom-call | flops 31457280 | bytes 8257536 | tf_op jit(solution)/shard_map/pallas_call | solution.py:189
  31.7 1.0 dynamic-slice_bitcast_fusion.3
  32.9 9.6 %shard_map.119 = f32[128,2048]{1,0:T(8,128)} custom-call(bf16[16,128,8192]{2,1,0:T(8,128)(2,1)} %cov_ref.15, f32[16,16,12,512]{3,2,1,0:T(8,128)} %fusion.a_ref), custom_call_target="tpu_custom_call" | custom-call | flops 41943040 | bytes 11010048 | tf_op jit(solution)/shard_map/pallas_call | solution.py:189
  42.4 1.9 %dynamic-slice_bitcast_fusion.2 = f32[64,2048]{1,0:T(8,128)} fusion(f32[2,64,2048]{2,1,0:T(8,128)} %bitcast.80, s32[]{:T(128)S(6)} %select_n.187), kind=kLoop, calls=%fused_computation.31 | loop fusion | bytes 1048580 | tf_op jit(solution)/shard_map/jit(dynamic_index_in_dim)/squeeze | solution.py:104
  44.3 0.5 collective-permute-start.4
  44.8 2.0 %collective-permute-start.3 = (f32[64,1536]{1,0:T(8,128)S(1)}, f32[64,1536]{1,0:T(8,128)}, u32[]{:S(2)}, u32[]{:S(2)}) collective-permute-start(f32[64,1536]{1,0:T(8,128)S(1)} %bitcast_add_fusion.3), channel_id=1, source_target_pairs={{0,2},{1,3},{2,0},{3,1},{4,6},{5,7},{6,4},{7,5},{8,10},{9,11},{10,... | collective-permute-start | bytes 1179656 | tf_op jit(solution)/shard_map/ppermute | solution.py:288
  46.8 9.5 %shard_map.120 = f32[128,2048]{1,0:T(8,128)} custom-call(bf16[16,128,8192]{2,1,0:T(8,128)(2,1)} %cov_ref.15, f32[16,16,12,512]{3,2,1,0:T(8,128)} %fusion.a_ref), custom_call_target="tpu_custom_call" | custom-call | flops 41943040 | bytes 11010048 | tf_op jit(solution)/shard_map/pallas_call | solution.py:189
  56.4 1.1 copy-done.4
  57.5 0.8 dynamic-slice_bitcast_fusion.1
  58.3 0.6 collective-permute-start.6
  58.9 1.1 add.299.t_ref
  60.0 0.3 collective-permute-start.5
  60.2 11.3 %shard_map.121 = f32[128,2560]{1,0:T(8,128)} custom-call(bf16[16,128,8192]{2,1,0:T(8,128)(2,1)} %cov_ref.15, f32[16,16,12,512]{3,2,1,0:T(8,128)} %fusion.a_ref), custom_call_target="tpu_custom_call" | custom-call | flops 52428800 | bytes 13762560 | tf_op jit(solution)/shard_map/pallas_call | solution.py:189
  71.5 1.1 collective-permute-done.6
  72.6 2.0 %dynamic-slice_bitcast_fusion = f32[64,2560]{1,0:T(8,128)} fusion(f32[2,64,2560]{2,1,0:T(8,128)} %bitcast.76, s32[]{:T(128)S(6)} %select_n.187), kind=kLoop, calls=%fused_computation.19 | loop fusion | bytes 1310724 | tf_op jit(solution)/shard_map/jit(dynamic_index_in_dim)/squeeze | solution.py:104
  74.6 1.9 %bitcast_add_fusion.1 = f32[64,2048]{1,0:T(8,128)} fusion(f32[64,2048]{1,0:T(8,128)} %collective-permute-done.7, f32[2,64,2048]{2,1,0:T(8,128)S(1)} %bitcast.79, s32[]{:T(128)S(6)} %select_n.186), kind=kLoop, calls=%fused_computation.28 | loop fusion | flops 131072 | bytes 1572868 | tf_op jit(solution)/shard_map/add | solution.py:105
  76.6 0.6 collective-permute-start.8
  77.2 0.6 collective-permute-start.9
  77.7 8.8 %shard_map.122 = f32[16,3,12,512]{3,2,1,0:T(8,128)} custom-call(s32[1]{0:T(128)} %bitcast.29.b_ref, bf16[16,128,8192]{2,1,0:T(8,128)(2,1)} %cov_ref.15, f32[64,1536]{1,0:T(8,128)} %copy-done.12, f32[64,1536]{1,0:T(8,128)} %copy-done.24, f32[128,8192]{1,0:T(8,128)} %y_ref.7, s32[128,8192]{1,0:T(8,128)} %g_ref.7), custom_call_target="tpu_custom_call" | custom-call | flops 31457280 | bytes 9830400 | tf_op jit(solution)/shard_map/pallas_call | solution.py:211
  86.5 4.8 %collective-permute-done.9 = f32[64,2048]{1,0:T(8,128)} collective-permute-done((f32[64,2048]{1,0:T(8,128)}, f32[64,2048]{1,0:T(8,128)}, u32[]{:S(2)}, u32[]{:S(2)}) %collective-permute-start.9) | collective-permute-done | bytes 524320 | tf_op jit(solution)/shard_map/ppermute | solution.py:288
  91.4 1.2 bitcast_add_fusion
  92.6 0.7 collective-permute-start.12
  93.3 1.3 add.304.t_ref
  94.7 1.7 %dynamic-slice_select_fusion.3 = f32[32,1536]{1,0:T(8,128)} fusion(f32[64,1536]{1,0:T(8,128)} %copy-done.24, s32[]{:T(128)S(6)} %select_n.189, f32[64,1536]{1,0:T(8,128)S(1)} %copy-done.13, pred[]{:T(512)S(6)} %eq.63), kind=kLoop, calls=%fused_computation.71 | loop fusion | flops 49152 | bytes 589829 | tf_op jit(solution)/shard_map/jit(_where)/select_n | solution.py:314
  96.4 10.8 %shard_map.123 = f32[16,4,12,512]{3,2,1,0:T(8,128)} custom-call(s32[1]{0:T(128)} %bitcast.29.b_ref, bf16[16,128,8192]{2,1,0:T(8,128)(2,1)} %cov_ref.15, f32[64,2048]{1,0:T(8,128)} %copy-done.7, f32[64,2048]{1,0:T(8,128)} %copy-done.19, f32[128,8192]{1,0:T(8,128)} %y_ref.7, s32[128,8192]{1,0:T(8,128)} %g_ref.7), custom_call_target="tpu_custom_call" | custom-call | flops 41943040 | bytes 13107200 | tf_op jit(solution)/shard_map/pallas_call | solution.py:211
  107.3 2.9 %fusion.19 = f32[16,12,3,128]{3,0,1,2:T(8,128)} fusion(f32[16,3,12,512]{3,2,1,0:T(8,128)S(1)} %copy-done.3, f32[512]{0:T(512)S(1)} %get-tuple-element.177, f32[512]{0:T(512)S(1)} %get-tuple-element.178, f32[512]{0:T(512)} %copy-done.27, f32[512]{0:T(512)S(1)} %get-tuple-element.175, s32[512]{0:T(512)S(1)} %add_select_fusion, s32[128]{0:T(128)} %copy-done.29), kind=kOutput, calls=%fused_computation.15 | convolution fusion | flops 227082240 | bytes 1485312 | tf_op jit(solution)/shard_map/pbkj,nj->pkbn/dot_general | solution.py:77
  110.1 1.2 add.306.t_ref
  111.3 0.5 collective-permute-start.13
  111.8 0.7 dynamic-slice_select_fusion.2
  112.5 10.9 %shard_map.124 = f32[16,4,12,512]{3,2,1,0:T(8,128)} custom-call(s32[1]{0:T(128)} %bitcast.29.b_ref, bf16[16,128,8192]{2,1,0:T(8,128)(2,1)} %cov_ref.15, f32[64,2048]{1,0:T(8,128)} %copy-done.9, f32[64,2048]{1,0:T(8,128)} %collective-permute-done.11.u_ref, f32[128,8192]{1,0:T(8,128)} %y_ref.7, s32[128,8192]{1,0:T(8,128)} %g_ref.7), custom_call_target="tpu_custom_call" | custom-call | flops 41943040 | bytes 13107200 | tf_op jit(solution)/shard_map/pallas_call | solution.py:211
  123.4 1.7 %dynamic-slice_select_fusion.1 = f32[32,2048]{1,0:T(8,128)} fusion(f32[64,2048]{1,0:T(8,128)} %collective-permute-done.11.u_ref, s32[]{:T(128)S(6)} %select_n.189, f32[64,2048]{1,0:T(8,128)S(1)} %copy-done.10, pred[]{:T(512)S(6)} %eq.63), kind=kLoop, calls=%fused_computation.59 | loop fusion | flops 65536 | bytes 786437 | tf_op jit(solution)/shard_map/jit(_where)/select_n | solution.py:314
  125.1 2.4 %fusion.11 = f32[16,12,4,128]{3,0,1,2:T(8,128)S(1)} fusion(f32[16,4,12,512]{3,2,1,0:T(8,128)S(1)} %copy-done, f32[512]{0:T(512)S(1)} %get-tuple-element.177, f32[512]{0:T(512)S(1)} %get-tuple-element.178, f32[512]{0:T(512)} %copy-done.27, f32[512]{0:T(512)S(1)} %get-tuple-element.175, s32[512]{0:T(512)S(1)} %add_select_fusion, s32[128]{0:T(128)} %copy-done.29), kind=kOutput, calls=%fused_computation.11 | convolution fusion | flops 302579712 | bytes 1976832 | tf_op jit(solution)/shard_map/pbkj,nj->pkbn/dot_general | solution.py:77
  127.5 1.7 %dynamic-slice_select_fusion = f32[32,2560]{1,0:T(8,128)} fusion(f32[64,2560]{1,0:T(8,128)} %collective-permute-done.13.u_ref, s32[]{:T(128)S(6)} %select_n.189, f32[64,2560]{1,0:T(8,128)S(1)} %add.306.t_ref, pred[]{:T(512)S(6)} %eq.63), kind=kLoop, calls=%fused_computation.40 | loop fusion | flops 81920 | bytes 983045 | tf_op jit(solution)/shard_map/jit(_where)/select_n | solution.py:314
  129.3 12.9 %shard_map.125 = f32[16,5,12,512]{3,2,1,0:T(8,128)} custom-call(s32[1]{0:T(128)} %bitcast.29.b_ref, bf16[16,128,8192]{2,1,0:T(8,128)(2,1)} %cov_ref.15, f32[64,2560]{1,0:T(8,128)} %copy-done.6, f32[64,2560]{1,0:T(8,128)} %collective-permute-done.13.u_ref, f32[128,8192]{1,0:T(8,128)} %y_ref.7, s32[128,8192]{1,0:T(8,128)} %g_ref.7), custom_call_target="tpu_custom_call" | custom-call | flops 52428800 | bytes 16384000 | tf_op jit(solution)/shard_map/pallas_call | solution.py:211
  142.2 1.7 %fusion.14 = f32[16,12,4,128]{3,0,1,2:T(8,128)S(1)} fusion(f32[16,4,12,512]{3,2,1,0:T(8,128)S(1)} %copy-done.1, f32[512]{0:T(512)S(1)} %get-tuple-element.177, f32[512]{0:T(512)S(1)} %get-tuple-element.178, f32[512]{0:T(512)S(1)} %copy-done.28, f32[512]{0:T(512)S(1)} %get-tuple-element.175, s32[512]{0:T(512)S(1)} %add_select_fusion, s32[128]{0:T(128)S(1)} %copy-done.30), kind=kOutput, calls=%fused_computation.12 | convolution fusion | flops 302579712 | bytes 1976832 | tf_op jit(solution)/shard_map/pbkj,nj->pkbn/dot_general | solution.py:77
  143.9 3.9 %fusion.8 = f32[16,12,5,128]{3,0,1,2:T(8,128)S(1)} fusion(f32[16,5,12,512]{3,2,1,0:T(8,128)} %shard_map.125, f32[512]{0:T(512)S(1)} %get-tuple-element.177, f32[512]{0:T(512)S(1)} %get-tuple-element.178, f32[512]{0:T(512)S(1)} %copy-done.28, f32[512]{0:T(512)S(1)} %get-tuple-element.175, s32[512]{0:T(512)S(1)} %add_select_fusion, s32[128]{0:T(128)S(1)} %copy-done.30), kind=kOutput, calls=%fused_computation.10 | convolution fusion | flops 378077184 | bytes 2468352 | tf_op jit(solution)/shard_map/pbkj,nj->pkbn/dot_general | solution.py:77
  147.8 0.2 pad_maximum_fusion
  147.9 1.4 fusion.89
  149.3 0.6 pad_add_fusion
  149.9 1.1 copy.738
  151.0 0.5 reshape.147
  151.5 0.2 slice_multiply_fusion
  151.7 4.3 %collective-permute-start.14 = (f32[16,2,512]{2,0,1:T(8,128)S(1)}, f32[16,2,512]{2,0,1:T(8,128)S(1)}, u32[]{:S(2)}, u32[]{:S(2)}) collective-permute-start(f32[16,2,512]{2,0,1:T(8,128)S(1)} %get-tuple-element.148), channel_id=1, source_target_pairs={{0,4},{4,8},{8,12},{12,16},{16,20},{20,24},{24,28},{1,5},{5,9},{9,... | collective-permute-start | bytes 196616 | tf_op jit(solution)/shard_map/ppermute | solution.py:31
  156.1 1.4 collective-permute-start.15
  157.5 3.3 %subtract_multiply_fusion = (f32[32,8192]{1,0:T(8,128)}, f32[32,8192]{1,0:T(8,128)}) fusion(f32[128,8192]{1,0:T(8,128)} %y_ref.7, s32[]{:T(128)S(6)} %select_n.195, s32[128,8192]{1,0:T(8,128)} %g_ref.7, f32[32,2560]{1,0:T(8,128)} %dynamic-slice_select_fusion, f32[32,2048]{1,0:T(8,128)} %dynamic-slice_select_fusion.1, ...), kind=kLoop, calls=%fused_computation.17 | loop fusion | flops 1572864 | bytes 5242884 | tf_op jit(solution)/shard_map/mul | solution.py:317
  160.8 2.8 %collective-permute-done.15 = f32[16,2,512]{2,0,1:T(8,128)S(1)} collective-permute-done((f32[16,2,512]{2,0,1:T(8,128)S(1)}, f32[16,2,512]{2,0,1:T(8,128)S(1)}, u32[]{:S(2)}, u32[]{:S(2)}) %collective-permute-start.15) | collective-permute-done | bytes 65568 | tf_op jit(solution)/shard_map/ppermute | solution.py:31
  163.7 0.8 divide_subtract_fusion
  164.5 0.9 copy.747
  165.3 0.9 copy.748
  166.2 0.9 copy.749
  167.0 0.9 copy.746
  (101 shorter events, 1.9 us)
Async XLA Ops:
  1.8 10.0 %collective-permute-start.1 = (f32[16,2,512]{2,0,1:T(8,128)S(1)}, f32[16,2,512]{2,0,1:T(8,128)S(1)}, u32[]{:S(2)}, u32[]{:S(2)}) collective-permute-start(f32[16,2,512]{2,0,1:T(8,128)S(1)} %get-tuple-element.169), channel_id=1, source_target_pairs={{4,0},{8,4},{12,8},{16,12},{20,16},{24,20},{28,24},{5,1},{9,5},{13... | collective-permute-start | bytes 196616 | tf_op jit(solution)/shard_map/ppermute | solution.py:23
  3.1 7.5 %collective-permute-start = (f32[16,2,512]{2,0,1:T(8,128)S(1)}, f32[16,2,512]{2,0,1:T(8,128)S(1)}, u32[]{:S(2)}, u32[]{:S(2)}) collective-permute-start(f32[16,2,512]{2,0,1:T(8,128)S(1)} %get-tuple-element.170), channel_id=1, source_target_pairs={{0,4},{4,8},{8,12},{12,16},{16,20},{20,24},{24,28},{1,5},{5,9},{9,... | collective-permute-start | bytes 196616 | tf_op jit(solution)/shard_map/ppermute | solution.py:22
  8.6 9.5 %copy-start.27 = (f32[512]{0:T(512)}, f32[512]{0:T(512)S(1)}, u32[]{:S(2)}) copy-start(f32[512]{0:T(512)S(1)} %get-tuple-element.176) | copy-start | bytes 6148
  8.6 9.5 %copy-start.29 = (s32[128]{0:T(128)}, s32[128]{0:T(128)S(1)}, u32[]{:S(2)}) copy-start(s32[128]{0:T(128)S(1)} %iota_add_fusion) | copy-start | bytes 1540
  11.7 0.7 copy-start.22
  12.4 0.7 copy-start.15
  32.8 9.7 %collective-permute-start.2 = (f32[64,1536]{1,0:T(8,128)S(1)}, f32[64,1536]{1,0:T(8,128)S(1)}, u32[]{:S(2)}, u32[]{:S(2)}) collective-permute-start(f32[64,1536]{1,0:T(8,128)S(1)} %dynamic-slice_bitcast_fusion.3), channel_id=1, source_target_pairs={{0,1},{1,0},{2,3},{3,2},{4,5},{5,4},{6,7},{7,6},{8,9},{9,8},{10,11... | collective-permute-start | bytes 1179656 | tf_op jit(solution)/shard_map/ppermute | solution.py:288
  32.8 11.9 %copy-start.11 = (f32[128,1536]{1,0:T(8,128)S(1)}, f32[128,1536]{1,0:T(8,128)}, u32[]{:S(2)}) copy-start(f32[128,1536]{1,0:T(8,128)} %shard_map.118) | copy-start | bytes 2359300
  44.3 12.0 %collective-permute-start.4 = (f32[64,2048]{1,0:T(8,128)}, f32[64,2048]{1,0:T(8,128)S(1)}, u32[]{:S(2)}, u32[]{:S(2)}) collective-permute-start(f32[64,2048]{1,0:T(8,128)} %dynamic-slice_bitcast_fusion.2), channel_id=1, source_target_pairs={{0,1},{1,0},{2,3},{3,2},{4,5},{5,4},{6,7},{7,6},{8,9},{9,8},{10,11... | collective-permute-start | bytes 1572872 | tf_op jit(solution)/shard_map/ppermute | solution.py:288
  44.8 11.4 %copy-start.17 = (f32[64,1536]{1,0:T(8,128)}, f32[64,1536]{1,0:T(8,128)S(1)}, u32[]{:S(2)}) copy-start(f32[64,1536]{1,0:T(8,128)S(1)} %bitcast_add_fusion.3) | copy-start | bytes 1179652
  44.8 11.5 %copy-start.5 = (f32[128,2048]{1,0:T(8,128)S(1)}, f32[128,2048]{1,0:T(8,128)}, u32[]{:S(2)}) copy-start(f32[128,2048]{1,0:T(8,128)} %shard_map.119) | copy-start | bytes 3145732
  44.8 11.4 %collective-permute-start.3 = (f32[64,1536]{1,0:T(8,128)S(1)}, f32[64,1536]{1,0:T(8,128)}, u32[]{:S(2)}, u32[]{:S(2)}) collective-permute-start(f32[64,1536]{1,0:T(8,128)S(1)} %bitcast_add_fusion.3), channel_id=1, source_target_pairs={{0,2},{1,3},{2,0},{3,1},{4,6},{5,7},{6,4},{7,5},{8,10},{9,11},{10,... | collective-permute-start | bytes 1179656 | tf_op jit(solution)/shard_map/ppermute | solution.py:288
  56.3 1.2 copy-start.4
  56.3 2.6 %copy-start.18 = (f32[64,1536]{1,0:T(8,128)S(1)}, f32[64,1536]{1,0:T(8,128)}, u32[]{:S(2)}) copy-start(f32[64,1536]{1,0:T(8,128)} %copy-done.17) | copy-start | bytes 1179652
  58.3 13.2 %collective-permute-start.7 = (f32[64,2048]{1,0:T(8,128)}, f32[64,2048]{1,0:T(8,128)}, u32[]{:S(2)}, u32[]{:S(2)}) collective-permute-start(f32[64,2048]{1,0:T(8,128)} %dynamic-slice_bitcast_fusion.1), channel_id=1, source_target_pairs={{0,1},{1,0},{2,3},{3,2},{4,5},{5,4},{6,7},{7,6},{8,9},{9,8},{10,11... | collective-permute-start | bytes 1572872 | tf_op jit(solution)/shard_map/ppermute | solution.py:288
  58.3 14.3 %collective-permute-start.6 = (f32[64,2048]{1,0:T(8,128)S(1)}, f32[64,2048]{1,0:T(8,128)S(1)}, u32[]{:S(2)}, u32[]{:S(2)}) collective-permute-start(f32[64,2048]{1,0:T(8,128)S(1)} %bitcast_add_fusion.2), channel_id=1, source_target_pairs={{0,2},{1,3},{2,0},{3,1},{4,6},{5,7},{6,4},{7,5},{8,10},{9,11},{10,... | collective-permute-start | bytes 1572872 | tf_op jit(solution)/shard_map/ppermute | solution.py:288
  59.9 11.6 %copy-start.12 = (f32[64,1536]{1,0:T(8,128)}, f32[64,1536]{1,0:T(8,128)S(1)}, u32[]{:S(2)}) copy-start(f32[64,1536]{1,0:T(8,128)S(1)} %add.299.t_ref) | copy-start | bytes 1179652
  60.0 11.6 %collective-permute-start.5 = (f32[64,1536]{1,0:T(8,128)S(1)}, f32[64,1536]{1,0:T(8,128)S(1)}, u32[]{:S(2)}, u32[]{:S(2)}) collective-permute-start(f32[64,1536]{1,0:T(8,128)S(1)} %add.299.t_ref), channel_id=1, source_target_pairs={{0,1},{1,0},{2,3},{3,2},{4,5},{5,4},{6,7},{7,6},{8,9},{9,8},{10,11... | collective-permute-start | bytes 1179656 | tf_op jit(solution)/shard_map/ppermute | solution.py:288
  71.5 5.1 %copy-start.24 = (f32[64,1536]{1,0:T(8,128)}, f32[64,1536]{1,0:T(8,128)S(1)}, u32[]{:S(2)}) copy-start(f32[64,1536]{1,0:T(8,128)S(1)} %collective-permute-done.5.u_ref) | copy-start | bytes 1179652
  74.6 16.8 %collective-permute-start.10 = (f32[64,2560]{1,0:T(8,128)}, f32[64,2560]{1,0:T(8,128)}, u32[]{:S(2)}, u32[]{:S(2)}) collective-permute-start(f32[64,2560]{1,0:T(8,128)} %dynamic-slice_bitcast_fusion), channel_id=1, source_target_pairs={{0,1},{1,0},{2,3},{3,2},{4,5},{5,4},{6,7},{7,6},{8,9},{9,8},{10,11... | collective-permute-start | bytes 1966088 | tf_op jit(solution)/shard_map/ppermute | solution.py:288
  76.6 9.9 %copy-start.7 = (f32[64,2048]{1,0:T(8,128)}, f32[64,2048]{1,0:T(8,128)S(1)}, u32[]{:S(2)}) copy-start(f32[64,2048]{1,0:T(8,128)S(1)} %add.302.t_ref) | copy-start | bytes 1572868
  76.6 9.9 %collective-permute-start.8 = (f32[64,2048]{1,0:T(8,128)S(1)}, f32[64,2048]{1,0:T(8,128)S(1)}, u32[]{:S(2)}, u32[]{:S(2)}) collective-permute-start(f32[64,2048]{1,0:T(8,128)S(1)} %add.302.t_ref), channel_id=1, source_target_pairs={{0,1},{1,0},{2,3},{3,2},{4,5},{5,4},{6,7},{7,6},{8,9},{9,8},{10,11... | collective-permute-start | bytes 1572872 | tf_op jit(solution)/shard_map/ppermute | solution.py:288
  77.2 14.2 %collective-permute-start.9 = (f32[64,2048]{1,0:T(8,128)}, f32[64,2048]{1,0:T(8,128)}, u32[]{:S(2)}, u32[]{:S(2)}) collective-permute-start(f32[64,2048]{1,0:T(8,128)} %bitcast_add_fusion.1), channel_id=1, source_target_pairs={{0,2},{1,3},{2,0},{3,1},{4,6},{5,7},{6,4},{7,5},{8,10},{9,11},{10,... | collective-permute-start | bytes 1572872 | tf_op jit(solution)/shard_map/ppermute | solution.py:288
  77.7 13.7 %copy-start.2 = (f32[128,2560]{1,0:T(8,128)S(1)}, f32[128,2560]{1,0:T(8,128)}, u32[]{:S(2)}) copy-start(f32[128,2560]{1,0:T(8,128)} %shard_map.121) | copy-start | bytes 3932164
  86.5 8.2 %copy-start.13 = (f32[64,1536]{1,0:T(8,128)S(1)}, f32[64,1536]{1,0:T(8,128)}, u32[]{:S(2)}) copy-start(f32[64,1536]{1,0:T(8,128)} %copy-done.12) | copy-start | bytes 1179652
  86.5 4.9 %copy-start.19 = (f32[64,2048]{1,0:T(8,128)}, f32[64,2048]{1,0:T(8,128)S(1)}, u32[]{:S(2)}) copy-start(f32[64,2048]{1,0:T(8,128)S(1)} %collective-permute-done.8.u_ref) | copy-start | bytes 1572868
  92.6 17.6 %collective-permute-start.12 = (f32[64,2560]{1,0:T(8,128)S(1)}, f32[64,2560]{1,0:T(8,128)}, u32[]{:S(2)}, u32[]{:S(2)}) collective-permute-start(f32[64,2560]{1,0:T(8,128)S(1)} %bitcast_add_fusion), channel_id=1, source_target_pairs={{0,2},{1,3},{2,0},{3,1},{4,6},{5,7},{6,4},{7,5},{8,10},{9,11},{10,... | collective-permute-start | bytes 1966088 | tf_op jit(solution)/shard_map/ppermute | solution.py:288
  94.6 12.7 %copy-start.9 = (f32[64,2048]{1,0:T(8,128)}, f32[64,2048]{1,0:T(8,128)S(1)}, u32[]{:S(2)}) copy-start(f32[64,2048]{1,0:T(8,128)S(1)} %add.304.t_ref) | copy-start | bytes 1572868
  94.6 15.5 %collective-permute-start.11 = (f32[64,2048]{1,0:T(8,128)S(1)}, f32[64,2048]{1,0:T(8,128)}, u32[]{:S(2)}, u32[]{:S(2)}) collective-permute-start(f32[64,2048]{1,0:T(8,128)S(1)} %add.304.t_ref), channel_id=1, source_target_pairs={{0,1},{1,0},{2,3},{3,2},{4,5},{5,4},{6,7},{7,6},{8,9},{9,8},{10,11... | collective-permute-start | bytes 1572872 | tf_op jit(solution)/shard_map/ppermute | solution.py:288
  96.4 10.8 %copy-start.3 = (f32[16,3,12,512]{3,2,1,0:T(8,128)S(1)}, f32[16,3,12,512]{3,2,1,0:T(8,128)}, u32[]{:S(2)}) copy-start(f32[16,3,12,512]{3,2,1,0:T(8,128)} %shard_map.122) | copy-start | bytes 3538948
  107.2 4.5 %copy-start.8 = (f32[64,2048]{1,0:T(8,128)S(1)}, f32[64,2048]{1,0:T(8,128)}, u32[]{:S(2)}) copy-start(f32[64,2048]{1,0:T(8,128)} %copy-done.7) | copy-start | bytes 1572868
  107.2 4.5 %copy-start.20 = (f32[64,2048]{1,0:T(8,128)S(1)}, f32[64,2048]{1,0:T(8,128)}, u32[]{:S(2)}) copy-start(f32[64,2048]{1,0:T(8,128)} %copy-done.19) | copy-start | bytes 1572868
  111.3 16.2 %copy-start.6 = (f32[64,2560]{1,0:T(8,128)}, f32[64,2560]{1,0:T(8,128)S(1)}, u32[]{:S(2)}) copy-start(f32[64,2560]{1,0:T(8,128)S(1)} %add.306.t_ref) | copy-start | bytes 1966084
  111.3 16.2 %collective-permute-start.13 = (f32[64,2560]{1,0:T(8,128)S(1)}, f32[64,2560]{1,0:T(8,128)}, u32[]{:S(2)}, u32[]{:S(2)}) collective-permute-start(f32[64,2560]{1,0:T(8,128)S(1)} %add.306.t_ref), channel_id=1, source_target_pairs={{0,1},{1,0},{2,3},{3,2},{4,5},{5,4},{6,7},{7,6},{8,9},{9,8},{10,11... | collective-permute-start | bytes 1966088 | tf_op jit(solution)/shard_map/ppermute | solution.py:288
  112.5 10.9 %copy-start.10 = (f32[64,2048]{1,0:T(8,128)S(1)}, f32[64,2048]{1,0:T(8,128)}, u32[]{:S(2)}) copy-start(f32[64,2048]{1,0:T(8,128)} %copy-done.9) | copy-start | bytes 1572868
  112.5 12.6 %copy-start = (f32[16,4,12,512]{3,2,1,0:T(8,128)S(1)}, f32[16,4,12,512]{3,2,1,0:T(8,128)}, u32[]{:S(2)}) copy-start(f32[16,4,12,512]{3,2,1,0:T(8,128)} %shard_map.123) | copy-start | bytes 4718596
  129.2 12.9 %copy-start.1 = (f32[16,4,12,512]{3,2,1,0:T(8,128)S(1)}, f32[16,4,12,512]{3,2,1,0:T(8,128)}, u32[]{:S(2)}) copy-start(f32[16,4,12,512]{3,2,1,0:T(8,128)} %shard_map.124) | copy-start | bytes 4718596
  129.2 12.9 %copy-start.28 = (f32[512]{0:T(512)S(1)}, f32[512]{0:T(512)}, u32[]{:S(2)}) copy-start(f32[512]{0:T(512)} %copy-done.27) | copy-start | bytes 6148
  129.3 12.9 %copy-start.30 = (s32[128]{0:T(128)S(1)}, s32[128]{0:T(128)}, u32[]{:S(2)}) copy-start(s32[128]{0:T(128)} %copy-done.29) | copy-start | bytes 1540
  143.9 3.9 %copy-start.21 = (f32[16,12,3,128]{3,0,1,2:T(8,128)S(1)}, f32[16,12,3,128]{3,0,1,2:T(8,128)}, u32[]{:S(2)}) copy-start(f32[16,12,3,128]{3,0,1,2:T(8,128)} %fusion.19) | copy-start | bytes 884740
  151.7 9.1 %collective-permute-start.14 = (f32[16,2,512]{2,0,1:T(8,128)S(1)}, f32[16,2,512]{2,0,1:T(8,128)S(1)}, u32[]{:S(2)}, u32[]{:S(2)}) collective-permute-start(f32[16,2,512]{2,0,1:T(8,128)S(1)} %get-tuple-element.148), channel_id=1, source_target_pairs={{0,4},{4,8},{8,12},{12,16},{16,20},{20,24},{24,28},{1,5},{5,9},{9,... | collective-permute-start | bytes 196616 | tf_op jit(solution)/shard_map/ppermute | solution.py:31
  156.0 7.6 %copy-start.14 = (f32[16,8,512]{2,1,0:T(8,128)S(1)}, f32[16,8,512]{2,1,0:T(8,128)}, u32[]{:S(2)}) copy-start(f32[16,8,512]{2,1,0:T(8,128)} %param.10) | copy-start | bytes 786436
  156.0 7.6 %copy-start.16 = (f32[16,10,512]{2,0,1:T(8,128)S(1)}, f32[16,10,512]{2,0,1:T(8,128)}, u32[]{:S(2)}) copy-start(f32[16,10,512]{2,0,1:T(8,128)} %copy-done.15) | copy-start | bytes 983044
  156.0 7.6 %copy-start.23 = (f32[16,10,512]{2,0,1:T(8,128)S(1)}, f32[16,10,512]{2,0,1:T(8,128)}, u32[]{:S(2)}) copy-start(f32[16,10,512]{2,0,1:T(8,128)} %copy-done.22) | copy-start | bytes 983044
  156.0 7.6 %copy-start.25 = (f32[16,8,512]{2,1,0:T(8,128)S(1)}, f32[16,8,512]{2,1,0:T(8,128)}, u32[]{:S(2)}) copy-start(f32[16,8,512]{2,1,0:T(8,128)} %param.11) | copy-start | bytes 786436
  156.1 7.6 %copy-start.26 = (f32[16,8,512]{2,1,0:T(8,128)S(1)}, f32[16,8,512]{2,1,0:T(8,128)}, u32[]{:S(2)}) copy-start(f32[16,8,512]{2,1,0:T(8,128)} %param.12) | copy-start | bytes 786436
  156.1 7.6 %copy-start.31 = (f32[16]{0:T(128)S(1)}, f32[16]{0:T(128)}, u32[]{:S(2)}) copy-start(f32[16]{0:T(128)} %param.13) | copy-start | bytes 196
  156.1 7.5 %collective-permute-start.15 = (f32[16,2,512]{2,0,1:T(8,128)S(1)}, f32[16,2,512]{2,0,1:T(8,128)S(1)}, u32[]{:S(2)}, u32[]{:S(2)}) collective-permute-start(f32[16,2,512]{2,0,1:T(8,128)S(1)} %get-tuple-element.149), channel_id=1, source_target_pairs={{4,0},{8,4},{12,8},{16,12},{20,16},{24,20},{28,24},{5,1},{9,5},{13... | collective-permute-start | bytes 196616 | tf_op jit(solution)/shard_map/ppermute | solution.py:31

commit v12 on v10

--- a/solution.py
+++ b/solution.py
@@ -174,7 +174,7 @@
                 o_ref[p, 0, pl.ds(r, 1), cols] = jnp.sum(accs[r], axis=0, keepdims=True)
             return carry
 
-        lax.fori_loop(0, npred, body, 0, unroll=4 if npred % 4 == 0 else 1)
+        lax.fori_loop(0, npred, body, 0, unroll=True)
 
 
 def fit_chunk(wl, cov, along, off, width):

time: 168 us -> 167 us (level)
  transfers between devices with their start and end apart: 16 -> 16, of which waited for: 5 -> 5; matrix products, arithmetic and copies ran while one was open for 11% -> 11% of each run, Pallas kernels for 35% -> 34%
where the time goes in v12:
time: 167 us; the launch traced here: 166 us
  Pallas kernels  76.8 us (46%)
  local copies, waits for them, and re-layouts  21.6 us (13%)
  starting transfers between devices  21.3 us (13%)
  other arithmetic  17.6 us (11%)
  matrix products  16.7 us (10%)
  waiting for transfers between devices  10.8 us (6%)
    pallas_call x4, Pallas kernels, back_chunk(): pl.pallas_call(back_kernel, grid=(width // TN,), in_specs=[pl.BlockSpec(m...  42.7 us
    pallas_call x4, Pallas kernels, fit_chunk(): pl.pallas_call(fit_kernel, grid=(width // TN,), in_specs=[pl.BlockSpec((4...  34.1 us
    dot_general x4, matrix products, banded_data(): jnp.einsum('pbkj,nj->pkbn', part, basis, precision=lax.Precision.HIGH)  10.8 us
    ppermute x12, starting transfers between devices, local(): pending.append((c, finish, lax.ppermute(send, 'pred', pairs)))  8.77 us
    unnamed x70, local copies, waits for them, and re-layouts  6.26 us
    ppermute x12, waiting for transfers between devices, local(): pending.append((c, finish, lax.ppermute(send, 'pred', pairs)))  6.12 us
    dot_general x1, matrix products, banded_along(): jnp.einsum('pbkn,nj->pbkj', cwin, block_basis(window), precision=lax.Prec...  5.94 us
    select_n x4, other arithmetic, local(): picked = jnp.where(bit0 == side, cur, other)  5.87 us
  transfers between devices with their start and end apart: 16, of which 5 were waited for; matrix products, arithmetic and copies ran while one was open for 11% of the time, Pallas kernels for 34%

profile of v12, /device:TPU:0, one launch (start us, length us, event | category | flops | bytes accessed | tf_op | source)
XLA Modules:
  0.0 166.1 jit_solution(12572104582434704876)
XLA Ops:
  0.6 1.1 copy.711
  1.8 1.3 collective-permute-start.1
  3.1 5.5 %collective-permute-start = (f32[16,2,512]{2,0,1:T(8,128)S(1)}, f32[16,2,512]{2,0,1:T(8,128)S(1)}, u32[]{:S(2)}, u32[]{:S(2)}) collective-permute-start(f32[16,2,512]{2,0,1:T(8,128)S(1)} %get-tuple-element.170), channel_id=1, source_target_pairs={{0,4},{4,8},{8,12},{12,16},{16,20},{20,24},{24,28},{1,5},{5,9},{9,... | collective-permute-start | bytes 196616 | tf_op jit(solution)/shard_map/ppermute | solution.py:22
  8.7 1.9 %collective-permute-done = f32[16,2,512]{2,0,1:T(8,128)S(1)} collective-permute-done((f32[16,2,512]{2,0,1:T(8,128)S(1)}, f32[16,2,512]{2,0,1:T(8,128)S(1)}, u32[]{:S(2)}, u32[]{:S(2)}) %collective-permute-start) | collective-permute-done | bytes 65568 | tf_op jit(solution)/shard_map/ppermute | solution.py:22
  10.6 1.1 constant_dynamic-update-slice_fusion.3
  11.8 0.7 copy-done.22
  12.5 0.7 copy-done.15
  13.2 0.5 fusion.45
  13.6 0.1 copy.729
  15.4 2.7 %stack.75 = f32[16,16,12,128]{3,1,2,0:T(8,128)S(1)} concatenate(f32[16,1,12,128]{3,1,2,0:T(1,128)S(1)} %copy.714, f32[16,1,12,128]{3,1,2,0:T(1,128)S(1)} %copy.715, f32[16,1,12,128]{3,1,2,0:T(1,128)S(1)} %copy.716, f32[16,1,12,128]{3,1,2,0:T(1,128)S(1)} %copy.717, f32[16,1,12,128]{3,1,2,0:T(1,128)S(1)} %copy.718, f32[16,1,12,128]{3,1,2,0:T(1,128)S(1)} %copy.719, ...), dimensions={1} | concatenate | bytes 3145728 | tf_op jit(solution)/shard_map/stack | solution.py:67
  18.1 5.9 %fusion.a_ref = f32[16,16,12,512]{3,2,1,0:T(8,128)} fusion(f32[16,16,12,128]{3,1,2,0:T(8,128)S(1)} %stack.75, f32[512]{0:T(512)S(1)} %get-tuple-element.177, f32[512]{0:T(512)S(1)} %get-tuple-element.178, f32[512]{0:T(512)S(1)} %get-tuple-element.176, f32[512]{0:T(512)S(1)} %get-tuple-element.175, s32[512]{0:T(512)S(1)} %add_select_fusion, ...), kind=kOutput, calls=%fused_computation | convolution fusion | flops 1208549376 | bytes 7875072 | tf_op jit(solution)/shard_map/pbkn,nj->pbkj/dot_general | solution.py:68
  24.0 0.7 broadcast_in_dim.79.w_ref
  24.7 6.9 %shard_map.118 = f32[128,1536]{1,0:T(8,128)} custom-call(f32[4,16,256]{2,1,0:T(8,128)} %broadcast_in_dim.79.w_ref, bf16[16,128,8192]{2,1,0:T(8,128)(2,1)} %cov_ref.15, f32[16,16,12,512]{3,2,1,0:T(8,128)} %fusion.a_ref), custom_call_target="tpu_custom_call" | custom-call | flops 31457280 | bytes 8257536 | tf_op jit(solution)/shard_map/pallas_call | solution.py:183
  31.7 1.0 dynamic-slice_bitcast_fusion.3
  32.8 8.5 %shard_map.119 = f32[128,2048]{1,0:T(8,128)} custom-call(f32[4,16,256]{2,1,0:T(8,128)} %broadcast_in_dim.79.w_ref, bf16[16,128,8192]{2,1,0:T(8,128)(2,1)} %cov_ref.15, f32[16,16,12,512]{3,2,1,0:T(8,128)} %fusion.a_ref), custom_call_target="tpu_custom_call" | custom-call | flops 41943040 | bytes 11010048 | tf_op jit(solution)/shard_map/pallas_call | solution.py:183
  41.3 1.9 %dynamic-slice_bitcast_fusion.2 = f32[64,2048]{1,0:T(8,128)} fusion(f32[2,64,2048]{2,1,0:T(8,128)} %bitcast.80, s32[]{:T(128)S(6)} %select_n.187), kind=kLoop, calls=%fused_computation.31 | loop fusion | bytes 1048580 | tf_op jit(solution)/shard_map/jit(dynamic_index_in_dim)/squeeze | solution.py:104
  43.2 0.5 collective-permute-start.4
  43.7 2.0 %collective-permute-start.3 = (f32[64,1536]{1,0:T(8,128)S(1)}, f32[64,1536]{1,0:T(8,128)}, u32[]{:S(2)}, u32[]{:S(2)}) collective-permute-start(f32[64,1536]{1,0:T(8,128)S(1)} %bitcast_add_fusion.3), channel_id=1, source_target_pairs={{0,2},{1,3},{2,0},{3,1},{4,6},{5,7},{6,4},{7,5},{8,10},{9,11},{10,... | collective-permute-start | bytes 1179656 | tf_op jit(solution)/shard_map/ppermute | solution.py:285
  45.7 8.4 %shard_map.120 = f32[128,2048]{1,0:T(8,128)} custom-call(f32[4,16,256]{2,1,0:T(8,128)} %broadcast_in_dim.79.w_ref, bf16[16,128,8192]{2,1,0:T(8,128)(2,1)} %cov_ref.15, f32[16,16,12,512]{3,2,1,0:T(8,128)} %fusion.a_ref), custom_call_target="tpu_custom_call" | custom-call | flops 41943040 | bytes 11010048 | tf_op jit(solution)/shard_map/pallas_call | solution.py:183
  54.1 1.0 collective-permute-done.3
  55.2 0.2 copy-done.4
  55.4 0.8 dynamic-slice_bitcast_fusion.1
  56.2 1.6 collective-permute-start.6
  57.8 1.1 add.372.t_ref
  58.9 0.3 collective-permute-start.5
  59.2 10.2 %shard_map.121 = f32[128,2560]{1,0:T(8,128)} custom-call(f32[4,16,256]{2,1,0:T(8,128)} %broadcast_in_dim.79.w_ref, bf16[16,128,8192]{2,1,0:T(8,128)(2,1)} %cov_ref.15, f32[16,16,12,512]{3,2,1,0:T(8,128)} %fusion.a_ref), custom_call_target="tpu_custom_call" | custom-call | flops 52428800 | bytes 13762560 | tf_op jit(solution)/shard_map/pallas_call | solution.py:183
  69.4 1.2 collective-permute-done.6
  70.5 2.0 %dynamic-slice_bitcast_fusion = f32[64,2560]{1,0:T(8,128)} fusion(f32[2,64,2560]{2,1,0:T(8,128)} %bitcast.76, s32[]{:T(128)S(6)} %select_n.187), kind=kLoop, calls=%fused_computation.19 | loop fusion | bytes 1310724 | tf_op jit(solution)/shard_map/jit(dynamic_index_in_dim)/squeeze | solution.py:104
  72.5 1.9 %bitcast_add_fusion.1 = f32[64,2048]{1,0:T(8,128)} fusion(f32[64,2048]{1,0:T(8,128)} %collective-permute-done.7, f32[2,64,2048]{2,1,0:T(8,128)S(1)} %bitcast.79, s32[]{:T(128)S(6)} %select_n.186), kind=kLoop, calls=%fused_computation.28 | loop fusion | flops 131072 | bytes 1572868 | tf_op jit(solution)/shard_map/add | solution.py:105
  74.5 0.6 collective-permute-start.8
  75.1 1.6 collective-permute-start.9
  76.7 8.7 %shard_map.122 = f32[16,3,12,512]{3,2,1,0:T(8,128)} custom-call(s32[1]{0:T(128)} %bitcast.29.b_ref, f32[4,16,256]{2,1,0:T(8,128)} %broadcast_in_dim.79.w_ref, bf16[16,128,8192]{2,1,0:T(8,128)(2,1)} %cov_ref.15, f32[64,1536]{1,0:T(8,128)} %copy-done.12, f32[64,1536]{1,0:T(8,128)} %copy-done.24, f32[128,8192]{1,0:T(8,128)} %y_ref.7, s32[128,8192]{1,0:T(8,128)} %g_ref.7), custom_call_target="tpu_custom_call" | custom-call | flops 31457280 | bytes 9830400 | tf_op jit(solution)/shard_map/pallas_call | solution.py:206
  85.3 3.9 %collective-permute-done.9 = f32[64,2048]{1,0:T(8,128)} collective-permute-done((f32[64,2048]{1,0:T(8,128)}, f32[64,2048]{1,0:T(8,128)}, u32[]{:S(2)}, u32[]{:S(2)}) %collective-permute-start.9) | collective-permute-done | bytes 524320 | tf_op jit(solution)/shard_map/ppermute | solution.py:285
  89.3 1.2 bitcast_add_fusion
  90.5 1.7 %collective-permute-start.12 = (f32[64,2560]{1,0:T(8,128)S(1)}, f32[64,2560]{1,0:T(8,128)}, u32[]{:S(2)}, u32[]{:S(2)}) collective-permute-start(f32[64,2560]{1,0:T(8,128)S(1)} %bitcast_add_fusion), channel_id=1, source_target_pairs={{0,2},{1,3},{2,0},{3,1},{4,6},{5,7},{6,4},{7,5},{8,10},{9,11},{10,... | collective-permute-start | bytes 1966088 | tf_op jit(solution)/shard_map/ppermute | solution.py:285
  92.1 1.3 add.377.t_ref
  93.5 1.7 %dynamic-slice_select_fusion.3 = f32[32,1536]{1,0:T(8,128)} fusion(f32[64,1536]{1,0:T(8,128)} %copy-done.24, s32[]{:T(128)S(6)} %select_n.189, f32[64,1536]{1,0:T(8,128)S(1)} %copy-done.13, pred[]{:T(512)S(6)} %eq.63), kind=kLoop, calls=%fused_computation.71 | loop fusion | flops 49152 | bytes 589829 | tf_op jit(solution)/shard_map/jit(_where)/select_n | solution.py:311
  95.2 10.6 %shard_map.123 = f32[16,4,12,512]{3,2,1,0:T(8,128)} custom-call(s32[1]{0:T(128)} %bitcast.29.b_ref, f32[4,16,256]{2,1,0:T(8,128)} %broadcast_in_dim.79.w_ref, bf16[16,128,8192]{2,1,0:T(8,128)(2,1)} %cov_ref.15, f32[64,2048]{1,0:T(8,128)} %copy-done.7, f32[64,2048]{1,0:T(8,128)} %copy-done.19, f32[128,8192]{1,0:T(8,128)} %y_ref.7, s32[128,8192]{1,0:T(8,128)} %g_ref.7), custom_call_target="tpu_custom_call" | custom-call | flops 41943040 | bytes 13107200 | tf_op jit(solution)/shard_map/pallas_call | solution.py:206
  105.9 2.8 %fusion.19 = f32[16,12,3,128]{3,0,1,2:T(8,128)} fusion(f32[16,3,12,512]{3,2,1,0:T(8,128)S(1)} %copy-done.3, f32[512]{0:T(512)S(1)} %get-tuple-element.177, f32[512]{0:T(512)S(1)} %get-tuple-element.178, f32[512]{0:T(512)} %copy-done.27, f32[512]{0:T(512)S(1)} %get-tuple-element.175, s32[512]{0:T(512)S(1)} %add_select_fusion, s32[128]{0:T(128)} %copy-done.29), kind=kOutput, calls=%fused_computation.15 | convolution fusion | flops 227082240 | bytes 1485312 | tf_op jit(solution)/shard_map/pbkj,nj->pkbn/dot_general | solution.py:77
  108.7 1.2 add.379.t_ref
  109.9 0.5 collective-permute-start.13
  110.3 0.7 dynamic-slice_select_fusion.2
  111.1 10.7 %shard_map.124 = f32[16,4,12,512]{3,2,1,0:T(8,128)} custom-call(s32[1]{0:T(128)} %bitcast.29.b_ref, f32[4,16,256]{2,1,0:T(8,128)} %broadcast_in_dim.79.w_ref, bf16[16,128,8192]{2,1,0:T(8,128)(2,1)} %cov_ref.15, f32[64,2048]{1,0:T(8,128)} %copy-done.9, f32[64,2048]{1,0:T(8,128)} %collective-permute-done.11.u_ref, f32[128,8192]{1,0:T(8,128)} %y_ref.7, ...), custom_call_target="tpu_custom_call" | custom-call | flops 41943040 | bytes 13107200 | tf_op jit(solution)/shard_map/pallas_call | solution.py:206
  121.8 1.7 %dynamic-slice_select_fusion.1 = f32[32,2048]{1,0:T(8,128)} fusion(f32[64,2048]{1,0:T(8,128)} %collective-permute-done.11.u_ref, s32[]{:T(128)S(6)} %select_n.189, f32[64,2048]{1,0:T(8,128)S(1)} %copy-done.10, pred[]{:T(512)S(6)} %eq.63), kind=kLoop, calls=%fused_computation.59 | loop fusion | flops 65536 | bytes 786437 | tf_op jit(solution)/shard_map/jit(_where)/select_n | solution.py:311
  123.5 2.4 %fusion.11 = f32[16,12,4,128]{3,0,1,2:T(8,128)S(1)} fusion(f32[16,4,12,512]{3,2,1,0:T(8,128)S(1)} %copy-done, f32[512]{0:T(512)S(1)} %get-tuple-element.177, f32[512]{0:T(512)S(1)} %get-tuple-element.178, f32[512]{0:T(512)} %copy-done.27, f32[512]{0:T(512)S(1)} %get-tuple-element.175, s32[512]{0:T(512)S(1)} %add_select_fusion, s32[128]{0:T(128)} %copy-done.29), kind=kOutput, calls=%fused_computation.11 | convolution fusion | flops 302579712 | bytes 1976832 | tf_op jit(solution)/shard_map/pbkj,nj->pkbn/dot_general | solution.py:77
  125.9 1.8 %dynamic-slice_select_fusion = f32[32,2560]{1,0:T(8,128)} fusion(f32[64,2560]{1,0:T(8,128)} %collective-permute-done.13.u_ref, s32[]{:T(128)S(6)} %select_n.189, f32[64,2560]{1,0:T(8,128)S(1)} %add.379.t_ref, pred[]{:T(512)S(6)} %eq.63), kind=kLoop, calls=%fused_computation.40 | loop fusion | flops 81920 | bytes 983045 | tf_op jit(solution)/shard_map/jit(_where)/select_n | solution.py:311
  127.7 12.7 %shard_map.125 = f32[16,5,12,512]{3,2,1,0:T(8,128)} custom-call(s32[1]{0:T(128)} %bitcast.29.b_ref, f32[4,16,256]{2,1,0:T(8,128)} %broadcast_in_dim.79.w_ref, bf16[16,128,8192]{2,1,0:T(8,128)(2,1)} %cov_ref.15, f32[64,2560]{1,0:T(8,128)} %copy-done.6, f32[64,2560]{1,0:T(8,128)} %collective-permute-done.13.u_ref, f32[128,8192]{1,0:T(8,128)} %y_ref.7, ...), custom_call_target="tpu_custom_call" | custom-call | flops 52428800 | bytes 16384000 | tf_op jit(solution)/shard_map/pallas_call | solution.py:206
  140.4 1.7 %fusion.14 = f32[16,12,4,128]{3,0,1,2:T(8,128)S(1)} fusion(f32[16,4,12,512]{3,2,1,0:T(8,128)S(1)} %copy-done.1, f32[512]{0:T(512)S(1)} %get-tuple-element.177, f32[512]{0:T(512)S(1)} %get-tuple-element.178, f32[512]{0:T(512)S(1)} %copy-done.28, f32[512]{0:T(512)S(1)} %get-tuple-element.175, s32[512]{0:T(512)S(1)} %add_select_fusion, s32[128]{0:T(128)S(1)} %copy-done.30), kind=kOutput, calls=%fused_computation.12 | convolution fusion | flops 302579712 | bytes 1976832 | tf_op jit(solution)/shard_map/pbkj,nj->pkbn/dot_general | solution.py:77
  142.1 3.9 %fusion.8 = f32[16,12,5,128]{3,0,1,2:T(8,128)S(1)} fusion(f32[16,5,12,512]{3,2,1,0:T(8,128)} %shard_map.125, f32[512]{0:T(512)S(1)} %get-tuple-element.177, f32[512]{0:T(512)S(1)} %get-tuple-element.178, f32[512]{0:T(512)S(1)} %copy-done.28, f32[512]{0:T(512)S(1)} %get-tuple-element.175, s32[512]{0:T(512)S(1)} %add_select_fusion, s32[128]{0:T(128)S(1)} %copy-done.30), kind=kOutput, calls=%fused_computation.10 | convolution fusion | flops 378077184 | bytes 2468352 | tf_op jit(solution)/shard_map/pbkj,nj->pkbn/dot_general | solution.py:77
  145.9 0.2 pad_maximum_fusion
  146.1 1.4 fusion.96
  147.5 0.6 pad_add_fusion
  148.1 1.1 copy.738
  149.2 0.5 reshape.227
  149.7 0.2 slice_multiply_fusion
  149.9 4.3 %collective-permute-start.14 = (f32[16,2,512]{2,0,1:T(8,128)S(1)}, f32[16,2,512]{2,0,1:T(8,128)S(1)}, u32[]{:S(2)}, u32[]{:S(2)}) collective-permute-start(f32[16,2,512]{2,0,1:T(8,128)S(1)} %get-tuple-element.148), channel_id=1, source_target_pairs={{0,4},{4,8},{8,12},{12,16},{16,20},{20,24},{24,28},{1,5},{5,9},{9,... | collective-permute-start | bytes 196616 | tf_op jit(solution)/shard_map/ppermute | solution.py:31
  154.3 1.4 collective-permute-start.15
  155.7 3.3 %subtract_multiply_fusion = (f32[32,8192]{1,0:T(8,128)}, f32[32,8192]{1,0:T(8,128)}) fusion(f32[128,8192]{1,0:T(8,128)} %y_ref.7, s32[]{:T(128)S(6)} %select_n.195, s32[128,8192]{1,0:T(8,128)} %g_ref.7, f32[32,2560]{1,0:T(8,128)} %dynamic-slice_select_fusion, f32[32,2048]{1,0:T(8,128)} %dynamic-slice_select_fusion.1, ...), kind=kLoop, calls=%fused_computation.17 | loop fusion | flops 1572864 | bytes 5242884 | tf_op jit(solution)/shard_map/mul | solution.py:314
  159.0 2.8 %collective-permute-done.15 = f32[16,2,512]{2,0,1:T(8,128)S(1)} collective-permute-done((f32[16,2,512]{2,0,1:T(8,128)S(1)}, f32[16,2,512]{2,0,1:T(8,128)S(1)}, u32[]{:S(2)}, u32[]{:S(2)}) %collective-permute-start.15) | collective-permute-done | bytes 65568 | tf_op jit(solution)/shard_map/ppermute | solution.py:31
  161.8 0.8 divide_subtract_fusion
  162.6 0.9 copy.747
  163.5 0.9 copy.748
  164.4 0.9 copy.749
  165.2 0.9 copy.746
  (105 shorter events, 2.1 us)
Async XLA Ops:
  1.8 10.0 %collective-permute-start.1 = (f32[16,2,512]{2,0,1:T(8,128)S(1)}, f32[16,2,512]{2,0,1:T(8,128)S(1)}, u32[]{:S(2)}, u32[]{:S(2)}) collective-permute-start(f32[16,2,512]{2,0,1:T(8,128)S(1)} %get-tuple-element.169), channel_id=1, source_target_pairs={{4,0},{8,4},{12,8},{16,12},{20,16},{24,20},{28,24},{5,1},{9,5},{13... | collective-permute-start | bytes 196616 | tf_op jit(solution)/shard_map/ppermute | solution.py:23
  3.1 7.5 %collective-permute-start = (f32[16,2,512]{2,0,1:T(8,128)S(1)}, f32[16,2,512]{2,0,1:T(8,128)S(1)}, u32[]{:S(2)}, u32[]{:S(2)}) collective-permute-start(f32[16,2,512]{2,0,1:T(8,128)S(1)} %get-tuple-element.170), channel_id=1, source_target_pairs={{0,4},{4,8},{8,12},{12,16},{16,20},{20,24},{24,28},{1,5},{5,9},{9,... | collective-permute-start | bytes 196616 | tf_op jit(solution)/shard_map/ppermute | solution.py:22
  8.6 9.5 %copy-start.27 = (f32[512]{0:T(512)}, f32[512]{0:T(512)S(1)}, u32[]{:S(2)}) copy-start(f32[512]{0:T(512)S(1)} %get-tuple-element.176) | copy-start | bytes 6148
  8.7 9.4 %copy-start.29 = (s32[128]{0:T(128)}, s32[128]{0:T(128)S(1)}, u32[]{:S(2)}) copy-start(s32[128]{0:T(128)S(1)} %iota_add_fusion) | copy-start | bytes 1540
  11.7 0.7 copy-start.22
  12.4 0.7 copy-start.15
  32.7 8.6 %collective-permute-start.2 = (f32[64,1536]{1,0:T(8,128)S(1)}, f32[64,1536]{1,0:T(8,128)S(1)}, u32[]{:S(2)}, u32[]{:S(2)}) collective-permute-start(f32[64,1536]{1,0:T(8,128)S(1)} %dynamic-slice_bitcast_fusion.3), channel_id=1, source_target_pairs={{0,1},{1,0},{2,3},{3,2},{4,5},{5,4},{6,7},{7,6},{8,9},{9,8},{10,11... | collective-permute-start | bytes 1179656 | tf_op jit(solution)/shard_map/ppermute | solution.py:285
  32.8 10.9 %copy-start.11 = (f32[128,1536]{1,0:T(8,128)S(1)}, f32[128,1536]{1,0:T(8,128)}, u32[]{:S(2)}) copy-start(f32[128,1536]{1,0:T(8,128)} %shard_map.118) | copy-start | bytes 2359300
  43.2 11.9 %collective-permute-start.4 = (f32[64,2048]{1,0:T(8,128)}, f32[64,2048]{1,0:T(8,128)S(1)}, u32[]{:S(2)}, u32[]{:S(2)}) collective-permute-start(f32[64,2048]{1,0:T(8,128)} %dynamic-slice_bitcast_fusion.2), channel_id=1, source_target_pairs={{0,1},{1,0},{2,3},{3,2},{4,5},{5,4},{6,7},{7,6},{8,9},{9,8},{10,11... | collective-permute-start | bytes 1572872 | tf_op jit(solution)/shard_map/ppermute | solution.py:285
  43.7 10.4 %copy-start.17 = (f32[64,1536]{1,0:T(8,128)}, f32[64,1536]{1,0:T(8,128)S(1)}, u32[]{:S(2)}) copy-start(f32[64,1536]{1,0:T(8,128)S(1)} %bitcast_add_fusion.3) | copy-start | bytes 1179652
  43.7 11.4 %copy-start.5 = (f32[128,2048]{1,0:T(8,128)S(1)}, f32[128,2048]{1,0:T(8,128)}, u32[]{:S(2)}) copy-start(f32[128,2048]{1,0:T(8,128)} %shard_map.119) | copy-start | bytes 3145732
  43.7 11.4 %collective-permute-start.3 = (f32[64,1536]{1,0:T(8,128)S(1)}, f32[64,1536]{1,0:T(8,128)}, u32[]{:S(2)}, u32[]{:S(2)}) collective-permute-start(f32[64,1536]{1,0:T(8,128)S(1)} %bitcast_add_fusion.3), channel_id=1, source_target_pairs={{0,2},{1,3},{2,0},{3,1},{4,6},{5,7},{6,4},{7,5},{8,10},{9,11},{10,... | collective-permute-start | bytes 1179656 | tf_op jit(solution)/shard_map/ppermute | solution.py:285
  54.1 1.2 copy-start.4
  55.1 2.7 %copy-start.18 = (f32[64,1536]{1,0:T(8,128)S(1)}, f32[64,1536]{1,0:T(8,128)}, u32[]{:S(2)}) copy-start(f32[64,1536]{1,0:T(8,128)} %copy-done.17) | copy-start | bytes 1179652
  56.2 13.2 %collective-permute-start.7 = (f32[64,2048]{1,0:T(8,128)}, f32[64,2048]{1,0:T(8,128)}, u32[]{:S(2)}, u32[]{:S(2)}) collective-permute-start(f32[64,2048]{1,0:T(8,128)} %dynamic-slice_bitcast_fusion.1), channel_id=1, source_target_pairs={{0,1},{1,0},{2,3},{3,2},{4,5},{5,4},{6,7},{7,6},{8,9},{9,8},{10,11... | collective-permute-start | bytes 1572872 | tf_op jit(solution)/shard_map/ppermute | solution.py:285
  56.2 14.3 %collective-permute-start.6 = (f32[64,2048]{1,0:T(8,128)S(1)}, f32[64,2048]{1,0:T(8,128)S(1)}, u32[]{:S(2)}, u32[]{:S(2)}) collective-permute-start(f32[64,2048]{1,0:T(8,128)S(1)} %bitcast_add_fusion.2), channel_id=1, source_target_pairs={{0,2},{1,3},{2,0},{3,1},{4,6},{5,7},{6,4},{7,5},{8,10},{9,11},{10,... | collective-permute-start | bytes 1572872 | tf_op jit(solution)/shard_map/ppermute | solution.py:285
  58.9 10.5 %copy-start.12 = (f32[64,1536]{1,0:T(8,128)}, f32[64,1536]{1,0:T(8,128)S(1)}, u32[]{:S(2)}) copy-start(f32[64,1536]{1,0:T(8,128)S(1)} %add.372.t_ref) | copy-start | bytes 1179652
  58.9 10.5 %collective-permute-start.5 = (f32[64,1536]{1,0:T(8,128)S(1)}, f32[64,1536]{1,0:T(8,128)S(1)}, u32[]{:S(2)}, u32[]{:S(2)}) collective-permute-start(f32[64,1536]{1,0:T(8,128)S(1)} %add.372.t_ref), channel_id=1, source_target_pairs={{0,1},{1,0},{2,3},{3,2},{4,5},{5,4},{6,7},{7,6},{8,9},{9,8},{10,11... | collective-permute-start | bytes 1179656 | tf_op jit(solution)/shard_map/ppermute | solution.py:285
  69.3 5.1 %copy-start.24 = (f32[64,1536]{1,0:T(8,128)}, f32[64,1536]{1,0:T(8,128)S(1)}, u32[]{:S(2)}) copy-start(f32[64,1536]{1,0:T(8,128)S(1)} %collective-permute-done.5.u_ref) | copy-start | bytes 1179652
  72.5 16.8 %collective-permute-start.10 = (f32[64,2560]{1,0:T(8,128)}, f32[64,2560]{1,0:T(8,128)}, u32[]{:S(2)}, u32[]{:S(2)}) collective-permute-start(f32[64,2560]{1,0:T(8,128)} %dynamic-slice_bitcast_fusion), channel_id=1, source_target_pairs={{0,1},{1,0},{2,3},{3,2},{4,5},{5,4},{6,7},{7,6},{8,9},{9,8},{10,11... | collective-permute-start | bytes 1966088 | tf_op jit(solution)/shard_map/ppermute | solution.py:285
  74.5 10.8 %copy-start.7 = (f32[64,2048]{1,0:T(8,128)}, f32[64,2048]{1,0:T(8,128)S(1)}, u32[]{:S(2)}) copy-start(f32[64,2048]{1,0:T(8,128)S(1)} %add.375.t_ref) | copy-start | bytes 1572868
  74.5 10.8 %collective-permute-start.8 = (f32[64,2048]{1,0:T(8,128)S(1)}, f32[64,2048]{1,0:T(8,128)S(1)}, u32[]{:S(2)}, u32[]{:S(2)}) collective-permute-start(f32[64,2048]{1,0:T(8,128)S(1)} %add.375.t_ref), channel_id=1, source_target_pairs={{0,1},{1,0},{2,3},{3,2},{4,5},{5,4},{6,7},{7,6},{8,9},{9,8},{10,11... | collective-permute-start | bytes 1572872 | tf_op jit(solution)/shard_map/ppermute | solution.py:285
  75.1 14.2 %collective-permute-start.9 = (f32[64,2048]{1,0:T(8,128)}, f32[64,2048]{1,0:T(8,128)}, u32[]{:S(2)}, u32[]{:S(2)}) collective-permute-start(f32[64,2048]{1,0:T(8,128)} %bitcast_add_fusion.1), channel_id=1, source_target_pairs={{0,2},{1,3},{2,0},{3,1},{4,6},{5,7},{6,4},{7,5},{8,10},{9,11},{10,... | collective-permute-start | bytes 1572872 | tf_op jit(solution)/shard_map/ppermute | solution.py:285
  76.7 12.6 %copy-start.2 = (f32[128,2560]{1,0:T(8,128)S(1)}, f32[128,2560]{1,0:T(8,128)}, u32[]{:S(2)}) copy-start(f32[128,2560]{1,0:T(8,128)} %shard_map.121) | copy-start | bytes 3932164
  85.3 8.2 %copy-start.13 = (f32[64,1536]{1,0:T(8,128)S(1)}, f32[64,1536]{1,0:T(8,128)}, u32[]{:S(2)}) copy-start(f32[64,1536]{1,0:T(8,128)} %copy-done.12) | copy-start | bytes 1179652
  85.3 3.9 %copy-start.19 = (f32[64,2048]{1,0:T(8,128)}, f32[64,2048]{1,0:T(8,128)S(1)}, u32[]{:S(2)}) copy-start(f32[64,2048]{1,0:T(8,128)S(1)} %collective-permute-done.8.u_ref) | copy-start | bytes 1572868
  90.5 18.3 %collective-permute-start.12 = (f32[64,2560]{1,0:T(8,128)S(1)}, f32[64,2560]{1,0:T(8,128)}, u32[]{:S(2)}, u32[]{:S(2)}) collective-permute-start(f32[64,2560]{1,0:T(8,128)S(1)} %bitcast_add_fusion), channel_id=1, source_target_pairs={{0,2},{1,3},{2,0},{3,1},{4,6},{5,7},{6,4},{7,5},{8,10},{9,11},{10,... | collective-permute-start | bytes 1966088 | tf_op jit(solution)/shard_map/ppermute | solution.py:285
  93.4 12.5 %copy-start.9 = (f32[64,2048]{1,0:T(8,128)}, f32[64,2048]{1,0:T(8,128)S(1)}, u32[]{:S(2)}) copy-start(f32[64,2048]{1,0:T(8,128)S(1)} %add.377.t_ref) | copy-start | bytes 1572868
  93.4 15.3 %collective-permute-start.11 = (f32[64,2048]{1,0:T(8,128)S(1)}, f32[64,2048]{1,0:T(8,128)}, u32[]{:S(2)}, u32[]{:S(2)}) collective-permute-start(f32[64,2048]{1,0:T(8,128)S(1)} %add.377.t_ref), channel_id=1, source_target_pairs={{0,1},{1,0},{2,3},{3,2},{4,5},{5,4},{6,7},{7,6},{8,9},{9,8},{10,11... | collective-permute-start | bytes 1572872 | tf_op jit(solution)/shard_map/ppermute | solution.py:285
  95.2 10.6 %copy-start.3 = (f32[16,3,12,512]{3,2,1,0:T(8,128)S(1)}, f32[16,3,12,512]{3,2,1,0:T(8,128)}, u32[]{:S(2)}) copy-start(f32[16,3,12,512]{3,2,1,0:T(8,128)} %shard_map.122) | copy-start | bytes 3538948
  105.9 4.5 %copy-start.8 = (f32[64,2048]{1,0:T(8,128)S(1)}, f32[64,2048]{1,0:T(8,128)}, u32[]{:S(2)}) copy-start(f32[64,2048]{1,0:T(8,128)} %copy-done.7) | copy-start | bytes 1572868
  105.9 4.5 %copy-start.20 = (f32[64,2048]{1,0:T(8,128)S(1)}, f32[64,2048]{1,0:T(8,128)}, u32[]{:S(2)}) copy-start(f32[64,2048]{1,0:T(8,128)} %copy-done.19) | copy-start | bytes 1572868
  109.9 16.0 %copy-start.6 = (f32[64,2560]{1,0:T(8,128)}, f32[64,2560]{1,0:T(8,128)S(1)}, u32[]{:S(2)}) copy-start(f32[64,2560]{1,0:T(8,128)S(1)} %add.379.t_ref) | copy-start | bytes 1966084
  109.9 16.0 %collective-permute-start.13 = (f32[64,2560]{1,0:T(8,128)S(1)}, f32[64,2560]{1,0:T(8,128)}, u32[]{:S(2)}, u32[]{:S(2)}) collective-permute-start(f32[64,2560]{1,0:T(8,128)S(1)} %add.379.t_ref), channel_id=1, source_target_pairs={{0,1},{1,0},{2,3},{3,2},{4,5},{5,4},{6,7},{7,6},{8,9},{9,8},{10,11... | collective-permute-start | bytes 1966088 | tf_op jit(solution)/shard_map/ppermute | solution.py:285
  111.1 10.8 %copy-start.10 = (f32[64,2048]{1,0:T(8,128)S(1)}, f32[64,2048]{1,0:T(8,128)}, u32[]{:S(2)}) copy-start(f32[64,2048]{1,0:T(8,128)} %copy-done.9) | copy-start | bytes 1572868
  111.1 12.4 %copy-start = (f32[16,4,12,512]{3,2,1,0:T(8,128)S(1)}, f32[16,4,12,512]{3,2,1,0:T(8,128)}, u32[]{:S(2)}) copy-start(f32[16,4,12,512]{3,2,1,0:T(8,128)} %shard_map.123) | copy-start | bytes 4718596
  127.7 12.7 %copy-start.1 = (f32[16,4,12,512]{3,2,1,0:T(8,128)S(1)}, f32[16,4,12,512]{3,2,1,0:T(8,128)}, u32[]{:S(2)}) copy-start(f32[16,4,12,512]{3,2,1,0:T(8,128)} %shard_map.124) | copy-start | bytes 4718596
  127.7 12.7 %copy-start.28 = (f32[512]{0:T(512)S(1)}, f32[512]{0:T(512)}, u32[]{:S(2)}) copy-start(f32[512]{0:T(512)} %copy-done.27) | copy-start | bytes 6148
  127.7 12.7 %copy-start.30 = (s32[128]{0:T(128)S(1)}, s32[128]{0:T(128)}, u32[]{:S(2)}) copy-start(s32[128]{0:T(128)} %copy-done.29) | copy-start | bytes 1540
  142.1 3.9 %copy-start.21 = (f32[16,12,3,128]{3,0,1,2:T(8,128)S(1)}, f32[16,12,3,128]{3,0,1,2:T(8,128)}, u32[]{:S(2)}) copy-start(f32[16,12,3,128]{3,0,1,2:T(8,128)} %fusion.19) | copy-start | bytes 884740
  149.9 9.1 %collective-permute-start.14 = (f32[16,2,512]{2,0,1:T(8,128)S(1)}, f32[16,2,512]{2,0,1:T(8,128)S(1)}, u32[]{:S(2)}, u32[]{:S(2)}) collective-permute-start(f32[16,2,512]{2,0,1:T(8,128)S(1)} %get-tuple-element.148), channel_id=1, source_target_pairs={{0,4},{4,8},{8,12},{12,16},{16,20},{20,24},{24,28},{1,5},{5,9},{9,... | collective-permute-start | bytes 196616 | tf_op jit(solution)/shard_map/ppermute | solution.py:31
  154.2 7.6 %copy-start.14 = (f32[16,8,512]{2,1,0:T(8,128)S(1)}, f32[16,8,512]{2,1,0:T(8,128)}, u32[]{:S(2)}) copy-start(f32[16,8,512]{2,1,0:T(8,128)} %param.10) | copy-start | bytes 786436
  154.2 7.6 %copy-start.16 = (f32[16,10,512]{2,0,1:T(8,128)S(1)}, f32[16,10,512]{2,0,1:T(8,128)}, u32[]{:S(2)}) copy-start(f32[16,10,512]{2,0,1:T(8,128)} %copy-done.15) | copy-start | bytes 983044
  154.2 7.6 %copy-start.23 = (f32[16,10,512]{2,0,1:T(8,128)S(1)}, f32[16,10,512]{2,0,1:T(8,128)}, u32[]{:S(2)}) copy-start(f32[16,10,512]{2,0,1:T(8,128)} %copy-done.22) | copy-start | bytes 983044
  154.2 7.6 %copy-start.25 = (f32[16,8,512]{2,1,0:T(8,128)S(1)}, f32[16,8,512]{2,1,0:T(8,128)}, u32[]{:S(2)}) copy-start(f32[16,8,512]{2,1,0:T(8,128)} %param.11) | copy-start | bytes 786436
  154.2 7.6 %copy-start.26 = (f32[16,8,512]{2,1,0:T(8,128)S(1)}, f32[16,8,512]{2,1,0:T(8,128)}, u32[]{:S(2)}) copy-start(f32[16,8,512]{2,1,0:T(8,128)} %param.12) | copy-start | bytes 786436
  154.2 7.6 %copy-start.31 = (f32[16]{0:T(128)S(1)}, f32[16]{0:T(128)}, u32[]{:S(2)}) copy-start(f32[16]{0:T(128)} %param.13) | copy-start | bytes 196
  154.3 7.5 %collective-permute-start.15 = (f32[16,2,512]{2,0,1:T(8,128)S(1)}, f32[16,2,512]{2,0,1:T(8,128)S(1)}, u32[]{:S(2)}, u32[]{:S(2)}) collective-permute-start(f32[16,2,512]{2,0,1:T(8,128)S(1)} %get-tuple-element.149), channel_id=1, source_target_pairs={{4,0},{8,4},{12,8},{16,12},{20,16},{24,20},{28,24},{5,1},{9,5},{13... | collective-permute-start | bytes 196616 | tf_op jit(solution)/shard_map/ppermute | solution.py:31
